TPU v7x, 256 devices: a whole 4x4x8 slice. The times are simulated.
256 devices in a mesh: node: 8 (over y, x_lo), gx: 32 (over z, x_hi, core).
Axes of the slice: x: 4 (x_hi: 2, x_lo: 2; x = x_hi * 2 + x_lo), y: 4, z: 8, core: 2. Of those that a mesh axis runs over, the one named last changes fastest.
Arguments:
- start_state: float32 [32, 8, 16, 512], P('gx'), may hold values from -6 to 6
- node_states: float32 [8, 32, 8, 16, 512], P('node', 'gx'), may hold values from -6 to 6
- reaction_rates: float32 [32, 8, 16, 512], P('gx'), may hold values from 0.1 to 1
- volume: bfloat16 [512, 512], replicated, may hold values from -0.25 to 0.25
- face_lift: bfloat16 [384, 512], replicated, may hold values from -0.3125 to 0.3125
Outputs:
- new_states: float32 [8, 32, 8, 16, 512], P('node', 'gx')
All inputs are finite; a program needn't handle non-finite values.
Results may differ from a plain program's by a relative error of at most 0.008.
Values may be sent and summed in bfloat16 or wider, within the bound.
No kernel may reach another device: no remote copies, remote signals or barrier semaphores. Data moves between devices by JAX's collectives and lax.ppermute only.
A program may use at most 64 MiB of HBM per device.

v0:
```python
import math

import jax
import jax.numpy as jnp
import numpy as np
from jax import lax
from jax.sharding import PartitionSpec as P

M = 8
NP = 8
SWEEPS = 2
INNER = 7
FACE = NP * NP


time_step = 0.45


def passed_along(array, axis, by):
    devices = lax.axis_size(axis)
    return lax.ppermute(array, axis, [(i, (i + by) % devices) for i in range(devices)])


def quadrature_table(node_count):
    roots_list = []
    for index in range(node_count):
        estimate = math.cos(math.pi * (index + 0.75) / (node_count + 0.5))
        for newton_step in range(60):
            previous, current = (1.0, estimate)
            for degree in range(2, node_count + 1):
                previous, current = (
                    current,
                    ((2 * degree - 1) * estimate * current - (degree - 1) * previous) / degree,
                )
            slope_value = node_count * (estimate * current - previous) / (estimate * estimate - 1.0)
            estimate = estimate - current / slope_value
        roots_list.append(0.5 * (estimate + 1.0))
    times_list = sorted(roots_list)
    weights_table = np.zeros((node_count, node_count))
    for column in range(node_count):
        coeffs = [1.0]
        scaling = 1.0
        for other in range(node_count):
            if other != column:
                point = times_list[other]
                widened = [0.0] * (len(coeffs) + 1)
                for power, entry in enumerate(coeffs):
                    widened[power + 1] += entry
                    widened[power] -= point * entry
                coeffs = widened
                scaling = scaling * (times_list[column] - point)
        for row in range(node_count):
            upper = times_list[row]
            total = 0.0
            for power, entry in enumerate(coeffs):
                total += entry / scaling * upper ** (power + 1) / (power + 1)
            weights_table[row, column] = total
    return (np.array(times_list), weights_table)


def face_selector(axis, value):
    a, b, c = np.meshgrid(np.arange(NP), np.arange(NP), np.arange(NP), indexing="ij")
    point = ((a * NP + b) * NP + c).reshape(-1)
    keep = [a, b, c][axis].reshape(-1) == value
    select = np.zeros((NP**3, FACE), np.float32)
    select[point[keep], np.arange(FACE)] = 1.0
    return select


def spread_weights(volume, face_lift):
    blocks = [volume]
    for index, (axis, value) in enumerate([(1, NP - 1), (1, 0), (2, NP - 1), (2, 0)]):
        rows = face_lift[(2 + index) * FACE : (3 + index) * FACE]
        select = jnp.asarray(face_selector(axis, value), jnp.bfloat16)
        blocks.append(jnp.dot(select, rows, preferred_element_type=jnp.float32).astype(jnp.bfloat16))
    return jnp.concatenate(blocks, axis=0)


def shifted_inputs(rounded, ny, nz):
    cube = rounded.reshape((ny, nz, -1))
    parts = [
        cube,
        jnp.roll(cube, 1, axis=0),
        jnp.roll(cube, -1, axis=0),
        jnp.roll(cube, 1, axis=1),
        jnp.roll(cube, -1, axis=1),
    ]
    return jnp.concatenate(parts, axis=-1).reshape((ny * nz, -1))


def local_terms(field, reaction, weights, ny, nz):
    rounded = field.astype(jnp.bfloat16)
    stacked = shifted_inputs(rounded, ny, nz)
    own = jnp.dot(stacked, weights, preferred_element_type=jnp.float32) - reaction * field
    return own, rounded


def swapped(array, axis, partner):
    devices = lax.axis_size(axis)
    return lax.ppermute(array, axis, [(i, partner(i) % devices) for i in range(devices)])


def exchange_faces(rounded):
    high = rounded[:, (NP - 1) * FACE :]
    low = rounded[:, :FACE]
    odd = lax.axis_index("gx") % 2 == 1
    first = swapped(jnp.where(odd, low, high), "gx", lambda i: i ^ 1)
    second = swapped(jnp.where(odd, high, low), "gx", lambda i: i + 1 if i % 2 else i - 1)
    below = jnp.where(odd, first, second)
    above = jnp.where(odd, second, first)
    return jnp.concatenate([below, above], axis=-1)


def apply_operator(field, reaction, weights, x_lift, ny, nz):
    own, rounded = local_terms(field, reaction, weights, ny, nz)
    faces = exchange_faces(rounded)
    return own + jnp.dot(faces, x_lift, preferred_element_type=jnp.float32)


def gather_nodes(rows):
    nodes = lax.axis_size("node")
    me = lax.axis_index("node")
    swaps = [rows] + [swapped(rows, "node", lambda i, k=k: i ^ k) for k in range(1, nodes)]
    return swaps, me ^ jnp.arange(nodes)


def local(start_state, node_states, reaction_rates, volume, face_lift):
    node_times, weights_table = quadrature_table(M)
    shape = node_states.shape
    ny, nz, points = shape[-3], shape[-2], shape[-1]
    rows = ny * nz
    local_count = shape[0]
    first_node = lax.axis_index("node") * local_count
    all_weights = jnp.asarray(weights_table, jnp.float32)
    own_weights = lax.dynamic_slice_in_dim(all_weights, first_node, local_count, 0)
    all_scales = jnp.asarray(time_step * node_times, jnp.float32)
    own_scale = lax.dynamic_slice_in_dim(all_scales, first_node, local_count, 0)[0]

    weights = spread_weights(volume, face_lift)
    x_lift = face_lift[: 2 * FACE]
    start = start_state.reshape((rows, points))
    reaction = reaction_rates.reshape((rows, points))
    states = node_states.reshape((rows, points))
    for sweep_index in range(SWEEPS):
        slopes = apply_operator(states, reaction, weights, x_lift, ny, nz)
        slope_rows = slopes.astype(jnp.bfloat16)
        received, sources = gather_nodes(slope_rows)
        source_weights = jnp.take(own_weights[0], sources)
        stacked = jnp.stack(received).astype(jnp.float32)
        running_sum = jnp.sum(source_weights[:, None, None] * stacked, axis=0)
        fixed_part = start + time_step * running_sum - own_scale * slopes
        iterate = start + time_step * running_sum
        for inner_step in range(INNER - 1):
            iterate = fixed_part + own_scale * apply_operator(iterate, reaction, weights, x_lift, ny, nz)
        states = iterate
    return states.reshape(shape)


def solution(mesh):
    in_specs = (
        P("gx", None, None, None),
        P("node", "gx", None, None, None),
        P("gx", None, None, None),
        P(),
        P(),
    )
    out_specs = P("node", "gx", None, None, None)
    return jax.shard_map(local, mesh=mesh, in_specs=in_specs, out_specs=out_specs, check_vma=False)
```

profile of v0, /device:TPU:1, one launch (start us, length us, event | category | flops | bytes accessed | tf_op | source)
XLA Modules:
  0.0 175.7 jit_solution(11484676286444129114)
XLA Ops:
  1.8 3.2 %collective-permute-start = (bf16[128,64]{1,0:T(8,128)(2,1)}, bf16[128,64]{1,0:T(8,128)(2,1)}, u32[]{:S(2)}, u32[]{:S(2)}) collective-permute-start(bf16[128,64]{1,0:T(8,128)(2,1)} %get-tuple-element.172), channel_id=1, source_target_pairs={{0,1},{1,0},{2,3},{3,2},{4,5},{5,4},{6,7},{7,6},{8,9},{9,8},{10,11... | collective-permute-start | bytes 49160 | tf_op jit(solution)/shard_map/ppermute | solution.py:100
  19.8 2.3 %convolution_subtract_fusion.2 = f32[128,512]{1,0:T(8,128)} fusion(f32[128,512]{1,0:T(8,128)S(1)} %copy-done.4, bf16[128,2560]{1,0:T(8,128)(2,1)} %constant_dynamic-update-slice_fusion, bf16[2560,512]{1,0:T(8,128)(2,1)S(1)} %fusion), kind=kOutput, calls=%fused_computation.51 | convolution fusion | flops 335609856 | bytes 3801088 | tf_op jit(solution)/shard_map/dot_general | solution.py:94
  29.0 2.9 %collective-permute-start.5 = (bf16[128,512]{1,0:T(8,128)(2,1)S(1)}, bf16[128,512]{1,0:T(8,128)(2,1)S(1)}, u32[]{:S(2)}, u32[]{:S(2)}) collective-permute-start(bf16[128,512]{1,0:T(8,128)(2,1)S(1)} %get-tuple-element.31), channel_id=1, source_target_pairs={{0,128},{32,160},{64,192},{96,224},{128,0},{160,32},{192,64},{224,... | collective-permute-start | bytes 393224 | tf_op jit(solution)/shard_map/ppermute | solution.py:100
  32.0 2.7 %collective-permute-start.7 = (bf16[128,512]{1,0:T(8,128)(2,1)S(1)}, bf16[128,512]{1,0:T(8,128)(2,1)S(1)}, u32[]{:S(2)}, u32[]{:S(2)}) collective-permute-start(bf16[128,512]{1,0:T(8,128)(2,1)S(1)} %get-tuple-element.31), channel_id=1, source_target_pairs={{0,192},{32,224},{64,128},{96,160},{128,64},{160,96},{192,0},{224,... | collective-permute-start | bytes 393224 | tf_op jit(solution)/shard_map/ppermute | solution.py:100
  35.8 2.9 %collective-permute-done.6 = bf16[128,512]{1,0:T(8,128)(2,1)S(1)} collective-permute-done((bf16[128,512]{1,0:T(8,128)(2,1)S(1)}, bf16[128,512]{1,0:T(8,128)(2,1)S(1)}, u32[]{:S(2)}, u32[]{:S(2)}) %collective-permute-start.6) | collective-permute-done | bytes 131104 | tf_op jit(solution)/shard_map/ppermute | solution.py:100
  38.7 3.6 %collective-permute-done.8 = bf16[128,512]{1,0:T(8,128)(2,1)S(1)} collective-permute-done((bf16[128,512]{1,0:T(8,128)(2,1)S(1)}, bf16[128,512]{1,0:T(8,128)(2,1)S(1)}, u32[]{:S(2)}, u32[]{:S(2)}) %collective-permute-start.8) | collective-permute-done | bytes 131104 | tf_op jit(solution)/shard_map/ppermute | solution.py:100
  43.6 8.4 %collective-permute-start.10 = (bf16[128,64]{1,0:T(8,128)(2,1)S(1)}, bf16[128,64]{1,0:T(8,128)(2,1)S(1)}, u32[]{:S(2)}, u32[]{:S(2)}) collective-permute-start(bf16[128,64]{1,0:T(8,128)(2,1)S(1)} %get-tuple-element.163), channel_id=1, source_target_pairs={{0,31},{1,2},{2,1},{3,4},{4,3},{5,6},{6,5},{7,8},{8,7},{9,10},{10,... | collective-permute-start | bytes 49160 | tf_op jit(solution)/shard_map/ppermute | solution.py:100
  54.7 4.2 %collective-permute-start.11 = (bf16[128,64]{1,0:T(8,128)(2,1)S(1)}, bf16[128,64]{1,0:T(8,128)(2,1)S(1)}, u32[]{:S(2)}, u32[]{:S(2)}) collective-permute-start(bf16[128,64]{1,0:T(8,128)(2,1)S(1)} %get-tuple-element.152), channel_id=1, source_target_pairs={{0,1},{1,0},{2,3},{3,2},{4,5},{5,4},{6,7},{7,6},{8,9},{9,8},{10,11... | collective-permute-start | bytes 49160 | tf_op jit(solution)/shard_map/ppermute | solution.py:100
  59.8 4.0 %collective-permute-done.12 = bf16[128,64]{1,0:T(8,128)(2,1)S(1)} collective-permute-done((bf16[128,64]{1,0:T(8,128)(2,1)S(1)}, bf16[128,64]{1,0:T(8,128)(2,1)S(1)}, u32[]{:S(2)}, u32[]{:S(2)}) %collective-permute-start.12) | collective-permute-done | bytes 16416 | tf_op jit(solution)/shard_map/ppermute | solution.py:100
  64.9 2.3 %collective-permute-start.13 = (bf16[128,64]{1,0:T(8,128)(2,1)S(1)}, bf16[128,64]{1,0:T(8,128)(2,1)S(1)}, u32[]{:S(2)}, u32[]{:S(2)}) collective-permute-start(bf16[128,64]{1,0:T(8,128)(2,1)S(1)} %get-tuple-element.142), channel_id=1, source_target_pairs={{0,1},{1,0},{2,3},{3,2},{4,5},{5,4},{6,7},{7,6},{8,9},{9,8},{10,11... | collective-permute-start | bytes 49160 | tf_op jit(solution)/shard_map/ppermute | solution.py:100
  68.0 4.0 %collective-permute-done.14 = bf16[128,64]{1,0:T(8,128)(2,1)S(1)} collective-permute-done((bf16[128,64]{1,0:T(8,128)(2,1)S(1)}, bf16[128,64]{1,0:T(8,128)(2,1)S(1)}, u32[]{:S(2)}, u32[]{:S(2)}) %collective-permute-start.14) | collective-permute-done | bytes 16416 | tf_op jit(solution)/shard_map/ppermute | solution.py:100
  73.1 2.5 %collective-permute-start.15 = (bf16[128,64]{1,0:T(8,128)(2,1)S(1)}, bf16[128,64]{1,0:T(8,128)(2,1)S(1)}, u32[]{:S(2)}, u32[]{:S(2)}) collective-permute-start(bf16[128,64]{1,0:T(8,128)(2,1)S(1)} %get-tuple-element.132), channel_id=1, source_target_pairs={{0,1},{1,0},{2,3},{3,2},{4,5},{5,4},{6,7},{7,6},{8,9},{9,8},{10,11... | collective-permute-start | bytes 49160 | tf_op jit(solution)/shard_map/ppermute | solution.py:100
  76.4 4.0 %collective-permute-done.16 = bf16[128,64]{1,0:T(8,128)(2,1)S(1)} collective-permute-done((bf16[128,64]{1,0:T(8,128)(2,1)S(1)}, bf16[128,64]{1,0:T(8,128)(2,1)S(1)}, u32[]{:S(2)}, u32[]{:S(2)}) %collective-permute-start.16) | collective-permute-done | bytes 16416 | tf_op jit(solution)/shard_map/ppermute | solution.py:100
  81.5 2.3 %collective-permute-start.17 = (bf16[128,64]{1,0:T(8,128)(2,1)S(1)}, bf16[128,64]{1,0:T(8,128)(2,1)S(1)}, u32[]{:S(2)}, u32[]{:S(2)}) collective-permute-start(bf16[128,64]{1,0:T(8,128)(2,1)S(1)} %get-tuple-element.122), channel_id=1, source_target_pairs={{0,1},{1,0},{2,3},{3,2},{4,5},{5,4},{6,7},{7,6},{8,9},{9,8},{10,11... | collective-permute-start | bytes 49160 | tf_op jit(solution)/shard_map/ppermute | solution.py:100
  84.7 4.0 %collective-permute-done.18 = bf16[128,64]{1,0:T(8,128)(2,1)S(1)} collective-permute-done((bf16[128,64]{1,0:T(8,128)(2,1)S(1)}, bf16[128,64]{1,0:T(8,128)(2,1)S(1)}, u32[]{:S(2)}, u32[]{:S(2)}) %collective-permute-start.18) | collective-permute-done | bytes 16416 | tf_op jit(solution)/shard_map/ppermute | solution.py:100
  92.9 4.0 %collective-permute-done.20 = bf16[128,64]{1,0:T(8,128)(2,1)S(1)} collective-permute-done((bf16[128,64]{1,0:T(8,128)(2,1)S(1)}, bf16[128,64]{1,0:T(8,128)(2,1)S(1)}, u32[]{:S(2)}, u32[]{:S(2)}) %collective-permute-start.20) | collective-permute-done | bytes 16416 | tf_op jit(solution)/shard_map/ppermute | solution.py:100
  98.0 2.3 %collective-permute-start.21 = (bf16[128,64]{1,0:T(8,128)(2,1)S(1)}, bf16[128,64]{1,0:T(8,128)(2,1)S(1)}, u32[]{:S(2)}, u32[]{:S(2)}) collective-permute-start(bf16[128,64]{1,0:T(8,128)(2,1)S(1)} %get-tuple-element.102), channel_id=1, source_target_pairs={{0,1},{1,0},{2,3},{3,2},{4,5},{5,4},{6,7},{7,6},{8,9},{9,8},{10,11... | collective-permute-start | bytes 49160 | tf_op jit(solution)/shard_map/ppermute | solution.py:100
  101.2 4.0 %collective-permute-done.22 = bf16[128,64]{1,0:T(8,128)(2,1)S(1)} collective-permute-done((bf16[128,64]{1,0:T(8,128)(2,1)S(1)}, bf16[128,64]{1,0:T(8,128)(2,1)S(1)}, u32[]{:S(2)}, u32[]{:S(2)}) %collective-permute-start.22) | collective-permute-done | bytes 16416 | tf_op jit(solution)/shard_map/ppermute | solution.py:100
  108.3 3.7 %collective-permute-start.27 = (bf16[128,512]{1,0:T(8,128)(2,1)S(1)}, bf16[128,512]{1,0:T(8,128)(2,1)S(1)}, u32[]{:S(2)}, u32[]{:S(2)}) collective-permute-start(bf16[128,512]{1,0:T(8,128)(2,1)S(1)} %get-tuple-element.17), channel_id=1, source_target_pairs={{0,160},{32,128},{64,224},{96,192},{128,32},{160,0},{192,96},{224,... | collective-permute-start | bytes 393224 | tf_op jit(solution)/shard_map/ppermute | solution.py:100
  112.2 2.9 %collective-permute-start.29 = (bf16[128,512]{1,0:T(8,128)(2,1)S(1)}, bf16[128,512]{1,0:T(8,128)(2,1)S(1)}, u32[]{:S(2)}, u32[]{:S(2)}) collective-permute-start(bf16[128,512]{1,0:T(8,128)(2,1)S(1)} %get-tuple-element.17), channel_id=1, source_target_pairs={{0,224},{32,192},{64,160},{96,128},{128,96},{160,64},{192,32},{224... | collective-permute-start | bytes 393224 | tf_op jit(solution)/shard_map/ppermute | solution.py:100
  115.1 5.0 %collective-permute-done.26 = bf16[128,512]{1,0:T(8,128)(2,1)S(1)} collective-permute-done((bf16[128,512]{1,0:T(8,128)(2,1)S(1)}, bf16[128,512]{1,0:T(8,128)(2,1)S(1)}, u32[]{:S(2)}, u32[]{:S(2)}) %collective-permute-start.26) | collective-permute-done | bytes 131104 | tf_op jit(solution)/shard_map/ppermute | solution.py:100
  120.1 3.5 %collective-permute-done.28 = bf16[128,512]{1,0:T(8,128)(2,1)S(1)} collective-permute-done((bf16[128,512]{1,0:T(8,128)(2,1)S(1)}, bf16[128,512]{1,0:T(8,128)(2,1)S(1)}, u32[]{:S(2)}, u32[]{:S(2)}) %collective-permute-start.28) | collective-permute-done | bytes 131104 | tf_op jit(solution)/shard_map/ppermute | solution.py:100
  124.9 3.2 %collective-permute-start.30 = (bf16[128,64]{1,0:T(8,128)(2,1)S(1)}, bf16[128,64]{1,0:T(8,128)(2,1)S(1)}, u32[]{:S(2)}, u32[]{:S(2)}) collective-permute-start(bf16[128,64]{1,0:T(8,128)(2,1)S(1)} %get-tuple-element.92), channel_id=1, source_target_pairs={{0,1},{1,0},{2,3},{3,2},{4,5},{5,4},{6,7},{7,6},{8,9},{9,8},{10,11... | collective-permute-start | bytes 49160 | tf_op jit(solution)/shard_map/ppermute | solution.py:100
  128.9 4.0 %collective-permute-done.31 = bf16[128,64]{1,0:T(8,128)(2,1)S(1)} collective-permute-done((bf16[128,64]{1,0:T(8,128)(2,1)S(1)}, bf16[128,64]{1,0:T(8,128)(2,1)S(1)}, u32[]{:S(2)}, u32[]{:S(2)}) %collective-permute-start.31) | collective-permute-done | bytes 16416 | tf_op jit(solution)/shard_map/ppermute | solution.py:100
  137.2 4.0 %collective-permute-done.33 = bf16[128,64]{1,0:T(8,128)(2,1)S(1)} collective-permute-done((bf16[128,64]{1,0:T(8,128)(2,1)S(1)}, bf16[128,64]{1,0:T(8,128)(2,1)S(1)}, u32[]{:S(2)}, u32[]{:S(2)}) %collective-permute-start.33) | collective-permute-done | bytes 16416 | tf_op jit(solution)/shard_map/ppermute | solution.py:100
  142.2 2.3 %collective-permute-start.34 = (bf16[128,64]{1,0:T(8,128)(2,1)S(1)}, bf16[128,64]{1,0:T(8,128)(2,1)S(1)}, u32[]{:S(2)}, u32[]{:S(2)}) collective-permute-start(bf16[128,64]{1,0:T(8,128)(2,1)S(1)} %get-tuple-element.72), channel_id=1, source_target_pairs={{0,1},{1,0},{2,3},{3,2},{4,5},{5,4},{6,7},{7,6},{8,9},{9,8},{10,11... | collective-permute-start | bytes 49160 | tf_op jit(solution)/shard_map/ppermute | solution.py:100
  145.4 4.0 %collective-permute-done.35 = bf16[128,64]{1,0:T(8,128)(2,1)S(1)} collective-permute-done((bf16[128,64]{1,0:T(8,128)(2,1)S(1)}, bf16[128,64]{1,0:T(8,128)(2,1)S(1)}, u32[]{:S(2)}, u32[]{:S(2)}) %collective-permute-start.35) | collective-permute-done | bytes 16416 | tf_op jit(solution)/shard_map/ppermute | solution.py:100
  150.5 2.3 %collective-permute-start.36 = (bf16[128,64]{1,0:T(8,128)(2,1)S(1)}, bf16[128,64]{1,0:T(8,128)(2,1)S(1)}, u32[]{:S(2)}, u32[]{:S(2)}) collective-permute-start(bf16[128,64]{1,0:T(8,128)(2,1)S(1)} %get-tuple-element.62), channel_id=1, source_target_pairs={{0,1},{1,0},{2,3},{3,2},{4,5},{5,4},{6,7},{7,6},{8,9},{9,8},{10,11... | collective-permute-start | bytes 49160 | tf_op jit(solution)/shard_map/ppermute | solution.py:100
  153.6 4.0 %collective-permute-done.37 = bf16[128,64]{1,0:T(8,128)(2,1)S(1)} collective-permute-done((bf16[128,64]{1,0:T(8,128)(2,1)S(1)}, bf16[128,64]{1,0:T(8,128)(2,1)S(1)}, u32[]{:S(2)}, u32[]{:S(2)}) %collective-permute-start.37) | collective-permute-done | bytes 16416 | tf_op jit(solution)/shard_map/ppermute | solution.py:100
  161.9 4.0 %collective-permute-done.39 = bf16[128,64]{1,0:T(8,128)(2,1)S(1)} collective-permute-done((bf16[128,64]{1,0:T(8,128)(2,1)S(1)}, bf16[128,64]{1,0:T(8,128)(2,1)S(1)}, u32[]{:S(2)}, u32[]{:S(2)}) %collective-permute-start.39) | collective-permute-done | bytes 16416 | tf_op jit(solution)/shard_map/ppermute | solution.py:100
  167.0 2.3 %collective-permute-start.40 = (bf16[128,64]{1,0:T(8,128)(2,1)S(1)}, bf16[128,64]{1,0:T(8,128)(2,1)S(1)}, u32[]{:S(2)}, u32[]{:S(2)}) collective-permute-start(bf16[128,64]{1,0:T(8,128)(2,1)S(1)} %get-tuple-element.42), channel_id=1, source_target_pairs={{0,1},{1,0},{2,3},{3,2},{4,5},{5,4},{6,7},{7,6},{8,9},{9,8},{10,11... | collective-permute-start | bytes 49160 | tf_op jit(solution)/shard_map/ppermute | solution.py:100
  170.1 4.0 %collective-permute-done.41 = bf16[128,64]{1,0:T(8,128)(2,1)S(1)} collective-permute-done((bf16[128,64]{1,0:T(8,128)(2,1)S(1)}, bf16[128,64]{1,0:T(8,128)(2,1)S(1)}, u32[]{:S(2)}, u32[]{:S(2)}) %collective-permute-start.41) | collective-permute-done | bytes 16416 | tf_op jit(solution)/shard_map/ppermute | solution.py:100
  (328 shorter events, 61.3 us)
Async XLA Ops:
  1.8 22.4 %collective-permute-start = (bf16[128,64]{1,0:T(8,128)(2,1)}, bf16[128,64]{1,0:T(8,128)(2,1)}, u32[]{:S(2)}, u32[]{:S(2)}) collective-permute-start(bf16[128,64]{1,0:T(8,128)(2,1)} %get-tuple-element.172), channel_id=1, source_target_pairs={{0,1},{1,0},{2,3},{3,2},{4,5},{5,4},{6,7},{7,6},{8,9},{9,8},{10,11... | collective-permute-start | bytes 49160 | tf_op jit(solution)/shard_map/ppermute | solution.py:100
  5.1 19.2 %collective-permute-start.1 = (bf16[128,64]{1,0:T(8,128)(2,1)}, bf16[128,64]{1,0:T(8,128)(2,1)}, u32[]{:S(2)}, u32[]{:S(2)}) collective-permute-start(bf16[128,64]{1,0:T(8,128)(2,1)} %get-tuple-element.173), channel_id=1, source_target_pairs={{0,31},{1,2},{2,1},{3,4},{4,3},{5,6},{6,5},{7,8},{8,7},{9,10},{10,... | collective-permute-start | bytes 49160 | tf_op jit(solution)/shard_map/ppermute | solution.py:100
  26.2 5.7 %collective-permute-start.2 = (bf16[128,512]{1,0:T(8,128)(2,1)S(1)}, bf16[128,512]{1,0:T(8,128)(2,1)S(1)}, u32[]{:S(2)}, u32[]{:S(2)}) collective-permute-start(bf16[128,512]{1,0:T(8,128)(2,1)S(1)} %get-tuple-element.31), channel_id=1, source_target_pairs={{0,32},{32,0},{64,96},{96,64},{128,160},{160,128},{192,224},{224,1... | collective-permute-start | bytes 393224 | tf_op jit(solution)/shard_map/ppermute | solution.py:100
  26.6 8.1 %collective-permute-start.3 = (bf16[128,512]{1,0:T(8,128)(2,1)S(1)}, bf16[128,512]{1,0:T(8,128)(2,1)S(1)}, u32[]{:S(2)}, u32[]{:S(2)}) collective-permute-start(bf16[128,512]{1,0:T(8,128)(2,1)S(1)} %get-tuple-element.31), channel_id=1, source_target_pairs={{0,64},{32,96},{64,0},{96,32},{128,192},{160,224},{192,128},{224,1... | collective-permute-start | bytes 393224 | tf_op jit(solution)/shard_map/ppermute | solution.py:100
  27.9 7.8 %collective-permute-start.4 = (bf16[128,512]{1,0:T(8,128)(2,1)S(1)}, bf16[128,512]{1,0:T(8,128)(2,1)S(1)}, u32[]{:S(2)}, u32[]{:S(2)}) collective-permute-start(bf16[128,512]{1,0:T(8,128)(2,1)S(1)} %get-tuple-element.31), channel_id=1, source_target_pairs={{0,96},{32,64},{64,32},{96,0},{128,224},{160,192},{192,160},{224,1... | collective-permute-start | bytes 393224 | tf_op jit(solution)/shard_map/ppermute | solution.py:100
  29.0 6.8 %collective-permute-start.5 = (bf16[128,512]{1,0:T(8,128)(2,1)S(1)}, bf16[128,512]{1,0:T(8,128)(2,1)S(1)}, u32[]{:S(2)}, u32[]{:S(2)}) collective-permute-start(bf16[128,512]{1,0:T(8,128)(2,1)S(1)} %get-tuple-element.31), channel_id=1, source_target_pairs={{0,128},{32,160},{64,192},{96,224},{128,0},{160,32},{192,64},{224,... | collective-permute-start | bytes 393224 | tf_op jit(solution)/shard_map/ppermute | solution.py:100
  31.9 6.7 %collective-permute-start.6 = (bf16[128,512]{1,0:T(8,128)(2,1)S(1)}, bf16[128,512]{1,0:T(8,128)(2,1)S(1)}, u32[]{:S(2)}, u32[]{:S(2)}) collective-permute-start(bf16[128,512]{1,0:T(8,128)(2,1)S(1)} %get-tuple-element.31), channel_id=1, source_target_pairs={{0,160},{32,128},{64,224},{96,192},{128,32},{160,0},{192,96},{224,... | collective-permute-start | bytes 393224 | tf_op jit(solution)/shard_map/ppermute | solution.py:100
  32.0 6.7 %collective-permute-start.7 = (bf16[128,512]{1,0:T(8,128)(2,1)S(1)}, bf16[128,512]{1,0:T(8,128)(2,1)S(1)}, u32[]{:S(2)}, u32[]{:S(2)}) collective-permute-start(bf16[128,512]{1,0:T(8,128)(2,1)S(1)} %get-tuple-element.31), channel_id=1, source_target_pairs={{0,192},{32,224},{64,128},{96,160},{128,64},{160,96},{192,0},{224,... | collective-permute-start | bytes 393224 | tf_op jit(solution)/shard_map/ppermute | solution.py:100
  34.7 7.5 %collective-permute-start.8 = (bf16[128,512]{1,0:T(8,128)(2,1)S(1)}, bf16[128,512]{1,0:T(8,128)(2,1)S(1)}, u32[]{:S(2)}, u32[]{:S(2)}) collective-permute-start(bf16[128,512]{1,0:T(8,128)(2,1)S(1)} %get-tuple-element.31), channel_id=1, source_target_pairs={{0,224},{32,192},{64,160},{96,128},{128,96},{160,64},{192,32},{224... | collective-permute-start | bytes 393224 | tf_op jit(solution)/shard_map/ppermute | solution.py:100
  43.6 10.0 %collective-permute-start.10 = (bf16[128,64]{1,0:T(8,128)(2,1)S(1)}, bf16[128,64]{1,0:T(8,128)(2,1)S(1)}, u32[]{:S(2)}, u32[]{:S(2)}) collective-permute-start(bf16[128,64]{1,0:T(8,128)(2,1)S(1)} %get-tuple-element.163), channel_id=1, source_target_pairs={{0,31},{1,2},{2,1},{3,4},{4,3},{5,6},{6,5},{7,8},{8,7},{9,10},{10,... | collective-permute-start | bytes 49160 | tf_op jit(solution)/shard_map/ppermute | solution.py:100
  54.7 5.1 %collective-permute-start.11 = (bf16[128,64]{1,0:T(8,128)(2,1)S(1)}, bf16[128,64]{1,0:T(8,128)(2,1)S(1)}, u32[]{:S(2)}, u32[]{:S(2)}) collective-permute-start(bf16[128,64]{1,0:T(8,128)(2,1)S(1)} %get-tuple-element.152), channel_id=1, source_target_pairs={{0,1},{1,0},{2,3},{3,2},{4,5},{5,4},{6,7},{7,6},{8,9},{9,8},{10,11... | collective-permute-start | bytes 49160 | tf_op jit(solution)/shard_map/ppermute | solution.py:100
  58.9 4.8 %collective-permute-start.12 = (bf16[128,64]{1,0:T(8,128)(2,1)S(1)}, bf16[128,64]{1,0:T(8,128)(2,1)S(1)}, u32[]{:S(2)}, u32[]{:S(2)}) collective-permute-start(bf16[128,64]{1,0:T(8,128)(2,1)S(1)} %get-tuple-element.153), channel_id=1, source_target_pairs={{0,31},{1,2},{2,1},{3,4},{4,3},{5,6},{6,5},{7,8},{8,7},{9,10},{10,... | collective-permute-start | bytes 49160 | tf_op jit(solution)/shard_map/ppermute | solution.py:100
  67.2 4.8 %collective-permute-start.14 = (bf16[128,64]{1,0:T(8,128)(2,1)S(1)}, bf16[128,64]{1,0:T(8,128)(2,1)S(1)}, u32[]{:S(2)}, u32[]{:S(2)}) collective-permute-start(bf16[128,64]{1,0:T(8,128)(2,1)S(1)} %get-tuple-element.143), channel_id=1, source_target_pairs={{0,31},{1,2},{2,1},{3,4},{4,3},{5,6},{6,5},{7,8},{8,7},{9,10},{10,... | collective-permute-start | bytes 49160 | tf_op jit(solution)/shard_map/ppermute | solution.py:100
  73.1 3.3 %collective-permute-start.15 = (bf16[128,64]{1,0:T(8,128)(2,1)S(1)}, bf16[128,64]{1,0:T(8,128)(2,1)S(1)}, u32[]{:S(2)}, u32[]{:S(2)}) collective-permute-start(bf16[128,64]{1,0:T(8,128)(2,1)S(1)} %get-tuple-element.132), channel_id=1, source_target_pairs={{0,1},{1,0},{2,3},{3,2},{4,5},{5,4},{6,7},{7,6},{8,9},{9,8},{10,11... | collective-permute-start | bytes 49160 | tf_op jit(solution)/shard_map/ppermute | solution.py:100
  75.6 4.8 %collective-permute-start.16 = (bf16[128,64]{1,0:T(8,128)(2,1)S(1)}, bf16[128,64]{1,0:T(8,128)(2,1)S(1)}, u32[]{:S(2)}, u32[]{:S(2)}) collective-permute-start(bf16[128,64]{1,0:T(8,128)(2,1)S(1)} %get-tuple-element.133), channel_id=1, source_target_pairs={{0,31},{1,2},{2,1},{3,4},{4,3},{5,6},{6,5},{7,8},{8,7},{9,10},{10,... | collective-permute-start | bytes 49160 | tf_op jit(solution)/shard_map/ppermute | solution.py:100
  83.8 4.8 %collective-permute-start.18 = (bf16[128,64]{1,0:T(8,128)(2,1)S(1)}, bf16[128,64]{1,0:T(8,128)(2,1)S(1)}, u32[]{:S(2)}, u32[]{:S(2)}) collective-permute-start(bf16[128,64]{1,0:T(8,128)(2,1)S(1)} %get-tuple-element.123), channel_id=1, source_target_pairs={{0,31},{1,2},{2,1},{3,4},{4,3},{5,6},{6,5},{7,8},{8,7},{9,10},{10,... | collective-permute-start | bytes 49160 | tf_op jit(solution)/shard_map/ppermute | solution.py:100
  92.1 4.8 %collective-permute-start.20 = (bf16[128,64]{1,0:T(8,128)(2,1)S(1)}, bf16[128,64]{1,0:T(8,128)(2,1)S(1)}, u32[]{:S(2)}, u32[]{:S(2)}) collective-permute-start(bf16[128,64]{1,0:T(8,128)(2,1)S(1)} %get-tuple-element.113), channel_id=1, source_target_pairs={{0,31},{1,2},{2,1},{3,4},{4,3},{5,6},{6,5},{7,8},{8,7},{9,10},{10,... | collective-permute-start | bytes 49160 | tf_op jit(solution)/shard_map/ppermute | solution.py:100
  100.3 4.8 %collective-permute-start.22 = (bf16[128,64]{1,0:T(8,128)(2,1)S(1)}, bf16[128,64]{1,0:T(8,128)(2,1)S(1)}, u32[]{:S(2)}, u32[]{:S(2)}) collective-permute-start(bf16[128,64]{1,0:T(8,128)(2,1)S(1)} %get-tuple-element.103), channel_id=1, source_target_pairs={{0,31},{1,2},{2,1},{3,4},{4,3},{5,6},{6,5},{7,8},{8,7},{9,10},{10,... | collective-permute-start | bytes 49160 | tf_op jit(solution)/shard_map/ppermute | solution.py:100
  105.4 6.6 %collective-permute-start.23 = (bf16[128,512]{1,0:T(8,128)(2,1)S(1)}, bf16[128,512]{1,0:T(8,128)(2,1)S(1)}, u32[]{:S(2)}, u32[]{:S(2)}) collective-permute-start(bf16[128,512]{1,0:T(8,128)(2,1)S(1)} %get-tuple-element.17), channel_id=1, source_target_pairs={{0,32},{32,0},{64,96},{96,64},{128,160},{160,128},{192,224},{224,1... | collective-permute-start | bytes 393224 | tf_op jit(solution)/shard_map/ppermute | solution.py:100
  106.6 5.5 %collective-permute-start.24 = (bf16[128,512]{1,0:T(8,128)(2,1)S(1)}, bf16[128,512]{1,0:T(8,128)(2,1)S(1)}, u32[]{:S(2)}, u32[]{:S(2)}) collective-permute-start(bf16[128,512]{1,0:T(8,128)(2,1)S(1)} %get-tuple-element.17), channel_id=1, source_target_pairs={{0,64},{32,96},{64,0},{96,32},{128,192},{160,224},{192,128},{224,1... | collective-permute-start | bytes 393224 | tf_op jit(solution)/shard_map/ppermute | solution.py:100
  106.6 8.4 %collective-permute-start.25 = (bf16[128,512]{1,0:T(8,128)(2,1)S(1)}, bf16[128,512]{1,0:T(8,128)(2,1)S(1)}, u32[]{:S(2)}, u32[]{:S(2)}) collective-permute-start(bf16[128,512]{1,0:T(8,128)(2,1)S(1)} %get-tuple-element.17), channel_id=1, source_target_pairs={{0,96},{32,64},{64,32},{96,0},{128,224},{160,192},{192,160},{224,1... | collective-permute-start | bytes 393224 | tf_op jit(solution)/shard_map/ppermute | solution.py:100
  108.1 11.9 %collective-permute-start.26 = (bf16[128,512]{1,0:T(8,128)(2,1)S(1)}, bf16[128,512]{1,0:T(8,128)(2,1)S(1)}, u32[]{:S(2)}, u32[]{:S(2)}) collective-permute-start(bf16[128,512]{1,0:T(8,128)(2,1)S(1)} %get-tuple-element.17), channel_id=1, source_target_pairs={{0,128},{32,160},{64,192},{96,224},{128,0},{160,32},{192,64},{224,... | collective-permute-start | bytes 393224 | tf_op jit(solution)/shard_map/ppermute | solution.py:100
  108.3 11.8 %collective-permute-start.27 = (bf16[128,512]{1,0:T(8,128)(2,1)S(1)}, bf16[128,512]{1,0:T(8,128)(2,1)S(1)}, u32[]{:S(2)}, u32[]{:S(2)}) collective-permute-start(bf16[128,512]{1,0:T(8,128)(2,1)S(1)} %get-tuple-element.17), channel_id=1, source_target_pairs={{0,160},{32,128},{64,224},{96,192},{128,32},{160,0},{192,96},{224,... | collective-permute-start | bytes 393224 | tf_op jit(solution)/shard_map/ppermute | solution.py:100
  112.0 11.6 %collective-permute-start.28 = (bf16[128,512]{1,0:T(8,128)(2,1)S(1)}, bf16[128,512]{1,0:T(8,128)(2,1)S(1)}, u32[]{:S(2)}, u32[]{:S(2)}) collective-permute-start(bf16[128,512]{1,0:T(8,128)(2,1)S(1)} %get-tuple-element.17), channel_id=1, source_target_pairs={{0,192},{32,224},{64,128},{96,160},{128,64},{160,96},{192,0},{224,... | collective-permute-start | bytes 393224 | tf_op jit(solution)/shard_map/ppermute | solution.py:100
  112.2 11.4 %collective-permute-start.29 = (bf16[128,512]{1,0:T(8,128)(2,1)S(1)}, bf16[128,512]{1,0:T(8,128)(2,1)S(1)}, u32[]{:S(2)}, u32[]{:S(2)}) collective-permute-start(bf16[128,512]{1,0:T(8,128)(2,1)S(1)} %get-tuple-element.17), channel_id=1, source_target_pairs={{0,224},{32,192},{64,160},{96,128},{128,96},{160,64},{192,32},{224... | collective-permute-start | bytes 393224 | tf_op jit(solution)/shard_map/ppermute | solution.py:100
  124.9 4.0 %collective-permute-start.30 = (bf16[128,64]{1,0:T(8,128)(2,1)S(1)}, bf16[128,64]{1,0:T(8,128)(2,1)S(1)}, u32[]{:S(2)}, u32[]{:S(2)}) collective-permute-start(bf16[128,64]{1,0:T(8,128)(2,1)S(1)} %get-tuple-element.92), channel_id=1, source_target_pairs={{0,1},{1,0},{2,3},{3,2},{4,5},{5,4},{6,7},{7,6},{8,9},{9,8},{10,11... | collective-permute-start | bytes 49160 | tf_op jit(solution)/shard_map/ppermute | solution.py:100
  128.1 4.8 %collective-permute-start.31 = (bf16[128,64]{1,0:T(8,128)(2,1)S(1)}, bf16[128,64]{1,0:T(8,128)(2,1)S(1)}, u32[]{:S(2)}, u32[]{:S(2)}) collective-permute-start(bf16[128,64]{1,0:T(8,128)(2,1)S(1)} %get-tuple-element.93), channel_id=1, source_target_pairs={{0,31},{1,2},{2,1},{3,4},{4,3},{5,6},{6,5},{7,8},{8,7},{9,10},{10,... | collective-permute-start | bytes 49160 | tf_op jit(solution)/shard_map/ppermute | solution.py:100
  136.3 4.8 %collective-permute-start.33 = (bf16[128,64]{1,0:T(8,128)(2,1)S(1)}, bf16[128,64]{1,0:T(8,128)(2,1)S(1)}, u32[]{:S(2)}, u32[]{:S(2)}) collective-permute-start(bf16[128,64]{1,0:T(8,128)(2,1)S(1)} %get-tuple-element.83), channel_id=1, source_target_pairs={{0,31},{1,2},{2,1},{3,4},{4,3},{5,6},{6,5},{7,8},{8,7},{9,10},{10,... | collective-permute-start | bytes 49160 | tf_op jit(solution)/shard_map/ppermute | solution.py:100
  144.5 4.8 %collective-permute-start.35 = (bf16[128,64]{1,0:T(8,128)(2,1)S(1)}, bf16[128,64]{1,0:T(8,128)(2,1)S(1)}, u32[]{:S(2)}, u32[]{:S(2)}) collective-permute-start(bf16[128,64]{1,0:T(8,128)(2,1)S(1)} %get-tuple-element.73), channel_id=1, source_target_pairs={{0,31},{1,2},{2,1},{3,4},{4,3},{5,6},{6,5},{7,8},{8,7},{9,10},{10,... | collective-permute-start | bytes 49160 | tf_op jit(solution)/shard_map/ppermute | solution.py:100
  152.8 4.8 %collective-permute-start.37 = (bf16[128,64]{1,0:T(8,128)(2,1)S(1)}, bf16[128,64]{1,0:T(8,128)(2,1)S(1)}, u32[]{:S(2)}, u32[]{:S(2)}) collective-permute-start(bf16[128,64]{1,0:T(8,128)(2,1)S(1)} %get-tuple-element.63), channel_id=1, source_target_pairs={{0,31},{1,2},{2,1},{3,4},{4,3},{5,6},{6,5},{7,8},{8,7},{9,10},{10,... | collective-permute-start | bytes 49160 | tf_op jit(solution)/shard_map/ppermute | solution.py:100
  161.0 4.8 %collective-permute-start.39 = (bf16[128,64]{1,0:T(8,128)(2,1)S(1)}, bf16[128,64]{1,0:T(8,128)(2,1)S(1)}, u32[]{:S(2)}, u32[]{:S(2)}) collective-permute-start(bf16[128,64]{1,0:T(8,128)(2,1)S(1)} %get-tuple-element.53), channel_id=1, source_target_pairs={{0,31},{1,2},{2,1},{3,4},{4,3},{5,6},{6,5},{7,8},{8,7},{9,10},{10,... | collective-permute-start | bytes 49160 | tf_op jit(solution)/shard_map/ppermute | solution.py:100
  169.3 4.8 %collective-permute-start.41 = (bf16[128,64]{1,0:T(8,128)(2,1)S(1)}, bf16[128,64]{1,0:T(8,128)(2,1)S(1)}, u32[]{:S(2)}, u32[]{:S(2)}) collective-permute-start(bf16[128,64]{1,0:T(8,128)(2,1)S(1)} %get-tuple-element.43), channel_id=1, source_target_pairs={{0,31},{1,2},{2,1},{3,4},{4,3},{5,6},{6,5},{7,8},{8,7},{9,10},{10,... | collective-permute-start | bytes 49160 | tf_op jit(solution)/shard_map/ppermute | solution.py:100
  (19 other events, 119.3 us)
where the time goes:
time: 177 us; the launch traced here: 176 us
  waiting for transfers between devices  65 us (37%)
  starting transfers between devices  62.1 us (35%)
  matrix products  23.5 us (13%)
  other arithmetic  12 us (7%)
  local copies, waits for them, and re-layouts  11.2 us (6%)
  between operations  1.83 us (1%)
    ppermute x42, waiting for transfers between devices, swapped(): lax.ppermute(array, axis, [(i, partner(i) % devices) for i in range(devic...  65 us
    ppermute x42, starting transfers between devices, swapped(): lax.ppermute(array, axis, [(i, partner(i) % devices) for i in range(devic...  62.1 us
    dot_general x14, matrix products, apply_operator(): return own + jnp.dot(faces, x_lift, preferred_element_type=jnp.float32)  12.6 us
    dot_general x14, matrix products, local_terms(): jnp.dot(stacked, weights, preferred_element_type=jnp.float32)  8.95 us
    unnamed x76, local copies, waits for them, and re-layouts  4.42 us
  transfers between devices with their start and end apart: 42, of which 29 were waited for; matrix products, arithmetic and copies ran while one was open for 15% of the time, Pallas kernels for 0%

commit v1 on v0

--- a/solution.py
+++ b/solution.py
@@ -150,8 +150,10 @@
         running_sum = jnp.sum(source_weights[:, None, None] * stacked, axis=0)
         fixed_part = start + time_step * running_sum - own_scale * slopes
         iterate = start + time_step * running_sum
-        for inner_step in range(INNER - 1):
-            iterate = fixed_part + own_scale * apply_operator(iterate, reaction, weights, x_lift, ny, nz)
+        def inner(step, value):
+            return fixed_part + own_scale * apply_operator(value, reaction, weights, x_lift, ny, nz)
+
+        iterate = lax.fori_loop(0, INNER - 1, inner, iterate)
         states = iterate
     return states.reshape(shape)
 

time: 177 us -> 223 us (1.26)
  waiting for transfers between devices: 65 us -> 16.3 us
  local copies, waits for them, and re-layouts: 11.2 us -> 50.3 us
  other arithmetic: 12 us -> 38.7 us
  matrix products: 23.5 us -> 47.1 us
  starting transfers between devices: 62.1 us -> 66.4 us
    ppermute x42, waiting for transfers between devices: 65 us -> 16.3 us  [swapped(): lax.ppermute(array, axis, [(i, partner(i) % devices) for i in range(devic...]
    while x0 -> x36, local copies, waits for them, and re-layouts: none -> 25.3 us
    dot_general x14, matrix products: 8.95 us -> 22 us  [local_terms(): jnp.dot(stacked, weights, preferred_element_type=jnp.float32)]
    dot_general x14, matrix products: 12.6 us -> 23.1 us  [apply_operator(): return own + jnp.dot(faces, x_lift, preferred_element_type=jnp.float32)]
    select_n x14, other arithmetic: 0.91 us -> 10.2 us  [exchange_faces(): below = jnp.where(odd, first, second)]
    while x0 -> x12, other arithmetic: none -> 8.16 us
    concatenate x14, local copies, waits for them, and re-layouts: 0.82 us -> 8.96 us  [shifted_inputs(): return jnp.concatenate(parts, axis=-1).reshape((ny * nz, -1))]
    select_n x14, other arithmetic: 1.76 us -> 9.37 us  [exchange_faces(): first = swapped(jnp.where(odd, low, high), 'gx', lambda i: i ^ 1)]
  transfers between devices with their start and end apart: 42 -> 42, of which waited for: 29 -> 8; matrix products, arithmetic and copies ran while one was open for 15% -> 35% of each run, Pallas kernels for 0% -> 0%
where the time goes in v1:
time: 223 us; the launch traced here: 220 us
  starting transfers between devices  66.4 us (30%)
  local copies, waits for them, and re-layouts  50.3 us (23%)
  matrix products  47.1 us (21%)
  other arithmetic  38.7 us (17%)
  waiting for transfers between devices  16.3 us (7%)
    ppermute x42, starting transfers between devices, swapped(): lax.ppermute(array, axis, [(i, partner(i) % devices) for i in range(devic...  66.4 us
    while x36, local copies, waits for them, and re-layouts  25.3 us
    dot_general x14, matrix products, apply_operator(): return own + jnp.dot(faces, x_lift, preferred_element_type=jnp.float32)  23.1 us
    dot_general x14, matrix products, local_terms(): jnp.dot(stacked, weights, preferred_element_type=jnp.float32)  22 us
    ppermute x42, waiting for transfers between devices, swapped(): lax.ppermute(array, axis, [(i, partner(i) % devices) for i in range(devic...  16.3 us
    select_n x14, other arithmetic, exchange_faces(): below = jnp.where(odd, first, second)  10.2 us
    unnamed x44, local copies, waits for them, and re-layouts  9.59 us
    select_n x14, other arithmetic, exchange_faces(): first = swapped(jnp.where(odd, low, high), 'gx', lambda i: i ^ 1)  9.37 us
  transfers between devices with their start and end apart: 42, of which 8 were waited for; matrix products, arithmetic and copies ran while one was open for 35% of the time, Pallas kernels for 0%

profile of v1, /device:TPU:1, one launch (start us, length us, event | category | flops | bytes accessed | tf_op | source)
XLA Modules:
  0.0 220.2 jit_solution(12922372678079249476)
XLA Ops:
  1.8 3.2 %collective-permute-start.4 = (bf16[128,64]{1,0:T(8,128)(2,1)}, bf16[128,64]{1,0:T(8,128)(2,1)}, u32[]{:S(2)}, u32[]{:S(2)}) collective-permute-start(bf16[128,64]{1,0:T(8,128)(2,1)} %get-tuple-element.274), channel_id=1, source_target_pairs={{0,1},{1,0},{2,3},{3,2},{4,5},{5,4},{6,7},{7,6},{8,9},{9,8},{10,11... | collective-permute-start | bytes 49160 | tf_op jit(solution)/shard_map/ppermute | solution.py:100
  18.3 2.3 %convolution_subtract_fusion.3 = f32[128,512]{1,0:T(8,128)} fusion(f32[128,512]{1,0:T(8,128)S(1)} %copy-done.7, bf16[128,2560]{1,0:T(8,128)(2,1)} %constant_dynamic-update-slice_fusion.10, bf16[2560,512]{1,0:T(8,128)(2,1)S(1)} %fusion.12), kind=kOutput, calls=%fused_computation.60 | convolution fusion | flops 335609856 | bytes 3801088 | tf_op jit(solution)/shard_map/dot_general | solution.py:94
  27.2 2.9 %collective-permute-start.9 = (bf16[128,512]{1,0:T(8,128)(2,1)S(1)}, bf16[128,512]{1,0:T(8,128)(2,1)S(1)}, u32[]{:S(2)}, u32[]{:S(2)}) collective-permute-start(bf16[128,512]{1,0:T(8,128)(2,1)S(1)} %get-tuple-element.229), channel_id=1, source_target_pairs={{0,128},{32,160},{64,192},{96,224},{128,0},{160,32},{192,64},{224,... | collective-permute-start | bytes 393224 | tf_op jit(solution)/shard_map/ppermute | solution.py:100
  30.3 2.8 %collective-permute-start.11 = (bf16[128,512]{1,0:T(8,128)(2,1)S(1)}, bf16[128,512]{1,0:T(8,128)(2,1)S(1)}, u32[]{:S(2)}, u32[]{:S(2)}) collective-permute-start(bf16[128,512]{1,0:T(8,128)(2,1)S(1)} %get-tuple-element.229), channel_id=1, source_target_pairs={{0,192},{32,224},{64,128},{96,160},{128,64},{160,96},{192,0},{224,... | collective-permute-start | bytes 393224 | tf_op jit(solution)/shard_map/ppermute | solution.py:100
  34.1 2.8 %collective-permute-done.10 = bf16[128,512]{1,0:T(8,128)(2,1)S(1)} collective-permute-done((bf16[128,512]{1,0:T(8,128)(2,1)S(1)}, bf16[128,512]{1,0:T(8,128)(2,1)S(1)}, u32[]{:S(2)}, u32[]{:S(2)}) %collective-permute-start.10) | collective-permute-done | bytes 131104 | tf_op jit(solution)/shard_map/ppermute | solution.py:100
  37.0 3.8 %collective-permute-done.12 = bf16[128,512]{1,0:T(8,128)(2,1)S(1)} collective-permute-done((bf16[128,512]{1,0:T(8,128)(2,1)S(1)}, bf16[128,512]{1,0:T(8,128)(2,1)S(1)}, u32[]{:S(2)}, u32[]{:S(2)}) %collective-permute-start.12) | collective-permute-done | bytes 131104 | tf_op jit(solution)/shard_map/ppermute | solution.py:100
  41.0 2.3 %multiply_subtract_fusion.1 = (f32[128,512]{1,0:T(8,128)}, f32[128,512]{1,0:T(8,128)S(1)}) fusion(f32[128,512]{1,0:T(8,128)S(1)} %get-tuple-element.288, f32[]{:T(128)} %bitcast.39, f32[128,512]{1,0:T(8,128)S(1)} %multiply_reduce_fusion.1, f32[1,8,16,512]{3,2,1,0:T(8,128)} %param.17), kind=kLoop, calls=%fused_computation.66 | loop fusion | flops 262144 | bytes 1310724 | tf_op jit(solution)/shard_map/sub | solution.py:151
  43.3 74.9 %while.24 = (s32[]{:T(128)}, f32[128,512]{1,0:T(8,128)S(1)}, f32[]{:T(128)}, bf16[2560,512]{1,0:T(8,128)(2,1)S(1)}, f32[128,512]{1,0:T(8,128)S(1)}, /*index=5*/b...) while((s32[]{:T(128)}, f32[128,512]{1,0:T(8,128)S(1)}, ...), condition=%wide.region_2.4_spmd, body=%wide.region_1.3_spmd.sunk | while | flops 353468416 | bytes 8945997 | solution.py:156
  44.7 7.0 %collective-permute-start = (bf16[128,64]{1,0:T(8,128)(2,1)}, bf16[128,64]{1,0:T(8,128)(2,1)}, u32[]{:S(2)}, u32[]{:S(2)}) collective-permute-start(bf16[128,64]{1,0:T(8,128)(2,1)} %get-tuple-element.423), channel_id=1, source_target_pairs={{0,1},{1,0},{2,3},{3,2},{4,5},{5,4},{6,7},{7,6},{8,9},{9,8},{10,11... | collective-permute-start | bytes 49160 | tf_op jit(solution)/shard_map/while/body/eval_jaxpr/ppermute | solution.py:100
  58.4 1.7 fusion.79
  61.6 2.7 %collective-permute-start = (bf16[128,64]{1,0:T(8,128)(2,1)}, bf16[128,64]{1,0:T(8,128)(2,1)}, u32[]{:S(2)}, u32[]{:S(2)}) collective-permute-start(bf16[128,64]{1,0:T(8,128)(2,1)} %get-tuple-element.423), channel_id=1, source_target_pairs={{0,1},{1,0},{2,3},{3,2},{4,5},{5,4},{6,7},{7,6},{8,9},{9,8},{10,11... | collective-permute-start | bytes 49160 | tf_op jit(solution)/shard_map/while/body/eval_jaxpr/ppermute | solution.py:100
  70.2 1.7 fusion.79
  73.3 2.1 collective-permute-start
  84.7 3.2 %collective-permute-start = (bf16[128,64]{1,0:T(8,128)(2,1)}, bf16[128,64]{1,0:T(8,128)(2,1)}, u32[]{:S(2)}, u32[]{:S(2)}) collective-permute-start(bf16[128,64]{1,0:T(8,128)(2,1)} %get-tuple-element.423), channel_id=1, source_target_pairs={{0,1},{1,0},{2,3},{3,2},{4,5},{5,4},{6,7},{7,6},{8,9},{9,8},{10,11... | collective-permute-start | bytes 49160 | tf_op jit(solution)/shard_map/while/body/eval_jaxpr/ppermute | solution.py:100
  93.8 1.7 fusion.79
  97.0 2.1 collective-permute-start
  105.2 1.7 fusion.79
  108.4 2.1 collective-permute-start
  118.5 2.2 collective-permute-start.13
  122.2 3.3 %collective-permute-done.14 = bf16[128,64]{1,0:T(8,128)(2,1)S(1)} collective-permute-done((bf16[128,64]{1,0:T(8,128)(2,1)S(1)}, bf16[128,64]{1,0:T(8,128)(2,1)S(1)}, u32[]{:S(2)}, u32[]{:S(2)}) %collective-permute-start.14) | collective-permute-done | bytes 16416 | tf_op jit(solution)/shard_map/ppermute | solution.py:100
  127.1 2.0 collective-permute-start.17
  133.9 2.2 collective-permute-start.20
  141.6 3.1 %collective-permute-done.20 = bf16[128,512]{1,0:T(8,128)(2,1)S(1)} collective-permute-done((bf16[128,512]{1,0:T(8,128)(2,1)S(1)}, bf16[128,512]{1,0:T(8,128)(2,1)S(1)}, u32[]{:S(2)}, u32[]{:S(2)}) %collective-permute-start.20) | collective-permute-done | bytes 131104 | tf_op jit(solution)/shard_map/ppermute | solution.py:100
  148.9 70.6 %while.25 = (s32[]{:T(128)}, f32[128,512]{1,0:T(8,128)S(1)}, f32[]{:T(128)}, bf16[2560,512]{1,0:T(8,128)(2,1)S(1)}, f32[128,512]{1,0:T(8,128)S(1)}, /*index=5*/b...) while((s32[]{:T(128)}, f32[128,512]{1,0:T(8,128)S(1)}, ...), condition=%wide.region_5.7_spmd, body=%wide.region_4.6_spmd.sunk | while | flops 353468416 | bytes 8945997 | solution.py:156
  150.3 2.4 %collective-permute-start.2 = (bf16[128,64]{1,0:T(8,128)(2,1)}, bf16[128,64]{1,0:T(8,128)(2,1)}, u32[]{:S(2)}, u32[]{:S(2)}) collective-permute-start(bf16[128,64]{1,0:T(8,128)(2,1)} %get-tuple-element.448), channel_id=1, source_target_pairs={{0,1},{1,0},{2,3},{3,2},{4,5},{5,4},{6,7},{7,6},{8,9},{9,8},{10,11... | collective-permute-start | bytes 49160 | tf_op jit(solution)/shard_map/while/body/eval_jaxpr/ppermute | solution.py:100
  152.7 2.1 collective-permute-start.3
  163.4 3.2 %collective-permute-start.2 = (bf16[128,64]{1,0:T(8,128)(2,1)}, bf16[128,64]{1,0:T(8,128)(2,1)}, u32[]{:S(2)}, u32[]{:S(2)}) collective-permute-start(bf16[128,64]{1,0:T(8,128)(2,1)} %get-tuple-element.448), channel_id=1, source_target_pairs={{0,1},{1,0},{2,3},{3,2},{4,5},{5,4},{6,7},{7,6},{8,9},{9,8},{10,11... | collective-permute-start | bytes 49160 | tf_op jit(solution)/shard_map/while/body/eval_jaxpr/ppermute | solution.py:100
  175.7 2.1 collective-permute-start.2
  187.1 2.1 collective-permute-start.2
  198.3 2.1 collective-permute-start.2
  209.7 2.1 collective-permute-start.2
  217.8 1.7 fusion.87
  (323 shorter events, 141.8 us)
Async XLA Ops:
  1.8 20.6 %collective-permute-start.4 = (bf16[128,64]{1,0:T(8,128)(2,1)}, bf16[128,64]{1,0:T(8,128)(2,1)}, u32[]{:S(2)}, u32[]{:S(2)}) collective-permute-start(bf16[128,64]{1,0:T(8,128)(2,1)} %get-tuple-element.274), channel_id=1, source_target_pairs={{0,1},{1,0},{2,3},{3,2},{4,5},{5,4},{6,7},{7,6},{8,9},{9,8},{10,11... | collective-permute-start | bytes 49160 | tf_op jit(solution)/shard_map/ppermute | solution.py:100
  5.1 17.4 %collective-permute-start.5 = (bf16[128,64]{1,0:T(8,128)(2,1)}, bf16[128,64]{1,0:T(8,128)(2,1)}, u32[]{:S(2)}, u32[]{:S(2)}) collective-permute-start(bf16[128,64]{1,0:T(8,128)(2,1)} %get-tuple-element.275), channel_id=1, source_target_pairs={{0,31},{1,2},{2,1},{3,4},{4,3},{5,6},{6,5},{7,8},{8,7},{9,10},{10,... | collective-permute-start | bytes 49160 | tf_op jit(solution)/shard_map/ppermute | solution.py:100
  24.5 5.8 %collective-permute-start.6 = (bf16[128,512]{1,0:T(8,128)(2,1)S(1)}, bf16[128,512]{1,0:T(8,128)(2,1)S(1)}, u32[]{:S(2)}, u32[]{:S(2)}) collective-permute-start(bf16[128,512]{1,0:T(8,128)(2,1)S(1)} %get-tuple-element.229), channel_id=1, source_target_pairs={{0,32},{32,0},{64,96},{96,64},{128,160},{160,128},{192,224},{224,1... | collective-permute-start | bytes 393224 | tf_op jit(solution)/shard_map/ppermute | solution.py:100
  24.9 8.2 %collective-permute-start.7 = (bf16[128,512]{1,0:T(8,128)(2,1)S(1)}, bf16[128,512]{1,0:T(8,128)(2,1)S(1)}, u32[]{:S(2)}, u32[]{:S(2)}) collective-permute-start(bf16[128,512]{1,0:T(8,128)(2,1)S(1)} %get-tuple-element.229), channel_id=1, source_target_pairs={{0,64},{32,96},{64,0},{96,32},{128,192},{160,224},{192,128},{224,1... | collective-permute-start | bytes 393224 | tf_op jit(solution)/shard_map/ppermute | solution.py:100
  26.2 7.9 %collective-permute-start.8 = (bf16[128,512]{1,0:T(8,128)(2,1)S(1)}, bf16[128,512]{1,0:T(8,128)(2,1)S(1)}, u32[]{:S(2)}, u32[]{:S(2)}) collective-permute-start(bf16[128,512]{1,0:T(8,128)(2,1)S(1)} %get-tuple-element.229), channel_id=1, source_target_pairs={{0,96},{32,64},{64,32},{96,0},{128,224},{160,192},{192,160},{224,1... | collective-permute-start | bytes 393224 | tf_op jit(solution)/shard_map/ppermute | solution.py:100
  27.2 6.9 %collective-permute-start.9 = (bf16[128,512]{1,0:T(8,128)(2,1)S(1)}, bf16[128,512]{1,0:T(8,128)(2,1)S(1)}, u32[]{:S(2)}, u32[]{:S(2)}) collective-permute-start(bf16[128,512]{1,0:T(8,128)(2,1)S(1)} %get-tuple-element.229), channel_id=1, source_target_pairs={{0,128},{32,160},{64,192},{96,224},{128,0},{160,32},{192,64},{224,... | collective-permute-start | bytes 393224 | tf_op jit(solution)/shard_map/ppermute | solution.py:100
  30.2 6.7 %collective-permute-start.10 = (bf16[128,512]{1,0:T(8,128)(2,1)S(1)}, bf16[128,512]{1,0:T(8,128)(2,1)S(1)}, u32[]{:S(2)}, u32[]{:S(2)}) collective-permute-start(bf16[128,512]{1,0:T(8,128)(2,1)S(1)} %get-tuple-element.229), channel_id=1, source_target_pairs={{0,160},{32,128},{64,224},{96,192},{128,32},{160,0},{192,96},{224,... | collective-permute-start | bytes 393224 | tf_op jit(solution)/shard_map/ppermute | solution.py:100
  30.3 6.7 %collective-permute-start.11 = (bf16[128,512]{1,0:T(8,128)(2,1)S(1)}, bf16[128,512]{1,0:T(8,128)(2,1)S(1)}, u32[]{:S(2)}, u32[]{:S(2)}) collective-permute-start(bf16[128,512]{1,0:T(8,128)(2,1)S(1)} %get-tuple-element.229), channel_id=1, source_target_pairs={{0,192},{32,224},{64,128},{96,160},{128,64},{160,96},{192,0},{224,... | collective-permute-start | bytes 393224 | tf_op jit(solution)/shard_map/ppermute | solution.py:100
  33.1 7.6 %collective-permute-start.12 = (bf16[128,512]{1,0:T(8,128)(2,1)S(1)}, bf16[128,512]{1,0:T(8,128)(2,1)S(1)}, u32[]{:S(2)}, u32[]{:S(2)}) collective-permute-start(bf16[128,512]{1,0:T(8,128)(2,1)S(1)} %get-tuple-element.229), channel_id=1, source_target_pairs={{0,224},{32,192},{64,160},{96,128},{128,96},{160,64},{192,32},{224... | collective-permute-start | bytes 393224 | tf_op jit(solution)/shard_map/ppermute | solution.py:100
  44.7 12.9 %collective-permute-start = (bf16[128,64]{1,0:T(8,128)(2,1)}, bf16[128,64]{1,0:T(8,128)(2,1)}, u32[]{:S(2)}, u32[]{:S(2)}) collective-permute-start(bf16[128,64]{1,0:T(8,128)(2,1)} %get-tuple-element.423), channel_id=1, source_target_pairs={{0,1},{1,0},{2,3},{3,2},{4,5},{5,4},{6,7},{7,6},{8,9},{9,8},{10,11... | collective-permute-start | bytes 49160 | tf_op jit(solution)/shard_map/while/body/eval_jaxpr/ppermute | solution.py:100
  51.7 5.9 %collective-permute-start.1 = (bf16[128,64]{1,0:T(8,128)(2,1)}, bf16[128,64]{1,0:T(8,128)(2,1)}, u32[]{:S(2)}, u32[]{:S(2)}) collective-permute-start(bf16[128,64]{1,0:T(8,128)(2,1)} %get-tuple-element.424), channel_id=1, source_target_pairs={{0,31},{1,2},{2,1},{3,4},{4,3},{5,6},{6,5},{7,8},{8,7},{9,10},{10,... | collective-permute-start | bytes 49160 | tf_op jit(solution)/shard_map/while/body/eval_jaxpr/ppermute | solution.py:100
  61.6 7.3 %collective-permute-start = (bf16[128,64]{1,0:T(8,128)(2,1)}, bf16[128,64]{1,0:T(8,128)(2,1)}, u32[]{:S(2)}, u32[]{:S(2)}) collective-permute-start(bf16[128,64]{1,0:T(8,128)(2,1)} %get-tuple-element.423), channel_id=1, source_target_pairs={{0,1},{1,0},{2,3},{3,2},{4,5},{5,4},{6,7},{7,6},{8,9},{9,8},{10,11... | collective-permute-start | bytes 49160 | tf_op jit(solution)/shard_map/while/body/eval_jaxpr/ppermute | solution.py:100
  73.3 7.4 %collective-permute-start = (bf16[128,64]{1,0:T(8,128)(2,1)}, bf16[128,64]{1,0:T(8,128)(2,1)}, u32[]{:S(2)}, u32[]{:S(2)}) collective-permute-start(bf16[128,64]{1,0:T(8,128)(2,1)} %get-tuple-element.423), channel_id=1, source_target_pairs={{0,1},{1,0},{2,3},{3,2},{4,5},{5,4},{6,7},{7,6},{8,9},{9,8},{10,11... | collective-permute-start | bytes 49160 | tf_op jit(solution)/shard_map/while/body/eval_jaxpr/ppermute | solution.py:100
  84.7 7.8 %collective-permute-start = (bf16[128,64]{1,0:T(8,128)(2,1)}, bf16[128,64]{1,0:T(8,128)(2,1)}, u32[]{:S(2)}, u32[]{:S(2)}) collective-permute-start(bf16[128,64]{1,0:T(8,128)(2,1)} %get-tuple-element.423), channel_id=1, source_target_pairs={{0,1},{1,0},{2,3},{3,2},{4,5},{5,4},{6,7},{7,6},{8,9},{9,8},{10,11... | collective-permute-start | bytes 49160 | tf_op jit(solution)/shard_map/while/body/eval_jaxpr/ppermute | solution.py:100
  97.0 7.4 %collective-permute-start = (bf16[128,64]{1,0:T(8,128)(2,1)}, bf16[128,64]{1,0:T(8,128)(2,1)}, u32[]{:S(2)}, u32[]{:S(2)}) collective-permute-start(bf16[128,64]{1,0:T(8,128)(2,1)} %get-tuple-element.423), channel_id=1, source_target_pairs={{0,1},{1,0},{2,3},{3,2},{4,5},{5,4},{6,7},{7,6},{8,9},{9,8},{10,11... | collective-permute-start | bytes 49160 | tf_op jit(solution)/shard_map/while/body/eval_jaxpr/ppermute | solution.py:100
  108.4 7.3 %collective-permute-start = (bf16[128,64]{1,0:T(8,128)(2,1)}, bf16[128,64]{1,0:T(8,128)(2,1)}, u32[]{:S(2)}, u32[]{:S(2)}) collective-permute-start(bf16[128,64]{1,0:T(8,128)(2,1)} %get-tuple-element.423), channel_id=1, source_target_pairs={{0,1},{1,0},{2,3},{3,2},{4,5},{5,4},{6,7},{7,6},{8,9},{9,8},{10,11... | collective-permute-start | bytes 49160 | tf_op jit(solution)/shard_map/while/body/eval_jaxpr/ppermute | solution.py:100
  126.5 5.9 %collective-permute-start.15 = (bf16[128,512]{1,0:T(8,128)(2,1)S(1)}, bf16[128,512]{1,0:T(8,128)(2,1)}, u32[]{:S(2)}, u32[]{:S(2)}) collective-permute-start(bf16[128,512]{1,0:T(8,128)(2,1)S(1)} %get-tuple-element.223), channel_id=1, source_target_pairs={{0,32},{32,0},{64,96},{96,64},{128,160},{160,128},{192,224},{224,1... | collective-permute-start | bytes 393224 | tf_op jit(solution)/shard_map/ppermute | solution.py:100
  127.0 9.1 %collective-permute-start.16 = (bf16[128,512]{1,0:T(8,128)(2,1)S(1)}, bf16[128,512]{1,0:T(8,128)(2,1)S(1)}, u32[]{:S(2)}, u32[]{:S(2)}) collective-permute-start(bf16[128,512]{1,0:T(8,128)(2,1)S(1)} %get-tuple-element.223), channel_id=1, source_target_pairs={{0,64},{32,96},{64,0},{96,32},{128,192},{160,224},{192,128},{224,1... | collective-permute-start | bytes 393224 | tf_op jit(solution)/shard_map/ppermute | solution.py:100
  127.1 10.8 %collective-permute-start.17 = (bf16[128,512]{1,0:T(8,128)(2,1)S(1)}, bf16[128,512]{1,0:T(8,128)(2,1)S(1)}, u32[]{:S(2)}, u32[]{:S(2)}) collective-permute-start(bf16[128,512]{1,0:T(8,128)(2,1)S(1)} %get-tuple-element.223), channel_id=1, source_target_pairs={{0,96},{32,64},{64,32},{96,0},{128,224},{160,192},{192,160},{224,1... | collective-permute-start | bytes 393224 | tf_op jit(solution)/shard_map/ppermute | solution.py:100
  129.1 11.2 %collective-permute-start.18 = (bf16[128,512]{1,0:T(8,128)(2,1)S(1)}, bf16[128,512]{1,0:T(8,128)(2,1)S(1)}, u32[]{:S(2)}, u32[]{:S(2)}) collective-permute-start(bf16[128,512]{1,0:T(8,128)(2,1)S(1)} %get-tuple-element.223), channel_id=1, source_target_pairs={{0,128},{32,160},{64,192},{96,224},{128,0},{160,32},{192,64},{224,... | collective-permute-start | bytes 393224 | tf_op jit(solution)/shard_map/ppermute | solution.py:100
  130.7 10.3 %collective-permute-start.19 = (bf16[128,512]{1,0:T(8,128)(2,1)S(1)}, bf16[128,512]{1,0:T(8,128)(2,1)S(1)}, u32[]{:S(2)}, u32[]{:S(2)}) collective-permute-start(bf16[128,512]{1,0:T(8,128)(2,1)S(1)} %get-tuple-element.223), channel_id=1, source_target_pairs={{0,160},{32,128},{64,224},{96,192},{128,32},{160,0},{192,96},{224,... | collective-permute-start | bytes 393224 | tf_op jit(solution)/shard_map/ppermute | solution.py:100
  133.9 10.8 %collective-permute-start.20 = (bf16[128,512]{1,0:T(8,128)(2,1)S(1)}, bf16[128,512]{1,0:T(8,128)(2,1)S(1)}, u32[]{:S(2)}, u32[]{:S(2)}) collective-permute-start(bf16[128,512]{1,0:T(8,128)(2,1)S(1)} %get-tuple-element.223), channel_id=1, source_target_pairs={{0,192},{32,224},{64,128},{96,160},{128,64},{160,96},{192,0},{224,... | collective-permute-start | bytes 393224 | tf_op jit(solution)/shard_map/ppermute | solution.py:100
  136.8 8.6 %collective-permute-start.21 = (bf16[128,512]{1,0:T(8,128)(2,1)S(1)}, bf16[128,512]{1,0:T(8,128)(2,1)S(1)}, u32[]{:S(2)}, u32[]{:S(2)}) collective-permute-start(bf16[128,512]{1,0:T(8,128)(2,1)S(1)} %get-tuple-element.223), channel_id=1, source_target_pairs={{0,224},{32,192},{64,160},{96,128},{128,96},{160,64},{192,32},{224... | collective-permute-start | bytes 393224 | tf_op jit(solution)/shard_map/ppermute | solution.py:100
  150.3 9.1 %collective-permute-start.2 = (bf16[128,64]{1,0:T(8,128)(2,1)}, bf16[128,64]{1,0:T(8,128)(2,1)}, u32[]{:S(2)}, u32[]{:S(2)}) collective-permute-start(bf16[128,64]{1,0:T(8,128)(2,1)} %get-tuple-element.448), channel_id=1, source_target_pairs={{0,1},{1,0},{2,3},{3,2},{4,5},{5,4},{6,7},{7,6},{8,9},{9,8},{10,11... | collective-permute-start | bytes 49160 | tf_op jit(solution)/shard_map/while/body/eval_jaxpr/ppermute | solution.py:100
  152.7 6.8 %collective-permute-start.3 = (bf16[128,64]{1,0:T(8,128)(2,1)}, bf16[128,64]{1,0:T(8,128)(2,1)}, u32[]{:S(2)}, u32[]{:S(2)}) collective-permute-start(bf16[128,64]{1,0:T(8,128)(2,1)} %get-tuple-element.449), channel_id=1, source_target_pairs={{0,31},{1,2},{2,1},{3,4},{4,3},{5,6},{6,5},{7,8},{8,7},{9,10},{10,... | collective-permute-start | bytes 49160 | tf_op jit(solution)/shard_map/while/body/eval_jaxpr/ppermute | solution.py:100
  163.4 7.9 %collective-permute-start.2 = (bf16[128,64]{1,0:T(8,128)(2,1)}, bf16[128,64]{1,0:T(8,128)(2,1)}, u32[]{:S(2)}, u32[]{:S(2)}) collective-permute-start(bf16[128,64]{1,0:T(8,128)(2,1)} %get-tuple-element.448), channel_id=1, source_target_pairs={{0,1},{1,0},{2,3},{3,2},{4,5},{5,4},{6,7},{7,6},{8,9},{9,8},{10,11... | collective-permute-start | bytes 49160 | tf_op jit(solution)/shard_map/while/body/eval_jaxpr/ppermute | solution.py:100
  175.7 7.4 %collective-permute-start.2 = (bf16[128,64]{1,0:T(8,128)(2,1)}, bf16[128,64]{1,0:T(8,128)(2,1)}, u32[]{:S(2)}, u32[]{:S(2)}) collective-permute-start(bf16[128,64]{1,0:T(8,128)(2,1)} %get-tuple-element.448), channel_id=1, source_target_pairs={{0,1},{1,0},{2,3},{3,2},{4,5},{5,4},{6,7},{7,6},{8,9},{9,8},{10,11... | collective-permute-start | bytes 49160 | tf_op jit(solution)/shard_map/while/body/eval_jaxpr/ppermute | solution.py:100
  177.9 5.3 %collective-permute-start.3 = (bf16[128,64]{1,0:T(8,128)(2,1)}, bf16[128,64]{1,0:T(8,128)(2,1)}, u32[]{:S(2)}, u32[]{:S(2)}) collective-permute-start(bf16[128,64]{1,0:T(8,128)(2,1)} %get-tuple-element.449), channel_id=1, source_target_pairs={{0,31},{1,2},{2,1},{3,4},{4,3},{5,6},{6,5},{7,8},{8,7},{9,10},{10,... | collective-permute-start | bytes 49160 | tf_op jit(solution)/shard_map/while/body/eval_jaxpr/ppermute | solution.py:100
  187.1 7.3 %collective-permute-start.2 = (bf16[128,64]{1,0:T(8,128)(2,1)}, bf16[128,64]{1,0:T(8,128)(2,1)}, u32[]{:S(2)}, u32[]{:S(2)}) collective-permute-start(bf16[128,64]{1,0:T(8,128)(2,1)} %get-tuple-element.448), channel_id=1, source_target_pairs={{0,1},{1,0},{2,3},{3,2},{4,5},{5,4},{6,7},{7,6},{8,9},{9,8},{10,11... | collective-permute-start | bytes 49160 | tf_op jit(solution)/shard_map/while/body/eval_jaxpr/ppermute | solution.py:100
  198.3 7.4 %collective-permute-start.2 = (bf16[128,64]{1,0:T(8,128)(2,1)}, bf16[128,64]{1,0:T(8,128)(2,1)}, u32[]{:S(2)}, u32[]{:S(2)}) collective-permute-start(bf16[128,64]{1,0:T(8,128)(2,1)} %get-tuple-element.448), channel_id=1, source_target_pairs={{0,1},{1,0},{2,3},{3,2},{4,5},{5,4},{6,7},{7,6},{8,9},{9,8},{10,11... | collective-permute-start | bytes 49160 | tf_op jit(solution)/shard_map/while/body/eval_jaxpr/ppermute | solution.py:100
  200.5 5.3 %collective-permute-start.3 = (bf16[128,64]{1,0:T(8,128)(2,1)}, bf16[128,64]{1,0:T(8,128)(2,1)}, u32[]{:S(2)}, u32[]{:S(2)}) collective-permute-start(bf16[128,64]{1,0:T(8,128)(2,1)} %get-tuple-element.449), channel_id=1, source_target_pairs={{0,31},{1,2},{2,1},{3,4},{4,3},{5,6},{6,5},{7,8},{8,7},{9,10},{10,... | collective-permute-start | bytes 49160 | tf_op jit(solution)/shard_map/while/body/eval_jaxpr/ppermute | solution.py:100
  209.7 7.2 %collective-permute-start.2 = (bf16[128,64]{1,0:T(8,128)(2,1)}, bf16[128,64]{1,0:T(8,128)(2,1)}, u32[]{:S(2)}, u32[]{:S(2)}) collective-permute-start(bf16[128,64]{1,0:T(8,128)(2,1)} %get-tuple-element.448), channel_id=1, source_target_pairs={{0,1},{1,0},{2,3},{3,2},{4,5},{5,4},{6,7},{7,6},{8,9},{9,8},{10,11... | collective-permute-start | bytes 49160 | tf_op jit(solution)/shard_map/while/body/eval_jaxpr/ppermute | solution.py:100
  (23 other events, 182.9 us)

commit v2 on v0

--- a/solution.py
+++ b/solution.py
@@ -117,6 +117,59 @@
     return own + jnp.dot(faces, x_lift, preferred_element_type=jnp.float32)
 
 
+def two_steps(field, fixed, scale, reaction, weights, x_lift, ny, nz, last_is_slope):
+    high_cols = slice((NP - 1) * FACE, NP * FACE)
+    low_cols = slice(0, FACE)
+    odd = lax.axis_index("gx") % 2 == 1
+    on_chip = lambda i: i ^ 1
+    far = lambda i: i + 1 if i % 2 else i - 1
+    rounded = field.astype(jnp.bfloat16)
+    high = rounded[:, high_cols]
+    low = rounded[:, low_cols]
+    chip_faces = swapped(jnp.where(odd, low, high), "gx", on_chip)
+    own, _ = local_terms(field, reaction, weights, ny, nz)
+    part_high = fixed[:, high_cols] + scale * own[:, high_cols]
+    part_low = fixed[:, low_cols] + scale * own[:, low_cols]
+    far_send = jnp.where(
+        odd,
+        jnp.concatenate([high.astype(jnp.float32), part_high, chip_faces.astype(jnp.float32)], -1),
+        jnp.concatenate([low.astype(jnp.float32), part_low, chip_faces.astype(jnp.float32)], -1),
+    )
+    far_got = swapped(far_send, "gx", far)
+    far_face = far_got[:, :FACE]
+    far_part = far_got[:, FACE : 2 * FACE]
+    far_second = far_got[:, 2 * FACE :].astype(jnp.bfloat16)
+    chip_send = jnp.where(
+        odd,
+        jnp.concatenate([part_low, far_face], -1),
+        jnp.concatenate([part_high, far_face], -1),
+    )
+    chip_got = swapped(chip_send, "gx", on_chip)
+    chip_part = chip_got[:, :FACE]
+    chip_second = chip_got[:, FACE:].astype(jnp.bfloat16)
+    far_face = far_face.astype(jnp.bfloat16)
+    below_1 = jnp.where(odd, chip_faces, far_face)
+    above_1 = jnp.where(odd, far_face, chip_faces)
+    below_part = jnp.where(odd, chip_part, far_part)
+    above_part = jnp.where(odd, far_part, chip_part)
+    below_2 = jnp.where(odd, chip_second, far_second)
+    above_2 = jnp.where(odd, far_second, chip_second)
+    x_terms = jnp.dot(jnp.concatenate([below_1, above_1], -1), x_lift, preferred_element_type=jnp.float32)
+    first = fixed + scale * (own + x_terms)
+    below_plane = below_part + scale * jnp.dot(
+        jnp.concatenate([below_2, low], -1), x_lift[:, high_cols], preferred_element_type=jnp.float32
+    )
+    above_plane = above_part + scale * jnp.dot(
+        jnp.concatenate([high, above_2], -1), x_lift[:, low_cols], preferred_element_type=jnp.float32
+    )
+    own_1, _ = local_terms(first, reaction, weights, ny, nz)
+    faces_1 = jnp.concatenate([below_plane.astype(jnp.bfloat16), above_plane.astype(jnp.bfloat16)], -1)
+    applied = own_1 + jnp.dot(faces_1, x_lift, preferred_element_type=jnp.float32)
+    if last_is_slope:
+        return applied
+    return fixed + scale * applied
+
+
 def gather_nodes(rows):
     nodes = lax.axis_size("node")
     me = lax.axis_index("node")
@@ -141,8 +194,8 @@
     start = start_state.reshape((rows, points))
     reaction = reaction_rates.reshape((rows, points))
     states = node_states.reshape((rows, points))
+    slopes = apply_operator(states, reaction, weights, x_lift, ny, nz)
     for sweep_index in range(SWEEPS):
-        slopes = apply_operator(states, reaction, weights, x_lift, ny, nz)
         slope_rows = slopes.astype(jnp.bfloat16)
         received, sources = gather_nodes(slope_rows)
         source_weights = jnp.take(own_weights[0], sources)
@@ -150,9 +203,18 @@
         running_sum = jnp.sum(source_weights[:, None, None] * stacked, axis=0)
         fixed_part = start + time_step * running_sum - own_scale * slopes
         iterate = start + time_step * running_sum
-        for inner_step in range(INNER - 1):
+        more = sweep_index + 1 < SWEEPS
+        steps = INNER - 1 + (1 if more else 0)
+        if steps % 2:
             iterate = fixed_part + own_scale * apply_operator(iterate, reaction, weights, x_lift, ny, nz)
-        states = iterate
+            steps -= 1
+        for pair in range(steps // 2):
+            last = more and pair == steps // 2 - 1
+            iterate = two_steps(iterate, fixed_part, own_scale, reaction, weights, x_lift, ny, nz, last)
+        if more:
+            slopes = iterate
+        else:
+            states = iterate
     return states.reshape(shape)
 
 

time: 177 us -> 176 us (level)
  matrix products: 23.5 us -> 34.6 us
  starting transfers between devices: 62.1 us -> 52.5 us
  waiting for transfers between devices: 65 us -> 58.9 us
  other arithmetic: 12 us -> 16.5 us
    dot_general x0 -> x24, matrix products: none -> 21.6 us  [the longest x6 5.54 us: two_steps(): jnp.dot(faces_1, x_lift, preferred_element_type=jnp.float32)]
    dot_general x14 -> x2, matrix products: 12.6 us -> 2.09 us  [apply_operator(): return own + jnp.dot(faces, x_lift, preferred_element_type=jnp.float32)]
    ppermute x42 -> x36, starting transfers between devices: 62.1 us -> 52.5 us  [swapped(): lax.ppermute(array, axis, [(i, partner(i) % devices) for i in range(devic...]
    ppermute x42 -> x36, waiting for transfers between devices: 65 us -> 58.9 us  [swapped(): lax.ppermute(array, axis, [(i, partner(i) % devices) for i in range(devic...]
    add x0 -> x6, other arithmetic: none -> 4.65 us  [two_steps(): part_low = fixed[:, low_cols] + scale * own[:, low_cols]]
    select_n x0 -> x18, other arithmetic: none -> 1.82 us  [the longest x6 0.81 us: two_steps(): jnp.where(odd, jnp.concatenate([high.astype(jnp.float32), part_high, chip...]
    unnamed x76 -> x80, local copies, waits for them, and re-layouts: 4.42 us -> 4.55 us
  transfers between devices with their start and end apart: 42 -> 36, of which waited for: 29 -> 18; matrix products, arithmetic and copies ran while one was open for 15% -> 15% of each run, Pallas kernels for 0% -> 0%
where the time goes in v2:
time: 176 us
  waiting for transfers between devices  58.9 us (33%)
  starting transfers between devices  52.5 us (30%)
  matrix products  34.6 us (20%)
  other arithmetic  16.5 us (9%)
  local copies, waits for them, and re-layouts  11.3 us (6%)
  between operations  2.15 us (1%)
    ppermute x36, waiting for transfers between devices, swapped(): lax.ppermute(array, axis, [(i, partner(i) % devices) for i in range(devic...  58.9 us
    ppermute x36, starting transfers between devices, swapped(): lax.ppermute(array, axis, [(i, partner(i) % devices) for i in range(devic...  52.5 us
    dot_general x14, matrix products, local_terms(): jnp.dot(stacked, weights, preferred_element_type=jnp.float32)  8.93 us
    dot_general x6, matrix products, two_steps(): jnp.dot(faces_1, x_lift, preferred_element_type=jnp.float32)  5.54 us
    dot_general x6, matrix products, two_steps(): jnp.dot(jnp.concatenate([below_1, above_1], -1), x_lift, preferred_elemen...  5.47 us
    dot_general x6, matrix products, two_steps(): jnp.dot(jnp.concatenate([below_2, low], -1), x_lift[:, high_cols], prefer...  5.31 us
    dot_general x6, matrix products, two_steps(): jnp.dot(jnp.concatenate([high, above_2], -1), x_lift[:, low_cols], prefer...  5.25 us
    add x6, other arithmetic, two_steps(): part_low = fixed[:, low_cols] + scale * own[:, low_cols]  4.65 us
  transfers between devices with their start and end apart: 36, of which 18 were waited for; matrix products, arithmetic and copies ran while one was open for 15% of the time, Pallas kernels for 0%

profile of v2, /device:TPU:1, one launch (start us, length us, event | category | flops | bytes accessed | tf_op | source)
XLA Modules:
  0.0 175.8 jit_solution(8131397385936689172)
XLA Ops:
  0.0 1.1 convert_bitcast_fusion
  1.8 3.2 %collective-permute-start = (bf16[128,64]{1,0:T(8,128)(2,1)}, bf16[128,64]{1,0:T(8,128)(2,1)}, u32[]{:S(2)}, u32[]{:S(2)}) collective-permute-start(bf16[128,64]{1,0:T(8,128)(2,1)} %get-tuple-element.226), channel_id=1, source_target_pairs={{0,1},{1,0},{2,3},{3,2},{4,5},{5,4},{6,7},{7,6},{8,9},{9,8},{10,11... | collective-permute-start | bytes 49160 | tf_op jit(solution)/shard_map/ppermute | solution.py:100
  16.2 1.2 fusion.3
  18.2 2.3 %convolution_subtract_fusion.6 = f32[128,512]{1,0:T(8,128)} fusion(f32[128,512]{1,0:T(8,128)S(1)} %copy-done.4, bf16[128,2560]{1,0:T(8,128)(2,1)} %constant_dynamic-update-slice_fusion, bf16[2560,512]{1,0:T(8,128)(2,1)S(1)} %fusion), kind=kOutput, calls=%fused_computation.55 | convolution fusion | flops 335609856 | bytes 3801088 | tf_op jit(solution)/shard_map/dot_general | solution.py:94
  23.3 1.2 constant_dynamic-update-slice_fusion.13
  24.9 1.3 collective-permute-start.3
  27.3 2.9 %collective-permute-start.5 = (bf16[128,512]{1,0:T(8,128)(2,1)S(1)}, bf16[128,512]{1,0:T(8,128)(2,1)S(1)}, u32[]{:S(2)}, u32[]{:S(2)}) collective-permute-start(bf16[128,512]{1,0:T(8,128)(2,1)S(1)} %get-tuple-element.31), channel_id=1, source_target_pairs={{0,128},{32,160},{64,192},{96,224},{128,0},{160,32},{192,64},{224,... | collective-permute-start | bytes 393224 | tf_op jit(solution)/shard_map/ppermute | solution.py:100
  30.3 2.7 %collective-permute-start.7 = (bf16[128,512]{1,0:T(8,128)(2,1)S(1)}, bf16[128,512]{1,0:T(8,128)(2,1)S(1)}, u32[]{:S(2)}, u32[]{:S(2)}) collective-permute-start(bf16[128,512]{1,0:T(8,128)(2,1)S(1)} %get-tuple-element.31), channel_id=1, source_target_pairs={{0,192},{32,224},{64,128},{96,160},{128,64},{160,96},{192,0},{224,... | collective-permute-start | bytes 393224 | tf_op jit(solution)/shard_map/ppermute | solution.py:100
  34.1 2.9 %collective-permute-done.6 = bf16[128,512]{1,0:T(8,128)(2,1)S(1)} collective-permute-done((bf16[128,512]{1,0:T(8,128)(2,1)S(1)}, bf16[128,512]{1,0:T(8,128)(2,1)S(1)}, u32[]{:S(2)}, u32[]{:S(2)}) %collective-permute-start.6) | collective-permute-done | bytes 131104 | tf_op jit(solution)/shard_map/ppermute | solution.py:100
  37.0 3.6 %collective-permute-done.8 = bf16[128,512]{1,0:T(8,128)(2,1)S(1)} collective-permute-done((bf16[128,512]{1,0:T(8,128)(2,1)S(1)}, bf16[128,512]{1,0:T(8,128)(2,1)S(1)}, u32[]{:S(2)}, u32[]{:S(2)}) %collective-permute-start.8) | collective-permute-done | bytes 131104 | tf_op jit(solution)/shard_map/ppermute | solution.py:100
  41.9 8.4 %collective-permute-start.10 = (bf16[128,64]{1,0:T(8,128)(2,1)S(1)}, bf16[128,64]{1,0:T(8,128)(2,1)S(1)}, u32[]{:S(2)}, u32[]{:S(2)}) collective-permute-start(bf16[128,64]{1,0:T(8,128)(2,1)S(1)} %get-tuple-element.217), channel_id=1, source_target_pairs={{0,31},{1,2},{2,1},{3,4},{4,3},{5,6},{6,5},{7,8},{8,7},{9,10},{10,... | collective-permute-start | bytes 49160 | tf_op jit(solution)/shard_map/ppermute | solution.py:100
  53.1 4.2 %collective-permute-start.11 = (bf16[128,64]{1,0:T(8,128)(2,1)S(1)}, bf16[128,64]{1,0:T(8,128)(2,1)S(1)}, u32[]{:S(2)}, u32[]{:S(2)}) collective-permute-start(bf16[128,64]{1,0:T(8,128)(2,1)S(1)} %get-tuple-element.196), channel_id=1, source_target_pairs={{0,1},{1,0},{2,3},{3,2},{4,5},{5,4},{6,7},{7,6},{8,9},{9,8},{10,11... | collective-permute-start | bytes 49160 | tf_op jit(solution)/shard_map/ppermute | solution.py:100
  59.1 5.9 %collective-permute-done.12 = f32[128,192]{1,0:T(8,128)S(1)} collective-permute-done((f32[128,192]{1,0:T(8,128)S(1)}, f32[128,192]{1,0:T(8,128)S(1)}, u32[]{:S(2)}, u32[]{:S(2)}) %collective-permute-start.12) | collective-permute-done | bytes 98336 | tf_op jit(solution)/shard_map/ppermute | solution.py:100
  65.1 2.4 %collective-permute-start.13 = (f32[128,128]{1,0:T(8,128)S(1)}, f32[128,128]{1,0:T(8,128)S(1)}, u32[]{:S(2)}, u32[]{:S(2)}) collective-permute-start(f32[128,128]{1,0:T(8,128)S(1)} %maximum_select_fusion), channel_id=1, source_target_pairs={{0,1},{1,0},{2,3},{3,2},{4,5},{5,4},{6,7},{7,6},{8,9},{9,8},{10,11... | collective-permute-start | bytes 196616 | tf_op jit(solution)/shard_map/ppermute | solution.py:100
  75.4 5.9 %collective-permute-done.15 = f32[128,192]{1,0:T(8,128)S(1)} collective-permute-done((f32[128,192]{1,0:T(8,128)S(1)}, f32[128,192]{1,0:T(8,128)S(1)}, u32[]{:S(2)}, u32[]{:S(2)}) %collective-permute-start.15) | collective-permute-done | bytes 98336 | tf_op jit(solution)/shard_map/ppermute | solution.py:100
  81.4 2.4 %collective-permute-start.16 = (f32[128,128]{1,0:T(8,128)S(1)}, f32[128,128]{1,0:T(8,128)S(1)}, u32[]{:S(2)}, u32[]{:S(2)}) collective-permute-start(f32[128,128]{1,0:T(8,128)S(1)} %maximum_select_fusion.1), channel_id=1, source_target_pairs={{0,1},{1,0},{2,3},{3,2},{4,5},{5,4},{6,7},{7,6},{8,9},{9,8},{10,11... | collective-permute-start | bytes 196616 | tf_op jit(solution)/shard_map/ppermute | solution.py:100
  91.7 5.9 %collective-permute-done.18 = f32[128,192]{1,0:T(8,128)S(1)} collective-permute-done((f32[128,192]{1,0:T(8,128)S(1)}, f32[128,192]{1,0:T(8,128)S(1)}, u32[]{:S(2)}, u32[]{:S(2)}) %collective-permute-start.18) | collective-permute-done | bytes 98336 | tf_op jit(solution)/shard_map/ppermute | solution.py:100
  97.7 2.3 %collective-permute-start.19 = (f32[128,128]{1,0:T(8,128)S(1)}, f32[128,128]{1,0:T(8,128)S(1)}, u32[]{:S(2)}, u32[]{:S(2)}) collective-permute-start(f32[128,128]{1,0:T(8,128)S(1)} %maximum_select_fusion.2), channel_id=1, source_target_pairs={{0,1},{1,0},{2,3},{3,2},{4,5},{5,4},{6,7},{7,6},{8,9},{9,8},{10,11... | collective-permute-start | bytes 196616 | tf_op jit(solution)/shard_map/ppermute | solution.py:100
  104.8 1.2 collective-permute-start.20
  106.1 1.5 collective-permute-start.22
  107.7 3.7 %collective-permute-start.24 = (bf16[128,512]{1,0:T(8,128)(2,1)S(1)}, bf16[128,512]{1,0:T(8,128)(2,1)S(1)}, u32[]{:S(2)}, u32[]{:S(2)}) collective-permute-start(bf16[128,512]{1,0:T(8,128)(2,1)S(1)} %get-tuple-element.17), channel_id=1, source_target_pairs={{0,160},{32,128},{64,224},{96,192},{128,32},{160,0},{192,96},{224,... | collective-permute-start | bytes 393224 | tf_op jit(solution)/shard_map/ppermute | solution.py:100
  111.6 4.6 %collective-permute-done.21 = bf16[128,512]{1,0:T(8,128)(2,1)S(1)} collective-permute-done((bf16[128,512]{1,0:T(8,128)(2,1)S(1)}, bf16[128,512]{1,0:T(8,128)(2,1)S(1)}, u32[]{:S(2)}, u32[]{:S(2)}) %collective-permute-start.21) | collective-permute-done | bytes 131104 | tf_op jit(solution)/shard_map/ppermute | solution.py:100
  116.2 2.6 %collective-permute-done.23 = bf16[128,512]{1,0:T(8,128)(2,1)S(1)} collective-permute-done((bf16[128,512]{1,0:T(8,128)(2,1)S(1)}, bf16[128,512]{1,0:T(8,128)(2,1)S(1)}, u32[]{:S(2)}, u32[]{:S(2)}) %collective-permute-start.23) | collective-permute-done | bytes 131104 | tf_op jit(solution)/shard_map/ppermute | solution.py:100
  118.9 3.6 %collective-permute-done.25 = bf16[128,512]{1,0:T(8,128)(2,1)S(1)} collective-permute-done((bf16[128,512]{1,0:T(8,128)(2,1)S(1)}, bf16[128,512]{1,0:T(8,128)(2,1)S(1)}, u32[]{:S(2)}, u32[]{:S(2)}) %collective-permute-start.25) | collective-permute-done | bytes 131104 | tf_op jit(solution)/shard_map/ppermute | solution.py:100
  123.9 3.2 %collective-permute-start.27 = (bf16[128,64]{1,0:T(8,128)(2,1)S(1)}, bf16[128,64]{1,0:T(8,128)(2,1)S(1)}, u32[]{:S(2)}, u32[]{:S(2)}) collective-permute-start(bf16[128,64]{1,0:T(8,128)(2,1)S(1)} %get-tuple-element.128), channel_id=1, source_target_pairs={{0,1},{1,0},{2,3},{3,2},{4,5},{5,4},{6,7},{7,6},{8,9},{9,8},{10,11... | collective-permute-start | bytes 49160 | tf_op jit(solution)/shard_map/ppermute | solution.py:100
  128.9 5.9 %collective-permute-done.28 = f32[128,192]{1,0:T(8,128)S(1)} collective-permute-done((f32[128,192]{1,0:T(8,128)S(1)}, f32[128,192]{1,0:T(8,128)S(1)}, u32[]{:S(2)}, u32[]{:S(2)}) %collective-permute-start.28) | collective-permute-done | bytes 98336 | tf_op jit(solution)/shard_map/ppermute | solution.py:100
  134.9 2.2 %collective-permute-start.29 = (f32[128,128]{1,0:T(8,128)S(1)}, f32[128,128]{1,0:T(8,128)S(1)}, u32[]{:S(2)}, u32[]{:S(2)}) collective-permute-start(f32[128,128]{1,0:T(8,128)S(1)} %maximum_select_fusion.3), channel_id=1, source_target_pairs={{0,1},{1,0},{2,3},{3,2},{4,5},{5,4},{6,7},{7,6},{8,9},{9,8},{10,11... | collective-permute-start | bytes 196616 | tf_op jit(solution)/shard_map/ppermute | solution.py:100
  145.1 5.9 %collective-permute-done.31 = f32[128,192]{1,0:T(8,128)S(1)} collective-permute-done((f32[128,192]{1,0:T(8,128)S(1)}, f32[128,192]{1,0:T(8,128)S(1)}, u32[]{:S(2)}, u32[]{:S(2)}) %collective-permute-start.31) | collective-permute-done | bytes 98336 | tf_op jit(solution)/shard_map/ppermute | solution.py:100
  151.1 2.3 %collective-permute-start.32 = (f32[128,128]{1,0:T(8,128)S(1)}, f32[128,128]{1,0:T(8,128)S(1)}, u32[]{:S(2)}, u32[]{:S(2)}) collective-permute-start(f32[128,128]{1,0:T(8,128)S(1)} %maximum_select_fusion.4), channel_id=1, source_target_pairs={{0,1},{1,0},{2,3},{3,2},{4,5},{5,4},{6,7},{7,6},{8,9},{9,8},{10,11... | collective-permute-start | bytes 196616 | tf_op jit(solution)/shard_map/ppermute | solution.py:100
  161.4 5.9 %collective-permute-done.34 = f32[128,192]{1,0:T(8,128)S(1)} collective-permute-done((f32[128,192]{1,0:T(8,128)S(1)}, f32[128,192]{1,0:T(8,128)S(1)}, u32[]{:S(2)}, u32[]{:S(2)}) %collective-permute-start.34) | collective-permute-done | bytes 98336 | tf_op jit(solution)/shard_map/ppermute | solution.py:100
  167.3 2.4 %collective-permute-start.35 = (f32[128,128]{1,0:T(8,128)S(1)}, f32[128,128]{1,0:T(8,128)S(1)}, u32[]{:S(2)}, u32[]{:S(2)}) collective-permute-start(f32[128,128]{1,0:T(8,128)S(1)} %maximum_select_fusion.5), channel_id=1, source_target_pairs={{0,1},{1,0},{2,3},{3,2},{4,5},{5,4},{6,7},{7,6},{8,9},{9,8},{10,11... | collective-permute-start | bytes 196616 | tf_op jit(solution)/shard_map/ppermute | solution.py:100
  174.2 1.6 fusion.5
  (350 shorter events, 67.2 us)
Async XLA Ops:
  1.8 20.7 %collective-permute-start = (bf16[128,64]{1,0:T(8,128)(2,1)}, bf16[128,64]{1,0:T(8,128)(2,1)}, u32[]{:S(2)}, u32[]{:S(2)}) collective-permute-start(bf16[128,64]{1,0:T(8,128)(2,1)} %get-tuple-element.226), channel_id=1, source_target_pairs={{0,1},{1,0},{2,3},{3,2},{4,5},{5,4},{6,7},{7,6},{8,9},{9,8},{10,11... | collective-permute-start | bytes 49160 | tf_op jit(solution)/shard_map/ppermute | solution.py:100
  5.1 17.5 %collective-permute-start.1 = (bf16[128,64]{1,0:T(8,128)(2,1)}, bf16[128,64]{1,0:T(8,128)(2,1)}, u32[]{:S(2)}, u32[]{:S(2)}) collective-permute-start(bf16[128,64]{1,0:T(8,128)(2,1)} %get-tuple-element.227), channel_id=1, source_target_pairs={{0,31},{1,2},{2,1},{3,4},{4,3},{5,6},{6,5},{7,8},{8,7},{9,10},{10,... | collective-permute-start | bytes 49160 | tf_op jit(solution)/shard_map/ppermute | solution.py:100
  24.5 5.7 %collective-permute-start.2 = (bf16[128,512]{1,0:T(8,128)(2,1)S(1)}, bf16[128,512]{1,0:T(8,128)(2,1)S(1)}, u32[]{:S(2)}, u32[]{:S(2)}) collective-permute-start(bf16[128,512]{1,0:T(8,128)(2,1)S(1)} %get-tuple-element.31), channel_id=1, source_target_pairs={{0,32},{32,0},{64,96},{96,64},{128,160},{160,128},{192,224},{224,1... | collective-permute-start | bytes 393224 | tf_op jit(solution)/shard_map/ppermute | solution.py:100
  24.9 8.1 %collective-permute-start.3 = (bf16[128,512]{1,0:T(8,128)(2,1)S(1)}, bf16[128,512]{1,0:T(8,128)(2,1)S(1)}, u32[]{:S(2)}, u32[]{:S(2)}) collective-permute-start(bf16[128,512]{1,0:T(8,128)(2,1)S(1)} %get-tuple-element.31), channel_id=1, source_target_pairs={{0,64},{32,96},{64,0},{96,32},{128,192},{160,224},{192,128},{224,1... | collective-permute-start | bytes 393224 | tf_op jit(solution)/shard_map/ppermute | solution.py:100
  26.2 7.8 %collective-permute-start.4 = (bf16[128,512]{1,0:T(8,128)(2,1)S(1)}, bf16[128,512]{1,0:T(8,128)(2,1)S(1)}, u32[]{:S(2)}, u32[]{:S(2)}) collective-permute-start(bf16[128,512]{1,0:T(8,128)(2,1)S(1)} %get-tuple-element.31), channel_id=1, source_target_pairs={{0,96},{32,64},{64,32},{96,0},{128,224},{160,192},{192,160},{224,1... | collective-permute-start | bytes 393224 | tf_op jit(solution)/shard_map/ppermute | solution.py:100
  27.3 6.8 %collective-permute-start.5 = (bf16[128,512]{1,0:T(8,128)(2,1)S(1)}, bf16[128,512]{1,0:T(8,128)(2,1)S(1)}, u32[]{:S(2)}, u32[]{:S(2)}) collective-permute-start(bf16[128,512]{1,0:T(8,128)(2,1)S(1)} %get-tuple-element.31), channel_id=1, source_target_pairs={{0,128},{32,160},{64,192},{96,224},{128,0},{160,32},{192,64},{224,... | collective-permute-start | bytes 393224 | tf_op jit(solution)/shard_map/ppermute | solution.py:100
  30.2 6.7 %collective-permute-start.6 = (bf16[128,512]{1,0:T(8,128)(2,1)S(1)}, bf16[128,512]{1,0:T(8,128)(2,1)S(1)}, u32[]{:S(2)}, u32[]{:S(2)}) collective-permute-start(bf16[128,512]{1,0:T(8,128)(2,1)S(1)} %get-tuple-element.31), channel_id=1, source_target_pairs={{0,160},{32,128},{64,224},{96,192},{128,32},{160,0},{192,96},{224,... | collective-permute-start | bytes 393224 | tf_op jit(solution)/shard_map/ppermute | solution.py:100
  30.3 6.7 %collective-permute-start.7 = (bf16[128,512]{1,0:T(8,128)(2,1)S(1)}, bf16[128,512]{1,0:T(8,128)(2,1)S(1)}, u32[]{:S(2)}, u32[]{:S(2)}) collective-permute-start(bf16[128,512]{1,0:T(8,128)(2,1)S(1)} %get-tuple-element.31), channel_id=1, source_target_pairs={{0,192},{32,224},{64,128},{96,160},{128,64},{160,96},{192,0},{224,... | collective-permute-start | bytes 393224 | tf_op jit(solution)/shard_map/ppermute | solution.py:100
  33.0 7.5 %collective-permute-start.8 = (bf16[128,512]{1,0:T(8,128)(2,1)S(1)}, bf16[128,512]{1,0:T(8,128)(2,1)S(1)}, u32[]{:S(2)}, u32[]{:S(2)}) collective-permute-start(bf16[128,512]{1,0:T(8,128)(2,1)S(1)} %get-tuple-element.31), channel_id=1, source_target_pairs={{0,224},{32,192},{64,160},{96,128},{128,96},{160,64},{192,32},{224... | collective-permute-start | bytes 393224 | tf_op jit(solution)/shard_map/ppermute | solution.py:100
  41.9 10.0 %collective-permute-start.10 = (bf16[128,64]{1,0:T(8,128)(2,1)S(1)}, bf16[128,64]{1,0:T(8,128)(2,1)S(1)}, u32[]{:S(2)}, u32[]{:S(2)}) collective-permute-start(bf16[128,64]{1,0:T(8,128)(2,1)S(1)} %get-tuple-element.217), channel_id=1, source_target_pairs={{0,31},{1,2},{2,1},{3,4},{4,3},{5,6},{6,5},{7,8},{8,7},{9,10},{10,... | collective-permute-start | bytes 49160 | tf_op jit(solution)/shard_map/ppermute | solution.py:100
  53.1 5.8 %collective-permute-start.11 = (bf16[128,64]{1,0:T(8,128)(2,1)S(1)}, bf16[128,64]{1,0:T(8,128)(2,1)S(1)}, u32[]{:S(2)}, u32[]{:S(2)}) collective-permute-start(bf16[128,64]{1,0:T(8,128)(2,1)S(1)} %get-tuple-element.196), channel_id=1, source_target_pairs={{0,1},{1,0},{2,3},{3,2},{4,5},{5,4},{6,7},{7,6},{8,9},{9,8},{10,11... | collective-permute-start | bytes 49160 | tf_op jit(solution)/shard_map/ppermute | solution.py:100
  59.0 6.0 %collective-permute-start.12 = (f32[128,192]{1,0:T(8,128)S(1)}, f32[128,192]{1,0:T(8,128)S(1)}, u32[]{:S(2)}, u32[]{:S(2)}) collective-permute-start(f32[128,192]{1,0:T(8,128)S(1)} %fusion.42), channel_id=1, source_target_pairs={{0,31},{1,2},{2,1},{3,4},{4,3},{5,6},{6,5},{7,8},{8,7},{9,10},{10,... | collective-permute-start | bytes 294920 | tf_op jit(solution)/shard_map/ppermute | solution.py:100
  65.1 3.3 %collective-permute-start.13 = (f32[128,128]{1,0:T(8,128)S(1)}, f32[128,128]{1,0:T(8,128)S(1)}, u32[]{:S(2)}, u32[]{:S(2)}) collective-permute-start(f32[128,128]{1,0:T(8,128)S(1)} %maximum_select_fusion), channel_id=1, source_target_pairs={{0,1},{1,0},{2,3},{3,2},{4,5},{5,4},{6,7},{7,6},{8,9},{9,8},{10,11... | collective-permute-start | bytes 196616 | tf_op jit(solution)/shard_map/ppermute | solution.py:100
  75.3 6.0 %collective-permute-start.15 = (f32[128,192]{1,0:T(8,128)S(1)}, f32[128,192]{1,0:T(8,128)S(1)}, u32[]{:S(2)}, u32[]{:S(2)}) collective-permute-start(f32[128,192]{1,0:T(8,128)S(1)} %fusion.41), channel_id=1, source_target_pairs={{0,31},{1,2},{2,1},{3,4},{4,3},{5,6},{6,5},{7,8},{8,7},{9,10},{10,... | collective-permute-start | bytes 294920 | tf_op jit(solution)/shard_map/ppermute | solution.py:100
  81.4 3.3 %collective-permute-start.16 = (f32[128,128]{1,0:T(8,128)S(1)}, f32[128,128]{1,0:T(8,128)S(1)}, u32[]{:S(2)}, u32[]{:S(2)}) collective-permute-start(f32[128,128]{1,0:T(8,128)S(1)} %maximum_select_fusion.1), channel_id=1, source_target_pairs={{0,1},{1,0},{2,3},{3,2},{4,5},{5,4},{6,7},{7,6},{8,9},{9,8},{10,11... | collective-permute-start | bytes 196616 | tf_op jit(solution)/shard_map/ppermute | solution.py:100
  89.5 2.0 %collective-permute-start.17 = (bf16[128,64]{1,0:T(8,128)(2,1)S(1)}, bf16[128,64]{1,0:T(8,128)(2,1)S(1)}, u32[]{:S(2)}, u32[]{:S(2)}) collective-permute-start(bf16[128,64]{1,0:T(8,128)(2,1)S(1)} %get-tuple-element.150), channel_id=1, source_target_pairs={{0,1},{1,0},{2,3},{3,2},{4,5},{5,4},{6,7},{7,6},{8,9},{9,8},{10,11... | collective-permute-start | bytes 49160 | tf_op jit(solution)/shard_map/ppermute | solution.py:100
  91.6 6.0 %collective-permute-start.18 = (f32[128,192]{1,0:T(8,128)S(1)}, f32[128,192]{1,0:T(8,128)S(1)}, u32[]{:S(2)}, u32[]{:S(2)}) collective-permute-start(f32[128,192]{1,0:T(8,128)S(1)} %fusion.40), channel_id=1, source_target_pairs={{0,31},{1,2},{2,1},{3,4},{4,3},{5,6},{6,5},{7,8},{8,7},{9,10},{10,... | collective-permute-start | bytes 294920 | tf_op jit(solution)/shard_map/ppermute | solution.py:100
  97.7 3.3 %collective-permute-start.19 = (f32[128,128]{1,0:T(8,128)S(1)}, f32[128,128]{1,0:T(8,128)S(1)}, u32[]{:S(2)}, u32[]{:S(2)}) collective-permute-start(f32[128,128]{1,0:T(8,128)S(1)} %maximum_select_fusion.2), channel_id=1, source_target_pairs={{0,1},{1,0},{2,3},{3,2},{4,5},{5,4},{6,7},{7,6},{8,9},{9,8},{10,11... | collective-permute-start | bytes 196616 | tf_op jit(solution)/shard_map/ppermute | solution.py:100
  104.8 6.6 %collective-permute-start.20 = (bf16[128,512]{1,0:T(8,128)(2,1)S(1)}, bf16[128,512]{1,0:T(8,128)(2,1)S(1)}, u32[]{:S(2)}, u32[]{:S(2)}) collective-permute-start(bf16[128,512]{1,0:T(8,128)(2,1)S(1)} %get-tuple-element.17), channel_id=1, source_target_pairs={{0,32},{32,0},{64,96},{96,64},{128,160},{160,128},{192,224},{224,1... | collective-permute-start | bytes 393224 | tf_op jit(solution)/shard_map/ppermute | solution.py:100
  106.1 10.1 %collective-permute-start.21 = (bf16[128,512]{1,0:T(8,128)(2,1)S(1)}, bf16[128,512]{1,0:T(8,128)(2,1)S(1)}, u32[]{:S(2)}, u32[]{:S(2)}) collective-permute-start(bf16[128,512]{1,0:T(8,128)(2,1)S(1)} %get-tuple-element.17), channel_id=1, source_target_pairs={{0,64},{32,96},{64,0},{96,32},{128,192},{160,224},{192,128},{224,1... | collective-permute-start | bytes 393224 | tf_op jit(solution)/shard_map/ppermute | solution.py:100
  106.1 10.1 %collective-permute-start.22 = (bf16[128,512]{1,0:T(8,128)(2,1)S(1)}, bf16[128,512]{1,0:T(8,128)(2,1)S(1)}, u32[]{:S(2)}, u32[]{:S(2)}) collective-permute-start(bf16[128,512]{1,0:T(8,128)(2,1)S(1)} %get-tuple-element.17), channel_id=1, source_target_pairs={{0,96},{32,64},{64,32},{96,0},{128,224},{160,192},{192,160},{224,1... | collective-permute-start | bytes 393224 | tf_op jit(solution)/shard_map/ppermute | solution.py:100
  107.6 11.3 %collective-permute-start.23 = (bf16[128,512]{1,0:T(8,128)(2,1)S(1)}, bf16[128,512]{1,0:T(8,128)(2,1)S(1)}, u32[]{:S(2)}, u32[]{:S(2)}) collective-permute-start(bf16[128,512]{1,0:T(8,128)(2,1)S(1)} %get-tuple-element.17), channel_id=1, source_target_pairs={{0,128},{32,160},{64,192},{96,224},{128,0},{160,32},{192,64},{224,... | collective-permute-start | bytes 393224 | tf_op jit(solution)/shard_map/ppermute | solution.py:100
  107.7 11.1 %collective-permute-start.24 = (bf16[128,512]{1,0:T(8,128)(2,1)S(1)}, bf16[128,512]{1,0:T(8,128)(2,1)S(1)}, u32[]{:S(2)}, u32[]{:S(2)}) collective-permute-start(bf16[128,512]{1,0:T(8,128)(2,1)S(1)} %get-tuple-element.17), channel_id=1, source_target_pairs={{0,160},{32,128},{64,224},{96,192},{128,32},{160,0},{192,96},{224,... | collective-permute-start | bytes 393224 | tf_op jit(solution)/shard_map/ppermute | solution.py:100
  111.4 11.1 %collective-permute-start.25 = (bf16[128,512]{1,0:T(8,128)(2,1)S(1)}, bf16[128,512]{1,0:T(8,128)(2,1)S(1)}, u32[]{:S(2)}, u32[]{:S(2)}) collective-permute-start(bf16[128,512]{1,0:T(8,128)(2,1)S(1)} %get-tuple-element.17), channel_id=1, source_target_pairs={{0,192},{32,224},{64,128},{96,160},{128,64},{160,96},{192,0},{224,... | collective-permute-start | bytes 393224 | tf_op jit(solution)/shard_map/ppermute | solution.py:100
  116.2 6.3 %collective-permute-start.26 = (bf16[128,512]{1,0:T(8,128)(2,1)S(1)}, bf16[128,512]{1,0:T(8,128)(2,1)S(1)}, u32[]{:S(2)}, u32[]{:S(2)}) collective-permute-start(bf16[128,512]{1,0:T(8,128)(2,1)S(1)} %get-tuple-element.17), channel_id=1, source_target_pairs={{0,224},{32,192},{64,160},{96,128},{128,96},{160,64},{192,32},{224... | collective-permute-start | bytes 393224 | tf_op jit(solution)/shard_map/ppermute | solution.py:100
  123.9 4.8 %collective-permute-start.27 = (bf16[128,64]{1,0:T(8,128)(2,1)S(1)}, bf16[128,64]{1,0:T(8,128)(2,1)S(1)}, u32[]{:S(2)}, u32[]{:S(2)}) collective-permute-start(bf16[128,64]{1,0:T(8,128)(2,1)S(1)} %get-tuple-element.128), channel_id=1, source_target_pairs={{0,1},{1,0},{2,3},{3,2},{4,5},{5,4},{6,7},{7,6},{8,9},{9,8},{10,11... | collective-permute-start | bytes 49160 | tf_op jit(solution)/shard_map/ppermute | solution.py:100
  128.8 6.0 %collective-permute-start.28 = (f32[128,192]{1,0:T(8,128)S(1)}, f32[128,192]{1,0:T(8,128)S(1)}, u32[]{:S(2)}, u32[]{:S(2)}) collective-permute-start(f32[128,192]{1,0:T(8,128)S(1)} %fusion.39), channel_id=1, source_target_pairs={{0,31},{1,2},{2,1},{3,4},{4,3},{5,6},{6,5},{7,8},{8,7},{9,10},{10,... | collective-permute-start | bytes 294920 | tf_op jit(solution)/shard_map/ppermute | solution.py:100
  134.9 3.1 %collective-permute-start.29 = (f32[128,128]{1,0:T(8,128)S(1)}, f32[128,128]{1,0:T(8,128)S(1)}, u32[]{:S(2)}, u32[]{:S(2)}) collective-permute-start(f32[128,128]{1,0:T(8,128)S(1)} %maximum_select_fusion.3), channel_id=1, source_target_pairs={{0,1},{1,0},{2,3},{3,2},{4,5},{5,4},{6,7},{7,6},{8,9},{9,8},{10,11... | collective-permute-start | bytes 196616 | tf_op jit(solution)/shard_map/ppermute | solution.py:100
  145.0 6.0 %collective-permute-start.31 = (f32[128,192]{1,0:T(8,128)S(1)}, f32[128,192]{1,0:T(8,128)S(1)}, u32[]{:S(2)}, u32[]{:S(2)}) collective-permute-start(f32[128,192]{1,0:T(8,128)S(1)} %fusion.38), channel_id=1, source_target_pairs={{0,31},{1,2},{2,1},{3,4},{4,3},{5,6},{6,5},{7,8},{8,7},{9,10},{10,... | collective-permute-start | bytes 294920 | tf_op jit(solution)/shard_map/ppermute | solution.py:100
  151.1 3.3 %collective-permute-start.32 = (f32[128,128]{1,0:T(8,128)S(1)}, f32[128,128]{1,0:T(8,128)S(1)}, u32[]{:S(2)}, u32[]{:S(2)}) collective-permute-start(f32[128,128]{1,0:T(8,128)S(1)} %maximum_select_fusion.4), channel_id=1, source_target_pairs={{0,1},{1,0},{2,3},{3,2},{4,5},{5,4},{6,7},{7,6},{8,9},{9,8},{10,11... | collective-permute-start | bytes 196616 | tf_op jit(solution)/shard_map/ppermute | solution.py:100
  161.3 6.0 %collective-permute-start.34 = (f32[128,192]{1,0:T(8,128)S(1)}, f32[128,192]{1,0:T(8,128)S(1)}, u32[]{:S(2)}, u32[]{:S(2)}) collective-permute-start(f32[128,192]{1,0:T(8,128)S(1)} %fusion.37), channel_id=1, source_target_pairs={{0,31},{1,2},{2,1},{3,4},{4,3},{5,6},{6,5},{7,8},{8,7},{9,10},{10,... | collective-permute-start | bytes 294920 | tf_op jit(solution)/shard_map/ppermute | solution.py:100
  167.3 3.3 %collective-permute-start.35 = (f32[128,128]{1,0:T(8,128)S(1)}, f32[128,128]{1,0:T(8,128)S(1)}, u32[]{:S(2)}, u32[]{:S(2)}) collective-permute-start(f32[128,128]{1,0:T(8,128)S(1)} %maximum_select_fusion.5), channel_id=1, source_target_pairs={{0,1},{1,0},{2,3},{3,2},{4,5},{5,4},{6,7},{7,6},{8,9},{9,8},{10,11... | collective-permute-start | bytes 196616 | tf_op jit(solution)/shard_map/ppermute | solution.py:100
  (13 other events, 89.8 us)

commit v3 on v0

--- a/solution.py
+++ b/solution.py
@@ -67,31 +67,30 @@
     return select
 
 
-def spread_weights(volume, face_lift):
-    blocks = [volume]
-    for index, (axis, value) in enumerate([(1, NP - 1), (1, 0), (2, NP - 1), (2, 0)]):
-        rows = face_lift[(2 + index) * FACE : (3 + index) * FACE]
-        select = jnp.asarray(face_selector(axis, value), jnp.bfloat16)
-        blocks.append(jnp.dot(select, rows, preferred_element_type=jnp.float32).astype(jnp.bfloat16))
-    return jnp.concatenate(blocks, axis=0)
-
-
-def shifted_inputs(rounded, ny, nz):
-    cube = rounded.reshape((ny, nz, -1))
-    parts = [
-        cube,
-        jnp.roll(cube, 1, axis=0),
-        jnp.roll(cube, -1, axis=0),
-        jnp.roll(cube, 1, axis=1),
-        jnp.roll(cube, -1, axis=1),
-    ]
-    return jnp.concatenate(parts, axis=-1).reshape((ny * nz, -1))
+def face_weights(volume, face_lift):
+    select = np.concatenate(
+        [face_selector(axis, value) for axis, value in [(1, NP - 1), (1, 0), (2, NP - 1), (2, 0)]], axis=1
+    )
+    stacked = jnp.concatenate([volume, face_lift[2 * FACE :]], axis=0)
+    return jnp.asarray(select, jnp.bfloat16), stacked
 
 
 def local_terms(field, reaction, weights, ny, nz):
+    select, stacked = weights
     rounded = field.astype(jnp.bfloat16)
-    stacked = shifted_inputs(rounded, ny, nz)
-    own = jnp.dot(stacked, weights, preferred_element_type=jnp.float32) - reaction * field
+    faces = jnp.dot(rounded, select, preferred_element_type=jnp.float32).astype(jnp.bfloat16)
+    cube = faces.reshape((ny, nz, 4, FACE))
+    moved = jnp.concatenate(
+        [
+            jnp.roll(cube[:, :, 0], 1, axis=0),
+            jnp.roll(cube[:, :, 1], -1, axis=0),
+            jnp.roll(cube[:, :, 2], 1, axis=1),
+            jnp.roll(cube[:, :, 3], -1, axis=1),
+        ],
+        axis=-1,
+    ).reshape((ny * nz, 4 * FACE))
+    inputs = jnp.concatenate([rounded, moved], axis=-1)
+    own = jnp.dot(inputs, stacked, preferred_element_type=jnp.float32) - reaction * field
     return own, rounded
 
 
@@ -136,7 +135,7 @@
     all_scales = jnp.asarray(time_step * node_times, jnp.float32)
     own_scale = lax.dynamic_slice_in_dim(all_scales, first_node, local_count, 0)[0]
 
-    weights = spread_weights(volume, face_lift)
+    weights = face_weights(volume, face_lift)
     x_lift = face_lift[: 2 * FACE]
     start = start_state.reshape((rows, points))
     reaction = reaction_rates.reshape((rows, points))

time: 177 us -> 168 us (0.949)
  other arithmetic: 12 us -> 5.89 us
  matrix products: 23.5 us -> 18.9 us
  starting transfers between devices: 62.1 us -> 65.3 us
  local copies, waits for them, and re-layouts: 11.2 us -> 8.64 us
  waiting for transfers between devices: 65 us -> 67.2 us
    dot_general x18 -> x28, matrix products: 10.9 us -> 7.48 us  [the longest x14 3.82 us: local_terms(): jnp.dot(inputs, stacked, preferred_element_type=jnp.float32)]
    ppermute x42, starting transfers between devices: 62.1 us -> 65.3 us  [swapped(): lax.ppermute(array, axis, [(i, partner(i) % devices) for i in range(devic...]
    unnamed x76 -> x107, local copies, waits for them, and re-layouts: 4.42 us -> 1.3 us
    ppermute x42, waiting for transfers between devices: 65 us -> 67.2 us  [swapped(): lax.ppermute(array, axis, [(i, partner(i) % devices) for i in range(devic...]
    concatenate x54 -> x14, other arithmetic: 3.64 us -> 1.52 us  [local_terms(): jnp.concatenate([jnp.roll(cube[:, :, 0], 1, axis=0), jnp.roll(cube[:, :,...]
    slice x56 -> x85, local copies, waits for them, and re-layouts: 3.81 us -> 3.62 us  [the longest x14 1.72 us: local_terms(): cube[:, :, 2]]
  transfers between devices with their start and end apart: 42 -> 42, of which waited for: 29 -> 29; matrix products, arithmetic and copies ran while one was open for 15% -> 6% of each run, Pallas kernels for 0% -> 0%
where the time goes in v3:
time: 168 us
  waiting for transfers between devices  67.2 us (40%)
  starting transfers between devices  65.3 us (39%)
  matrix products  18.9 us (11%)
  local copies, waits for them, and re-layouts  8.64 us (5%)
  other arithmetic  5.89 us (4%)
  between operations  2.11 us (1%)
    ppermute x42, waiting for transfers between devices, swapped(): lax.ppermute(array, axis, [(i, partner(i) % devices) for i in range(devic...  67.2 us
    ppermute x42, starting transfers between devices, swapped(): lax.ppermute(array, axis, [(i, partner(i) % devices) for i in range(devic...  65.3 us
    dot_general x14, matrix products, apply_operator(): return own + jnp.dot(faces, x_lift, preferred_element_type=jnp.float32)  11.4 us
    dot_general x14, matrix products, local_terms(): jnp.dot(inputs, stacked, preferred_element_type=jnp.float32)  3.82 us
    dot_general x14, matrix products, local_terms(): jnp.dot(rounded, select, preferred_element_type=jnp.float32)  3.66 us
  transfers between devices with their start and end apart: 42, of which 29 were waited for; matrix products, arithmetic and copies ran while one was open for 6% of the time, Pallas kernels for 0%

profile of v3, /device:TPU:1, one launch (start us, length us, event | category | flops | bytes accessed | tf_op | source)
XLA Modules:
  0.0 168.0 jit_solution(15898702326158264947)
XLA Ops:
  1.1 3.3 %collective-permute-start = (bf16[128,64]{1,0:T(8,128)(2,1)S(1)}, bf16[128,64]{1,0:T(8,128)(2,1)S(1)}, u32[]{:S(2)}, u32[]{:S(2)}) collective-permute-start(bf16[128,64]{1,0:T(8,128)(2,1)S(1)} %get-tuple-element.120), channel_id=1, source_target_pairs={{0,1},{1,0},{2,3},{3,2},{4,5},{5,4},{6,7},{7,6},{8,9},{9,8},{10,11... | collective-permute-start | bytes 49160 | tf_op jit(solution)/shard_map/ppermute | solution.py:99
  13.4 2.9 %collective-permute-start.5 = (bf16[128,512]{1,0:T(8,128)(2,1)S(1)}, bf16[128,512]{1,0:T(8,128)(2,1)S(1)}, u32[]{:S(2)}, u32[]{:S(2)}) collective-permute-start(bf16[128,512]{1,0:T(8,128)(2,1)S(1)} %get-tuple-element.9), channel_id=1, source_target_pairs={{0,128},{32,160},{64,192},{96,224},{128,0},{160,32},{192,64},{224,... | collective-permute-start | bytes 393224 | tf_op jit(solution)/shard_map/ppermute | solution.py:99
  16.4 2.7 %collective-permute-start.7 = (bf16[128,512]{1,0:T(8,128)(2,1)S(1)}, bf16[128,512]{1,0:T(8,128)(2,1)S(1)}, u32[]{:S(2)}, u32[]{:S(2)}) collective-permute-start(bf16[128,512]{1,0:T(8,128)(2,1)S(1)} %get-tuple-element.9), channel_id=1, source_target_pairs={{0,192},{32,224},{64,128},{96,160},{128,64},{160,96},{192,0},{224,... | collective-permute-start | bytes 393224 | tf_op jit(solution)/shard_map/ppermute | solution.py:99
  20.2 3.0 %collective-permute-done.6 = bf16[128,512]{1,0:T(8,128)(2,1)S(1)} collective-permute-done((bf16[128,512]{1,0:T(8,128)(2,1)S(1)}, bf16[128,512]{1,0:T(8,128)(2,1)S(1)}, u32[]{:S(2)}, u32[]{:S(2)}) %collective-permute-start.6) | collective-permute-done | bytes 131104 | tf_op jit(solution)/shard_map/ppermute | solution.py:99
  23.2 3.6 %collective-permute-done.8 = bf16[128,512]{1,0:T(8,128)(2,1)S(1)} collective-permute-done((bf16[128,512]{1,0:T(8,128)(2,1)S(1)}, bf16[128,512]{1,0:T(8,128)(2,1)S(1)}, u32[]{:S(2)}, u32[]{:S(2)}) %collective-permute-start.8) | collective-permute-done | bytes 131104 | tf_op jit(solution)/shard_map/ppermute | solution.py:99
  28.7 8.3 %collective-permute-start.10 = (bf16[128,64]{1,0:T(8,128)(2,1)S(1)}, bf16[128,64]{1,0:T(8,128)(2,1)S(1)}, u32[]{:S(2)}, u32[]{:S(2)}) collective-permute-start(bf16[128,64]{1,0:T(8,128)(2,1)S(1)} %get-tuple-element.113), channel_id=1, source_target_pairs={{0,31},{1,2},{2,1},{3,4},{4,3},{5,6},{6,5},{7,8},{8,7},{9,10},{10,... | collective-permute-start | bytes 49160 | tf_op jit(solution)/shard_map/ppermute | solution.py:99
  37.0 4.4 %collective-permute-start.9 = (bf16[128,64]{1,0:T(8,128)(2,1)S(1)}, bf16[128,64]{1,0:T(8,128)(2,1)S(1)}, u32[]{:S(2)}, u32[]{:S(2)}) collective-permute-start(bf16[128,64]{1,0:T(8,128)(2,1)S(1)} %get-tuple-element.112), channel_id=1, source_target_pairs={{0,1},{1,0},{2,3},{3,2},{4,5},{5,4},{6,7},{7,6},{8,9},{9,8},{10,11... | collective-permute-start | bytes 49160 | tf_op jit(solution)/shard_map/ppermute | solution.py:99
  45.5 4.0 %collective-permute-done.12 = bf16[128,64]{1,0:T(8,128)(2,1)S(1)} collective-permute-done((bf16[128,64]{1,0:T(8,128)(2,1)S(1)}, bf16[128,64]{1,0:T(8,128)(2,1)S(1)}, u32[]{:S(2)}, u32[]{:S(2)}) %collective-permute-start.12) | collective-permute-done | bytes 16416 | tf_op jit(solution)/shard_map/ppermute | solution.py:99
  51.0 2.3 %collective-permute-start.13 = (bf16[128,64]{1,0:T(8,128)(2,1)S(1)}, bf16[128,64]{1,0:T(8,128)(2,1)S(1)}, u32[]{:S(2)}, u32[]{:S(2)}) collective-permute-start(bf16[128,64]{1,0:T(8,128)(2,1)S(1)} %get-tuple-element.96), channel_id=1, source_target_pairs={{0,1},{1,0},{2,3},{3,2},{4,5},{5,4},{6,7},{7,6},{8,9},{9,8},{10,11... | collective-permute-start | bytes 49160 | tf_op jit(solution)/shard_map/ppermute | solution.py:99
  54.2 4.0 %collective-permute-done.14 = bf16[128,64]{1,0:T(8,128)(2,1)S(1)} collective-permute-done((bf16[128,64]{1,0:T(8,128)(2,1)S(1)}, bf16[128,64]{1,0:T(8,128)(2,1)S(1)}, u32[]{:S(2)}, u32[]{:S(2)}) %collective-permute-start.14) | collective-permute-done | bytes 16416 | tf_op jit(solution)/shard_map/ppermute | solution.py:99
  59.7 2.5 %collective-permute-start.15 = (bf16[128,64]{1,0:T(8,128)(2,1)S(1)}, bf16[128,64]{1,0:T(8,128)(2,1)S(1)}, u32[]{:S(2)}, u32[]{:S(2)}) collective-permute-start(bf16[128,64]{1,0:T(8,128)(2,1)S(1)} %get-tuple-element.88), channel_id=1, source_target_pairs={{0,1},{1,0},{2,3},{3,2},{4,5},{5,4},{6,7},{7,6},{8,9},{9,8},{10,11... | collective-permute-start | bytes 49160 | tf_op jit(solution)/shard_map/ppermute | solution.py:99
  63.1 4.0 %collective-permute-done.16 = bf16[128,64]{1,0:T(8,128)(2,1)S(1)} collective-permute-done((bf16[128,64]{1,0:T(8,128)(2,1)S(1)}, bf16[128,64]{1,0:T(8,128)(2,1)S(1)}, u32[]{:S(2)}, u32[]{:S(2)}) %collective-permute-start.16) | collective-permute-done | bytes 16416 | tf_op jit(solution)/shard_map/ppermute | solution.py:99
  68.6 2.3 %collective-permute-start.17 = (bf16[128,64]{1,0:T(8,128)(2,1)S(1)}, bf16[128,64]{1,0:T(8,128)(2,1)S(1)}, u32[]{:S(2)}, u32[]{:S(2)}) collective-permute-start(bf16[128,64]{1,0:T(8,128)(2,1)S(1)} %get-tuple-element.80), channel_id=1, source_target_pairs={{0,1},{1,0},{2,3},{3,2},{4,5},{5,4},{6,7},{7,6},{8,9},{9,8},{10,11... | collective-permute-start | bytes 49160 | tf_op jit(solution)/shard_map/ppermute | solution.py:99
  71.8 4.0 %collective-permute-done.18 = bf16[128,64]{1,0:T(8,128)(2,1)S(1)} collective-permute-done((bf16[128,64]{1,0:T(8,128)(2,1)S(1)}, bf16[128,64]{1,0:T(8,128)(2,1)S(1)}, u32[]{:S(2)}, u32[]{:S(2)}) %collective-permute-start.18) | collective-permute-done | bytes 16416 | tf_op jit(solution)/shard_map/ppermute | solution.py:99
  77.4 2.3 %collective-permute-start.19 = (bf16[128,64]{1,0:T(8,128)(2,1)S(1)}, bf16[128,64]{1,0:T(8,128)(2,1)S(1)}, u32[]{:S(2)}, u32[]{:S(2)}) collective-permute-start(bf16[128,64]{1,0:T(8,128)(2,1)S(1)} %get-tuple-element.72), channel_id=1, source_target_pairs={{0,1},{1,0},{2,3},{3,2},{4,5},{5,4},{6,7},{7,6},{8,9},{9,8},{10,11... | collective-permute-start | bytes 49160 | tf_op jit(solution)/shard_map/ppermute | solution.py:99
  80.5 4.0 %collective-permute-done.20 = bf16[128,64]{1,0:T(8,128)(2,1)S(1)} collective-permute-done((bf16[128,64]{1,0:T(8,128)(2,1)S(1)}, bf16[128,64]{1,0:T(8,128)(2,1)S(1)}, u32[]{:S(2)}, u32[]{:S(2)}) %collective-permute-start.20) | collective-permute-done | bytes 16416 | tf_op jit(solution)/shard_map/ppermute | solution.py:99
  86.1 2.3 %collective-permute-start.21 = (bf16[128,64]{1,0:T(8,128)(2,1)S(1)}, bf16[128,64]{1,0:T(8,128)(2,1)S(1)}, u32[]{:S(2)}, u32[]{:S(2)}) collective-permute-start(bf16[128,64]{1,0:T(8,128)(2,1)S(1)} %get-tuple-element.64), channel_id=1, source_target_pairs={{0,1},{1,0},{2,3},{3,2},{4,5},{5,4},{6,7},{7,6},{8,9},{9,8},{10,11... | collective-permute-start | bytes 49160 | tf_op jit(solution)/shard_map/ppermute | solution.py:99
  89.2 4.0 %collective-permute-done.22 = bf16[128,64]{1,0:T(8,128)(2,1)S(1)} collective-permute-done((bf16[128,64]{1,0:T(8,128)(2,1)S(1)}, bf16[128,64]{1,0:T(8,128)(2,1)S(1)}, u32[]{:S(2)}, u32[]{:S(2)}) %collective-permute-start.22) | collective-permute-done | bytes 16416 | tf_op jit(solution)/shard_map/ppermute | solution.py:99
  103.1 2.9 %collective-permute-done.26 = bf16[128,512]{1,0:T(8,128)(2,1)S(1)} collective-permute-done((bf16[128,512]{1,0:T(8,128)(2,1)S(1)}, bf16[128,512]{1,0:T(8,128)(2,1)S(1)}, u32[]{:S(2)}, u32[]{:S(2)}) %collective-permute-start.26) | collective-permute-done | bytes 131104 | tf_op jit(solution)/shard_map/ppermute | solution.py:99
  106.0 4.9 %collective-permute-done.28 = bf16[128,512]{1,0:T(8,128)(2,1)S(1)} collective-permute-done((bf16[128,512]{1,0:T(8,128)(2,1)S(1)}, bf16[128,512]{1,0:T(8,128)(2,1)S(1)}, u32[]{:S(2)}, u32[]{:S(2)}) %collective-permute-start.28) | collective-permute-done | bytes 131104 | tf_op jit(solution)/shard_map/ppermute | solution.py:99
  112.7 3.9 %collective-permute-start.30 = (bf16[128,64]{1,0:T(8,128)(2,1)S(1)}, bf16[128,64]{1,0:T(8,128)(2,1)S(1)}, u32[]{:S(2)}, u32[]{:S(2)}) collective-permute-start(bf16[128,64]{1,0:T(8,128)(2,1)S(1)} %get-tuple-element.56), channel_id=1, source_target_pairs={{0,1},{1,0},{2,3},{3,2},{4,5},{5,4},{6,7},{7,6},{8,9},{9,8},{10,11... | collective-permute-start | bytes 49160 | tf_op jit(solution)/shard_map/ppermute | solution.py:99
  117.5 4.0 %collective-permute-done.31 = bf16[128,64]{1,0:T(8,128)(2,1)S(1)} collective-permute-done((bf16[128,64]{1,0:T(8,128)(2,1)S(1)}, bf16[128,64]{1,0:T(8,128)(2,1)S(1)}, u32[]{:S(2)}, u32[]{:S(2)}) %collective-permute-start.31) | collective-permute-done | bytes 16416 | tf_op jit(solution)/shard_map/ppermute | solution.py:99
  123.1 3.7 %collective-permute-start.32 = (bf16[128,64]{1,0:T(8,128)(2,1)S(1)}, bf16[128,64]{1,0:T(8,128)(2,1)S(1)}, u32[]{:S(2)}, u32[]{:S(2)}) collective-permute-start(bf16[128,64]{1,0:T(8,128)(2,1)S(1)} %get-tuple-element.48), channel_id=1, source_target_pairs={{0,1},{1,0},{2,3},{3,2},{4,5},{5,4},{6,7},{7,6},{8,9},{9,8},{10,11... | collective-permute-start | bytes 49160 | tf_op jit(solution)/shard_map/ppermute | solution.py:99
  127.6 4.0 %collective-permute-done.33 = bf16[128,64]{1,0:T(8,128)(2,1)S(1)} collective-permute-done((bf16[128,64]{1,0:T(8,128)(2,1)S(1)}, bf16[128,64]{1,0:T(8,128)(2,1)S(1)}, u32[]{:S(2)}, u32[]{:S(2)}) %collective-permute-start.33) | collective-permute-done | bytes 16416 | tf_op jit(solution)/shard_map/ppermute | solution.py:99
  133.2 2.3 %collective-permute-start.34 = (bf16[128,64]{1,0:T(8,128)(2,1)S(1)}, bf16[128,64]{1,0:T(8,128)(2,1)S(1)}, u32[]{:S(2)}, u32[]{:S(2)}) collective-permute-start(bf16[128,64]{1,0:T(8,128)(2,1)S(1)} %get-tuple-element.40), channel_id=1, source_target_pairs={{0,1},{1,0},{2,3},{3,2},{4,5},{5,4},{6,7},{7,6},{8,9},{9,8},{10,11... | collective-permute-start | bytes 49160 | tf_op jit(solution)/shard_map/ppermute | solution.py:99
  136.3 4.0 %collective-permute-done.35 = bf16[128,64]{1,0:T(8,128)(2,1)S(1)} collective-permute-done((bf16[128,64]{1,0:T(8,128)(2,1)S(1)}, bf16[128,64]{1,0:T(8,128)(2,1)S(1)}, u32[]{:S(2)}, u32[]{:S(2)}) %collective-permute-start.35) | collective-permute-done | bytes 16416 | tf_op jit(solution)/shard_map/ppermute | solution.py:99
  141.9 2.3 %collective-permute-start.36 = (bf16[128,64]{1,0:T(8,128)(2,1)S(1)}, bf16[128,64]{1,0:T(8,128)(2,1)S(1)}, u32[]{:S(2)}, u32[]{:S(2)}) collective-permute-start(bf16[128,64]{1,0:T(8,128)(2,1)S(1)} %get-tuple-element.32), channel_id=1, source_target_pairs={{0,1},{1,0},{2,3},{3,2},{4,5},{5,4},{6,7},{7,6},{8,9},{9,8},{10,11... | collective-permute-start | bytes 49160 | tf_op jit(solution)/shard_map/ppermute | solution.py:99
  145.0 4.0 %collective-permute-done.37 = bf16[128,64]{1,0:T(8,128)(2,1)S(1)} collective-permute-done((bf16[128,64]{1,0:T(8,128)(2,1)S(1)}, bf16[128,64]{1,0:T(8,128)(2,1)S(1)}, u32[]{:S(2)}, u32[]{:S(2)}) %collective-permute-start.37) | collective-permute-done | bytes 16416 | tf_op jit(solution)/shard_map/ppermute | solution.py:99
  150.6 2.3 %collective-permute-start.38 = (bf16[128,64]{1,0:T(8,128)(2,1)S(1)}, bf16[128,64]{1,0:T(8,128)(2,1)S(1)}, u32[]{:S(2)}, u32[]{:S(2)}) collective-permute-start(bf16[128,64]{1,0:T(8,128)(2,1)S(1)} %get-tuple-element.24), channel_id=1, source_target_pairs={{0,1},{1,0},{2,3},{3,2},{4,5},{5,4},{6,7},{7,6},{8,9},{9,8},{10,11... | collective-permute-start | bytes 49160 | tf_op jit(solution)/shard_map/ppermute | solution.py:99
  153.8 4.0 %collective-permute-done.39 = bf16[128,64]{1,0:T(8,128)(2,1)S(1)} collective-permute-done((bf16[128,64]{1,0:T(8,128)(2,1)S(1)}, bf16[128,64]{1,0:T(8,128)(2,1)S(1)}, u32[]{:S(2)}, u32[]{:S(2)}) %collective-permute-start.39) | collective-permute-done | bytes 16416 | tf_op jit(solution)/shard_map/ppermute | solution.py:99
  159.3 2.3 %collective-permute-start.40 = (bf16[128,64]{1,0:T(8,128)(2,1)S(1)}, bf16[128,64]{1,0:T(8,128)(2,1)S(1)}, u32[]{:S(2)}, u32[]{:S(2)}) collective-permute-start(bf16[128,64]{1,0:T(8,128)(2,1)S(1)} %get-tuple-element.16), channel_id=1, source_target_pairs={{0,1},{1,0},{2,3},{3,2},{4,5},{5,4},{6,7},{7,6},{8,9},{9,8},{10,11... | collective-permute-start | bytes 49160 | tf_op jit(solution)/shard_map/ppermute | solution.py:99
  162.5 4.0 %collective-permute-done.41 = bf16[128,64]{1,0:T(8,128)(2,1)S(1)} collective-permute-done((bf16[128,64]{1,0:T(8,128)(2,1)S(1)}, bf16[128,64]{1,0:T(8,128)(2,1)S(1)}, u32[]{:S(2)}, u32[]{:S(2)}) %collective-permute-start.41) | collective-permute-done | bytes 16416 | tf_op jit(solution)/shard_map/ppermute | solution.py:99
  (357 shorter events, 53.7 us)
Async XLA Ops:
  1.1 9.3 %collective-permute-start = (bf16[128,64]{1,0:T(8,128)(2,1)S(1)}, bf16[128,64]{1,0:T(8,128)(2,1)S(1)}, u32[]{:S(2)}, u32[]{:S(2)}) collective-permute-start(bf16[128,64]{1,0:T(8,128)(2,1)S(1)} %get-tuple-element.120), channel_id=1, source_target_pairs={{0,1},{1,0},{2,3},{3,2},{4,5},{5,4},{6,7},{7,6},{8,9},{9,8},{10,11... | collective-permute-start | bytes 49160 | tf_op jit(solution)/shard_map/ppermute | solution.py:99
  4.4 5.9 %collective-permute-start.1 = (bf16[128,64]{1,0:T(8,128)(2,1)S(1)}, bf16[128,64]{1,0:T(8,128)(2,1)S(1)}, u32[]{:S(2)}, u32[]{:S(2)}) collective-permute-start(bf16[128,64]{1,0:T(8,128)(2,1)S(1)} %get-tuple-element.121), channel_id=1, source_target_pairs={{0,31},{1,2},{2,1},{3,4},{4,3},{5,6},{6,5},{7,8},{8,7},{9,10},{10,... | collective-permute-start | bytes 49160 | tf_op jit(solution)/shard_map/ppermute | solution.py:99
  10.6 5.7 %collective-permute-start.2 = (bf16[128,512]{1,0:T(8,128)(2,1)S(1)}, bf16[128,512]{1,0:T(8,128)(2,1)S(1)}, u32[]{:S(2)}, u32[]{:S(2)}) collective-permute-start(bf16[128,512]{1,0:T(8,128)(2,1)S(1)} %get-tuple-element.9), channel_id=1, source_target_pairs={{0,32},{32,0},{64,96},{96,64},{128,160},{160,128},{192,224},{224,1... | collective-permute-start | bytes 393224 | tf_op jit(solution)/shard_map/ppermute | solution.py:99
  11.1 8.1 %collective-permute-start.3 = (bf16[128,512]{1,0:T(8,128)(2,1)S(1)}, bf16[128,512]{1,0:T(8,128)(2,1)S(1)}, u32[]{:S(2)}, u32[]{:S(2)}) collective-permute-start(bf16[128,512]{1,0:T(8,128)(2,1)S(1)} %get-tuple-element.9), channel_id=1, source_target_pairs={{0,64},{32,96},{64,0},{96,32},{128,192},{160,224},{192,128},{224,1... | collective-permute-start | bytes 393224 | tf_op jit(solution)/shard_map/ppermute | solution.py:99
  12.3 7.8 %collective-permute-start.4 = (bf16[128,512]{1,0:T(8,128)(2,1)S(1)}, bf16[128,512]{1,0:T(8,128)(2,1)S(1)}, u32[]{:S(2)}, u32[]{:S(2)}) collective-permute-start(bf16[128,512]{1,0:T(8,128)(2,1)S(1)} %get-tuple-element.9), channel_id=1, source_target_pairs={{0,96},{32,64},{64,32},{96,0},{128,224},{160,192},{192,160},{224,1... | collective-permute-start | bytes 393224 | tf_op jit(solution)/shard_map/ppermute | solution.py:99
  13.4 6.8 %collective-permute-start.5 = (bf16[128,512]{1,0:T(8,128)(2,1)S(1)}, bf16[128,512]{1,0:T(8,128)(2,1)S(1)}, u32[]{:S(2)}, u32[]{:S(2)}) collective-permute-start(bf16[128,512]{1,0:T(8,128)(2,1)S(1)} %get-tuple-element.9), channel_id=1, source_target_pairs={{0,128},{32,160},{64,192},{96,224},{128,0},{160,32},{192,64},{224,... | collective-permute-start | bytes 393224 | tf_op jit(solution)/shard_map/ppermute | solution.py:99
  16.3 6.9 %collective-permute-start.6 = (bf16[128,512]{1,0:T(8,128)(2,1)S(1)}, bf16[128,512]{1,0:T(8,128)(2,1)S(1)}, u32[]{:S(2)}, u32[]{:S(2)}) collective-permute-start(bf16[128,512]{1,0:T(8,128)(2,1)S(1)} %get-tuple-element.9), channel_id=1, source_target_pairs={{0,160},{32,128},{64,224},{96,192},{128,32},{160,0},{192,96},{224,... | collective-permute-start | bytes 393224 | tf_op jit(solution)/shard_map/ppermute | solution.py:99
  16.4 6.8 %collective-permute-start.7 = (bf16[128,512]{1,0:T(8,128)(2,1)S(1)}, bf16[128,512]{1,0:T(8,128)(2,1)S(1)}, u32[]{:S(2)}, u32[]{:S(2)}) collective-permute-start(bf16[128,512]{1,0:T(8,128)(2,1)S(1)} %get-tuple-element.9), channel_id=1, source_target_pairs={{0,192},{32,224},{64,128},{96,160},{128,64},{160,96},{192,0},{224,... | collective-permute-start | bytes 393224 | tf_op jit(solution)/shard_map/ppermute | solution.py:99
  19.2 7.7 %collective-permute-start.8 = (bf16[128,512]{1,0:T(8,128)(2,1)S(1)}, bf16[128,512]{1,0:T(8,128)(2,1)S(1)}, u32[]{:S(2)}, u32[]{:S(2)}) collective-permute-start(bf16[128,512]{1,0:T(8,128)(2,1)S(1)} %get-tuple-element.9), channel_id=1, source_target_pairs={{0,224},{32,192},{64,160},{96,128},{128,96},{160,64},{192,32},{224... | collective-permute-start | bytes 393224 | tf_op jit(solution)/shard_map/ppermute | solution.py:99
  28.7 13.1 %collective-permute-start.10 = (bf16[128,64]{1,0:T(8,128)(2,1)S(1)}, bf16[128,64]{1,0:T(8,128)(2,1)S(1)}, u32[]{:S(2)}, u32[]{:S(2)}) collective-permute-start(bf16[128,64]{1,0:T(8,128)(2,1)S(1)} %get-tuple-element.113), channel_id=1, source_target_pairs={{0,31},{1,2},{2,1},{3,4},{4,3},{5,6},{6,5},{7,8},{8,7},{9,10},{10,... | collective-permute-start | bytes 49160 | tf_op jit(solution)/shard_map/ppermute | solution.py:99
  37.0 5.2 %collective-permute-start.9 = (bf16[128,64]{1,0:T(8,128)(2,1)S(1)}, bf16[128,64]{1,0:T(8,128)(2,1)S(1)}, u32[]{:S(2)}, u32[]{:S(2)}) collective-permute-start(bf16[128,64]{1,0:T(8,128)(2,1)S(1)} %get-tuple-element.112), channel_id=1, source_target_pairs={{0,1},{1,0},{2,3},{3,2},{4,5},{5,4},{6,7},{7,6},{8,9},{9,8},{10,11... | collective-permute-start | bytes 49160 | tf_op jit(solution)/shard_map/ppermute | solution.py:99
  44.6 4.8 %collective-permute-start.12 = (bf16[128,64]{1,0:T(8,128)(2,1)S(1)}, bf16[128,64]{1,0:T(8,128)(2,1)S(1)}, u32[]{:S(2)}, u32[]{:S(2)}) collective-permute-start(bf16[128,64]{1,0:T(8,128)(2,1)S(1)} %get-tuple-element.105), channel_id=1, source_target_pairs={{0,31},{1,2},{2,1},{3,4},{4,3},{5,6},{6,5},{7,8},{8,7},{9,10},{10,... | collective-permute-start | bytes 49160 | tf_op jit(solution)/shard_map/ppermute | solution.py:99
  53.3 4.8 %collective-permute-start.14 = (bf16[128,64]{1,0:T(8,128)(2,1)S(1)}, bf16[128,64]{1,0:T(8,128)(2,1)S(1)}, u32[]{:S(2)}, u32[]{:S(2)}) collective-permute-start(bf16[128,64]{1,0:T(8,128)(2,1)S(1)} %get-tuple-element.97), channel_id=1, source_target_pairs={{0,31},{1,2},{2,1},{3,4},{4,3},{5,6},{6,5},{7,8},{8,7},{9,10},{10,... | collective-permute-start | bytes 49160 | tf_op jit(solution)/shard_map/ppermute | solution.py:99
  62.2 4.8 %collective-permute-start.16 = (bf16[128,64]{1,0:T(8,128)(2,1)S(1)}, bf16[128,64]{1,0:T(8,128)(2,1)S(1)}, u32[]{:S(2)}, u32[]{:S(2)}) collective-permute-start(bf16[128,64]{1,0:T(8,128)(2,1)S(1)} %get-tuple-element.89), channel_id=1, source_target_pairs={{0,31},{1,2},{2,1},{3,4},{4,3},{5,6},{6,5},{7,8},{8,7},{9,10},{10,... | collective-permute-start | bytes 49160 | tf_op jit(solution)/shard_map/ppermute | solution.py:99
  70.9 4.8 %collective-permute-start.18 = (bf16[128,64]{1,0:T(8,128)(2,1)S(1)}, bf16[128,64]{1,0:T(8,128)(2,1)S(1)}, u32[]{:S(2)}, u32[]{:S(2)}) collective-permute-start(bf16[128,64]{1,0:T(8,128)(2,1)S(1)} %get-tuple-element.81), channel_id=1, source_target_pairs={{0,31},{1,2},{2,1},{3,4},{4,3},{5,6},{6,5},{7,8},{8,7},{9,10},{10,... | collective-permute-start | bytes 49160 | tf_op jit(solution)/shard_map/ppermute | solution.py:99
  79.7 4.8 %collective-permute-start.20 = (bf16[128,64]{1,0:T(8,128)(2,1)S(1)}, bf16[128,64]{1,0:T(8,128)(2,1)S(1)}, u32[]{:S(2)}, u32[]{:S(2)}) collective-permute-start(bf16[128,64]{1,0:T(8,128)(2,1)S(1)} %get-tuple-element.73), channel_id=1, source_target_pairs={{0,31},{1,2},{2,1},{3,4},{4,3},{5,6},{6,5},{7,8},{8,7},{9,10},{10,... | collective-permute-start | bytes 49160 | tf_op jit(solution)/shard_map/ppermute | solution.py:99
  88.4 4.8 %collective-permute-start.22 = (bf16[128,64]{1,0:T(8,128)(2,1)S(1)}, bf16[128,64]{1,0:T(8,128)(2,1)S(1)}, u32[]{:S(2)}, u32[]{:S(2)}) collective-permute-start(bf16[128,64]{1,0:T(8,128)(2,1)S(1)} %get-tuple-element.65), channel_id=1, source_target_pairs={{0,31},{1,2},{2,1},{3,4},{4,3},{5,6},{6,5},{7,8},{8,7},{9,10},{10,... | collective-permute-start | bytes 49160 | tf_op jit(solution)/shard_map/ppermute | solution.py:99
  93.5 6.2 %collective-permute-start.23 = (bf16[128,512]{1,0:T(8,128)(2,1)S(1)}, bf16[128,512]{1,0:T(8,128)(2,1)S(1)}, u32[]{:S(2)}, u32[]{:S(2)}) collective-permute-start(bf16[128,512]{1,0:T(8,128)(2,1)S(1)} %get-tuple-element.7), channel_id=1, source_target_pairs={{0,32},{32,0},{64,96},{96,64},{128,160},{160,128},{192,224},{224,1... | collective-permute-start | bytes 393224 | tf_op jit(solution)/shard_map/ppermute | solution.py:99
  94.4 6.8 %collective-permute-start.24 = (bf16[128,512]{1,0:T(8,128)(2,1)S(1)}, bf16[128,512]{1,0:T(8,128)(2,1)S(1)}, u32[]{:S(2)}, u32[]{:S(2)}) collective-permute-start(bf16[128,512]{1,0:T(8,128)(2,1)S(1)} %get-tuple-element.7), channel_id=1, source_target_pairs={{0,64},{32,96},{64,0},{96,32},{128,192},{160,224},{192,128},{224,1... | collective-permute-start | bytes 393224 | tf_op jit(solution)/shard_map/ppermute | solution.py:99
  94.4 8.7 %collective-permute-start.25 = (bf16[128,512]{1,0:T(8,128)(2,1)S(1)}, bf16[128,512]{1,0:T(8,128)(2,1)S(1)}, u32[]{:S(2)}, u32[]{:S(2)}) collective-permute-start(bf16[128,512]{1,0:T(8,128)(2,1)S(1)} %get-tuple-element.7), channel_id=1, source_target_pairs={{0,96},{32,64},{64,32},{96,0},{128,224},{160,192},{192,160},{224,1... | collective-permute-start | bytes 393224 | tf_op jit(solution)/shard_map/ppermute | solution.py:99
  96.2 9.8 %collective-permute-start.26 = (bf16[128,512]{1,0:T(8,128)(2,1)S(1)}, bf16[128,512]{1,0:T(8,128)(2,1)S(1)}, u32[]{:S(2)}, u32[]{:S(2)}) collective-permute-start(bf16[128,512]{1,0:T(8,128)(2,1)S(1)} %get-tuple-element.7), channel_id=1, source_target_pairs={{0,128},{32,160},{64,192},{96,224},{128,0},{160,32},{192,64},{224,... | collective-permute-start | bytes 393224 | tf_op jit(solution)/shard_map/ppermute | solution.py:99
  97.6 8.4 %collective-permute-start.27 = (bf16[128,512]{1,0:T(8,128)(2,1)S(1)}, bf16[128,512]{1,0:T(8,128)(2,1)S(1)}, u32[]{:S(2)}, u32[]{:S(2)}) collective-permute-start(bf16[128,512]{1,0:T(8,128)(2,1)S(1)} %get-tuple-element.7), channel_id=1, source_target_pairs={{0,160},{32,128},{64,224},{96,192},{128,32},{160,0},{192,96},{224,... | collective-permute-start | bytes 393224 | tf_op jit(solution)/shard_map/ppermute | solution.py:99
  99.7 11.2 %collective-permute-start.28 = (bf16[128,512]{1,0:T(8,128)(2,1)S(1)}, bf16[128,512]{1,0:T(8,128)(2,1)S(1)}, u32[]{:S(2)}, u32[]{:S(2)}) collective-permute-start(bf16[128,512]{1,0:T(8,128)(2,1)S(1)} %get-tuple-element.7), channel_id=1, source_target_pairs={{0,192},{32,224},{64,128},{96,160},{128,64},{160,96},{192,0},{224,... | collective-permute-start | bytes 393224 | tf_op jit(solution)/shard_map/ppermute | solution.py:99
  101.2 9.8 %collective-permute-start.29 = (bf16[128,512]{1,0:T(8,128)(2,1)S(1)}, bf16[128,512]{1,0:T(8,128)(2,1)S(1)}, u32[]{:S(2)}, u32[]{:S(2)}) collective-permute-start(bf16[128,512]{1,0:T(8,128)(2,1)S(1)} %get-tuple-element.7), channel_id=1, source_target_pairs={{0,224},{32,192},{64,160},{96,128},{128,96},{160,64},{192,32},{224... | collective-permute-start | bytes 393224 | tf_op jit(solution)/shard_map/ppermute | solution.py:99
  112.7 4.8 %collective-permute-start.30 = (bf16[128,64]{1,0:T(8,128)(2,1)S(1)}, bf16[128,64]{1,0:T(8,128)(2,1)S(1)}, u32[]{:S(2)}, u32[]{:S(2)}) collective-permute-start(bf16[128,64]{1,0:T(8,128)(2,1)S(1)} %get-tuple-element.56), channel_id=1, source_target_pairs={{0,1},{1,0},{2,3},{3,2},{4,5},{5,4},{6,7},{7,6},{8,9},{9,8},{10,11... | collective-permute-start | bytes 49160 | tf_op jit(solution)/shard_map/ppermute | solution.py:99
  116.6 4.8 %collective-permute-start.31 = (bf16[128,64]{1,0:T(8,128)(2,1)S(1)}, bf16[128,64]{1,0:T(8,128)(2,1)S(1)}, u32[]{:S(2)}, u32[]{:S(2)}) collective-permute-start(bf16[128,64]{1,0:T(8,128)(2,1)S(1)} %get-tuple-element.57), channel_id=1, source_target_pairs={{0,31},{1,2},{2,1},{3,4},{4,3},{5,6},{6,5},{7,8},{8,7},{9,10},{10,... | collective-permute-start | bytes 49160 | tf_op jit(solution)/shard_map/ppermute | solution.py:99
  123.1 4.5 %collective-permute-start.32 = (bf16[128,64]{1,0:T(8,128)(2,1)S(1)}, bf16[128,64]{1,0:T(8,128)(2,1)S(1)}, u32[]{:S(2)}, u32[]{:S(2)}) collective-permute-start(bf16[128,64]{1,0:T(8,128)(2,1)S(1)} %get-tuple-element.48), channel_id=1, source_target_pairs={{0,1},{1,0},{2,3},{3,2},{4,5},{5,4},{6,7},{7,6},{8,9},{9,8},{10,11... | collective-permute-start | bytes 49160 | tf_op jit(solution)/shard_map/ppermute | solution.py:99
  126.7 4.8 %collective-permute-start.33 = (bf16[128,64]{1,0:T(8,128)(2,1)S(1)}, bf16[128,64]{1,0:T(8,128)(2,1)S(1)}, u32[]{:S(2)}, u32[]{:S(2)}) collective-permute-start(bf16[128,64]{1,0:T(8,128)(2,1)S(1)} %get-tuple-element.49), channel_id=1, source_target_pairs={{0,31},{1,2},{2,1},{3,4},{4,3},{5,6},{6,5},{7,8},{8,7},{9,10},{10,... | collective-permute-start | bytes 49160 | tf_op jit(solution)/shard_map/ppermute | solution.py:99
  135.5 4.8 %collective-permute-start.35 = (bf16[128,64]{1,0:T(8,128)(2,1)S(1)}, bf16[128,64]{1,0:T(8,128)(2,1)S(1)}, u32[]{:S(2)}, u32[]{:S(2)}) collective-permute-start(bf16[128,64]{1,0:T(8,128)(2,1)S(1)} %get-tuple-element.41), channel_id=1, source_target_pairs={{0,31},{1,2},{2,1},{3,4},{4,3},{5,6},{6,5},{7,8},{8,7},{9,10},{10,... | collective-permute-start | bytes 49160 | tf_op jit(solution)/shard_map/ppermute | solution.py:99
  144.2 4.8 %collective-permute-start.37 = (bf16[128,64]{1,0:T(8,128)(2,1)S(1)}, bf16[128,64]{1,0:T(8,128)(2,1)S(1)}, u32[]{:S(2)}, u32[]{:S(2)}) collective-permute-start(bf16[128,64]{1,0:T(8,128)(2,1)S(1)} %get-tuple-element.33), channel_id=1, source_target_pairs={{0,31},{1,2},{2,1},{3,4},{4,3},{5,6},{6,5},{7,8},{8,7},{9,10},{10,... | collective-permute-start | bytes 49160 | tf_op jit(solution)/shard_map/ppermute | solution.py:99
  152.9 4.8 %collective-permute-start.39 = (bf16[128,64]{1,0:T(8,128)(2,1)S(1)}, bf16[128,64]{1,0:T(8,128)(2,1)S(1)}, u32[]{:S(2)}, u32[]{:S(2)}) collective-permute-start(bf16[128,64]{1,0:T(8,128)(2,1)S(1)} %get-tuple-element.25), channel_id=1, source_target_pairs={{0,31},{1,2},{2,1},{3,4},{4,3},{5,6},{6,5},{7,8},{8,7},{9,10},{10,... | collective-permute-start | bytes 49160 | tf_op jit(solution)/shard_map/ppermute | solution.py:99
  161.6 4.8 %collective-permute-start.41 = (bf16[128,64]{1,0:T(8,128)(2,1)S(1)}, bf16[128,64]{1,0:T(8,128)(2,1)S(1)}, u32[]{:S(2)}, u32[]{:S(2)}) collective-permute-start(bf16[128,64]{1,0:T(8,128)(2,1)S(1)} %get-tuple-element.17), channel_id=1, source_target_pairs={{0,31},{1,2},{2,1},{3,4},{4,3},{5,6},{6,5},{7,8},{8,7},{9,10},{10,... | collective-permute-start | bytes 49160 | tf_op jit(solution)/shard_map/ppermute | solution.py:99
  (17 other events, 54.0 us)

commit v4 on v3

--- a/solution.py
+++ b/solution.py
@@ -68,27 +68,31 @@
 
 
 def face_weights(volume, face_lift):
-    select = np.concatenate(
+    picks = np.concatenate(
         [face_selector(axis, value) for axis, value in [(1, NP - 1), (1, 0), (2, NP - 1), (2, 0)]], axis=1
-    )
+    ).argmax(axis=0)
+    rows = lax.broadcasted_iota(jnp.int32, (NP**3, 4 * FACE), 0)
+    select = (rows == jnp.asarray(picks, jnp.int32)[None, :]).astype(jnp.bfloat16)
     stacked = jnp.concatenate([volume, face_lift[2 * FACE :]], axis=0)
-    return jnp.asarray(select, jnp.bfloat16), stacked
+    return select, stacked
 
 
 def local_terms(field, reaction, weights, ny, nz):
     select, stacked = weights
     rounded = field.astype(jnp.bfloat16)
     faces = jnp.dot(rounded, select, preferred_element_type=jnp.float32).astype(jnp.bfloat16)
-    cube = faces.reshape((ny, nz, 4, FACE))
+    z = lax.broadcasted_iota(jnp.int32, (ny * nz, FACE), 0) % nz
+    z_low = faces[:, 2 * FACE : 3 * FACE]
+    z_high = faces[:, 3 * FACE :]
     moved = jnp.concatenate(
         [
-            jnp.roll(cube[:, :, 0], 1, axis=0),
-            jnp.roll(cube[:, :, 1], -1, axis=0),
-            jnp.roll(cube[:, :, 2], 1, axis=1),
-            jnp.roll(cube[:, :, 3], -1, axis=1),
+            jnp.roll(faces[:, :FACE], nz, axis=0),
+            jnp.roll(faces[:, FACE : 2 * FACE], -nz, axis=0),
+            jnp.where(z == 0, jnp.roll(z_low, 1 - nz, axis=0), jnp.roll(z_low, 1, axis=0)),
+            jnp.where(z == nz - 1, jnp.roll(z_high, nz - 1, axis=0), jnp.roll(z_high, -1, axis=0)),
         ],
         axis=-1,
-    ).reshape((ny * nz, 4 * FACE))
+    )
     inputs = jnp.concatenate([rounded, moved], axis=-1)
     own = jnp.dot(inputs, stacked, preferred_element_type=jnp.float32) - reaction * field
     return own, rounded

time: 168 us -> 171 us (1.018)
  waiting for transfers between devices: 67.2 us -> 58.5 us
  local copies, waits for them, and re-layouts: 8.64 us -> 17 us
  matrix products: 18.9 us -> 21.5 us
  other arithmetic: 5.89 us -> 8.18 us
    ppermute x42, waiting for transfers between devices: 67.2 us -> 58.5 us  [swapped(): lax.ppermute(array, axis, [(i, partner(i) % devices) for i in range(devic...]
    concatenate x0 -> x42, local copies, waits for them, and re-layouts: none -> 4.92 us  [the longest x14 1.65 us: local_terms(): jnp.roll(faces[:, FACE:2 * FACE], -nz, axis=0)]
    select_n x0 -> x28, local copies, waits for them, and re-layouts: none -> 3.28 us  [the longest x14 1.69 us: local_terms(): jnp.where(z == nz - 1, jnp.roll(z_high, nz - 1, axis=0), jnp.roll(z_high,...]
    slice x84, local copies, waits for them, and re-layouts: 3.6 us -> 6.4 us  [the longest x28 2.14 us: local_terms(): jnp.roll(faces[:, FACE:2 * FACE], -nz, axis=0)]
    dot_general x14, matrix products: 3.66 us -> 5.45 us  [local_terms(): jnp.dot(rounded, select, preferred_element_type=jnp.float32)]
  transfers between devices with their start and end apart: 42 -> 42, of which waited for: 29 -> 16; matrix products, arithmetic and copies ran while one was open for 6% -> 11% of each run, Pallas kernels for 0% -> 0%
where the time goes in v4:
time: 171 us
  starting transfers between devices  64.2 us (38%)
  waiting for transfers between devices  58.5 us (34%)
  matrix products  21.5 us (13%)
  local copies, waits for them, and re-layouts  17 us (10%)
  other arithmetic  8.18 us (5%)
    ppermute x42, starting transfers between devices, swapped(): lax.ppermute(array, axis, [(i, partner(i) % devices) for i in range(devic...  64.2 us
    ppermute x42, waiting for transfers between devices, swapped(): lax.ppermute(array, axis, [(i, partner(i) % devices) for i in range(devic...  58.5 us
    dot_general x14, matrix products, apply_operator(): return own + jnp.dot(faces, x_lift, preferred_element_type=jnp.float32)  12.2 us
    dot_general x14, matrix products, local_terms(): jnp.dot(rounded, select, preferred_element_type=jnp.float32)  5.45 us
    dot_general x14, matrix products, local_terms(): jnp.dot(inputs, stacked, preferred_element_type=jnp.float32)  3.81 us
  transfers between devices with their start and end apart: 42, of which 16 were waited for; matrix products, arithmetic and copies ran while one was open for 11% of the time, Pallas kernels for 0%

profile of v4, /device:TPU:1, one launch (start us, length us, event | category | flops | bytes accessed | tf_op | source)
XLA Modules:
  0.0 170.7 jit_solution(15091329532206142409)
XLA Ops:
  1.1 3.3 %collective-permute-start = (bf16[128,64]{1,0:T(8,128)(2,1)S(1)}, bf16[128,64]{1,0:T(8,128)(2,1)S(1)}, u32[]{:S(2)}, u32[]{:S(2)}) collective-permute-start(bf16[128,64]{1,0:T(8,128)(2,1)S(1)} %get-tuple-element.42), channel_id=1, source_target_pairs={{0,1},{1,0},{2,3},{3,2},{4,5},{5,4},{6,7},{7,6},{8,9},{9,8},{10,11... | collective-permute-start | bytes 49160 | tf_op jit(solution)/shard_map/ppermute | solution.py:103
  13.3 2.9 %collective-permute-start.5 = (bf16[128,512]{1,0:T(8,128)(2,1)S(1)}, bf16[128,512]{1,0:T(8,128)(2,1)S(1)}, u32[]{:S(2)}, u32[]{:S(2)}) collective-permute-start(bf16[128,512]{1,0:T(8,128)(2,1)S(1)} %get-tuple-element.9), channel_id=1, source_target_pairs={{0,128},{32,160},{64,192},{96,224},{128,0},{160,32},{192,64},{224,... | collective-permute-start | bytes 393224 | tf_op jit(solution)/shard_map/ppermute | solution.py:103
  16.3 2.7 %collective-permute-start.7 = (bf16[128,512]{1,0:T(8,128)(2,1)S(1)}, bf16[128,512]{1,0:T(8,128)(2,1)S(1)}, u32[]{:S(2)}, u32[]{:S(2)}) collective-permute-start(bf16[128,512]{1,0:T(8,128)(2,1)S(1)} %get-tuple-element.9), channel_id=1, source_target_pairs={{0,192},{32,224},{64,128},{96,160},{128,64},{160,96},{192,0},{224,... | collective-permute-start | bytes 393224 | tf_op jit(solution)/shard_map/ppermute | solution.py:103
  20.1 2.9 %collective-permute-done.6 = bf16[128,512]{1,0:T(8,128)(2,1)S(1)} collective-permute-done((bf16[128,512]{1,0:T(8,128)(2,1)S(1)}, bf16[128,512]{1,0:T(8,128)(2,1)S(1)}, u32[]{:S(2)}, u32[]{:S(2)}) %collective-permute-start.6) | collective-permute-done | bytes 131104 | tf_op jit(solution)/shard_map/ppermute | solution.py:103
  23.1 3.6 %collective-permute-done.8 = bf16[128,512]{1,0:T(8,128)(2,1)S(1)} collective-permute-done((bf16[128,512]{1,0:T(8,128)(2,1)S(1)}, bf16[128,512]{1,0:T(8,128)(2,1)S(1)}, u32[]{:S(2)}, u32[]{:S(2)}) %collective-permute-start.8) | collective-permute-done | bytes 131104 | tf_op jit(solution)/shard_map/ppermute | solution.py:103
  28.8 8.2 %collective-permute-start.10 = (bf16[128,64]{1,0:T(8,128)(2,1)S(1)}, bf16[128,64]{1,0:T(8,128)(2,1)S(1)}, u32[]{:S(2)}, u32[]{:S(2)}) collective-permute-start(bf16[128,64]{1,0:T(8,128)(2,1)S(1)} %get-tuple-element.41), channel_id=1, source_target_pairs={{0,31},{1,2},{2,1},{3,4},{4,3},{5,6},{6,5},{7,8},{8,7},{9,10},{10,... | collective-permute-start | bytes 49160 | tf_op jit(solution)/shard_map/ppermute | solution.py:103
  37.0 4.4 %collective-permute-start.9 = (bf16[128,64]{1,0:T(8,128)(2,1)S(1)}, bf16[128,64]{1,0:T(8,128)(2,1)S(1)}, u32[]{:S(2)}, u32[]{:S(2)}) collective-permute-start(bf16[128,64]{1,0:T(8,128)(2,1)S(1)} %get-tuple-element.40), channel_id=1, source_target_pairs={{0,1},{1,0},{2,3},{3,2},{4,5},{5,4},{6,7},{7,6},{8,9},{9,8},{10,11... | collective-permute-start | bytes 49160 | tf_op jit(solution)/shard_map/ppermute | solution.py:103
  46.1 3.7 %collective-permute-done.12 = bf16[128,64]{1,0:T(8,128)(2,1)S(1)} collective-permute-done((bf16[128,64]{1,0:T(8,128)(2,1)S(1)}, bf16[128,64]{1,0:T(8,128)(2,1)S(1)}, u32[]{:S(2)}, u32[]{:S(2)}) %collective-permute-start.12) | collective-permute-done | bytes 16416 | tf_op jit(solution)/shard_map/ppermute | solution.py:103
  51.6 2.2 %collective-permute-start.13 = (bf16[128,64]{1,0:T(8,128)(2,1)S(1)}, bf16[128,64]{1,0:T(8,128)(2,1)S(1)}, u32[]{:S(2)}, u32[]{:S(2)}) collective-permute-start(bf16[128,64]{1,0:T(8,128)(2,1)S(1)} %get-tuple-element.36), channel_id=1, source_target_pairs={{0,1},{1,0},{2,3},{3,2},{4,5},{5,4},{6,7},{7,6},{8,9},{9,8},{10,11... | collective-permute-start | bytes 49160 | tf_op jit(solution)/shard_map/ppermute | solution.py:103
  55.0 3.7 %collective-permute-done.14 = bf16[128,64]{1,0:T(8,128)(2,1)S(1)} collective-permute-done((bf16[128,64]{1,0:T(8,128)(2,1)S(1)}, bf16[128,64]{1,0:T(8,128)(2,1)S(1)}, u32[]{:S(2)}, u32[]{:S(2)}) %collective-permute-start.14) | collective-permute-done | bytes 16416 | tf_op jit(solution)/shard_map/ppermute | solution.py:103
  60.5 2.4 %collective-permute-start.15 = (bf16[128,64]{1,0:T(8,128)(2,1)S(1)}, bf16[128,64]{1,0:T(8,128)(2,1)S(1)}, u32[]{:S(2)}, u32[]{:S(2)}) collective-permute-start(bf16[128,64]{1,0:T(8,128)(2,1)S(1)} %get-tuple-element.34), channel_id=1, source_target_pairs={{0,1},{1,0},{2,3},{3,2},{4,5},{5,4},{6,7},{7,6},{8,9},{9,8},{10,11... | collective-permute-start | bytes 49160 | tf_op jit(solution)/shard_map/ppermute | solution.py:103
  64.1 3.7 %collective-permute-done.16 = bf16[128,64]{1,0:T(8,128)(2,1)S(1)} collective-permute-done((bf16[128,64]{1,0:T(8,128)(2,1)S(1)}, bf16[128,64]{1,0:T(8,128)(2,1)S(1)}, u32[]{:S(2)}, u32[]{:S(2)}) %collective-permute-start.16) | collective-permute-done | bytes 16416 | tf_op jit(solution)/shard_map/ppermute | solution.py:103
  69.7 2.2 %collective-permute-start.17 = (bf16[128,64]{1,0:T(8,128)(2,1)S(1)}, bf16[128,64]{1,0:T(8,128)(2,1)S(1)}, u32[]{:S(2)}, u32[]{:S(2)}) collective-permute-start(bf16[128,64]{1,0:T(8,128)(2,1)S(1)} %get-tuple-element.32), channel_id=1, source_target_pairs={{0,1},{1,0},{2,3},{3,2},{4,5},{5,4},{6,7},{7,6},{8,9},{9,8},{10,11... | collective-permute-start | bytes 49160 | tf_op jit(solution)/shard_map/ppermute | solution.py:103
  73.1 3.7 %collective-permute-done.18 = bf16[128,64]{1,0:T(8,128)(2,1)S(1)} collective-permute-done((bf16[128,64]{1,0:T(8,128)(2,1)S(1)}, bf16[128,64]{1,0:T(8,128)(2,1)S(1)}, u32[]{:S(2)}, u32[]{:S(2)}) %collective-permute-start.18) | collective-permute-done | bytes 16416 | tf_op jit(solution)/shard_map/ppermute | solution.py:103
  78.6 2.2 %collective-permute-start.19 = (bf16[128,64]{1,0:T(8,128)(2,1)S(1)}, bf16[128,64]{1,0:T(8,128)(2,1)S(1)}, u32[]{:S(2)}, u32[]{:S(2)}) collective-permute-start(bf16[128,64]{1,0:T(8,128)(2,1)S(1)} %get-tuple-element.30), channel_id=1, source_target_pairs={{0,1},{1,0},{2,3},{3,2},{4,5},{5,4},{6,7},{7,6},{8,9},{9,8},{10,11... | collective-permute-start | bytes 49160 | tf_op jit(solution)/shard_map/ppermute | solution.py:103
  82.0 3.7 %collective-permute-done.20 = bf16[128,64]{1,0:T(8,128)(2,1)S(1)} collective-permute-done((bf16[128,64]{1,0:T(8,128)(2,1)S(1)}, bf16[128,64]{1,0:T(8,128)(2,1)S(1)}, u32[]{:S(2)}, u32[]{:S(2)}) %collective-permute-start.20) | collective-permute-done | bytes 16416 | tf_op jit(solution)/shard_map/ppermute | solution.py:103
  87.5 2.2 %collective-permute-start.21 = (bf16[128,64]{1,0:T(8,128)(2,1)S(1)}, bf16[128,64]{1,0:T(8,128)(2,1)S(1)}, u32[]{:S(2)}, u32[]{:S(2)}) collective-permute-start(bf16[128,64]{1,0:T(8,128)(2,1)S(1)} %get-tuple-element.28), channel_id=1, source_target_pairs={{0,1},{1,0},{2,3},{3,2},{4,5},{5,4},{6,7},{7,6},{8,9},{9,8},{10,11... | collective-permute-start | bytes 49160 | tf_op jit(solution)/shard_map/ppermute | solution.py:103
  90.9 3.7 %collective-permute-done.22 = bf16[128,64]{1,0:T(8,128)(2,1)S(1)} collective-permute-done((bf16[128,64]{1,0:T(8,128)(2,1)S(1)}, bf16[128,64]{1,0:T(8,128)(2,1)S(1)}, u32[]{:S(2)}, u32[]{:S(2)}) %collective-permute-start.22) | collective-permute-done | bytes 16416 | tf_op jit(solution)/shard_map/ppermute | solution.py:103
  104.5 2.8 %collective-permute-done.26 = bf16[128,512]{1,0:T(8,128)(2,1)S(1)} collective-permute-done((bf16[128,512]{1,0:T(8,128)(2,1)S(1)}, bf16[128,512]{1,0:T(8,128)(2,1)S(1)}, u32[]{:S(2)}, u32[]{:S(2)}) %collective-permute-start.26) | collective-permute-done | bytes 131104 | tf_op jit(solution)/shard_map/ppermute | solution.py:103
  107.4 5.0 %collective-permute-done.28 = bf16[128,512]{1,0:T(8,128)(2,1)S(1)} collective-permute-done((bf16[128,512]{1,0:T(8,128)(2,1)S(1)}, bf16[128,512]{1,0:T(8,128)(2,1)S(1)}, u32[]{:S(2)}, u32[]{:S(2)}) %collective-permute-start.28) | collective-permute-done | bytes 131104 | tf_op jit(solution)/shard_map/ppermute | solution.py:103
  114.4 3.8 %collective-permute-start.30 = (bf16[128,64]{1,0:T(8,128)(2,1)S(1)}, bf16[128,64]{1,0:T(8,128)(2,1)S(1)}, u32[]{:S(2)}, u32[]{:S(2)}) collective-permute-start(bf16[128,64]{1,0:T(8,128)(2,1)S(1)} %get-tuple-element.26), channel_id=1, source_target_pairs={{0,1},{1,0},{2,3},{3,2},{4,5},{5,4},{6,7},{7,6},{8,9},{9,8},{10,11... | collective-permute-start | bytes 49160 | tf_op jit(solution)/shard_map/ppermute | solution.py:103
  119.4 3.7 %collective-permute-done.31 = bf16[128,64]{1,0:T(8,128)(2,1)S(1)} collective-permute-done((bf16[128,64]{1,0:T(8,128)(2,1)S(1)}, bf16[128,64]{1,0:T(8,128)(2,1)S(1)}, u32[]{:S(2)}, u32[]{:S(2)}) %collective-permute-start.31) | collective-permute-done | bytes 16416 | tf_op jit(solution)/shard_map/ppermute | solution.py:103
  124.9 3.6 %collective-permute-start.32 = (bf16[128,64]{1,0:T(8,128)(2,1)S(1)}, bf16[128,64]{1,0:T(8,128)(2,1)S(1)}, u32[]{:S(2)}, u32[]{:S(2)}) collective-permute-start(bf16[128,64]{1,0:T(8,128)(2,1)S(1)} %get-tuple-element.24), channel_id=1, source_target_pairs={{0,1},{1,0},{2,3},{3,2},{4,5},{5,4},{6,7},{7,6},{8,9},{9,8},{10,11... | collective-permute-start | bytes 49160 | tf_op jit(solution)/shard_map/ppermute | solution.py:103
  129.7 3.7 %collective-permute-done.33 = bf16[128,64]{1,0:T(8,128)(2,1)S(1)} collective-permute-done((bf16[128,64]{1,0:T(8,128)(2,1)S(1)}, bf16[128,64]{1,0:T(8,128)(2,1)S(1)}, u32[]{:S(2)}, u32[]{:S(2)}) %collective-permute-start.33) | collective-permute-done | bytes 16416 | tf_op jit(solution)/shard_map/ppermute | solution.py:103
  135.2 2.2 %collective-permute-start.34 = (bf16[128,64]{1,0:T(8,128)(2,1)S(1)}, bf16[128,64]{1,0:T(8,128)(2,1)S(1)}, u32[]{:S(2)}, u32[]{:S(2)}) collective-permute-start(bf16[128,64]{1,0:T(8,128)(2,1)S(1)} %get-tuple-element.22), channel_id=1, source_target_pairs={{0,1},{1,0},{2,3},{3,2},{4,5},{5,4},{6,7},{7,6},{8,9},{9,8},{10,11... | collective-permute-start | bytes 49160 | tf_op jit(solution)/shard_map/ppermute | solution.py:103
  138.6 3.7 %collective-permute-done.35 = bf16[128,64]{1,0:T(8,128)(2,1)S(1)} collective-permute-done((bf16[128,64]{1,0:T(8,128)(2,1)S(1)}, bf16[128,64]{1,0:T(8,128)(2,1)S(1)}, u32[]{:S(2)}, u32[]{:S(2)}) %collective-permute-start.35) | collective-permute-done | bytes 16416 | tf_op jit(solution)/shard_map/ppermute | solution.py:103
  144.1 2.2 %collective-permute-start.36 = (bf16[128,64]{1,0:T(8,128)(2,1)S(1)}, bf16[128,64]{1,0:T(8,128)(2,1)S(1)}, u32[]{:S(2)}, u32[]{:S(2)}) collective-permute-start(bf16[128,64]{1,0:T(8,128)(2,1)S(1)} %get-tuple-element.20), channel_id=1, source_target_pairs={{0,1},{1,0},{2,3},{3,2},{4,5},{5,4},{6,7},{7,6},{8,9},{9,8},{10,11... | collective-permute-start | bytes 49160 | tf_op jit(solution)/shard_map/ppermute | solution.py:103
  147.6 3.7 %collective-permute-done.37 = bf16[128,64]{1,0:T(8,128)(2,1)S(1)} collective-permute-done((bf16[128,64]{1,0:T(8,128)(2,1)S(1)}, bf16[128,64]{1,0:T(8,128)(2,1)S(1)}, u32[]{:S(2)}, u32[]{:S(2)}) %collective-permute-start.37) | collective-permute-done | bytes 16416 | tf_op jit(solution)/shard_map/ppermute | solution.py:103
  153.1 2.2 %collective-permute-start.38 = (bf16[128,64]{1,0:T(8,128)(2,1)S(1)}, bf16[128,64]{1,0:T(8,128)(2,1)S(1)}, u32[]{:S(2)}, u32[]{:S(2)}) collective-permute-start(bf16[128,64]{1,0:T(8,128)(2,1)S(1)} %get-tuple-element.18), channel_id=1, source_target_pairs={{0,1},{1,0},{2,3},{3,2},{4,5},{5,4},{6,7},{7,6},{8,9},{9,8},{10,11... | collective-permute-start | bytes 49160 | tf_op jit(solution)/shard_map/ppermute | solution.py:103
  156.5 3.7 %collective-permute-done.39 = bf16[128,64]{1,0:T(8,128)(2,1)S(1)} collective-permute-done((bf16[128,64]{1,0:T(8,128)(2,1)S(1)}, bf16[128,64]{1,0:T(8,128)(2,1)S(1)}, u32[]{:S(2)}, u32[]{:S(2)}) %collective-permute-start.39) | collective-permute-done | bytes 16416 | tf_op jit(solution)/shard_map/ppermute | solution.py:103
  162.0 2.2 %collective-permute-start.40 = (bf16[128,64]{1,0:T(8,128)(2,1)S(1)}, bf16[128,64]{1,0:T(8,128)(2,1)S(1)}, u32[]{:S(2)}, u32[]{:S(2)}) collective-permute-start(bf16[128,64]{1,0:T(8,128)(2,1)S(1)} %get-tuple-element.16), channel_id=1, source_target_pairs={{0,1},{1,0},{2,3},{3,2},{4,5},{5,4},{6,7},{7,6},{8,9},{9,8},{10,11... | collective-permute-start | bytes 49160 | tf_op jit(solution)/shard_map/ppermute | solution.py:103
  165.4 3.7 %collective-permute-done.41 = bf16[128,64]{1,0:T(8,128)(2,1)S(1)} collective-permute-done((bf16[128,64]{1,0:T(8,128)(2,1)S(1)}, bf16[128,64]{1,0:T(8,128)(2,1)S(1)}, u32[]{:S(2)}, u32[]{:S(2)}) %collective-permute-start.41) | collective-permute-done | bytes 16416 | tf_op jit(solution)/shard_map/ppermute | solution.py:103
  (360 shorter events, 61.6 us)
Async XLA Ops:
  1.1 9.2 %collective-permute-start = (bf16[128,64]{1,0:T(8,128)(2,1)S(1)}, bf16[128,64]{1,0:T(8,128)(2,1)S(1)}, u32[]{:S(2)}, u32[]{:S(2)}) collective-permute-start(bf16[128,64]{1,0:T(8,128)(2,1)S(1)} %get-tuple-element.42), channel_id=1, source_target_pairs={{0,1},{1,0},{2,3},{3,2},{4,5},{5,4},{6,7},{7,6},{8,9},{9,8},{10,11... | collective-permute-start | bytes 49160 | tf_op jit(solution)/shard_map/ppermute | solution.py:103
  4.5 5.9 %collective-permute-start.1 = (bf16[128,64]{1,0:T(8,128)(2,1)S(1)}, bf16[128,64]{1,0:T(8,128)(2,1)S(1)}, u32[]{:S(2)}, u32[]{:S(2)}) collective-permute-start(bf16[128,64]{1,0:T(8,128)(2,1)S(1)} %get-tuple-element.43), channel_id=1, source_target_pairs={{0,31},{1,2},{2,1},{3,4},{4,3},{5,6},{6,5},{7,8},{8,7},{9,10},{10,... | collective-permute-start | bytes 49160 | tf_op jit(solution)/shard_map/ppermute | solution.py:103
  10.6 5.7 %collective-permute-start.2 = (bf16[128,512]{1,0:T(8,128)(2,1)S(1)}, bf16[128,512]{1,0:T(8,128)(2,1)S(1)}, u32[]{:S(2)}, u32[]{:S(2)}) collective-permute-start(bf16[128,512]{1,0:T(8,128)(2,1)S(1)} %get-tuple-element.9), channel_id=1, source_target_pairs={{0,32},{32,0},{64,96},{96,64},{128,160},{160,128},{192,224},{224,1... | collective-permute-start | bytes 393224 | tf_op jit(solution)/shard_map/ppermute | solution.py:103
  11.0 8.1 %collective-permute-start.3 = (bf16[128,512]{1,0:T(8,128)(2,1)S(1)}, bf16[128,512]{1,0:T(8,128)(2,1)S(1)}, u32[]{:S(2)}, u32[]{:S(2)}) collective-permute-start(bf16[128,512]{1,0:T(8,128)(2,1)S(1)} %get-tuple-element.9), channel_id=1, source_target_pairs={{0,64},{32,96},{64,0},{96,32},{128,192},{160,224},{192,128},{224,1... | collective-permute-start | bytes 393224 | tf_op jit(solution)/shard_map/ppermute | solution.py:103
  12.3 7.8 %collective-permute-start.4 = (bf16[128,512]{1,0:T(8,128)(2,1)S(1)}, bf16[128,512]{1,0:T(8,128)(2,1)S(1)}, u32[]{:S(2)}, u32[]{:S(2)}) collective-permute-start(bf16[128,512]{1,0:T(8,128)(2,1)S(1)} %get-tuple-element.9), channel_id=1, source_target_pairs={{0,96},{32,64},{64,32},{96,0},{128,224},{160,192},{192,160},{224,1... | collective-permute-start | bytes 393224 | tf_op jit(solution)/shard_map/ppermute | solution.py:103
  13.3 6.8 %collective-permute-start.5 = (bf16[128,512]{1,0:T(8,128)(2,1)S(1)}, bf16[128,512]{1,0:T(8,128)(2,1)S(1)}, u32[]{:S(2)}, u32[]{:S(2)}) collective-permute-start(bf16[128,512]{1,0:T(8,128)(2,1)S(1)} %get-tuple-element.9), channel_id=1, source_target_pairs={{0,128},{32,160},{64,192},{96,224},{128,0},{160,32},{192,64},{224,... | collective-permute-start | bytes 393224 | tf_op jit(solution)/shard_map/ppermute | solution.py:103
  16.2 6.8 %collective-permute-start.6 = (bf16[128,512]{1,0:T(8,128)(2,1)S(1)}, bf16[128,512]{1,0:T(8,128)(2,1)S(1)}, u32[]{:S(2)}, u32[]{:S(2)}) collective-permute-start(bf16[128,512]{1,0:T(8,128)(2,1)S(1)} %get-tuple-element.9), channel_id=1, source_target_pairs={{0,160},{32,128},{64,224},{96,192},{128,32},{160,0},{192,96},{224,... | collective-permute-start | bytes 393224 | tf_op jit(solution)/shard_map/ppermute | solution.py:103
  16.3 6.8 %collective-permute-start.7 = (bf16[128,512]{1,0:T(8,128)(2,1)S(1)}, bf16[128,512]{1,0:T(8,128)(2,1)S(1)}, u32[]{:S(2)}, u32[]{:S(2)}) collective-permute-start(bf16[128,512]{1,0:T(8,128)(2,1)S(1)} %get-tuple-element.9), channel_id=1, source_target_pairs={{0,192},{32,224},{64,128},{96,160},{128,64},{160,96},{192,0},{224,... | collective-permute-start | bytes 393224 | tf_op jit(solution)/shard_map/ppermute | solution.py:103
  19.1 7.7 %collective-permute-start.8 = (bf16[128,512]{1,0:T(8,128)(2,1)S(1)}, bf16[128,512]{1,0:T(8,128)(2,1)S(1)}, u32[]{:S(2)}, u32[]{:S(2)}) collective-permute-start(bf16[128,512]{1,0:T(8,128)(2,1)S(1)} %get-tuple-element.9), channel_id=1, source_target_pairs={{0,224},{32,192},{64,160},{96,128},{128,96},{160,64},{192,32},{224... | collective-permute-start | bytes 393224 | tf_op jit(solution)/shard_map/ppermute | solution.py:103
  28.8 13.8 %collective-permute-start.10 = (bf16[128,64]{1,0:T(8,128)(2,1)S(1)}, bf16[128,64]{1,0:T(8,128)(2,1)S(1)}, u32[]{:S(2)}, u32[]{:S(2)}) collective-permute-start(bf16[128,64]{1,0:T(8,128)(2,1)S(1)} %get-tuple-element.41), channel_id=1, source_target_pairs={{0,31},{1,2},{2,1},{3,4},{4,3},{5,6},{6,5},{7,8},{8,7},{9,10},{10,... | collective-permute-start | bytes 49160 | tf_op jit(solution)/shard_map/ppermute | solution.py:103
  37.0 5.6 %collective-permute-start.9 = (bf16[128,64]{1,0:T(8,128)(2,1)S(1)}, bf16[128,64]{1,0:T(8,128)(2,1)S(1)}, u32[]{:S(2)}, u32[]{:S(2)}) collective-permute-start(bf16[128,64]{1,0:T(8,128)(2,1)S(1)} %get-tuple-element.40), channel_id=1, source_target_pairs={{0,1},{1,0},{2,3},{3,2},{4,5},{5,4},{6,7},{7,6},{8,9},{9,8},{10,11... | collective-permute-start | bytes 49160 | tf_op jit(solution)/shard_map/ppermute | solution.py:103
  44.9 4.8 %collective-permute-start.12 = (bf16[128,64]{1,0:T(8,128)(2,1)S(1)}, bf16[128,64]{1,0:T(8,128)(2,1)S(1)}, u32[]{:S(2)}, u32[]{:S(2)}) collective-permute-start(bf16[128,64]{1,0:T(8,128)(2,1)S(1)} %get-tuple-element.39), channel_id=1, source_target_pairs={{0,31},{1,2},{2,1},{3,4},{4,3},{5,6},{6,5},{7,8},{8,7},{9,10},{10,... | collective-permute-start | bytes 49160 | tf_op jit(solution)/shard_map/ppermute | solution.py:103
  53.9 4.8 %collective-permute-start.14 = (bf16[128,64]{1,0:T(8,128)(2,1)S(1)}, bf16[128,64]{1,0:T(8,128)(2,1)S(1)}, u32[]{:S(2)}, u32[]{:S(2)}) collective-permute-start(bf16[128,64]{1,0:T(8,128)(2,1)S(1)} %get-tuple-element.37), channel_id=1, source_target_pairs={{0,31},{1,2},{2,1},{3,4},{4,3},{5,6},{6,5},{7,8},{8,7},{9,10},{10,... | collective-permute-start | bytes 49160 | tf_op jit(solution)/shard_map/ppermute | solution.py:103
  63.0 4.8 %collective-permute-start.16 = (bf16[128,64]{1,0:T(8,128)(2,1)S(1)}, bf16[128,64]{1,0:T(8,128)(2,1)S(1)}, u32[]{:S(2)}, u32[]{:S(2)}) collective-permute-start(bf16[128,64]{1,0:T(8,128)(2,1)S(1)} %get-tuple-element.35), channel_id=1, source_target_pairs={{0,31},{1,2},{2,1},{3,4},{4,3},{5,6},{6,5},{7,8},{8,7},{9,10},{10,... | collective-permute-start | bytes 49160 | tf_op jit(solution)/shard_map/ppermute | solution.py:103
  71.9 4.8 %collective-permute-start.18 = (bf16[128,64]{1,0:T(8,128)(2,1)S(1)}, bf16[128,64]{1,0:T(8,128)(2,1)S(1)}, u32[]{:S(2)}, u32[]{:S(2)}) collective-permute-start(bf16[128,64]{1,0:T(8,128)(2,1)S(1)} %get-tuple-element.33), channel_id=1, source_target_pairs={{0,31},{1,2},{2,1},{3,4},{4,3},{5,6},{6,5},{7,8},{8,7},{9,10},{10,... | collective-permute-start | bytes 49160 | tf_op jit(solution)/shard_map/ppermute | solution.py:103
  80.8 4.8 %collective-permute-start.20 = (bf16[128,64]{1,0:T(8,128)(2,1)S(1)}, bf16[128,64]{1,0:T(8,128)(2,1)S(1)}, u32[]{:S(2)}, u32[]{:S(2)}) collective-permute-start(bf16[128,64]{1,0:T(8,128)(2,1)S(1)} %get-tuple-element.31), channel_id=1, source_target_pairs={{0,31},{1,2},{2,1},{3,4},{4,3},{5,6},{6,5},{7,8},{8,7},{9,10},{10,... | collective-permute-start | bytes 49160 | tf_op jit(solution)/shard_map/ppermute | solution.py:103
  89.7 4.8 %collective-permute-start.22 = (bf16[128,64]{1,0:T(8,128)(2,1)S(1)}, bf16[128,64]{1,0:T(8,128)(2,1)S(1)}, u32[]{:S(2)}, u32[]{:S(2)}) collective-permute-start(bf16[128,64]{1,0:T(8,128)(2,1)S(1)} %get-tuple-element.29), channel_id=1, source_target_pairs={{0,31},{1,2},{2,1},{3,4},{4,3},{5,6},{6,5},{7,8},{8,7},{9,10},{10,... | collective-permute-start | bytes 49160 | tf_op jit(solution)/shard_map/ppermute | solution.py:103
  94.8 6.2 %collective-permute-start.23 = (bf16[128,512]{1,0:T(8,128)(2,1)S(1)}, bf16[128,512]{1,0:T(8,128)(2,1)S(1)}, u32[]{:S(2)}, u32[]{:S(2)}) collective-permute-start(bf16[128,512]{1,0:T(8,128)(2,1)S(1)} %get-tuple-element.7), channel_id=1, source_target_pairs={{0,32},{32,0},{64,96},{96,64},{128,160},{160,128},{192,224},{224,1... | collective-permute-start | bytes 393224 | tf_op jit(solution)/shard_map/ppermute | solution.py:103
  95.7 6.8 %collective-permute-start.24 = (bf16[128,512]{1,0:T(8,128)(2,1)S(1)}, bf16[128,512]{1,0:T(8,128)(2,1)S(1)}, u32[]{:S(2)}, u32[]{:S(2)}) collective-permute-start(bf16[128,512]{1,0:T(8,128)(2,1)S(1)} %get-tuple-element.7), channel_id=1, source_target_pairs={{0,64},{32,96},{64,0},{96,32},{128,192},{160,224},{192,128},{224,1... | collective-permute-start | bytes 393224 | tf_op jit(solution)/shard_map/ppermute | solution.py:103
  95.7 8.8 %collective-permute-start.25 = (bf16[128,512]{1,0:T(8,128)(2,1)S(1)}, bf16[128,512]{1,0:T(8,128)(2,1)S(1)}, u32[]{:S(2)}, u32[]{:S(2)}) collective-permute-start(bf16[128,512]{1,0:T(8,128)(2,1)S(1)} %get-tuple-element.7), channel_id=1, source_target_pairs={{0,96},{32,64},{64,32},{96,0},{128,224},{160,192},{192,160},{224,1... | collective-permute-start | bytes 393224 | tf_op jit(solution)/shard_map/ppermute | solution.py:103
  97.6 9.7 %collective-permute-start.26 = (bf16[128,512]{1,0:T(8,128)(2,1)S(1)}, bf16[128,512]{1,0:T(8,128)(2,1)S(1)}, u32[]{:S(2)}, u32[]{:S(2)}) collective-permute-start(bf16[128,512]{1,0:T(8,128)(2,1)S(1)} %get-tuple-element.7), channel_id=1, source_target_pairs={{0,128},{32,160},{64,192},{96,224},{128,0},{160,32},{192,64},{224,... | collective-permute-start | bytes 393224 | tf_op jit(solution)/shard_map/ppermute | solution.py:103
  99.0 8.3 %collective-permute-start.27 = (bf16[128,512]{1,0:T(8,128)(2,1)S(1)}, bf16[128,512]{1,0:T(8,128)(2,1)S(1)}, u32[]{:S(2)}, u32[]{:S(2)}) collective-permute-start(bf16[128,512]{1,0:T(8,128)(2,1)S(1)} %get-tuple-element.7), channel_id=1, source_target_pairs={{0,160},{32,128},{64,224},{96,192},{128,32},{160,0},{192,96},{224,... | collective-permute-start | bytes 393224 | tf_op jit(solution)/shard_map/ppermute | solution.py:103
  101.0 11.4 %collective-permute-start.28 = (bf16[128,512]{1,0:T(8,128)(2,1)S(1)}, bf16[128,512]{1,0:T(8,128)(2,1)S(1)}, u32[]{:S(2)}, u32[]{:S(2)}) collective-permute-start(bf16[128,512]{1,0:T(8,128)(2,1)S(1)} %get-tuple-element.7), channel_id=1, source_target_pairs={{0,192},{32,224},{64,128},{96,160},{128,64},{160,96},{192,0},{224,... | collective-permute-start | bytes 393224 | tf_op jit(solution)/shard_map/ppermute | solution.py:103
  102.5 9.9 %collective-permute-start.29 = (bf16[128,512]{1,0:T(8,128)(2,1)S(1)}, bf16[128,512]{1,0:T(8,128)(2,1)S(1)}, u32[]{:S(2)}, u32[]{:S(2)}) collective-permute-start(bf16[128,512]{1,0:T(8,128)(2,1)S(1)} %get-tuple-element.7), channel_id=1, source_target_pairs={{0,224},{32,192},{64,160},{96,128},{128,96},{160,64},{192,32},{224... | collective-permute-start | bytes 393224 | tf_op jit(solution)/shard_map/ppermute | solution.py:103
  114.4 4.9 %collective-permute-start.30 = (bf16[128,64]{1,0:T(8,128)(2,1)S(1)}, bf16[128,64]{1,0:T(8,128)(2,1)S(1)}, u32[]{:S(2)}, u32[]{:S(2)}) collective-permute-start(bf16[128,64]{1,0:T(8,128)(2,1)S(1)} %get-tuple-element.26), channel_id=1, source_target_pairs={{0,1},{1,0},{2,3},{3,2},{4,5},{5,4},{6,7},{7,6},{8,9},{9,8},{10,11... | collective-permute-start | bytes 49160 | tf_op jit(solution)/shard_map/ppermute | solution.py:103
  118.2 4.8 %collective-permute-start.31 = (bf16[128,64]{1,0:T(8,128)(2,1)S(1)}, bf16[128,64]{1,0:T(8,128)(2,1)S(1)}, u32[]{:S(2)}, u32[]{:S(2)}) collective-permute-start(bf16[128,64]{1,0:T(8,128)(2,1)S(1)} %get-tuple-element.27), channel_id=1, source_target_pairs={{0,31},{1,2},{2,1},{3,4},{4,3},{5,6},{6,5},{7,8},{8,7},{9,10},{10,... | collective-permute-start | bytes 49160 | tf_op jit(solution)/shard_map/ppermute | solution.py:103
  124.9 4.8 %collective-permute-start.32 = (bf16[128,64]{1,0:T(8,128)(2,1)S(1)}, bf16[128,64]{1,0:T(8,128)(2,1)S(1)}, u32[]{:S(2)}, u32[]{:S(2)}) collective-permute-start(bf16[128,64]{1,0:T(8,128)(2,1)S(1)} %get-tuple-element.24), channel_id=1, source_target_pairs={{0,1},{1,0},{2,3},{3,2},{4,5},{5,4},{6,7},{7,6},{8,9},{9,8},{10,11... | collective-permute-start | bytes 49160 | tf_op jit(solution)/shard_map/ppermute | solution.py:103
  128.5 4.8 %collective-permute-start.33 = (bf16[128,64]{1,0:T(8,128)(2,1)S(1)}, bf16[128,64]{1,0:T(8,128)(2,1)S(1)}, u32[]{:S(2)}, u32[]{:S(2)}) collective-permute-start(bf16[128,64]{1,0:T(8,128)(2,1)S(1)} %get-tuple-element.25), channel_id=1, source_target_pairs={{0,31},{1,2},{2,1},{3,4},{4,3},{5,6},{6,5},{7,8},{8,7},{9,10},{10,... | collective-permute-start | bytes 49160 | tf_op jit(solution)/shard_map/ppermute | solution.py:103
  137.5 4.8 %collective-permute-start.35 = (bf16[128,64]{1,0:T(8,128)(2,1)S(1)}, bf16[128,64]{1,0:T(8,128)(2,1)S(1)}, u32[]{:S(2)}, u32[]{:S(2)}) collective-permute-start(bf16[128,64]{1,0:T(8,128)(2,1)S(1)} %get-tuple-element.23), channel_id=1, source_target_pairs={{0,31},{1,2},{2,1},{3,4},{4,3},{5,6},{6,5},{7,8},{8,7},{9,10},{10,... | collective-permute-start | bytes 49160 | tf_op jit(solution)/shard_map/ppermute | solution.py:103
  146.4 4.8 %collective-permute-start.37 = (bf16[128,64]{1,0:T(8,128)(2,1)S(1)}, bf16[128,64]{1,0:T(8,128)(2,1)S(1)}, u32[]{:S(2)}, u32[]{:S(2)}) collective-permute-start(bf16[128,64]{1,0:T(8,128)(2,1)S(1)} %get-tuple-element.21), channel_id=1, source_target_pairs={{0,31},{1,2},{2,1},{3,4},{4,3},{5,6},{6,5},{7,8},{8,7},{9,10},{10,... | collective-permute-start | bytes 49160 | tf_op jit(solution)/shard_map/ppermute | solution.py:103
  155.3 4.8 %collective-permute-start.39 = (bf16[128,64]{1,0:T(8,128)(2,1)S(1)}, bf16[128,64]{1,0:T(8,128)(2,1)S(1)}, u32[]{:S(2)}, u32[]{:S(2)}) collective-permute-start(bf16[128,64]{1,0:T(8,128)(2,1)S(1)} %get-tuple-element.19), channel_id=1, source_target_pairs={{0,31},{1,2},{2,1},{3,4},{4,3},{5,6},{6,5},{7,8},{8,7},{9,10},{10,... | collective-permute-start | bytes 49160 | tf_op jit(solution)/shard_map/ppermute | solution.py:103
  164.2 4.8 %collective-permute-start.41 = (bf16[128,64]{1,0:T(8,128)(2,1)S(1)}, bf16[128,64]{1,0:T(8,128)(2,1)S(1)}, u32[]{:S(2)}, u32[]{:S(2)}) collective-permute-start(bf16[128,64]{1,0:T(8,128)(2,1)S(1)} %get-tuple-element.17), channel_id=1, source_target_pairs={{0,31},{1,2},{2,1},{3,4},{4,3},{5,6},{6,5},{7,8},{8,7},{9,10},{10,... | collective-permute-start | bytes 49160 | tf_op jit(solution)/shard_map/ppermute | solution.py:103
  (17 other events, 63.5 us)

commit v5 on v3

--- a/solution.py
+++ b/solution.py
@@ -119,8 +119,9 @@
 def gather_nodes(rows):
     nodes = lax.axis_size("node")
     me = lax.axis_index("node")
-    swaps = [rows] + [swapped(rows, "node", lambda i, k=k: i ^ k) for k in range(1, nodes)]
-    return swaps, me ^ jnp.arange(nodes)
+    masks = [5, 4, 3, 7, 2, 6, 1] if nodes == 8 else list(range(1, nodes))
+    swaps = [rows] + [swapped(rows, "node", lambda i, k=k: i ^ k) for k in masks]
+    return swaps, me ^ jnp.asarray([0] + masks)
 
 
 def local(start_state, node_states, reaction_rates, volume, face_lift):

time: 168 us -> 167 us (level); the launches traced: 168 us -> 165 us
  waiting for transfers between devices: 67.2 us -> 65 us
    ppermute x42, waiting for transfers between devices: 67.2 us -> 65 us  [swapped(): lax.ppermute(array, axis, [(i, partner(i) % devices) for i in range(devic...]
  transfers between devices with their start and end apart: 42 -> 42, of which waited for: 29 -> 31; matrix products, arithmetic and copies ran while one was open for 6% -> 6% of each run, Pallas kernels for 0% -> 0%
where the time goes in v5:
time: 167 us; the launch traced here: 165 us
  waiting for transfers between devices  65 us (39%)
  starting transfers between devices  64.6 us (39%)
  matrix products  18.9 us (11%)
  local copies, waits for them, and re-layouts  8.6 us (5%)
  other arithmetic  5.9 us (4%)
  between operations  2.09 us (1%)
    ppermute x42, waiting for transfers between devices, swapped(): lax.ppermute(array, axis, [(i, partner(i) % devices) for i in range(devic...  65 us
    ppermute x42, starting transfers between devices, swapped(): lax.ppermute(array, axis, [(i, partner(i) % devices) for i in range(devic...  64.6 us
    dot_general x14, matrix products, apply_operator(): return own + jnp.dot(faces, x_lift, preferred_element_type=jnp.float32)  11.4 us
    dot_general x14, matrix products, local_terms(): jnp.dot(inputs, stacked, preferred_element_type=jnp.float32)  3.82 us
    dot_general x14, matrix products, local_terms(): jnp.dot(rounded, select, preferred_element_type=jnp.float32)  3.67 us
  transfers between devices with their start and end apart: 42, of which 31 were waited for; matrix products, arithmetic and copies ran while one was open for 6% of the time, Pallas kernels for 0%

profile of v5, /device:TPU:1, one launch (start us, length us, event | category | flops | bytes accessed | tf_op | source)
XLA Modules:
  0.0 165.0 jit_solution(12345359499633547213)
XLA Ops:
  1.1 3.3 %collective-permute-start = (bf16[128,64]{1,0:T(8,128)(2,1)S(1)}, bf16[128,64]{1,0:T(8,128)(2,1)S(1)}, u32[]{:S(2)}, u32[]{:S(2)}) collective-permute-start(bf16[128,64]{1,0:T(8,128)(2,1)S(1)} %get-tuple-element.120), channel_id=1, source_target_pairs={{0,1},{1,0},{2,3},{3,2},{4,5},{5,4},{6,7},{7,6},{8,9},{9,8},{10,11... | collective-permute-start | bytes 49160 | tf_op jit(solution)/shard_map/ppermute | solution.py:99
  10.6 3.0 %collective-permute-start.2 = (bf16[128,512]{1,0:T(8,128)(2,1)S(1)}, bf16[128,512]{1,0:T(8,128)(2,1)S(1)}, u32[]{:S(2)}, u32[]{:S(2)}) collective-permute-start(bf16[128,512]{1,0:T(8,128)(2,1)S(1)} %get-tuple-element.9), channel_id=1, source_target_pairs={{0,160},{32,128},{64,224},{96,192},{128,32},{160,0},{192,96},{224,... | collective-permute-start | bytes 393224 | tf_op jit(solution)/shard_map/ppermute | solution.py:99
  13.7 2.1 %collective-permute-start.4 = (bf16[128,512]{1,0:T(8,128)(2,1)S(1)}, bf16[128,512]{1,0:T(8,128)(2,1)S(1)}, u32[]{:S(2)}, u32[]{:S(2)}) collective-permute-start(bf16[128,512]{1,0:T(8,128)(2,1)S(1)} %get-tuple-element.9), channel_id=1, source_target_pairs={{0,96},{32,64},{64,32},{96,0},{128,224},{160,192},{192,160},{224,1... | collective-permute-start | bytes 393224 | tf_op jit(solution)/shard_map/ppermute | solution.py:99
  22.2 4.0 %collective-permute-done.7 = bf16[128,512]{1,0:T(8,128)(2,1)S(1)} collective-permute-done((bf16[128,512]{1,0:T(8,128)(2,1)S(1)}, bf16[128,512]{1,0:T(8,128)(2,1)S(1)}, u32[]{:S(2)}, u32[]{:S(2)}) %collective-permute-start.7) | collective-permute-done | bytes 131104 | tf_op jit(solution)/shard_map/ppermute | solution.py:99
  28.1 6.9 %collective-permute-start.10 = (bf16[128,64]{1,0:T(8,128)(2,1)S(1)}, bf16[128,64]{1,0:T(8,128)(2,1)S(1)}, u32[]{:S(2)}, u32[]{:S(2)}) collective-permute-start(bf16[128,64]{1,0:T(8,128)(2,1)S(1)} %get-tuple-element.113), channel_id=1, source_target_pairs={{0,31},{1,2},{2,1},{3,4},{4,3},{5,6},{6,5},{7,8},{8,7},{9,10},{10,... | collective-permute-start | bytes 49160 | tf_op jit(solution)/shard_map/ppermute | solution.py:99
  34.9 4.6 %collective-permute-start.9 = (bf16[128,64]{1,0:T(8,128)(2,1)S(1)}, bf16[128,64]{1,0:T(8,128)(2,1)S(1)}, u32[]{:S(2)}, u32[]{:S(2)}) collective-permute-start(bf16[128,64]{1,0:T(8,128)(2,1)S(1)} %get-tuple-element.112), channel_id=1, source_target_pairs={{0,1},{1,0},{2,3},{3,2},{4,5},{5,4},{6,7},{7,6},{8,9},{9,8},{10,11... | collective-permute-start | bytes 49160 | tf_op jit(solution)/shard_map/ppermute | solution.py:99
  43.7 4.0 %collective-permute-done.12 = bf16[128,64]{1,0:T(8,128)(2,1)S(1)} collective-permute-done((bf16[128,64]{1,0:T(8,128)(2,1)S(1)}, bf16[128,64]{1,0:T(8,128)(2,1)S(1)}, u32[]{:S(2)}, u32[]{:S(2)}) %collective-permute-start.12) | collective-permute-done | bytes 16416 | tf_op jit(solution)/shard_map/ppermute | solution.py:99
  49.3 2.3 %collective-permute-start.13 = (bf16[128,64]{1,0:T(8,128)(2,1)S(1)}, bf16[128,64]{1,0:T(8,128)(2,1)S(1)}, u32[]{:S(2)}, u32[]{:S(2)}) collective-permute-start(bf16[128,64]{1,0:T(8,128)(2,1)S(1)} %get-tuple-element.96), channel_id=1, source_target_pairs={{0,1},{1,0},{2,3},{3,2},{4,5},{5,4},{6,7},{7,6},{8,9},{9,8},{10,11... | collective-permute-start | bytes 49160 | tf_op jit(solution)/shard_map/ppermute | solution.py:99
  52.4 4.0 %collective-permute-done.14 = bf16[128,64]{1,0:T(8,128)(2,1)S(1)} collective-permute-done((bf16[128,64]{1,0:T(8,128)(2,1)S(1)}, bf16[128,64]{1,0:T(8,128)(2,1)S(1)}, u32[]{:S(2)}, u32[]{:S(2)}) %collective-permute-start.14) | collective-permute-done | bytes 16416 | tf_op jit(solution)/shard_map/ppermute | solution.py:99
  58.0 2.5 %collective-permute-start.15 = (bf16[128,64]{1,0:T(8,128)(2,1)S(1)}, bf16[128,64]{1,0:T(8,128)(2,1)S(1)}, u32[]{:S(2)}, u32[]{:S(2)}) collective-permute-start(bf16[128,64]{1,0:T(8,128)(2,1)S(1)} %get-tuple-element.88), channel_id=1, source_target_pairs={{0,1},{1,0},{2,3},{3,2},{4,5},{5,4},{6,7},{7,6},{8,9},{9,8},{10,11... | collective-permute-start | bytes 49160 | tf_op jit(solution)/shard_map/ppermute | solution.py:99
  61.3 4.0 %collective-permute-done.16 = bf16[128,64]{1,0:T(8,128)(2,1)S(1)} collective-permute-done((bf16[128,64]{1,0:T(8,128)(2,1)S(1)}, bf16[128,64]{1,0:T(8,128)(2,1)S(1)}, u32[]{:S(2)}, u32[]{:S(2)}) %collective-permute-start.16) | collective-permute-done | bytes 16416 | tf_op jit(solution)/shard_map/ppermute | solution.py:99
  66.9 2.3 %collective-permute-start.17 = (bf16[128,64]{1,0:T(8,128)(2,1)S(1)}, bf16[128,64]{1,0:T(8,128)(2,1)S(1)}, u32[]{:S(2)}, u32[]{:S(2)}) collective-permute-start(bf16[128,64]{1,0:T(8,128)(2,1)S(1)} %get-tuple-element.80), channel_id=1, source_target_pairs={{0,1},{1,0},{2,3},{3,2},{4,5},{5,4},{6,7},{7,6},{8,9},{9,8},{10,11... | collective-permute-start | bytes 49160 | tf_op jit(solution)/shard_map/ppermute | solution.py:99
  70.0 4.0 %collective-permute-done.18 = bf16[128,64]{1,0:T(8,128)(2,1)S(1)} collective-permute-done((bf16[128,64]{1,0:T(8,128)(2,1)S(1)}, bf16[128,64]{1,0:T(8,128)(2,1)S(1)}, u32[]{:S(2)}, u32[]{:S(2)}) %collective-permute-start.18) | collective-permute-done | bytes 16416 | tf_op jit(solution)/shard_map/ppermute | solution.py:99
  75.6 2.3 %collective-permute-start.19 = (bf16[128,64]{1,0:T(8,128)(2,1)S(1)}, bf16[128,64]{1,0:T(8,128)(2,1)S(1)}, u32[]{:S(2)}, u32[]{:S(2)}) collective-permute-start(bf16[128,64]{1,0:T(8,128)(2,1)S(1)} %get-tuple-element.72), channel_id=1, source_target_pairs={{0,1},{1,0},{2,3},{3,2},{4,5},{5,4},{6,7},{7,6},{8,9},{9,8},{10,11... | collective-permute-start | bytes 49160 | tf_op jit(solution)/shard_map/ppermute | solution.py:99
  78.8 4.0 %collective-permute-done.20 = bf16[128,64]{1,0:T(8,128)(2,1)S(1)} collective-permute-done((bf16[128,64]{1,0:T(8,128)(2,1)S(1)}, bf16[128,64]{1,0:T(8,128)(2,1)S(1)}, u32[]{:S(2)}, u32[]{:S(2)}) %collective-permute-start.20) | collective-permute-done | bytes 16416 | tf_op jit(solution)/shard_map/ppermute | solution.py:99
  84.3 2.3 %collective-permute-start.21 = (bf16[128,64]{1,0:T(8,128)(2,1)S(1)}, bf16[128,64]{1,0:T(8,128)(2,1)S(1)}, u32[]{:S(2)}, u32[]{:S(2)}) collective-permute-start(bf16[128,64]{1,0:T(8,128)(2,1)S(1)} %get-tuple-element.64), channel_id=1, source_target_pairs={{0,1},{1,0},{2,3},{3,2},{4,5},{5,4},{6,7},{7,6},{8,9},{9,8},{10,11... | collective-permute-start | bytes 49160 | tf_op jit(solution)/shard_map/ppermute | solution.py:99
  87.5 4.0 %collective-permute-done.22 = bf16[128,64]{1,0:T(8,128)(2,1)S(1)} collective-permute-done((bf16[128,64]{1,0:T(8,128)(2,1)S(1)}, bf16[128,64]{1,0:T(8,128)(2,1)S(1)}, u32[]{:S(2)}, u32[]{:S(2)}) %collective-permute-start.22) | collective-permute-done | bytes 16416 | tf_op jit(solution)/shard_map/ppermute | solution.py:99
  91.7 3.2 %collective-permute-start.23 = (bf16[128,512]{1,0:T(8,128)(2,1)S(1)}, bf16[128,512]{1,0:T(8,128)(2,1)S(1)}, u32[]{:S(2)}, u32[]{:S(2)}) collective-permute-start(bf16[128,512]{1,0:T(8,128)(2,1)S(1)} %get-tuple-element.7), channel_id=1, source_target_pairs={{0,160},{32,128},{64,224},{96,192},{128,32},{160,0},{192,96},{224,... | collective-permute-start | bytes 393224 | tf_op jit(solution)/shard_map/ppermute | solution.py:99
  95.1 2.4 %collective-permute-start.25 = (bf16[128,512]{1,0:T(8,128)(2,1)S(1)}, bf16[128,512]{1,0:T(8,128)(2,1)S(1)}, u32[]{:S(2)}, u32[]{:S(2)}) collective-permute-start(bf16[128,512]{1,0:T(8,128)(2,1)S(1)} %get-tuple-element.7), channel_id=1, source_target_pairs={{0,96},{32,64},{64,32},{96,0},{128,224},{160,192},{192,160},{224,1... | collective-permute-start | bytes 393224 | tf_op jit(solution)/shard_map/ppermute | solution.py:99
  105.5 3.2 %collective-permute-done.27 = bf16[128,512]{1,0:T(8,128)(2,1)S(1)} collective-permute-done((bf16[128,512]{1,0:T(8,128)(2,1)S(1)}, bf16[128,512]{1,0:T(8,128)(2,1)S(1)}, u32[]{:S(2)}, u32[]{:S(2)}) %collective-permute-start.27) | collective-permute-done | bytes 131104 | tf_op jit(solution)/shard_map/ppermute | solution.py:99
  110.8 4.2 %collective-permute-start.30 = (bf16[128,64]{1,0:T(8,128)(2,1)S(1)}, bf16[128,64]{1,0:T(8,128)(2,1)S(1)}, u32[]{:S(2)}, u32[]{:S(2)}) collective-permute-start(bf16[128,64]{1,0:T(8,128)(2,1)S(1)} %get-tuple-element.56), channel_id=1, source_target_pairs={{0,1},{1,0},{2,3},{3,2},{4,5},{5,4},{6,7},{7,6},{8,9},{9,8},{10,11... | collective-permute-start | bytes 49160 | tf_op jit(solution)/shard_map/ppermute | solution.py:99
  115.9 4.0 %collective-permute-done.31 = bf16[128,64]{1,0:T(8,128)(2,1)S(1)} collective-permute-done((bf16[128,64]{1,0:T(8,128)(2,1)S(1)}, bf16[128,64]{1,0:T(8,128)(2,1)S(1)}, u32[]{:S(2)}, u32[]{:S(2)}) %collective-permute-start.31) | collective-permute-done | bytes 16416 | tf_op jit(solution)/shard_map/ppermute | solution.py:99
  121.4 2.3 %collective-permute-start.32 = (bf16[128,64]{1,0:T(8,128)(2,1)S(1)}, bf16[128,64]{1,0:T(8,128)(2,1)S(1)}, u32[]{:S(2)}, u32[]{:S(2)}) collective-permute-start(bf16[128,64]{1,0:T(8,128)(2,1)S(1)} %get-tuple-element.48), channel_id=1, source_target_pairs={{0,1},{1,0},{2,3},{3,2},{4,5},{5,4},{6,7},{7,6},{8,9},{9,8},{10,11... | collective-permute-start | bytes 49160 | tf_op jit(solution)/shard_map/ppermute | solution.py:99
  124.6 4.0 %collective-permute-done.33 = bf16[128,64]{1,0:T(8,128)(2,1)S(1)} collective-permute-done((bf16[128,64]{1,0:T(8,128)(2,1)S(1)}, bf16[128,64]{1,0:T(8,128)(2,1)S(1)}, u32[]{:S(2)}, u32[]{:S(2)}) %collective-permute-start.33) | collective-permute-done | bytes 16416 | tf_op jit(solution)/shard_map/ppermute | solution.py:99
  130.2 2.3 %collective-permute-start.34 = (bf16[128,64]{1,0:T(8,128)(2,1)S(1)}, bf16[128,64]{1,0:T(8,128)(2,1)S(1)}, u32[]{:S(2)}, u32[]{:S(2)}) collective-permute-start(bf16[128,64]{1,0:T(8,128)(2,1)S(1)} %get-tuple-element.40), channel_id=1, source_target_pairs={{0,1},{1,0},{2,3},{3,2},{4,5},{5,4},{6,7},{7,6},{8,9},{9,8},{10,11... | collective-permute-start | bytes 49160 | tf_op jit(solution)/shard_map/ppermute | solution.py:99
  133.3 4.0 %collective-permute-done.35 = bf16[128,64]{1,0:T(8,128)(2,1)S(1)} collective-permute-done((bf16[128,64]{1,0:T(8,128)(2,1)S(1)}, bf16[128,64]{1,0:T(8,128)(2,1)S(1)}, u32[]{:S(2)}, u32[]{:S(2)}) %collective-permute-start.35) | collective-permute-done | bytes 16416 | tf_op jit(solution)/shard_map/ppermute | solution.py:99
  138.9 2.3 %collective-permute-start.36 = (bf16[128,64]{1,0:T(8,128)(2,1)S(1)}, bf16[128,64]{1,0:T(8,128)(2,1)S(1)}, u32[]{:S(2)}, u32[]{:S(2)}) collective-permute-start(bf16[128,64]{1,0:T(8,128)(2,1)S(1)} %get-tuple-element.32), channel_id=1, source_target_pairs={{0,1},{1,0},{2,3},{3,2},{4,5},{5,4},{6,7},{7,6},{8,9},{9,8},{10,11... | collective-permute-start | bytes 49160 | tf_op jit(solution)/shard_map/ppermute | solution.py:99
  142.0 4.0 %collective-permute-done.37 = bf16[128,64]{1,0:T(8,128)(2,1)S(1)} collective-permute-done((bf16[128,64]{1,0:T(8,128)(2,1)S(1)}, bf16[128,64]{1,0:T(8,128)(2,1)S(1)}, u32[]{:S(2)}, u32[]{:S(2)}) %collective-permute-start.37) | collective-permute-done | bytes 16416 | tf_op jit(solution)/shard_map/ppermute | solution.py:99
  147.6 2.3 %collective-permute-start.38 = (bf16[128,64]{1,0:T(8,128)(2,1)S(1)}, bf16[128,64]{1,0:T(8,128)(2,1)S(1)}, u32[]{:S(2)}, u32[]{:S(2)}) collective-permute-start(bf16[128,64]{1,0:T(8,128)(2,1)S(1)} %get-tuple-element.24), channel_id=1, source_target_pairs={{0,1},{1,0},{2,3},{3,2},{4,5},{5,4},{6,7},{7,6},{8,9},{9,8},{10,11... | collective-permute-start | bytes 49160 | tf_op jit(solution)/shard_map/ppermute | solution.py:99
  150.8 4.0 %collective-permute-done.39 = bf16[128,64]{1,0:T(8,128)(2,1)S(1)} collective-permute-done((bf16[128,64]{1,0:T(8,128)(2,1)S(1)}, bf16[128,64]{1,0:T(8,128)(2,1)S(1)}, u32[]{:S(2)}, u32[]{:S(2)}) %collective-permute-start.39) | collective-permute-done | bytes 16416 | tf_op jit(solution)/shard_map/ppermute | solution.py:99
  156.3 2.3 %collective-permute-start.40 = (bf16[128,64]{1,0:T(8,128)(2,1)S(1)}, bf16[128,64]{1,0:T(8,128)(2,1)S(1)}, u32[]{:S(2)}, u32[]{:S(2)}) collective-permute-start(bf16[128,64]{1,0:T(8,128)(2,1)S(1)} %get-tuple-element.16), channel_id=1, source_target_pairs={{0,1},{1,0},{2,3},{3,2},{4,5},{5,4},{6,7},{7,6},{8,9},{9,8},{10,11... | collective-permute-start | bytes 49160 | tf_op jit(solution)/shard_map/ppermute | solution.py:99
  159.5 4.0 %collective-permute-done.41 = bf16[128,64]{1,0:T(8,128)(2,1)S(1)} collective-permute-done((bf16[128,64]{1,0:T(8,128)(2,1)S(1)}, bf16[128,64]{1,0:T(8,128)(2,1)S(1)}, u32[]{:S(2)}, u32[]{:S(2)}) %collective-permute-start.41) | collective-permute-done | bytes 16416 | tf_op jit(solution)/shard_map/ppermute | solution.py:99
  (359 shorter events, 55.0 us)
Async XLA Ops:
  1.1 9.2 %collective-permute-start = (bf16[128,64]{1,0:T(8,128)(2,1)S(1)}, bf16[128,64]{1,0:T(8,128)(2,1)S(1)}, u32[]{:S(2)}, u32[]{:S(2)}) collective-permute-start(bf16[128,64]{1,0:T(8,128)(2,1)S(1)} %get-tuple-element.120), channel_id=1, source_target_pairs={{0,1},{1,0},{2,3},{3,2},{4,5},{5,4},{6,7},{7,6},{8,9},{9,8},{10,11... | collective-permute-start | bytes 49160 | tf_op jit(solution)/shard_map/ppermute | solution.py:99
  4.4 5.9 %collective-permute-start.1 = (bf16[128,64]{1,0:T(8,128)(2,1)S(1)}, bf16[128,64]{1,0:T(8,128)(2,1)S(1)}, u32[]{:S(2)}, u32[]{:S(2)}) collective-permute-start(bf16[128,64]{1,0:T(8,128)(2,1)S(1)} %get-tuple-element.121), channel_id=1, source_target_pairs={{0,31},{1,2},{2,1},{3,4},{4,3},{5,6},{6,5},{7,8},{8,7},{9,10},{10,... | collective-permute-start | bytes 49160 | tf_op jit(solution)/shard_map/ppermute | solution.py:99
  10.6 7.6 %collective-permute-start.2 = (bf16[128,512]{1,0:T(8,128)(2,1)S(1)}, bf16[128,512]{1,0:T(8,128)(2,1)S(1)}, u32[]{:S(2)}, u32[]{:S(2)}) collective-permute-start(bf16[128,512]{1,0:T(8,128)(2,1)S(1)} %get-tuple-element.9), channel_id=1, source_target_pairs={{0,160},{32,128},{64,224},{96,192},{128,32},{160,0},{192,96},{224,... | collective-permute-start | bytes 393224 | tf_op jit(solution)/shard_map/ppermute | solution.py:99
  13.7 6.1 %collective-permute-start.3 = (bf16[128,512]{1,0:T(8,128)(2,1)S(1)}, bf16[128,512]{1,0:T(8,128)(2,1)S(1)}, u32[]{:S(2)}, u32[]{:S(2)}) collective-permute-start(bf16[128,512]{1,0:T(8,128)(2,1)S(1)} %get-tuple-element.9), channel_id=1, source_target_pairs={{0,128},{32,160},{64,192},{96,224},{128,0},{160,32},{192,64},{224,... | collective-permute-start | bytes 393224 | tf_op jit(solution)/shard_map/ppermute | solution.py:99
  13.7 6.4 %collective-permute-start.4 = (bf16[128,512]{1,0:T(8,128)(2,1)S(1)}, bf16[128,512]{1,0:T(8,128)(2,1)S(1)}, u32[]{:S(2)}, u32[]{:S(2)}) collective-permute-start(bf16[128,512]{1,0:T(8,128)(2,1)S(1)} %get-tuple-element.9), channel_id=1, source_target_pairs={{0,96},{32,64},{64,32},{96,0},{128,224},{160,192},{192,160},{224,1... | collective-permute-start | bytes 393224 | tf_op jit(solution)/shard_map/ppermute | solution.py:99
  15.9 6.2 %collective-permute-start.5 = (bf16[128,512]{1,0:T(8,128)(2,1)S(1)}, bf16[128,512]{1,0:T(8,128)(2,1)S(1)}, u32[]{:S(2)}, u32[]{:S(2)}) collective-permute-start(bf16[128,512]{1,0:T(8,128)(2,1)S(1)} %get-tuple-element.9), channel_id=1, source_target_pairs={{0,224},{32,192},{64,160},{96,128},{128,96},{160,64},{192,32},{224... | collective-permute-start | bytes 393224 | tf_op jit(solution)/shard_map/ppermute | solution.py:99
  17.8 4.3 %collective-permute-start.6 = (bf16[128,512]{1,0:T(8,128)(2,1)S(1)}, bf16[128,512]{1,0:T(8,128)(2,1)S(1)}, u32[]{:S(2)}, u32[]{:S(2)}) collective-permute-start(bf16[128,512]{1,0:T(8,128)(2,1)S(1)} %get-tuple-element.9), channel_id=1, source_target_pairs={{0,64},{32,96},{64,0},{96,32},{128,192},{160,224},{192,128},{224,1... | collective-permute-start | bytes 393224 | tf_op jit(solution)/shard_map/ppermute | solution.py:99
  18.2 7.9 %collective-permute-start.7 = (bf16[128,512]{1,0:T(8,128)(2,1)S(1)}, bf16[128,512]{1,0:T(8,128)(2,1)S(1)}, u32[]{:S(2)}, u32[]{:S(2)}) collective-permute-start(bf16[128,512]{1,0:T(8,128)(2,1)S(1)} %get-tuple-element.9), channel_id=1, source_target_pairs={{0,192},{32,224},{64,128},{96,160},{128,64},{160,96},{192,0},{224,... | collective-permute-start | bytes 393224 | tf_op jit(solution)/shard_map/ppermute | solution.py:99
  19.8 6.4 %collective-permute-start.8 = (bf16[128,512]{1,0:T(8,128)(2,1)S(1)}, bf16[128,512]{1,0:T(8,128)(2,1)S(1)}, u32[]{:S(2)}, u32[]{:S(2)}) collective-permute-start(bf16[128,512]{1,0:T(8,128)(2,1)S(1)} %get-tuple-element.9), channel_id=1, source_target_pairs={{0,32},{32,0},{64,96},{96,64},{128,160},{160,128},{192,224},{224,1... | collective-permute-start | bytes 393224 | tf_op jit(solution)/shard_map/ppermute | solution.py:99
  28.1 12.0 %collective-permute-start.10 = (bf16[128,64]{1,0:T(8,128)(2,1)S(1)}, bf16[128,64]{1,0:T(8,128)(2,1)S(1)}, u32[]{:S(2)}, u32[]{:S(2)}) collective-permute-start(bf16[128,64]{1,0:T(8,128)(2,1)S(1)} %get-tuple-element.113), channel_id=1, source_target_pairs={{0,31},{1,2},{2,1},{3,4},{4,3},{5,6},{6,5},{7,8},{8,7},{9,10},{10,... | collective-permute-start | bytes 49160 | tf_op jit(solution)/shard_map/ppermute | solution.py:99
  34.9 5.5 %collective-permute-start.9 = (bf16[128,64]{1,0:T(8,128)(2,1)S(1)}, bf16[128,64]{1,0:T(8,128)(2,1)S(1)}, u32[]{:S(2)}, u32[]{:S(2)}) collective-permute-start(bf16[128,64]{1,0:T(8,128)(2,1)S(1)} %get-tuple-element.112), channel_id=1, source_target_pairs={{0,1},{1,0},{2,3},{3,2},{4,5},{5,4},{6,7},{7,6},{8,9},{9,8},{10,11... | collective-permute-start | bytes 49160 | tf_op jit(solution)/shard_map/ppermute | solution.py:99
  42.8 4.8 %collective-permute-start.12 = (bf16[128,64]{1,0:T(8,128)(2,1)S(1)}, bf16[128,64]{1,0:T(8,128)(2,1)S(1)}, u32[]{:S(2)}, u32[]{:S(2)}) collective-permute-start(bf16[128,64]{1,0:T(8,128)(2,1)S(1)} %get-tuple-element.105), channel_id=1, source_target_pairs={{0,31},{1,2},{2,1},{3,4},{4,3},{5,6},{6,5},{7,8},{8,7},{9,10},{10,... | collective-permute-start | bytes 49160 | tf_op jit(solution)/shard_map/ppermute | solution.py:99
  51.5 4.8 %collective-permute-start.14 = (bf16[128,64]{1,0:T(8,128)(2,1)S(1)}, bf16[128,64]{1,0:T(8,128)(2,1)S(1)}, u32[]{:S(2)}, u32[]{:S(2)}) collective-permute-start(bf16[128,64]{1,0:T(8,128)(2,1)S(1)} %get-tuple-element.97), channel_id=1, source_target_pairs={{0,31},{1,2},{2,1},{3,4},{4,3},{5,6},{6,5},{7,8},{8,7},{9,10},{10,... | collective-permute-start | bytes 49160 | tf_op jit(solution)/shard_map/ppermute | solution.py:99
  58.0 3.3 %collective-permute-start.15 = (bf16[128,64]{1,0:T(8,128)(2,1)S(1)}, bf16[128,64]{1,0:T(8,128)(2,1)S(1)}, u32[]{:S(2)}, u32[]{:S(2)}) collective-permute-start(bf16[128,64]{1,0:T(8,128)(2,1)S(1)} %get-tuple-element.88), channel_id=1, source_target_pairs={{0,1},{1,0},{2,3},{3,2},{4,5},{5,4},{6,7},{7,6},{8,9},{9,8},{10,11... | collective-permute-start | bytes 49160 | tf_op jit(solution)/shard_map/ppermute | solution.py:99
  60.5 4.8 %collective-permute-start.16 = (bf16[128,64]{1,0:T(8,128)(2,1)S(1)}, bf16[128,64]{1,0:T(8,128)(2,1)S(1)}, u32[]{:S(2)}, u32[]{:S(2)}) collective-permute-start(bf16[128,64]{1,0:T(8,128)(2,1)S(1)} %get-tuple-element.89), channel_id=1, source_target_pairs={{0,31},{1,2},{2,1},{3,4},{4,3},{5,6},{6,5},{7,8},{8,7},{9,10},{10,... | collective-permute-start | bytes 49160 | tf_op jit(solution)/shard_map/ppermute | solution.py:99
  69.2 4.8 %collective-permute-start.18 = (bf16[128,64]{1,0:T(8,128)(2,1)S(1)}, bf16[128,64]{1,0:T(8,128)(2,1)S(1)}, u32[]{:S(2)}, u32[]{:S(2)}) collective-permute-start(bf16[128,64]{1,0:T(8,128)(2,1)S(1)} %get-tuple-element.81), channel_id=1, source_target_pairs={{0,31},{1,2},{2,1},{3,4},{4,3},{5,6},{6,5},{7,8},{8,7},{9,10},{10,... | collective-permute-start | bytes 49160 | tf_op jit(solution)/shard_map/ppermute | solution.py:99
  77.9 4.8 %collective-permute-start.20 = (bf16[128,64]{1,0:T(8,128)(2,1)S(1)}, bf16[128,64]{1,0:T(8,128)(2,1)S(1)}, u32[]{:S(2)}, u32[]{:S(2)}) collective-permute-start(bf16[128,64]{1,0:T(8,128)(2,1)S(1)} %get-tuple-element.73), channel_id=1, source_target_pairs={{0,31},{1,2},{2,1},{3,4},{4,3},{5,6},{6,5},{7,8},{8,7},{9,10},{10,... | collective-permute-start | bytes 49160 | tf_op jit(solution)/shard_map/ppermute | solution.py:99
  86.6 4.8 %collective-permute-start.22 = (bf16[128,64]{1,0:T(8,128)(2,1)S(1)}, bf16[128,64]{1,0:T(8,128)(2,1)S(1)}, u32[]{:S(2)}, u32[]{:S(2)}) collective-permute-start(bf16[128,64]{1,0:T(8,128)(2,1)S(1)} %get-tuple-element.65), channel_id=1, source_target_pairs={{0,31},{1,2},{2,1},{3,4},{4,3},{5,6},{6,5},{7,8},{8,7},{9,10},{10,... | collective-permute-start | bytes 49160 | tf_op jit(solution)/shard_map/ppermute | solution.py:99
  91.7 9.0 %collective-permute-start.23 = (bf16[128,512]{1,0:T(8,128)(2,1)S(1)}, bf16[128,512]{1,0:T(8,128)(2,1)S(1)}, u32[]{:S(2)}, u32[]{:S(2)}) collective-permute-start(bf16[128,512]{1,0:T(8,128)(2,1)S(1)} %get-tuple-element.7), channel_id=1, source_target_pairs={{0,160},{32,128},{64,224},{96,192},{128,32},{160,0},{192,96},{224,... | collective-permute-start | bytes 393224 | tf_op jit(solution)/shard_map/ppermute | solution.py:99
  95.0 6.7 %collective-permute-start.24 = (bf16[128,512]{1,0:T(8,128)(2,1)S(1)}, bf16[128,512]{1,0:T(8,128)(2,1)S(1)}, u32[]{:S(2)}, u32[]{:S(2)}) collective-permute-start(bf16[128,512]{1,0:T(8,128)(2,1)S(1)} %get-tuple-element.7), channel_id=1, source_target_pairs={{0,128},{32,160},{64,192},{96,224},{128,0},{160,32},{192,64},{224,... | collective-permute-start | bytes 393224 | tf_op jit(solution)/shard_map/ppermute | solution.py:99
  95.1 8.4 %collective-permute-start.25 = (bf16[128,512]{1,0:T(8,128)(2,1)S(1)}, bf16[128,512]{1,0:T(8,128)(2,1)S(1)}, u32[]{:S(2)}, u32[]{:S(2)}) collective-permute-start(bf16[128,512]{1,0:T(8,128)(2,1)S(1)} %get-tuple-element.7), channel_id=1, source_target_pairs={{0,96},{32,64},{64,32},{96,0},{128,224},{160,192},{192,160},{224,1... | collective-permute-start | bytes 393224 | tf_op jit(solution)/shard_map/ppermute | solution.py:99
  97.5 8.0 %collective-permute-start.26 = (bf16[128,512]{1,0:T(8,128)(2,1)S(1)}, bf16[128,512]{1,0:T(8,128)(2,1)S(1)}, u32[]{:S(2)}, u32[]{:S(2)}) collective-permute-start(bf16[128,512]{1,0:T(8,128)(2,1)S(1)} %get-tuple-element.7), channel_id=1, source_target_pairs={{0,224},{32,192},{64,160},{96,128},{128,96},{160,64},{192,32},{224... | collective-permute-start | bytes 393224 | tf_op jit(solution)/shard_map/ppermute | solution.py:99
  99.1 9.6 %collective-permute-start.27 = (bf16[128,512]{1,0:T(8,128)(2,1)S(1)}, bf16[128,512]{1,0:T(8,128)(2,1)S(1)}, u32[]{:S(2)}, u32[]{:S(2)}) collective-permute-start(bf16[128,512]{1,0:T(8,128)(2,1)S(1)} %get-tuple-element.7), channel_id=1, source_target_pairs={{0,64},{32,96},{64,0},{96,32},{128,192},{160,224},{192,128},{224,1... | collective-permute-start | bytes 393224 | tf_op jit(solution)/shard_map/ppermute | solution.py:99
  100.7 8.4 %collective-permute-start.28 = (bf16[128,512]{1,0:T(8,128)(2,1)S(1)}, bf16[128,512]{1,0:T(8,128)(2,1)S(1)}, u32[]{:S(2)}, u32[]{:S(2)}) collective-permute-start(bf16[128,512]{1,0:T(8,128)(2,1)S(1)} %get-tuple-element.7), channel_id=1, source_target_pairs={{0,192},{32,224},{64,128},{96,160},{128,64},{160,96},{192,0},{224,... | collective-permute-start | bytes 393224 | tf_op jit(solution)/shard_map/ppermute | solution.py:99
  101.7 7.4 %collective-permute-start.29 = (bf16[128,512]{1,0:T(8,128)(2,1)S(1)}, bf16[128,512]{1,0:T(8,128)(2,1)S(1)}, u32[]{:S(2)}, u32[]{:S(2)}) collective-permute-start(bf16[128,512]{1,0:T(8,128)(2,1)S(1)} %get-tuple-element.7), channel_id=1, source_target_pairs={{0,32},{32,0},{64,96},{96,64},{128,160},{160,128},{192,224},{224,1... | collective-permute-start | bytes 393224 | tf_op jit(solution)/shard_map/ppermute | solution.py:99
  110.8 5.0 %collective-permute-start.30 = (bf16[128,64]{1,0:T(8,128)(2,1)S(1)}, bf16[128,64]{1,0:T(8,128)(2,1)S(1)}, u32[]{:S(2)}, u32[]{:S(2)}) collective-permute-start(bf16[128,64]{1,0:T(8,128)(2,1)S(1)} %get-tuple-element.56), channel_id=1, source_target_pairs={{0,1},{1,0},{2,3},{3,2},{4,5},{5,4},{6,7},{7,6},{8,9},{9,8},{10,11... | collective-permute-start | bytes 49160 | tf_op jit(solution)/shard_map/ppermute | solution.py:99
  115.0 4.8 %collective-permute-start.31 = (bf16[128,64]{1,0:T(8,128)(2,1)S(1)}, bf16[128,64]{1,0:T(8,128)(2,1)S(1)}, u32[]{:S(2)}, u32[]{:S(2)}) collective-permute-start(bf16[128,64]{1,0:T(8,128)(2,1)S(1)} %get-tuple-element.57), channel_id=1, source_target_pairs={{0,31},{1,2},{2,1},{3,4},{4,3},{5,6},{6,5},{7,8},{8,7},{9,10},{10,... | collective-permute-start | bytes 49160 | tf_op jit(solution)/shard_map/ppermute | solution.py:99
  123.7 4.8 %collective-permute-start.33 = (bf16[128,64]{1,0:T(8,128)(2,1)S(1)}, bf16[128,64]{1,0:T(8,128)(2,1)S(1)}, u32[]{:S(2)}, u32[]{:S(2)}) collective-permute-start(bf16[128,64]{1,0:T(8,128)(2,1)S(1)} %get-tuple-element.49), channel_id=1, source_target_pairs={{0,31},{1,2},{2,1},{3,4},{4,3},{5,6},{6,5},{7,8},{8,7},{9,10},{10,... | collective-permute-start | bytes 49160 | tf_op jit(solution)/shard_map/ppermute | solution.py:99
  132.5 4.8 %collective-permute-start.35 = (bf16[128,64]{1,0:T(8,128)(2,1)S(1)}, bf16[128,64]{1,0:T(8,128)(2,1)S(1)}, u32[]{:S(2)}, u32[]{:S(2)}) collective-permute-start(bf16[128,64]{1,0:T(8,128)(2,1)S(1)} %get-tuple-element.41), channel_id=1, source_target_pairs={{0,31},{1,2},{2,1},{3,4},{4,3},{5,6},{6,5},{7,8},{8,7},{9,10},{10,... | collective-permute-start | bytes 49160 | tf_op jit(solution)/shard_map/ppermute | solution.py:99
  141.2 4.8 %collective-permute-start.37 = (bf16[128,64]{1,0:T(8,128)(2,1)S(1)}, bf16[128,64]{1,0:T(8,128)(2,1)S(1)}, u32[]{:S(2)}, u32[]{:S(2)}) collective-permute-start(bf16[128,64]{1,0:T(8,128)(2,1)S(1)} %get-tuple-element.33), channel_id=1, source_target_pairs={{0,31},{1,2},{2,1},{3,4},{4,3},{5,6},{6,5},{7,8},{8,7},{9,10},{10,... | collective-permute-start | bytes 49160 | tf_op jit(solution)/shard_map/ppermute | solution.py:99
  149.9 4.8 %collective-permute-start.39 = (bf16[128,64]{1,0:T(8,128)(2,1)S(1)}, bf16[128,64]{1,0:T(8,128)(2,1)S(1)}, u32[]{:S(2)}, u32[]{:S(2)}) collective-permute-start(bf16[128,64]{1,0:T(8,128)(2,1)S(1)} %get-tuple-element.25), channel_id=1, source_target_pairs={{0,31},{1,2},{2,1},{3,4},{4,3},{5,6},{6,5},{7,8},{8,7},{9,10},{10,... | collective-permute-start | bytes 49160 | tf_op jit(solution)/shard_map/ppermute | solution.py:99
  158.6 4.8 %collective-permute-start.41 = (bf16[128,64]{1,0:T(8,128)(2,1)S(1)}, bf16[128,64]{1,0:T(8,128)(2,1)S(1)}, u32[]{:S(2)}, u32[]{:S(2)}) collective-permute-start(bf16[128,64]{1,0:T(8,128)(2,1)S(1)} %get-tuple-element.17), channel_id=1, source_target_pairs={{0,31},{1,2},{2,1},{3,4},{4,3},{5,6},{6,5},{7,8},{8,7},{9,10},{10,... | collective-permute-start | bytes 49160 | tf_op jit(solution)/shard_map/ppermute | solution.py:99
  (18 other events, 51.6 us)

commit v6 on v5

--- a/solution.py
+++ b/solution.py
@@ -89,9 +89,7 @@
         ],
         axis=-1,
     ).reshape((ny * nz, 4 * FACE))
-    inputs = jnp.concatenate([rounded, moved], axis=-1)
-    own = jnp.dot(inputs, stacked, preferred_element_type=jnp.float32) - reaction * field
-    return own, rounded
+    return jnp.concatenate([rounded, moved], axis=-1), rounded
 
 
 def swapped(array, axis, partner):
@@ -111,9 +109,10 @@
 
 
 def apply_operator(field, reaction, weights, x_lift, ny, nz):
-    own, rounded = local_terms(field, reaction, weights, ny, nz)
+    inputs, rounded = local_terms(field, reaction, weights, ny, nz)
     faces = exchange_faces(rounded)
-    return own + jnp.dot(faces, x_lift, preferred_element_type=jnp.float32)
+    every = jnp.concatenate([inputs, faces], axis=-1)
+    return jnp.dot(every, x_lift, preferred_element_type=jnp.float32) - reaction * field
 
 
 def gather_nodes(rows):
@@ -137,7 +136,7 @@
     own_scale = lax.dynamic_slice_in_dim(all_scales, first_node, local_count, 0)[0]
 
     weights = face_weights(volume, face_lift)
-    x_lift = face_lift[: 2 * FACE]
+    x_lift = jnp.concatenate([weights[1], face_lift[: 2 * FACE]], axis=0)
     start = start_state.reshape((rows, points))
     reaction = reaction_rates.reshape((rows, points))
     states = node_states.reshape((rows, points))

time: 167 us -> 169 us (1.012)
  waiting for transfers between devices: 65 us -> 72.2 us
  matrix products: 18.9 us -> 16.4 us
  starting transfers between devices: 64.6 us -> 62.2 us
    ppermute x42, waiting for transfers between devices: 65 us -> 72.2 us  [swapped(): lax.ppermute(array, axis, [(i, partner(i) % devices) for i in range(devic...]
    dot_general x28 -> x14, matrix products: 15.3 us -> 12.7 us  [apply_operator(): jnp.dot(every, x_lift, preferred_element_type=jnp.float32)]
    ppermute x42, starting transfers between devices: 64.6 us -> 62.2 us  [swapped(): lax.ppermute(array, axis, [(i, partner(i) % devices) for i in range(devic...]
  transfers between devices with their start and end apart: 42 -> 42, of which waited for: 31 -> 31; matrix products, arithmetic and copies ran while one was open for 6% -> 3% of each run, Pallas kernels for 0% -> 0%
where the time goes in v6:
time: 169 us; the launch traced here: 167 us
  waiting for transfers between devices  72.2 us (43%)
  starting transfers between devices  62.2 us (37%)
  matrix products  16.4 us (10%)
  local copies, waits for them, and re-layouts  8.13 us (5%)
  other arithmetic  5.89 us (3%)
  between operations  2.1 us (1%)
    ppermute x42, waiting for transfers between devices, swapped(): lax.ppermute(array, axis, [(i, partner(i) % devices) for i in range(devic...  72.2 us
    ppermute x42, starting transfers between devices, swapped(): lax.ppermute(array, axis, [(i, partner(i) % devices) for i in range(devic...  62.2 us
    dot_general x14, matrix products, apply_operator(): jnp.dot(every, x_lift, preferred_element_type=jnp.float32)  12.7 us
    dot_general x14, matrix products, local_terms(): jnp.dot(rounded, select, preferred_element_type=jnp.float32)  3.67 us
  transfers between devices with their start and end apart: 42, of which 31 were waited for; matrix products, arithmetic and copies ran while one was open for 3% of the time, Pallas kernels for 0%

profile of v6, /device:TPU:1, one launch (start us, length us, event | category | flops | bytes accessed | tf_op | source)
XLA Modules:
  0.0 166.9 jit_solution(1734684163035657681)
XLA Ops:
  1.1 3.3 %collective-permute-start = (bf16[128,64]{1,0:T(8,128)(2,1)S(1)}, bf16[128,64]{1,0:T(8,128)(2,1)S(1)}, u32[]{:S(2)}, u32[]{:S(2)}) collective-permute-start(bf16[128,64]{1,0:T(8,128)(2,1)S(1)} %get-tuple-element.148), channel_id=1, source_target_pairs={{0,1},{1,0},{2,3},{3,2},{4,5},{5,4},{6,7},{7,6},{8,9},{9,8},{10,11... | collective-permute-start | bytes 49160 | tf_op jit(solution)/shard_map/ppermute | solution.py:97
  9.9 3.0 %collective-permute-start.2 = (bf16[128,512]{1,0:T(8,128)(2,1)S(1)}, bf16[128,512]{1,0:T(8,128)(2,1)S(1)}, u32[]{:S(2)}, u32[]{:S(2)}) collective-permute-start(bf16[128,512]{1,0:T(8,128)(2,1)S(1)} %get-tuple-element.9), channel_id=1, source_target_pairs={{0,160},{32,128},{64,224},{96,192},{128,32},{160,0},{192,96},{224,... | collective-permute-start | bytes 393224 | tf_op jit(solution)/shard_map/ppermute | solution.py:97
  21.4 4.0 %collective-permute-done.7 = bf16[128,512]{1,0:T(8,128)(2,1)S(1)} collective-permute-done((bf16[128,512]{1,0:T(8,128)(2,1)S(1)}, bf16[128,512]{1,0:T(8,128)(2,1)S(1)}, u32[]{:S(2)}, u32[]{:S(2)}) %collective-permute-start.7) | collective-permute-done | bytes 131104 | tf_op jit(solution)/shard_map/ppermute | solution.py:97
  27.5 6.8 %collective-permute-start.10 = (bf16[128,64]{1,0:T(8,128)(2,1)S(1)}, bf16[128,64]{1,0:T(8,128)(2,1)S(1)}, u32[]{:S(2)}, u32[]{:S(2)}) collective-permute-start(bf16[128,64]{1,0:T(8,128)(2,1)S(1)} %get-tuple-element.141), channel_id=1, source_target_pairs={{0,31},{1,2},{2,1},{3,4},{4,3},{5,6},{6,5},{7,8},{8,7},{9,10},{10,... | collective-permute-start | bytes 49160 | tf_op jit(solution)/shard_map/ppermute | solution.py:97
  34.4 5.2 %collective-permute-start.9 = (bf16[128,64]{1,0:T(8,128)(2,1)S(1)}, bf16[128,64]{1,0:T(8,128)(2,1)S(1)}, u32[]{:S(2)}, u32[]{:S(2)}) collective-permute-start(bf16[128,64]{1,0:T(8,128)(2,1)S(1)} %get-tuple-element.140), channel_id=1, source_target_pairs={{0,1},{1,0},{2,3},{3,2},{4,5},{5,4},{6,7},{7,6},{8,9},{9,8},{10,11... | collective-permute-start | bytes 49160 | tf_op jit(solution)/shard_map/ppermute | solution.py:97
  43.8 4.0 %collective-permute-done.12 = bf16[128,64]{1,0:T(8,128)(2,1)S(1)} collective-permute-done((bf16[128,64]{1,0:T(8,128)(2,1)S(1)}, bf16[128,64]{1,0:T(8,128)(2,1)S(1)}, u32[]{:S(2)}, u32[]{:S(2)}) %collective-permute-start.12) | collective-permute-done | bytes 16416 | tf_op jit(solution)/shard_map/ppermute | solution.py:97
  49.6 2.3 %collective-permute-start.13 = (bf16[128,64]{1,0:T(8,128)(2,1)S(1)}, bf16[128,64]{1,0:T(8,128)(2,1)S(1)}, u32[]{:S(2)}, u32[]{:S(2)}) collective-permute-start(bf16[128,64]{1,0:T(8,128)(2,1)S(1)} %get-tuple-element.124), channel_id=1, source_target_pairs={{0,1},{1,0},{2,3},{3,2},{4,5},{5,4},{6,7},{7,6},{8,9},{9,8},{10,11... | collective-permute-start | bytes 49160 | tf_op jit(solution)/shard_map/ppermute | solution.py:97
  52.7 4.0 %collective-permute-done.14 = bf16[128,64]{1,0:T(8,128)(2,1)S(1)} collective-permute-done((bf16[128,64]{1,0:T(8,128)(2,1)S(1)}, bf16[128,64]{1,0:T(8,128)(2,1)S(1)}, u32[]{:S(2)}, u32[]{:S(2)}) %collective-permute-start.14) | collective-permute-done | bytes 16416 | tf_op jit(solution)/shard_map/ppermute | solution.py:97
  58.5 2.5 %collective-permute-start.15 = (bf16[128,64]{1,0:T(8,128)(2,1)S(1)}, bf16[128,64]{1,0:T(8,128)(2,1)S(1)}, u32[]{:S(2)}, u32[]{:S(2)}) collective-permute-start(bf16[128,64]{1,0:T(8,128)(2,1)S(1)} %get-tuple-element.116), channel_id=1, source_target_pairs={{0,1},{1,0},{2,3},{3,2},{4,5},{5,4},{6,7},{7,6},{8,9},{9,8},{10,11... | collective-permute-start | bytes 49160 | tf_op jit(solution)/shard_map/ppermute | solution.py:97
  61.8 4.0 %collective-permute-done.16 = bf16[128,64]{1,0:T(8,128)(2,1)S(1)} collective-permute-done((bf16[128,64]{1,0:T(8,128)(2,1)S(1)}, bf16[128,64]{1,0:T(8,128)(2,1)S(1)}, u32[]{:S(2)}, u32[]{:S(2)}) %collective-permute-start.16) | collective-permute-done | bytes 16416 | tf_op jit(solution)/shard_map/ppermute | solution.py:97
  67.6 2.3 %collective-permute-start.17 = (bf16[128,64]{1,0:T(8,128)(2,1)S(1)}, bf16[128,64]{1,0:T(8,128)(2,1)S(1)}, u32[]{:S(2)}, u32[]{:S(2)}) collective-permute-start(bf16[128,64]{1,0:T(8,128)(2,1)S(1)} %get-tuple-element.108), channel_id=1, source_target_pairs={{0,1},{1,0},{2,3},{3,2},{4,5},{5,4},{6,7},{7,6},{8,9},{9,8},{10,11... | collective-permute-start | bytes 49160 | tf_op jit(solution)/shard_map/ppermute | solution.py:97
  70.7 4.0 %collective-permute-done.18 = bf16[128,64]{1,0:T(8,128)(2,1)S(1)} collective-permute-done((bf16[128,64]{1,0:T(8,128)(2,1)S(1)}, bf16[128,64]{1,0:T(8,128)(2,1)S(1)}, u32[]{:S(2)}, u32[]{:S(2)}) %collective-permute-start.18) | collective-permute-done | bytes 16416 | tf_op jit(solution)/shard_map/ppermute | solution.py:97
  76.5 2.3 %collective-permute-start.19 = (bf16[128,64]{1,0:T(8,128)(2,1)S(1)}, bf16[128,64]{1,0:T(8,128)(2,1)S(1)}, u32[]{:S(2)}, u32[]{:S(2)}) collective-permute-start(bf16[128,64]{1,0:T(8,128)(2,1)S(1)} %get-tuple-element.100), channel_id=1, source_target_pairs={{0,1},{1,0},{2,3},{3,2},{4,5},{5,4},{6,7},{7,6},{8,9},{9,8},{10,11... | collective-permute-start | bytes 49160 | tf_op jit(solution)/shard_map/ppermute | solution.py:97
  79.6 4.0 %collective-permute-done.20 = bf16[128,64]{1,0:T(8,128)(2,1)S(1)} collective-permute-done((bf16[128,64]{1,0:T(8,128)(2,1)S(1)}, bf16[128,64]{1,0:T(8,128)(2,1)S(1)}, u32[]{:S(2)}, u32[]{:S(2)}) %collective-permute-start.20) | collective-permute-done | bytes 16416 | tf_op jit(solution)/shard_map/ppermute | solution.py:97
  85.4 2.3 %collective-permute-start.21 = (bf16[128,64]{1,0:T(8,128)(2,1)S(1)}, bf16[128,64]{1,0:T(8,128)(2,1)S(1)}, u32[]{:S(2)}, u32[]{:S(2)}) collective-permute-start(bf16[128,64]{1,0:T(8,128)(2,1)S(1)} %get-tuple-element.92), channel_id=1, source_target_pairs={{0,1},{1,0},{2,3},{3,2},{4,5},{5,4},{6,7},{7,6},{8,9},{9,8},{10,11... | collective-permute-start | bytes 49160 | tf_op jit(solution)/shard_map/ppermute | solution.py:97
  88.5 4.0 %collective-permute-done.22 = bf16[128,64]{1,0:T(8,128)(2,1)S(1)} collective-permute-done((bf16[128,64]{1,0:T(8,128)(2,1)S(1)}, bf16[128,64]{1,0:T(8,128)(2,1)S(1)}, u32[]{:S(2)}, u32[]{:S(2)}) %collective-permute-start.22) | collective-permute-done | bytes 16416 | tf_op jit(solution)/shard_map/ppermute | solution.py:97
  92.9 3.1 %collective-permute-start.23 = (bf16[128,512]{1,0:T(8,128)(2,1)S(1)}, bf16[128,512]{1,0:T(8,128)(2,1)S(1)}, u32[]{:S(2)}, u32[]{:S(2)}) collective-permute-start(bf16[128,512]{1,0:T(8,128)(2,1)S(1)} %get-tuple-element.7), channel_id=1, source_target_pairs={{0,160},{32,128},{64,224},{96,192},{128,32},{160,0},{192,96},{224,... | collective-permute-start | bytes 393224 | tf_op jit(solution)/shard_map/ppermute | solution.py:97
  97.8 2.3 %collective-permute-start.26 = (bf16[128,512]{1,0:T(8,128)(2,1)S(1)}, bf16[128,512]{1,0:T(8,128)(2,1)S(1)}, u32[]{:S(2)}, u32[]{:S(2)}) collective-permute-start(bf16[128,512]{1,0:T(8,128)(2,1)S(1)} %get-tuple-element.7), channel_id=1, source_target_pairs={{0,224},{32,192},{64,160},{96,128},{128,96},{160,64},{192,32},{224... | collective-permute-start | bytes 393224 | tf_op jit(solution)/shard_map/ppermute | solution.py:97
  102.0 3.3 %collective-permute-done.24 = bf16[128,512]{1,0:T(8,128)(2,1)S(1)} collective-permute-done((bf16[128,512]{1,0:T(8,128)(2,1)S(1)}, bf16[128,512]{1,0:T(8,128)(2,1)S(1)}, u32[]{:S(2)}, u32[]{:S(2)}) %collective-permute-start.24) | collective-permute-done | bytes 131104 | tf_op jit(solution)/shard_map/ppermute | solution.py:97
  106.6 3.4 %collective-permute-done.27 = bf16[128,512]{1,0:T(8,128)(2,1)S(1)} collective-permute-done((bf16[128,512]{1,0:T(8,128)(2,1)S(1)}, bf16[128,512]{1,0:T(8,128)(2,1)S(1)}, u32[]{:S(2)}, u32[]{:S(2)}) %collective-permute-start.27) | collective-permute-done | bytes 131104 | tf_op jit(solution)/shard_map/ppermute | solution.py:97
  112.7 3.1 %collective-permute-start.30 = (bf16[128,64]{1,0:T(8,128)(2,1)S(1)}, bf16[128,64]{1,0:T(8,128)(2,1)S(1)}, u32[]{:S(2)}, u32[]{:S(2)}) collective-permute-start(bf16[128,64]{1,0:T(8,128)(2,1)S(1)} %get-tuple-element.84), channel_id=1, source_target_pairs={{0,1},{1,0},{2,3},{3,2},{4,5},{5,4},{6,7},{7,6},{8,9},{9,8},{10,11... | collective-permute-start | bytes 49160 | tf_op jit(solution)/shard_map/ppermute | solution.py:97
  116.7 4.0 %collective-permute-done.31 = bf16[128,64]{1,0:T(8,128)(2,1)S(1)} collective-permute-done((bf16[128,64]{1,0:T(8,128)(2,1)S(1)}, bf16[128,64]{1,0:T(8,128)(2,1)S(1)}, u32[]{:S(2)}, u32[]{:S(2)}) %collective-permute-start.31) | collective-permute-done | bytes 16416 | tf_op jit(solution)/shard_map/ppermute | solution.py:97
  122.5 2.3 %collective-permute-start.32 = (bf16[128,64]{1,0:T(8,128)(2,1)S(1)}, bf16[128,64]{1,0:T(8,128)(2,1)S(1)}, u32[]{:S(2)}, u32[]{:S(2)}) collective-permute-start(bf16[128,64]{1,0:T(8,128)(2,1)S(1)} %get-tuple-element.76), channel_id=1, source_target_pairs={{0,1},{1,0},{2,3},{3,2},{4,5},{5,4},{6,7},{7,6},{8,9},{9,8},{10,11... | collective-permute-start | bytes 49160 | tf_op jit(solution)/shard_map/ppermute | solution.py:97
  125.6 4.0 %collective-permute-done.33 = bf16[128,64]{1,0:T(8,128)(2,1)S(1)} collective-permute-done((bf16[128,64]{1,0:T(8,128)(2,1)S(1)}, bf16[128,64]{1,0:T(8,128)(2,1)S(1)}, u32[]{:S(2)}, u32[]{:S(2)}) %collective-permute-start.33) | collective-permute-done | bytes 16416 | tf_op jit(solution)/shard_map/ppermute | solution.py:97
  131.4 2.3 %collective-permute-start.34 = (bf16[128,64]{1,0:T(8,128)(2,1)S(1)}, bf16[128,64]{1,0:T(8,128)(2,1)S(1)}, u32[]{:S(2)}, u32[]{:S(2)}) collective-permute-start(bf16[128,64]{1,0:T(8,128)(2,1)S(1)} %get-tuple-element.68), channel_id=1, source_target_pairs={{0,1},{1,0},{2,3},{3,2},{4,5},{5,4},{6,7},{7,6},{8,9},{9,8},{10,11... | collective-permute-start | bytes 49160 | tf_op jit(solution)/shard_map/ppermute | solution.py:97
  134.5 4.0 %collective-permute-done.35 = bf16[128,64]{1,0:T(8,128)(2,1)S(1)} collective-permute-done((bf16[128,64]{1,0:T(8,128)(2,1)S(1)}, bf16[128,64]{1,0:T(8,128)(2,1)S(1)}, u32[]{:S(2)}, u32[]{:S(2)}) %collective-permute-start.35) | collective-permute-done | bytes 16416 | tf_op jit(solution)/shard_map/ppermute | solution.py:97
  140.3 2.3 %collective-permute-start.36 = (bf16[128,64]{1,0:T(8,128)(2,1)S(1)}, bf16[128,64]{1,0:T(8,128)(2,1)S(1)}, u32[]{:S(2)}, u32[]{:S(2)}) collective-permute-start(bf16[128,64]{1,0:T(8,128)(2,1)S(1)} %get-tuple-element.60), channel_id=1, source_target_pairs={{0,1},{1,0},{2,3},{3,2},{4,5},{5,4},{6,7},{7,6},{8,9},{9,8},{10,11... | collective-permute-start | bytes 49160 | tf_op jit(solution)/shard_map/ppermute | solution.py:97
  143.5 4.0 %collective-permute-done.37 = bf16[128,64]{1,0:T(8,128)(2,1)S(1)} collective-permute-done((bf16[128,64]{1,0:T(8,128)(2,1)S(1)}, bf16[128,64]{1,0:T(8,128)(2,1)S(1)}, u32[]{:S(2)}, u32[]{:S(2)}) %collective-permute-start.37) | collective-permute-done | bytes 16416 | tf_op jit(solution)/shard_map/ppermute | solution.py:97
  149.2 2.3 %collective-permute-start.38 = (bf16[128,64]{1,0:T(8,128)(2,1)S(1)}, bf16[128,64]{1,0:T(8,128)(2,1)S(1)}, u32[]{:S(2)}, u32[]{:S(2)}) collective-permute-start(bf16[128,64]{1,0:T(8,128)(2,1)S(1)} %get-tuple-element.52), channel_id=1, source_target_pairs={{0,1},{1,0},{2,3},{3,2},{4,5},{5,4},{6,7},{7,6},{8,9},{9,8},{10,11... | collective-permute-start | bytes 49160 | tf_op jit(solution)/shard_map/ppermute | solution.py:97
  152.4 4.0 %collective-permute-done.39 = bf16[128,64]{1,0:T(8,128)(2,1)S(1)} collective-permute-done((bf16[128,64]{1,0:T(8,128)(2,1)S(1)}, bf16[128,64]{1,0:T(8,128)(2,1)S(1)}, u32[]{:S(2)}, u32[]{:S(2)}) %collective-permute-start.39) | collective-permute-done | bytes 16416 | tf_op jit(solution)/shard_map/ppermute | solution.py:97
  158.1 2.3 %collective-permute-start.40 = (bf16[128,64]{1,0:T(8,128)(2,1)S(1)}, bf16[128,64]{1,0:T(8,128)(2,1)S(1)}, u32[]{:S(2)}, u32[]{:S(2)}) collective-permute-start(bf16[128,64]{1,0:T(8,128)(2,1)S(1)} %get-tuple-element.44), channel_id=1, source_target_pairs={{0,1},{1,0},{2,3},{3,2},{4,5},{5,4},{6,7},{7,6},{8,9},{9,8},{10,11... | collective-permute-start | bytes 49160 | tf_op jit(solution)/shard_map/ppermute | solution.py:97
  161.3 4.0 %collective-permute-done.41 = bf16[128,64]{1,0:T(8,128)(2,1)S(1)} collective-permute-done((bf16[128,64]{1,0:T(8,128)(2,1)S(1)}, bf16[128,64]{1,0:T(8,128)(2,1)S(1)}, u32[]{:S(2)}, u32[]{:S(2)}) %collective-permute-start.41) | collective-permute-done | bytes 16416 | tf_op jit(solution)/shard_map/ppermute | solution.py:97
  (346 shorter events, 56.2 us)
Async XLA Ops:
  1.1 8.4 %collective-permute-start = (bf16[128,64]{1,0:T(8,128)(2,1)S(1)}, bf16[128,64]{1,0:T(8,128)(2,1)S(1)}, u32[]{:S(2)}, u32[]{:S(2)}) collective-permute-start(bf16[128,64]{1,0:T(8,128)(2,1)S(1)} %get-tuple-element.148), channel_id=1, source_target_pairs={{0,1},{1,0},{2,3},{3,2},{4,5},{5,4},{6,7},{7,6},{8,9},{9,8},{10,11... | collective-permute-start | bytes 49160 | tf_op jit(solution)/shard_map/ppermute | solution.py:97
  4.5 5.1 %collective-permute-start.1 = (bf16[128,64]{1,0:T(8,128)(2,1)S(1)}, bf16[128,64]{1,0:T(8,128)(2,1)S(1)}, u32[]{:S(2)}, u32[]{:S(2)}) collective-permute-start(bf16[128,64]{1,0:T(8,128)(2,1)S(1)} %get-tuple-element.149), channel_id=1, source_target_pairs={{0,31},{1,2},{2,1},{3,4},{4,3},{5,6},{6,5},{7,8},{8,7},{9,10},{10,... | collective-permute-start | bytes 49160 | tf_op jit(solution)/shard_map/ppermute | solution.py:97
  9.9 7.6 %collective-permute-start.2 = (bf16[128,512]{1,0:T(8,128)(2,1)S(1)}, bf16[128,512]{1,0:T(8,128)(2,1)S(1)}, u32[]{:S(2)}, u32[]{:S(2)}) collective-permute-start(bf16[128,512]{1,0:T(8,128)(2,1)S(1)} %get-tuple-element.9), channel_id=1, source_target_pairs={{0,160},{32,128},{64,224},{96,192},{128,32},{160,0},{192,96},{224,... | collective-permute-start | bytes 393224 | tf_op jit(solution)/shard_map/ppermute | solution.py:97
  12.9 6.1 %collective-permute-start.3 = (bf16[128,512]{1,0:T(8,128)(2,1)S(1)}, bf16[128,512]{1,0:T(8,128)(2,1)S(1)}, u32[]{:S(2)}, u32[]{:S(2)}) collective-permute-start(bf16[128,512]{1,0:T(8,128)(2,1)S(1)} %get-tuple-element.9), channel_id=1, source_target_pairs={{0,128},{32,160},{64,192},{96,224},{128,0},{160,32},{192,64},{224,... | collective-permute-start | bytes 393224 | tf_op jit(solution)/shard_map/ppermute | solution.py:97
  13.0 6.4 %collective-permute-start.4 = (bf16[128,512]{1,0:T(8,128)(2,1)S(1)}, bf16[128,512]{1,0:T(8,128)(2,1)S(1)}, u32[]{:S(2)}, u32[]{:S(2)}) collective-permute-start(bf16[128,512]{1,0:T(8,128)(2,1)S(1)} %get-tuple-element.9), channel_id=1, source_target_pairs={{0,96},{32,64},{64,32},{96,0},{128,224},{160,192},{192,160},{224,1... | collective-permute-start | bytes 393224 | tf_op jit(solution)/shard_map/ppermute | solution.py:97
  15.2 6.2 %collective-permute-start.5 = (bf16[128,512]{1,0:T(8,128)(2,1)S(1)}, bf16[128,512]{1,0:T(8,128)(2,1)S(1)}, u32[]{:S(2)}, u32[]{:S(2)}) collective-permute-start(bf16[128,512]{1,0:T(8,128)(2,1)S(1)} %get-tuple-element.9), channel_id=1, source_target_pairs={{0,224},{32,192},{64,160},{96,128},{128,96},{160,64},{192,32},{224... | collective-permute-start | bytes 393224 | tf_op jit(solution)/shard_map/ppermute | solution.py:97
  17.1 4.3 %collective-permute-start.6 = (bf16[128,512]{1,0:T(8,128)(2,1)S(1)}, bf16[128,512]{1,0:T(8,128)(2,1)S(1)}, u32[]{:S(2)}, u32[]{:S(2)}) collective-permute-start(bf16[128,512]{1,0:T(8,128)(2,1)S(1)} %get-tuple-element.9), channel_id=1, source_target_pairs={{0,64},{32,96},{64,0},{96,32},{128,192},{160,224},{192,128},{224,1... | collective-permute-start | bytes 393224 | tf_op jit(solution)/shard_map/ppermute | solution.py:97
  17.5 7.9 %collective-permute-start.7 = (bf16[128,512]{1,0:T(8,128)(2,1)S(1)}, bf16[128,512]{1,0:T(8,128)(2,1)S(1)}, u32[]{:S(2)}, u32[]{:S(2)}) collective-permute-start(bf16[128,512]{1,0:T(8,128)(2,1)S(1)} %get-tuple-element.9), channel_id=1, source_target_pairs={{0,192},{32,224},{64,128},{96,160},{128,64},{160,96},{192,0},{224,... | collective-permute-start | bytes 393224 | tf_op jit(solution)/shard_map/ppermute | solution.py:97
  19.1 6.4 %collective-permute-start.8 = (bf16[128,512]{1,0:T(8,128)(2,1)S(1)}, bf16[128,512]{1,0:T(8,128)(2,1)S(1)}, u32[]{:S(2)}, u32[]{:S(2)}) collective-permute-start(bf16[128,512]{1,0:T(8,128)(2,1)S(1)} %get-tuple-element.9), channel_id=1, source_target_pairs={{0,32},{32,0},{64,96},{96,64},{128,160},{160,128},{192,224},{224,1... | collective-permute-start | bytes 393224 | tf_op jit(solution)/shard_map/ppermute | solution.py:97
  27.5 12.1 %collective-permute-start.10 = (bf16[128,64]{1,0:T(8,128)(2,1)S(1)}, bf16[128,64]{1,0:T(8,128)(2,1)S(1)}, u32[]{:S(2)}, u32[]{:S(2)}) collective-permute-start(bf16[128,64]{1,0:T(8,128)(2,1)S(1)} %get-tuple-element.141), channel_id=1, source_target_pairs={{0,31},{1,2},{2,1},{3,4},{4,3},{5,6},{6,5},{7,8},{8,7},{9,10},{10,... | collective-permute-start | bytes 49160 | tf_op jit(solution)/shard_map/ppermute | solution.py:97
  34.4 6.0 %collective-permute-start.9 = (bf16[128,64]{1,0:T(8,128)(2,1)S(1)}, bf16[128,64]{1,0:T(8,128)(2,1)S(1)}, u32[]{:S(2)}, u32[]{:S(2)}) collective-permute-start(bf16[128,64]{1,0:T(8,128)(2,1)S(1)} %get-tuple-element.140), channel_id=1, source_target_pairs={{0,1},{1,0},{2,3},{3,2},{4,5},{5,4},{6,7},{7,6},{8,9},{9,8},{10,11... | collective-permute-start | bytes 49160 | tf_op jit(solution)/shard_map/ppermute | solution.py:97
  43.0 4.8 %collective-permute-start.12 = (bf16[128,64]{1,0:T(8,128)(2,1)S(1)}, bf16[128,64]{1,0:T(8,128)(2,1)S(1)}, u32[]{:S(2)}, u32[]{:S(2)}) collective-permute-start(bf16[128,64]{1,0:T(8,128)(2,1)S(1)} %get-tuple-element.133), channel_id=1, source_target_pairs={{0,31},{1,2},{2,1},{3,4},{4,3},{5,6},{6,5},{7,8},{8,7},{9,10},{10,... | collective-permute-start | bytes 49160 | tf_op jit(solution)/shard_map/ppermute | solution.py:97
  51.9 4.8 %collective-permute-start.14 = (bf16[128,64]{1,0:T(8,128)(2,1)S(1)}, bf16[128,64]{1,0:T(8,128)(2,1)S(1)}, u32[]{:S(2)}, u32[]{:S(2)}) collective-permute-start(bf16[128,64]{1,0:T(8,128)(2,1)S(1)} %get-tuple-element.125), channel_id=1, source_target_pairs={{0,31},{1,2},{2,1},{3,4},{4,3},{5,6},{6,5},{7,8},{8,7},{9,10},{10,... | collective-permute-start | bytes 49160 | tf_op jit(solution)/shard_map/ppermute | solution.py:97
  58.5 3.3 %collective-permute-start.15 = (bf16[128,64]{1,0:T(8,128)(2,1)S(1)}, bf16[128,64]{1,0:T(8,128)(2,1)S(1)}, u32[]{:S(2)}, u32[]{:S(2)}) collective-permute-start(bf16[128,64]{1,0:T(8,128)(2,1)S(1)} %get-tuple-element.116), channel_id=1, source_target_pairs={{0,1},{1,0},{2,3},{3,2},{4,5},{5,4},{6,7},{7,6},{8,9},{9,8},{10,11... | collective-permute-start | bytes 49160 | tf_op jit(solution)/shard_map/ppermute | solution.py:97
  61.0 4.8 %collective-permute-start.16 = (bf16[128,64]{1,0:T(8,128)(2,1)S(1)}, bf16[128,64]{1,0:T(8,128)(2,1)S(1)}, u32[]{:S(2)}, u32[]{:S(2)}) collective-permute-start(bf16[128,64]{1,0:T(8,128)(2,1)S(1)} %get-tuple-element.117), channel_id=1, source_target_pairs={{0,31},{1,2},{2,1},{3,4},{4,3},{5,6},{6,5},{7,8},{8,7},{9,10},{10,... | collective-permute-start | bytes 49160 | tf_op jit(solution)/shard_map/ppermute | solution.py:97
  69.9 4.8 %collective-permute-start.18 = (bf16[128,64]{1,0:T(8,128)(2,1)S(1)}, bf16[128,64]{1,0:T(8,128)(2,1)S(1)}, u32[]{:S(2)}, u32[]{:S(2)}) collective-permute-start(bf16[128,64]{1,0:T(8,128)(2,1)S(1)} %get-tuple-element.109), channel_id=1, source_target_pairs={{0,31},{1,2},{2,1},{3,4},{4,3},{5,6},{6,5},{7,8},{8,7},{9,10},{10,... | collective-permute-start | bytes 49160 | tf_op jit(solution)/shard_map/ppermute | solution.py:97
  78.8 4.8 %collective-permute-start.20 = (bf16[128,64]{1,0:T(8,128)(2,1)S(1)}, bf16[128,64]{1,0:T(8,128)(2,1)S(1)}, u32[]{:S(2)}, u32[]{:S(2)}) collective-permute-start(bf16[128,64]{1,0:T(8,128)(2,1)S(1)} %get-tuple-element.101), channel_id=1, source_target_pairs={{0,31},{1,2},{2,1},{3,4},{4,3},{5,6},{6,5},{7,8},{8,7},{9,10},{10,... | collective-permute-start | bytes 49160 | tf_op jit(solution)/shard_map/ppermute | solution.py:97
  87.7 4.8 %collective-permute-start.22 = (bf16[128,64]{1,0:T(8,128)(2,1)S(1)}, bf16[128,64]{1,0:T(8,128)(2,1)S(1)}, u32[]{:S(2)}, u32[]{:S(2)}) collective-permute-start(bf16[128,64]{1,0:T(8,128)(2,1)S(1)} %get-tuple-element.93), channel_id=1, source_target_pairs={{0,31},{1,2},{2,1},{3,4},{4,3},{5,6},{6,5},{7,8},{8,7},{9,10},{10,... | collective-permute-start | bytes 49160 | tf_op jit(solution)/shard_map/ppermute | solution.py:97
  92.9 8.0 %collective-permute-start.23 = (bf16[128,512]{1,0:T(8,128)(2,1)S(1)}, bf16[128,512]{1,0:T(8,128)(2,1)S(1)}, u32[]{:S(2)}, u32[]{:S(2)}) collective-permute-start(bf16[128,512]{1,0:T(8,128)(2,1)S(1)} %get-tuple-element.7), channel_id=1, source_target_pairs={{0,160},{32,128},{64,224},{96,192},{128,32},{160,0},{192,96},{224,... | collective-permute-start | bytes 393224 | tf_op jit(solution)/shard_map/ppermute | solution.py:97
  95.9 9.4 %collective-permute-start.24 = (bf16[128,512]{1,0:T(8,128)(2,1)S(1)}, bf16[128,512]{1,0:T(8,128)(2,1)S(1)}, u32[]{:S(2)}, u32[]{:S(2)}) collective-permute-start(bf16[128,512]{1,0:T(8,128)(2,1)S(1)} %get-tuple-element.7), channel_id=1, source_target_pairs={{0,128},{32,160},{64,192},{96,224},{128,0},{160,32},{192,64},{224,... | collective-permute-start | bytes 393224 | tf_op jit(solution)/shard_map/ppermute | solution.py:97
  95.9 9.6 %collective-permute-start.25 = (bf16[128,512]{1,0:T(8,128)(2,1)S(1)}, bf16[128,512]{1,0:T(8,128)(2,1)S(1)}, u32[]{:S(2)}, u32[]{:S(2)}) collective-permute-start(bf16[128,512]{1,0:T(8,128)(2,1)S(1)} %get-tuple-element.7), channel_id=1, source_target_pairs={{0,96},{32,64},{64,32},{96,0},{128,224},{160,192},{192,160},{224,1... | collective-permute-start | bytes 393224 | tf_op jit(solution)/shard_map/ppermute | solution.py:97
  97.8 8.7 %collective-permute-start.26 = (bf16[128,512]{1,0:T(8,128)(2,1)S(1)}, bf16[128,512]{1,0:T(8,128)(2,1)S(1)}, u32[]{:S(2)}, u32[]{:S(2)}) collective-permute-start(bf16[128,512]{1,0:T(8,128)(2,1)S(1)} %get-tuple-element.7), channel_id=1, source_target_pairs={{0,224},{32,192},{64,160},{96,128},{128,96},{160,64},{192,32},{224... | collective-permute-start | bytes 393224 | tf_op jit(solution)/shard_map/ppermute | solution.py:97
  100.1 9.9 %collective-permute-start.27 = (bf16[128,512]{1,0:T(8,128)(2,1)S(1)}, bf16[128,512]{1,0:T(8,128)(2,1)S(1)}, u32[]{:S(2)}, u32[]{:S(2)}) collective-permute-start(bf16[128,512]{1,0:T(8,128)(2,1)S(1)} %get-tuple-element.7), channel_id=1, source_target_pairs={{0,64},{32,96},{64,0},{96,32},{128,192},{160,224},{192,128},{224,1... | collective-permute-start | bytes 393224 | tf_op jit(solution)/shard_map/ppermute | solution.py:97
  100.9 10.0 %collective-permute-start.28 = (bf16[128,512]{1,0:T(8,128)(2,1)S(1)}, bf16[128,512]{1,0:T(8,128)(2,1)S(1)}, u32[]{:S(2)}, u32[]{:S(2)}) collective-permute-start(bf16[128,512]{1,0:T(8,128)(2,1)S(1)} %get-tuple-element.7), channel_id=1, source_target_pairs={{0,192},{32,224},{64,128},{96,160},{128,64},{160,96},{192,0},{224,... | collective-permute-start | bytes 393224 | tf_op jit(solution)/shard_map/ppermute | solution.py:97
  105.3 5.6 %collective-permute-start.29 = (bf16[128,512]{1,0:T(8,128)(2,1)S(1)}, bf16[128,512]{1,0:T(8,128)(2,1)S(1)}, u32[]{:S(2)}, u32[]{:S(2)}) collective-permute-start(bf16[128,512]{1,0:T(8,128)(2,1)S(1)} %get-tuple-element.7), channel_id=1, source_target_pairs={{0,32},{32,0},{64,96},{96,64},{128,160},{160,128},{192,224},{224,1... | collective-permute-start | bytes 393224 | tf_op jit(solution)/shard_map/ppermute | solution.py:97
  112.7 4.0 %collective-permute-start.30 = (bf16[128,64]{1,0:T(8,128)(2,1)S(1)}, bf16[128,64]{1,0:T(8,128)(2,1)S(1)}, u32[]{:S(2)}, u32[]{:S(2)}) collective-permute-start(bf16[128,64]{1,0:T(8,128)(2,1)S(1)} %get-tuple-element.84), channel_id=1, source_target_pairs={{0,1},{1,0},{2,3},{3,2},{4,5},{5,4},{6,7},{7,6},{8,9},{9,8},{10,11... | collective-permute-start | bytes 49160 | tf_op jit(solution)/shard_map/ppermute | solution.py:97
  115.9 4.8 %collective-permute-start.31 = (bf16[128,64]{1,0:T(8,128)(2,1)S(1)}, bf16[128,64]{1,0:T(8,128)(2,1)S(1)}, u32[]{:S(2)}, u32[]{:S(2)}) collective-permute-start(bf16[128,64]{1,0:T(8,128)(2,1)S(1)} %get-tuple-element.85), channel_id=1, source_target_pairs={{0,31},{1,2},{2,1},{3,4},{4,3},{5,6},{6,5},{7,8},{8,7},{9,10},{10,... | collective-permute-start | bytes 49160 | tf_op jit(solution)/shard_map/ppermute | solution.py:97
  124.8 4.8 %collective-permute-start.33 = (bf16[128,64]{1,0:T(8,128)(2,1)S(1)}, bf16[128,64]{1,0:T(8,128)(2,1)S(1)}, u32[]{:S(2)}, u32[]{:S(2)}) collective-permute-start(bf16[128,64]{1,0:T(8,128)(2,1)S(1)} %get-tuple-element.77), channel_id=1, source_target_pairs={{0,31},{1,2},{2,1},{3,4},{4,3},{5,6},{6,5},{7,8},{8,7},{9,10},{10,... | collective-permute-start | bytes 49160 | tf_op jit(solution)/shard_map/ppermute | solution.py:97
  133.7 4.8 %collective-permute-start.35 = (bf16[128,64]{1,0:T(8,128)(2,1)S(1)}, bf16[128,64]{1,0:T(8,128)(2,1)S(1)}, u32[]{:S(2)}, u32[]{:S(2)}) collective-permute-start(bf16[128,64]{1,0:T(8,128)(2,1)S(1)} %get-tuple-element.69), channel_id=1, source_target_pairs={{0,31},{1,2},{2,1},{3,4},{4,3},{5,6},{6,5},{7,8},{8,7},{9,10},{10,... | collective-permute-start | bytes 49160 | tf_op jit(solution)/shard_map/ppermute | solution.py:97
  142.6 4.8 %collective-permute-start.37 = (bf16[128,64]{1,0:T(8,128)(2,1)S(1)}, bf16[128,64]{1,0:T(8,128)(2,1)S(1)}, u32[]{:S(2)}, u32[]{:S(2)}) collective-permute-start(bf16[128,64]{1,0:T(8,128)(2,1)S(1)} %get-tuple-element.61), channel_id=1, source_target_pairs={{0,31},{1,2},{2,1},{3,4},{4,3},{5,6},{6,5},{7,8},{8,7},{9,10},{10,... | collective-permute-start | bytes 49160 | tf_op jit(solution)/shard_map/ppermute | solution.py:97
  151.5 4.8 %collective-permute-start.39 = (bf16[128,64]{1,0:T(8,128)(2,1)S(1)}, bf16[128,64]{1,0:T(8,128)(2,1)S(1)}, u32[]{:S(2)}, u32[]{:S(2)}) collective-permute-start(bf16[128,64]{1,0:T(8,128)(2,1)S(1)} %get-tuple-element.53), channel_id=1, source_target_pairs={{0,31},{1,2},{2,1},{3,4},{4,3},{5,6},{6,5},{7,8},{8,7},{9,10},{10,... | collective-permute-start | bytes 49160 | tf_op jit(solution)/shard_map/ppermute | solution.py:97
  160.4 4.8 %collective-permute-start.41 = (bf16[128,64]{1,0:T(8,128)(2,1)S(1)}, bf16[128,64]{1,0:T(8,128)(2,1)S(1)}, u32[]{:S(2)}, u32[]{:S(2)}) collective-permute-start(bf16[128,64]{1,0:T(8,128)(2,1)S(1)} %get-tuple-element.45), channel_id=1, source_target_pairs={{0,31},{1,2},{2,1},{3,4},{4,3},{5,6},{6,5},{7,8},{8,7},{9,10},{10,... | collective-permute-start | bytes 49160 | tf_op jit(solution)/shard_map/ppermute | solution.py:97
  (18 other events, 55.3 us)

commit v7 on v3

--- a/solution.py
+++ b/solution.py
@@ -119,8 +119,15 @@
 def gather_nodes(rows):
     nodes = lax.axis_size("node")
     me = lax.axis_index("node")
-    swaps = [rows] + [swapped(rows, "node", lambda i, k=k: i ^ k) for k in range(1, nodes)]
-    return swaps, me ^ jnp.arange(nodes)
+    pair = swapped(rows, "node", lambda i: i ^ 1)
+    both = jnp.concatenate([rows, pair], axis=-1)
+    width = rows.shape[-1]
+    swaps, masks = [rows, pair], [0, 1]
+    for k in [4, 6, 2] if nodes == 8 else range(2, nodes, 2):
+        got = swapped(both, "node", lambda i, k=k: i ^ k)
+        swaps += [got[:, :width], got[:, width:]]
+        masks += [k, k ^ 1]
+    return swaps, me ^ jnp.asarray(masks)
 
 
 def local(start_state, node_states, reaction_rates, volume, face_lift):

time: 168 us -> 168 us (level)
  starting transfers between devices: 65.3 us -> 53.6 us
  waiting for transfers between devices: 67.2 us -> 78 us
    ppermute x42 -> x36, starting transfers between devices: 65.3 us -> 53.6 us  [swapped(): lax.ppermute(array, axis, [(i, partner(i) % devices) for i in range(devic...]
    ppermute x42 -> x36, waiting for transfers between devices: 67.2 us -> 78 us  [swapped(): lax.ppermute(array, axis, [(i, partner(i) % devices) for i in range(devic...]
  transfers between devices with their start and end apart: 42 -> 36, of which waited for: 29 -> 32; matrix products, arithmetic and copies ran while one was open for 6% -> 5% of each run, Pallas kernels for 0% -> 0%
where the time goes in v7:
time: 168 us; the launch traced here: 167 us
  waiting for transfers between devices  78 us (46%)
  starting transfers between devices  53.6 us (32%)
  matrix products  18.2 us (11%)
  local copies, waits for them, and re-layouts  9.17 us (5%)
  other arithmetic  5.75 us (3%)
  between operations  2.18 us (1%)
    ppermute x36, waiting for transfers between devices, swapped(): lax.ppermute(array, axis, [(i, partner(i) % devices) for i in range(devic...  78 us
    ppermute x36, starting transfers between devices, swapped(): lax.ppermute(array, axis, [(i, partner(i) % devices) for i in range(devic...  53.6 us
    dot_general x14, matrix products, apply_operator(): return own + jnp.dot(faces, x_lift, preferred_element_type=jnp.float32)  10.7 us
    dot_general x14, matrix products, local_terms(): jnp.dot(inputs, stacked, preferred_element_type=jnp.float32)  3.83 us
    dot_general x14, matrix products, local_terms(): jnp.dot(rounded, select, preferred_element_type=jnp.float32)  3.66 us
  transfers between devices with their start and end apart: 36, of which 32 were waited for; matrix products, arithmetic and copies ran while one was open for 5% of the time, Pallas kernels for 0%

profile of v7, /device:TPU:1, one launch (start us, length us, event | category | flops | bytes accessed | tf_op | source)
XLA Modules:
  0.0 166.8 jit_solution(4674756328693806880)
XLA Ops:
  1.1 3.3 %collective-permute-start = (bf16[128,64]{1,0:T(8,128)(2,1)S(1)}, bf16[128,64]{1,0:T(8,128)(2,1)S(1)}, u32[]{:S(2)}, u32[]{:S(2)}) collective-permute-start(bf16[128,64]{1,0:T(8,128)(2,1)S(1)} %get-tuple-element.120), channel_id=1, source_target_pairs={{0,1},{1,0},{2,3},{3,2},{4,5},{5,4},{6,7},{7,6},{8,9},{9,8},{10,11... | collective-permute-start | bytes 49160 | tf_op jit(solution)/shard_map/ppermute | solution.py:99
  11.0 2.5 %collective-permute-done.2 = bf16[128,512]{1,0:T(8,128)(2,1)S(1)} collective-permute-done((bf16[128,512]{1,0:T(8,128)(2,1)S(1)}, bf16[128,512]{1,0:T(8,128)(2,1)S(1)}, u32[]{:S(2)}, u32[]{:S(2)}) %collective-permute-start.2) | collective-permute-done | bytes 131104 | tf_op jit(solution)/shard_map/ppermute | solution.py:99
  17.1 3.3 %collective-permute-done.3 = bf16[128,1024]{1,0:T(8,128)(2,1)S(1)} collective-permute-done((bf16[128,1024]{1,0:T(8,128)(2,1)S(1)}, bf16[128,1024]{1,0:T(8,128)(2,1)S(1)}, u32[]{:S(2)}, u32[]{:S(2)}) %collective-permute-start.3) | collective-permute-done | bytes 262176 | tf_op jit(solution)/shard_map/ppermute | solution.py:99
  20.4 2.7 %collective-permute-done.4 = bf16[128,1024]{1,0:T(8,128)(2,1)S(1)} collective-permute-done((bf16[128,1024]{1,0:T(8,128)(2,1)S(1)}, bf16[128,1024]{1,0:T(8,128)(2,1)S(1)}, u32[]{:S(2)}, u32[]{:S(2)}) %collective-permute-start.4) | collective-permute-done | bytes 262176 | tf_op jit(solution)/shard_map/ppermute | solution.py:99
  25.6 7.9 %collective-permute-start.6 = (bf16[128,64]{1,0:T(8,128)(2,1)S(1)}, bf16[128,64]{1,0:T(8,128)(2,1)S(1)}, u32[]{:S(2)}, u32[]{:S(2)}) collective-permute-start(bf16[128,64]{1,0:T(8,128)(2,1)S(1)} %get-tuple-element.112), channel_id=1, source_target_pairs={{0,1},{1,0},{2,3},{3,2},{4,5},{5,4},{6,7},{7,6},{8,9},{9,8},{10,11... | collective-permute-start | bytes 49160 | tf_op jit(solution)/shard_map/ppermute | solution.py:99
  35.9 2.5 %collective-permute-done.7 = bf16[128,64]{1,0:T(8,128)(2,1)S(1)} collective-permute-done((bf16[128,64]{1,0:T(8,128)(2,1)S(1)}, bf16[128,64]{1,0:T(8,128)(2,1)S(1)}, u32[]{:S(2)}, u32[]{:S(2)}) %collective-permute-start.7) | collective-permute-done | bytes 16416 | tf_op jit(solution)/shard_map/ppermute | solution.py:99
  40.0 3.7 %collective-permute-start.8 = (bf16[128,64]{1,0:T(8,128)(2,1)S(1)}, bf16[128,64]{1,0:T(8,128)(2,1)S(1)}, u32[]{:S(2)}, u32[]{:S(2)}) collective-permute-start(bf16[128,64]{1,0:T(8,128)(2,1)S(1)} %get-tuple-element.104), channel_id=1, source_target_pairs={{0,1},{1,0},{2,3},{3,2},{4,5},{5,4},{6,7},{7,6},{8,9},{9,8},{10,11... | collective-permute-start | bytes 49160 | tf_op jit(solution)/shard_map/ppermute | solution.py:99
  44.5 4.0 %collective-permute-done.9 = bf16[128,64]{1,0:T(8,128)(2,1)S(1)} collective-permute-done((bf16[128,64]{1,0:T(8,128)(2,1)S(1)}, bf16[128,64]{1,0:T(8,128)(2,1)S(1)}, u32[]{:S(2)}, u32[]{:S(2)}) %collective-permute-start.9) | collective-permute-done | bytes 16416 | tf_op jit(solution)/shard_map/ppermute | solution.py:99
  50.1 2.3 %collective-permute-start.10 = (bf16[128,64]{1,0:T(8,128)(2,1)S(1)}, bf16[128,64]{1,0:T(8,128)(2,1)S(1)}, u32[]{:S(2)}, u32[]{:S(2)}) collective-permute-start(bf16[128,64]{1,0:T(8,128)(2,1)S(1)} %get-tuple-element.96), channel_id=1, source_target_pairs={{0,1},{1,0},{2,3},{3,2},{4,5},{5,4},{6,7},{7,6},{8,9},{9,8},{10,11... | collective-permute-start | bytes 49160 | tf_op jit(solution)/shard_map/ppermute | solution.py:99
  53.3 4.0 %collective-permute-done.11 = bf16[128,64]{1,0:T(8,128)(2,1)S(1)} collective-permute-done((bf16[128,64]{1,0:T(8,128)(2,1)S(1)}, bf16[128,64]{1,0:T(8,128)(2,1)S(1)}, u32[]{:S(2)}, u32[]{:S(2)}) %collective-permute-start.11) | collective-permute-done | bytes 16416 | tf_op jit(solution)/shard_map/ppermute | solution.py:99
  58.8 2.3 %collective-permute-start.12 = (bf16[128,64]{1,0:T(8,128)(2,1)S(1)}, bf16[128,64]{1,0:T(8,128)(2,1)S(1)}, u32[]{:S(2)}, u32[]{:S(2)}) collective-permute-start(bf16[128,64]{1,0:T(8,128)(2,1)S(1)} %get-tuple-element.88), channel_id=1, source_target_pairs={{0,1},{1,0},{2,3},{3,2},{4,5},{5,4},{6,7},{7,6},{8,9},{9,8},{10,11... | collective-permute-start | bytes 49160 | tf_op jit(solution)/shard_map/ppermute | solution.py:99
  62.0 4.0 %collective-permute-done.13 = bf16[128,64]{1,0:T(8,128)(2,1)S(1)} collective-permute-done((bf16[128,64]{1,0:T(8,128)(2,1)S(1)}, bf16[128,64]{1,0:T(8,128)(2,1)S(1)}, u32[]{:S(2)}, u32[]{:S(2)}) %collective-permute-start.13) | collective-permute-done | bytes 16416 | tf_op jit(solution)/shard_map/ppermute | solution.py:99
  67.6 2.5 %collective-permute-start.14 = (bf16[128,64]{1,0:T(8,128)(2,1)S(1)}, bf16[128,64]{1,0:T(8,128)(2,1)S(1)}, u32[]{:S(2)}, u32[]{:S(2)}) collective-permute-start(bf16[128,64]{1,0:T(8,128)(2,1)S(1)} %get-tuple-element.80), channel_id=1, source_target_pairs={{0,1},{1,0},{2,3},{3,2},{4,5},{5,4},{6,7},{7,6},{8,9},{9,8},{10,11... | collective-permute-start | bytes 49160 | tf_op jit(solution)/shard_map/ppermute | solution.py:99
  70.9 4.0 %collective-permute-done.15 = bf16[128,64]{1,0:T(8,128)(2,1)S(1)} collective-permute-done((bf16[128,64]{1,0:T(8,128)(2,1)S(1)}, bf16[128,64]{1,0:T(8,128)(2,1)S(1)}, u32[]{:S(2)}, u32[]{:S(2)}) %collective-permute-start.15) | collective-permute-done | bytes 16416 | tf_op jit(solution)/shard_map/ppermute | solution.py:99
  76.5 2.3 %collective-permute-start.16 = (bf16[128,64]{1,0:T(8,128)(2,1)S(1)}, bf16[128,64]{1,0:T(8,128)(2,1)S(1)}, u32[]{:S(2)}, u32[]{:S(2)}) collective-permute-start(bf16[128,64]{1,0:T(8,128)(2,1)S(1)} %get-tuple-element.72), channel_id=1, source_target_pairs={{0,1},{1,0},{2,3},{3,2},{4,5},{5,4},{6,7},{7,6},{8,9},{9,8},{10,11... | collective-permute-start | bytes 49160 | tf_op jit(solution)/shard_map/ppermute | solution.py:99
  79.7 4.0 %collective-permute-done.17 = bf16[128,64]{1,0:T(8,128)(2,1)S(1)} collective-permute-done((bf16[128,64]{1,0:T(8,128)(2,1)S(1)}, bf16[128,64]{1,0:T(8,128)(2,1)S(1)}, u32[]{:S(2)}, u32[]{:S(2)}) %collective-permute-start.17) | collective-permute-done | bytes 16416 | tf_op jit(solution)/shard_map/ppermute | solution.py:99
  88.4 4.0 %collective-permute-done.19 = bf16[128,64]{1,0:T(8,128)(2,1)S(1)} collective-permute-done((bf16[128,64]{1,0:T(8,128)(2,1)S(1)}, bf16[128,64]{1,0:T(8,128)(2,1)S(1)}, u32[]{:S(2)}, u32[]{:S(2)}) %collective-permute-start.19) | collective-permute-done | bytes 16416 | tf_op jit(solution)/shard_map/ppermute | solution.py:99
  93.1 3.5 %collective-permute-done.20 = bf16[128,512]{1,0:T(8,128)(2,1)S(1)} collective-permute-done((bf16[128,512]{1,0:T(8,128)(2,1)S(1)}, bf16[128,512]{1,0:T(8,128)(2,1)S(1)}, u32[]{:S(2)}, u32[]{:S(2)}) %collective-permute-start.20) | collective-permute-done | bytes 131104 | tf_op jit(solution)/shard_map/ppermute | solution.py:99
  96.6 2.5 %collective-permute-start.21 = (bf16[128,1024]{1,0:T(8,128)(2,1)S(1)}, bf16[128,1024]{1,0:T(8,128)(2,1)S(1)}, u32[]{:S(2)}, u32[]{:S(2)}) collective-permute-start(bf16[128,1024]{1,0:T(8,128)(2,1)S(1)} %pad_maximum_fusion.2), channel_id=1, source_target_pairs={{0,128},{32,160},{64,192},{96,224},{128,0},{160,32},{192,64},{224,... | collective-permute-start | bytes 786440 | tf_op jit(solution)/shard_map/ppermute | solution.py:99
  100.4 3.1 %collective-permute-done.21 = bf16[128,1024]{1,0:T(8,128)(2,1)S(1)} collective-permute-done((bf16[128,1024]{1,0:T(8,128)(2,1)S(1)}, bf16[128,1024]{1,0:T(8,128)(2,1)S(1)}, u32[]{:S(2)}, u32[]{:S(2)}) %collective-permute-start.21) | collective-permute-done | bytes 262176 | tf_op jit(solution)/shard_map/ppermute | solution.py:99
  103.5 6.1 %collective-permute-done.22 = bf16[128,1024]{1,0:T(8,128)(2,1)S(1)} collective-permute-done((bf16[128,1024]{1,0:T(8,128)(2,1)S(1)}, bf16[128,1024]{1,0:T(8,128)(2,1)S(1)}, u32[]{:S(2)}, u32[]{:S(2)}) %collective-permute-start.22) | collective-permute-done | bytes 262176 | tf_op jit(solution)/shard_map/ppermute | solution.py:99
  111.4 3.4 %collective-permute-start.24 = (bf16[128,64]{1,0:T(8,128)(2,1)S(1)}, bf16[128,64]{1,0:T(8,128)(2,1)S(1)}, u32[]{:S(2)}, u32[]{:S(2)}) collective-permute-start(bf16[128,64]{1,0:T(8,128)(2,1)S(1)} %get-tuple-element.56), channel_id=1, source_target_pairs={{0,1},{1,0},{2,3},{3,2},{4,5},{5,4},{6,7},{7,6},{8,9},{9,8},{10,11... | collective-permute-start | bytes 49160 | tf_op jit(solution)/shard_map/ppermute | solution.py:99
  115.7 4.0 %collective-permute-done.25 = bf16[128,64]{1,0:T(8,128)(2,1)S(1)} collective-permute-done((bf16[128,64]{1,0:T(8,128)(2,1)S(1)}, bf16[128,64]{1,0:T(8,128)(2,1)S(1)}, u32[]{:S(2)}, u32[]{:S(2)}) %collective-permute-start.25) | collective-permute-done | bytes 16416 | tf_op jit(solution)/shard_map/ppermute | solution.py:99
  121.3 4.0 %collective-permute-start.26 = (bf16[128,64]{1,0:T(8,128)(2,1)S(1)}, bf16[128,64]{1,0:T(8,128)(2,1)S(1)}, u32[]{:S(2)}, u32[]{:S(2)}) collective-permute-start(bf16[128,64]{1,0:T(8,128)(2,1)S(1)} %get-tuple-element.48), channel_id=1, source_target_pairs={{0,1},{1,0},{2,3},{3,2},{4,5},{5,4},{6,7},{7,6},{8,9},{9,8},{10,11... | collective-permute-start | bytes 49160 | tf_op jit(solution)/shard_map/ppermute | solution.py:99
  126.1 4.0 %collective-permute-done.27 = bf16[128,64]{1,0:T(8,128)(2,1)S(1)} collective-permute-done((bf16[128,64]{1,0:T(8,128)(2,1)S(1)}, bf16[128,64]{1,0:T(8,128)(2,1)S(1)}, u32[]{:S(2)}, u32[]{:S(2)}) %collective-permute-start.27) | collective-permute-done | bytes 16416 | tf_op jit(solution)/shard_map/ppermute | solution.py:99
  131.7 2.5 %collective-permute-start.28 = (bf16[128,64]{1,0:T(8,128)(2,1)S(1)}, bf16[128,64]{1,0:T(8,128)(2,1)S(1)}, u32[]{:S(2)}, u32[]{:S(2)}) collective-permute-start(bf16[128,64]{1,0:T(8,128)(2,1)S(1)} %get-tuple-element.40), channel_id=1, source_target_pairs={{0,1},{1,0},{2,3},{3,2},{4,5},{5,4},{6,7},{7,6},{8,9},{9,8},{10,11... | collective-permute-start | bytes 49160 | tf_op jit(solution)/shard_map/ppermute | solution.py:99
  135.1 4.0 %collective-permute-done.29 = bf16[128,64]{1,0:T(8,128)(2,1)S(1)} collective-permute-done((bf16[128,64]{1,0:T(8,128)(2,1)S(1)}, bf16[128,64]{1,0:T(8,128)(2,1)S(1)}, u32[]{:S(2)}, u32[]{:S(2)}) %collective-permute-start.29) | collective-permute-done | bytes 16416 | tf_op jit(solution)/shard_map/ppermute | solution.py:99
  140.7 2.3 %collective-permute-start.30 = (bf16[128,64]{1,0:T(8,128)(2,1)S(1)}, bf16[128,64]{1,0:T(8,128)(2,1)S(1)}, u32[]{:S(2)}, u32[]{:S(2)}) collective-permute-start(bf16[128,64]{1,0:T(8,128)(2,1)S(1)} %get-tuple-element.32), channel_id=1, source_target_pairs={{0,1},{1,0},{2,3},{3,2},{4,5},{5,4},{6,7},{7,6},{8,9},{9,8},{10,11... | collective-permute-start | bytes 49160 | tf_op jit(solution)/shard_map/ppermute | solution.py:99
  143.8 4.0 %collective-permute-done.31 = bf16[128,64]{1,0:T(8,128)(2,1)S(1)} collective-permute-done((bf16[128,64]{1,0:T(8,128)(2,1)S(1)}, bf16[128,64]{1,0:T(8,128)(2,1)S(1)}, u32[]{:S(2)}, u32[]{:S(2)}) %collective-permute-start.31) | collective-permute-done | bytes 16416 | tf_op jit(solution)/shard_map/ppermute | solution.py:99
  152.6 4.0 %collective-permute-done.33 = bf16[128,64]{1,0:T(8,128)(2,1)S(1)} collective-permute-done((bf16[128,64]{1,0:T(8,128)(2,1)S(1)}, bf16[128,64]{1,0:T(8,128)(2,1)S(1)}, u32[]{:S(2)}, u32[]{:S(2)}) %collective-permute-start.33) | collective-permute-done | bytes 16416 | tf_op jit(solution)/shard_map/ppermute | solution.py:99
  158.2 2.3 %collective-permute-start.34 = (bf16[128,64]{1,0:T(8,128)(2,1)S(1)}, bf16[128,64]{1,0:T(8,128)(2,1)S(1)}, u32[]{:S(2)}, u32[]{:S(2)}) collective-permute-start(bf16[128,64]{1,0:T(8,128)(2,1)S(1)} %get-tuple-element.16), channel_id=1, source_target_pairs={{0,1},{1,0},{2,3},{3,2},{4,5},{5,4},{6,7},{7,6},{8,9},{9,8},{10,11... | collective-permute-start | bytes 49160 | tf_op jit(solution)/shard_map/ppermute | solution.py:99
  161.3 4.0 %collective-permute-done.35 = bf16[128,64]{1,0:T(8,128)(2,1)S(1)} collective-permute-done((bf16[128,64]{1,0:T(8,128)(2,1)S(1)}, bf16[128,64]{1,0:T(8,128)(2,1)S(1)}, u32[]{:S(2)}, u32[]{:S(2)}) %collective-permute-start.35) | collective-permute-done | bytes 16416 | tf_op jit(solution)/shard_map/ppermute | solution.py:99
  (349 shorter events, 51.8 us)
Async XLA Ops:
  1.1 7.3 %collective-permute-start = (bf16[128,64]{1,0:T(8,128)(2,1)S(1)}, bf16[128,64]{1,0:T(8,128)(2,1)S(1)}, u32[]{:S(2)}, u32[]{:S(2)}) collective-permute-start(bf16[128,64]{1,0:T(8,128)(2,1)S(1)} %get-tuple-element.120), channel_id=1, source_target_pairs={{0,1},{1,0},{2,3},{3,2},{4,5},{5,4},{6,7},{7,6},{8,9},{9,8},{10,11... | collective-permute-start | bytes 49160 | tf_op jit(solution)/shard_map/ppermute | solution.py:99
  4.5 4.8 %collective-permute-start.1 = (bf16[128,64]{1,0:T(8,128)(2,1)S(1)}, bf16[128,64]{1,0:T(8,128)(2,1)S(1)}, u32[]{:S(2)}, u32[]{:S(2)}) collective-permute-start(bf16[128,64]{1,0:T(8,128)(2,1)S(1)} %get-tuple-element.121), channel_id=1, source_target_pairs={{0,31},{1,2},{2,1},{3,4},{4,3},{5,6},{6,5},{7,8},{8,7},{9,10},{10,... | collective-permute-start | bytes 49160 | tf_op jit(solution)/shard_map/ppermute | solution.py:99
  9.6 3.9 %collective-permute-start.2 = (bf16[128,512]{1,0:T(8,128)(2,1)S(1)}, bf16[128,512]{1,0:T(8,128)(2,1)S(1)}, u32[]{:S(2)}, u32[]{:S(2)}) collective-permute-start(bf16[128,512]{1,0:T(8,128)(2,1)S(1)} %get-tuple-element.9), channel_id=1, source_target_pairs={{0,32},{32,0},{64,96},{96,64},{128,160},{160,128},{192,224},{224,1... | collective-permute-start | bytes 393224 | tf_op jit(solution)/shard_map/ppermute | solution.py:99
  13.5 6.9 %collective-permute-start.3 = (bf16[128,1024]{1,0:T(8,128)(2,1)S(1)}, bf16[128,1024]{1,0:T(8,128)(2,1)S(1)}, u32[]{:S(2)}, u32[]{:S(2)}) collective-permute-start(bf16[128,1024]{1,0:T(8,128)(2,1)S(1)} %pad_maximum_fusion.1), channel_id=1, source_target_pairs={{0,128},{32,160},{64,192},{96,224},{128,0},{160,32},{192,64},{224,... | collective-permute-start | bytes 786440 | tf_op jit(solution)/shard_map/ppermute | solution.py:99
  16.3 6.9 %collective-permute-start.4 = (bf16[128,1024]{1,0:T(8,128)(2,1)S(1)}, bf16[128,1024]{1,0:T(8,128)(2,1)S(1)}, u32[]{:S(2)}, u32[]{:S(2)}) collective-permute-start(bf16[128,1024]{1,0:T(8,128)(2,1)S(1)} %pad_maximum_fusion.1), channel_id=1, source_target_pairs={{0,192},{32,224},{64,128},{96,160},{128,64},{160,96},{192,0},{224,... | collective-permute-start | bytes 786440 | tf_op jit(solution)/shard_map/ppermute | solution.py:99
  17.1 6.1 %collective-permute-start.5 = (bf16[128,1024]{1,0:T(8,128)(2,1)S(1)}, bf16[128,1024]{1,0:T(8,128)(2,1)S(1)}, u32[]{:S(2)}, u32[]{:S(2)}) collective-permute-start(bf16[128,1024]{1,0:T(8,128)(2,1)S(1)} %pad_maximum_fusion.1), channel_id=1, source_target_pairs={{0,64},{32,96},{64,0},{96,32},{128,192},{160,224},{192,128},{224,1... | collective-permute-start | bytes 786440 | tf_op jit(solution)/shard_map/ppermute | solution.py:99
  25.6 10.3 %collective-permute-start.6 = (bf16[128,64]{1,0:T(8,128)(2,1)S(1)}, bf16[128,64]{1,0:T(8,128)(2,1)S(1)}, u32[]{:S(2)}, u32[]{:S(2)}) collective-permute-start(bf16[128,64]{1,0:T(8,128)(2,1)S(1)} %get-tuple-element.112), channel_id=1, source_target_pairs={{0,1},{1,0},{2,3},{3,2},{4,5},{5,4},{6,7},{7,6},{8,9},{9,8},{10,11... | collective-permute-start | bytes 49160 | tf_op jit(solution)/shard_map/ppermute | solution.py:99
  33.5 4.8 %collective-permute-start.7 = (bf16[128,64]{1,0:T(8,128)(2,1)S(1)}, bf16[128,64]{1,0:T(8,128)(2,1)S(1)}, u32[]{:S(2)}, u32[]{:S(2)}) collective-permute-start(bf16[128,64]{1,0:T(8,128)(2,1)S(1)} %get-tuple-element.113), channel_id=1, source_target_pairs={{0,31},{1,2},{2,1},{3,4},{4,3},{5,6},{6,5},{7,8},{8,7},{9,10},{10,... | collective-permute-start | bytes 49160 | tf_op jit(solution)/shard_map/ppermute | solution.py:99
  40.0 4.5 %collective-permute-start.8 = (bf16[128,64]{1,0:T(8,128)(2,1)S(1)}, bf16[128,64]{1,0:T(8,128)(2,1)S(1)}, u32[]{:S(2)}, u32[]{:S(2)}) collective-permute-start(bf16[128,64]{1,0:T(8,128)(2,1)S(1)} %get-tuple-element.104), channel_id=1, source_target_pairs={{0,1},{1,0},{2,3},{3,2},{4,5},{5,4},{6,7},{7,6},{8,9},{9,8},{10,11... | collective-permute-start | bytes 49160 | tf_op jit(solution)/shard_map/ppermute | solution.py:99
  43.7 4.8 %collective-permute-start.9 = (bf16[128,64]{1,0:T(8,128)(2,1)S(1)}, bf16[128,64]{1,0:T(8,128)(2,1)S(1)}, u32[]{:S(2)}, u32[]{:S(2)}) collective-permute-start(bf16[128,64]{1,0:T(8,128)(2,1)S(1)} %get-tuple-element.105), channel_id=1, source_target_pairs={{0,31},{1,2},{2,1},{3,4},{4,3},{5,6},{6,5},{7,8},{8,7},{9,10},{10,... | collective-permute-start | bytes 49160 | tf_op jit(solution)/shard_map/ppermute | solution.py:99
  50.1 3.2 %collective-permute-start.10 = (bf16[128,64]{1,0:T(8,128)(2,1)S(1)}, bf16[128,64]{1,0:T(8,128)(2,1)S(1)}, u32[]{:S(2)}, u32[]{:S(2)}) collective-permute-start(bf16[128,64]{1,0:T(8,128)(2,1)S(1)} %get-tuple-element.96), channel_id=1, source_target_pairs={{0,1},{1,0},{2,3},{3,2},{4,5},{5,4},{6,7},{7,6},{8,9},{9,8},{10,11... | collective-permute-start | bytes 49160 | tf_op jit(solution)/shard_map/ppermute | solution.py:99
  52.4 4.8 %collective-permute-start.11 = (bf16[128,64]{1,0:T(8,128)(2,1)S(1)}, bf16[128,64]{1,0:T(8,128)(2,1)S(1)}, u32[]{:S(2)}, u32[]{:S(2)}) collective-permute-start(bf16[128,64]{1,0:T(8,128)(2,1)S(1)} %get-tuple-element.97), channel_id=1, source_target_pairs={{0,31},{1,2},{2,1},{3,4},{4,3},{5,6},{6,5},{7,8},{8,7},{9,10},{10,... | collective-permute-start | bytes 49160 | tf_op jit(solution)/shard_map/ppermute | solution.py:99
  61.1 4.8 %collective-permute-start.13 = (bf16[128,64]{1,0:T(8,128)(2,1)S(1)}, bf16[128,64]{1,0:T(8,128)(2,1)S(1)}, u32[]{:S(2)}, u32[]{:S(2)}) collective-permute-start(bf16[128,64]{1,0:T(8,128)(2,1)S(1)} %get-tuple-element.89), channel_id=1, source_target_pairs={{0,31},{1,2},{2,1},{3,4},{4,3},{5,6},{6,5},{7,8},{8,7},{9,10},{10,... | collective-permute-start | bytes 49160 | tf_op jit(solution)/shard_map/ppermute | solution.py:99
  67.6 3.3 %collective-permute-start.14 = (bf16[128,64]{1,0:T(8,128)(2,1)S(1)}, bf16[128,64]{1,0:T(8,128)(2,1)S(1)}, u32[]{:S(2)}, u32[]{:S(2)}) collective-permute-start(bf16[128,64]{1,0:T(8,128)(2,1)S(1)} %get-tuple-element.80), channel_id=1, source_target_pairs={{0,1},{1,0},{2,3},{3,2},{4,5},{5,4},{6,7},{7,6},{8,9},{9,8},{10,11... | collective-permute-start | bytes 49160 | tf_op jit(solution)/shard_map/ppermute | solution.py:99
  70.1 4.8 %collective-permute-start.15 = (bf16[128,64]{1,0:T(8,128)(2,1)S(1)}, bf16[128,64]{1,0:T(8,128)(2,1)S(1)}, u32[]{:S(2)}, u32[]{:S(2)}) collective-permute-start(bf16[128,64]{1,0:T(8,128)(2,1)S(1)} %get-tuple-element.81), channel_id=1, source_target_pairs={{0,31},{1,2},{2,1},{3,4},{4,3},{5,6},{6,5},{7,8},{8,7},{9,10},{10,... | collective-permute-start | bytes 49160 | tf_op jit(solution)/shard_map/ppermute | solution.py:99
  76.5 3.2 %collective-permute-start.16 = (bf16[128,64]{1,0:T(8,128)(2,1)S(1)}, bf16[128,64]{1,0:T(8,128)(2,1)S(1)}, u32[]{:S(2)}, u32[]{:S(2)}) collective-permute-start(bf16[128,64]{1,0:T(8,128)(2,1)S(1)} %get-tuple-element.72), channel_id=1, source_target_pairs={{0,1},{1,0},{2,3},{3,2},{4,5},{5,4},{6,7},{7,6},{8,9},{9,8},{10,11... | collective-permute-start | bytes 49160 | tf_op jit(solution)/shard_map/ppermute | solution.py:99
  78.8 4.8 %collective-permute-start.17 = (bf16[128,64]{1,0:T(8,128)(2,1)S(1)}, bf16[128,64]{1,0:T(8,128)(2,1)S(1)}, u32[]{:S(2)}, u32[]{:S(2)}) collective-permute-start(bf16[128,64]{1,0:T(8,128)(2,1)S(1)} %get-tuple-element.73), channel_id=1, source_target_pairs={{0,31},{1,2},{2,1},{3,4},{4,3},{5,6},{6,5},{7,8},{8,7},{9,10},{10,... | collective-permute-start | bytes 49160 | tf_op jit(solution)/shard_map/ppermute | solution.py:99
  87.6 4.8 %collective-permute-start.19 = (bf16[128,64]{1,0:T(8,128)(2,1)S(1)}, bf16[128,64]{1,0:T(8,128)(2,1)S(1)}, u32[]{:S(2)}, u32[]{:S(2)}) collective-permute-start(bf16[128,64]{1,0:T(8,128)(2,1)S(1)} %get-tuple-element.65), channel_id=1, source_target_pairs={{0,31},{1,2},{2,1},{3,4},{4,3},{5,6},{6,5},{7,8},{8,7},{9,10},{10,... | collective-permute-start | bytes 49160 | tf_op jit(solution)/shard_map/ppermute | solution.py:99
  92.7 3.9 %collective-permute-start.20 = (bf16[128,512]{1,0:T(8,128)(2,1)S(1)}, bf16[128,512]{1,0:T(8,128)(2,1)S(1)}, u32[]{:S(2)}, u32[]{:S(2)}) collective-permute-start(bf16[128,512]{1,0:T(8,128)(2,1)S(1)} %get-tuple-element.7), channel_id=1, source_target_pairs={{0,32},{32,0},{64,96},{96,64},{128,160},{160,128},{192,224},{224,1... | collective-permute-start | bytes 393224 | tf_op jit(solution)/shard_map/ppermute | solution.py:99
  96.6 6.9 %collective-permute-start.21 = (bf16[128,1024]{1,0:T(8,128)(2,1)S(1)}, bf16[128,1024]{1,0:T(8,128)(2,1)S(1)}, u32[]{:S(2)}, u32[]{:S(2)}) collective-permute-start(bf16[128,1024]{1,0:T(8,128)(2,1)S(1)} %pad_maximum_fusion.2), channel_id=1, source_target_pairs={{0,128},{32,160},{64,192},{96,224},{128,0},{160,32},{192,64},{224,... | collective-permute-start | bytes 786440 | tf_op jit(solution)/shard_map/ppermute | solution.py:99
  99.1 10.5 %collective-permute-start.22 = (bf16[128,1024]{1,0:T(8,128)(2,1)S(1)}, bf16[128,1024]{1,0:T(8,128)(2,1)S(1)}, u32[]{:S(2)}, u32[]{:S(2)}) collective-permute-start(bf16[128,1024]{1,0:T(8,128)(2,1)S(1)} %pad_maximum_fusion.2), channel_id=1, source_target_pairs={{0,192},{32,224},{64,128},{96,160},{128,64},{160,96},{192,0},{224,... | collective-permute-start | bytes 786440 | tf_op jit(solution)/shard_map/ppermute | solution.py:99
  100.4 9.3 %collective-permute-start.23 = (bf16[128,1024]{1,0:T(8,128)(2,1)S(1)}, bf16[128,1024]{1,0:T(8,128)(2,1)S(1)}, u32[]{:S(2)}, u32[]{:S(2)}) collective-permute-start(bf16[128,1024]{1,0:T(8,128)(2,1)S(1)} %pad_maximum_fusion.2), channel_id=1, source_target_pairs={{0,64},{32,96},{64,0},{96,32},{128,192},{160,224},{192,128},{224,1... | collective-permute-start | bytes 786440 | tf_op jit(solution)/shard_map/ppermute | solution.py:99
  111.4 4.2 %collective-permute-start.24 = (bf16[128,64]{1,0:T(8,128)(2,1)S(1)}, bf16[128,64]{1,0:T(8,128)(2,1)S(1)}, u32[]{:S(2)}, u32[]{:S(2)}) collective-permute-start(bf16[128,64]{1,0:T(8,128)(2,1)S(1)} %get-tuple-element.56), channel_id=1, source_target_pairs={{0,1},{1,0},{2,3},{3,2},{4,5},{5,4},{6,7},{7,6},{8,9},{9,8},{10,11... | collective-permute-start | bytes 49160 | tf_op jit(solution)/shard_map/ppermute | solution.py:99
  114.8 4.8 %collective-permute-start.25 = (bf16[128,64]{1,0:T(8,128)(2,1)S(1)}, bf16[128,64]{1,0:T(8,128)(2,1)S(1)}, u32[]{:S(2)}, u32[]{:S(2)}) collective-permute-start(bf16[128,64]{1,0:T(8,128)(2,1)S(1)} %get-tuple-element.57), channel_id=1, source_target_pairs={{0,31},{1,2},{2,1},{3,4},{4,3},{5,6},{6,5},{7,8},{8,7},{9,10},{10,... | collective-permute-start | bytes 49160 | tf_op jit(solution)/shard_map/ppermute | solution.py:99
  121.3 4.9 %collective-permute-start.26 = (bf16[128,64]{1,0:T(8,128)(2,1)S(1)}, bf16[128,64]{1,0:T(8,128)(2,1)S(1)}, u32[]{:S(2)}, u32[]{:S(2)}) collective-permute-start(bf16[128,64]{1,0:T(8,128)(2,1)S(1)} %get-tuple-element.48), channel_id=1, source_target_pairs={{0,1},{1,0},{2,3},{3,2},{4,5},{5,4},{6,7},{7,6},{8,9},{9,8},{10,11... | collective-permute-start | bytes 49160 | tf_op jit(solution)/shard_map/ppermute | solution.py:99
  125.3 4.8 %collective-permute-start.27 = (bf16[128,64]{1,0:T(8,128)(2,1)S(1)}, bf16[128,64]{1,0:T(8,128)(2,1)S(1)}, u32[]{:S(2)}, u32[]{:S(2)}) collective-permute-start(bf16[128,64]{1,0:T(8,128)(2,1)S(1)} %get-tuple-element.49), channel_id=1, source_target_pairs={{0,31},{1,2},{2,1},{3,4},{4,3},{5,6},{6,5},{7,8},{8,7},{9,10},{10,... | collective-permute-start | bytes 49160 | tf_op jit(solution)/shard_map/ppermute | solution.py:99
  131.7 3.4 %collective-permute-start.28 = (bf16[128,64]{1,0:T(8,128)(2,1)S(1)}, bf16[128,64]{1,0:T(8,128)(2,1)S(1)}, u32[]{:S(2)}, u32[]{:S(2)}) collective-permute-start(bf16[128,64]{1,0:T(8,128)(2,1)S(1)} %get-tuple-element.40), channel_id=1, source_target_pairs={{0,1},{1,0},{2,3},{3,2},{4,5},{5,4},{6,7},{7,6},{8,9},{9,8},{10,11... | collective-permute-start | bytes 49160 | tf_op jit(solution)/shard_map/ppermute | solution.py:99
  134.2 4.8 %collective-permute-start.29 = (bf16[128,64]{1,0:T(8,128)(2,1)S(1)}, bf16[128,64]{1,0:T(8,128)(2,1)S(1)}, u32[]{:S(2)}, u32[]{:S(2)}) collective-permute-start(bf16[128,64]{1,0:T(8,128)(2,1)S(1)} %get-tuple-element.41), channel_id=1, source_target_pairs={{0,31},{1,2},{2,1},{3,4},{4,3},{5,6},{6,5},{7,8},{8,7},{9,10},{10,... | collective-permute-start | bytes 49160 | tf_op jit(solution)/shard_map/ppermute | solution.py:99
  140.7 3.2 %collective-permute-start.30 = (bf16[128,64]{1,0:T(8,128)(2,1)S(1)}, bf16[128,64]{1,0:T(8,128)(2,1)S(1)}, u32[]{:S(2)}, u32[]{:S(2)}) collective-permute-start(bf16[128,64]{1,0:T(8,128)(2,1)S(1)} %get-tuple-element.32), channel_id=1, source_target_pairs={{0,1},{1,0},{2,3},{3,2},{4,5},{5,4},{6,7},{7,6},{8,9},{9,8},{10,11... | collective-permute-start | bytes 49160 | tf_op jit(solution)/shard_map/ppermute | solution.py:99
  143.0 4.8 %collective-permute-start.31 = (bf16[128,64]{1,0:T(8,128)(2,1)S(1)}, bf16[128,64]{1,0:T(8,128)(2,1)S(1)}, u32[]{:S(2)}, u32[]{:S(2)}) collective-permute-start(bf16[128,64]{1,0:T(8,128)(2,1)S(1)} %get-tuple-element.33), channel_id=1, source_target_pairs={{0,31},{1,2},{2,1},{3,4},{4,3},{5,6},{6,5},{7,8},{8,7},{9,10},{10,... | collective-permute-start | bytes 49160 | tf_op jit(solution)/shard_map/ppermute | solution.py:99
  151.7 4.8 %collective-permute-start.33 = (bf16[128,64]{1,0:T(8,128)(2,1)S(1)}, bf16[128,64]{1,0:T(8,128)(2,1)S(1)}, u32[]{:S(2)}, u32[]{:S(2)}) collective-permute-start(bf16[128,64]{1,0:T(8,128)(2,1)S(1)} %get-tuple-element.25), channel_id=1, source_target_pairs={{0,31},{1,2},{2,1},{3,4},{4,3},{5,6},{6,5},{7,8},{8,7},{9,10},{10,... | collective-permute-start | bytes 49160 | tf_op jit(solution)/shard_map/ppermute | solution.py:99
  160.5 4.8 %collective-permute-start.35 = (bf16[128,64]{1,0:T(8,128)(2,1)S(1)}, bf16[128,64]{1,0:T(8,128)(2,1)S(1)}, u32[]{:S(2)}, u32[]{:S(2)}) collective-permute-start(bf16[128,64]{1,0:T(8,128)(2,1)S(1)} %get-tuple-element.17), channel_id=1, source_target_pairs={{0,31},{1,2},{2,1},{3,4},{4,3},{5,6},{6,5},{7,8},{8,7},{9,10},{10,... | collective-permute-start | bytes 49160 | tf_op jit(solution)/shard_map/ppermute | solution.py:99
  (12 other events, 38.5 us)

commit v8 on v5

--- a/solution.py
+++ b/solution.py
@@ -151,7 +151,10 @@
         fixed_part = start + time_step * running_sum - own_scale * slopes
         iterate = start + time_step * running_sum
         for inner_step in range(INNER - 1):
-            iterate = fixed_part + own_scale * apply_operator(iterate, reaction, weights, x_lift, ny, nz)
+            own, rounded = local_terms(iterate, reaction, weights, ny, nz)
+            base = fixed_part + own_scale * own
+            faces = exchange_faces(rounded)
+            iterate = base + own_scale * jnp.dot(faces, x_lift, preferred_element_type=jnp.float32)
         states = iterate
     return states.reshape(shape)
 

time: 167 us -> 167 us (level)
  matrix products: 18.9 us -> 26.3 us
  waiting for transfers between devices: 65 us -> 57.7 us
    dot_general x14 -> x2, matrix products: 11.4 us -> 0.47 us  [apply_operator(): return own + jnp.dot(faces, x_lift, preferred_element_type=jnp.float32)]
    dot_general x0 -> x12, matrix products: none -> 10.9 us  [local(): jnp.dot(faces, x_lift, preferred_element_type=jnp.float32)]
    dot_general x14, matrix products: 3.82 us -> 11.3 us  [local_terms(): jnp.dot(inputs, stacked, preferred_element_type=jnp.float32)]
    ppermute x42, waiting for transfers between devices: 65 us -> 57.7 us  [swapped(): lax.ppermute(array, axis, [(i, partner(i) % devices) for i in range(devic...]
  transfers between devices with their start and end apart: 42 -> 42, of which waited for: 31 -> 19; matrix products, arithmetic and copies ran while one was open for 6% -> 10% of each run, Pallas kernels for 0% -> 0%
where the time goes in v8:
time: 167 us; the launch traced here: 165 us
  starting transfers between devices  64.4 us (39%)
  waiting for transfers between devices  57.7 us (35%)
  matrix products  26.3 us (16%)
  local copies, waits for them, and re-layouts  8.6 us (5%)
  other arithmetic  5.91 us (4%)
  between operations  2.2 us (1%)
    ppermute x42, starting transfers between devices, swapped(): lax.ppermute(array, axis, [(i, partner(i) % devices) for i in range(devic...  64.4 us
    ppermute x42, waiting for transfers between devices, swapped(): lax.ppermute(array, axis, [(i, partner(i) % devices) for i in range(devic...  57.7 us
    dot_general x14, matrix products, local_terms(): jnp.dot(inputs, stacked, preferred_element_type=jnp.float32)  11.3 us
    dot_general x12, matrix products, local(): jnp.dot(faces, x_lift, preferred_element_type=jnp.float32)  10.9 us
    dot_general x14, matrix products, local_terms(): jnp.dot(rounded, select, preferred_element_type=jnp.float32)  3.65 us
  transfers between devices with their start and end apart: 42, of which 19 were waited for; matrix products, arithmetic and copies ran while one was open for 10% of the time, Pallas kernels for 0%

profile of v8, /device:TPU:1, one launch (start us, length us, event | category | flops | bytes accessed | tf_op | source)
XLA Modules:
  0.0 165.2 jit_solution(14129819929222210412)
XLA Ops:
  1.1 3.3 %collective-permute-start = (bf16[128,64]{1,0:T(8,128)(2,1)S(1)}, bf16[128,64]{1,0:T(8,128)(2,1)S(1)}, u32[]{:S(2)}, u32[]{:S(2)}) collective-permute-start(bf16[128,64]{1,0:T(8,128)(2,1)S(1)} %get-tuple-element.120), channel_id=1, source_target_pairs={{0,1},{1,0},{2,3},{3,2},{4,5},{5,4},{6,7},{7,6},{8,9},{9,8},{10,11... | collective-permute-start | bytes 49160 | tf_op jit(solution)/shard_map/ppermute | solution.py:99
  10.6 3.0 %collective-permute-start.2 = (bf16[128,512]{1,0:T(8,128)(2,1)S(1)}, bf16[128,512]{1,0:T(8,128)(2,1)S(1)}, u32[]{:S(2)}, u32[]{:S(2)}) collective-permute-start(bf16[128,512]{1,0:T(8,128)(2,1)S(1)} %get-tuple-element.9), channel_id=1, source_target_pairs={{0,160},{32,128},{64,224},{96,192},{128,32},{160,0},{192,96},{224,... | collective-permute-start | bytes 393224 | tf_op jit(solution)/shard_map/ppermute | solution.py:99
  13.7 2.1 %collective-permute-start.4 = (bf16[128,512]{1,0:T(8,128)(2,1)S(1)}, bf16[128,512]{1,0:T(8,128)(2,1)S(1)}, u32[]{:S(2)}, u32[]{:S(2)}) collective-permute-start(bf16[128,512]{1,0:T(8,128)(2,1)S(1)} %get-tuple-element.9), channel_id=1, source_target_pairs={{0,96},{32,64},{64,32},{96,0},{128,224},{160,192},{192,160},{224,1... | collective-permute-start | bytes 393224 | tf_op jit(solution)/shard_map/ppermute | solution.py:99
  22.1 4.0 %collective-permute-done.7 = bf16[128,512]{1,0:T(8,128)(2,1)S(1)} collective-permute-done((bf16[128,512]{1,0:T(8,128)(2,1)S(1)}, bf16[128,512]{1,0:T(8,128)(2,1)S(1)}, u32[]{:S(2)}, u32[]{:S(2)}) %collective-permute-start.7) | collective-permute-done | bytes 131104 | tf_op jit(solution)/shard_map/ppermute | solution.py:99
  28.1 6.9 %collective-permute-start.10 = (bf16[128,64]{1,0:T(8,128)(2,1)S(1)}, bf16[128,64]{1,0:T(8,128)(2,1)S(1)}, u32[]{:S(2)}, u32[]{:S(2)}) collective-permute-start(bf16[128,64]{1,0:T(8,128)(2,1)S(1)} %get-tuple-element.113), channel_id=1, source_target_pairs={{0,31},{1,2},{2,1},{3,4},{4,3},{5,6},{6,5},{7,8},{8,7},{9,10},{10,... | collective-permute-start | bytes 49160 | tf_op jit(solution)/shard_map/ppermute | solution.py:99
  34.9 4.6 %collective-permute-start.9 = (bf16[128,64]{1,0:T(8,128)(2,1)S(1)}, bf16[128,64]{1,0:T(8,128)(2,1)S(1)}, u32[]{:S(2)}, u32[]{:S(2)}) collective-permute-start(bf16[128,64]{1,0:T(8,128)(2,1)S(1)} %get-tuple-element.112), channel_id=1, source_target_pairs={{0,1},{1,0},{2,3},{3,2},{4,5},{5,4},{6,7},{7,6},{8,9},{9,8},{10,11... | collective-permute-start | bytes 49160 | tf_op jit(solution)/shard_map/ppermute | solution.py:99
  43.9 3.7 %collective-permute-done.12 = bf16[128,64]{1,0:T(8,128)(2,1)S(1)} collective-permute-done((bf16[128,64]{1,0:T(8,128)(2,1)S(1)}, bf16[128,64]{1,0:T(8,128)(2,1)S(1)}, u32[]{:S(2)}, u32[]{:S(2)}) %collective-permute-start.12) | collective-permute-done | bytes 16416 | tf_op jit(solution)/shard_map/ppermute | solution.py:99
  49.2 2.3 %collective-permute-start.13 = (bf16[128,64]{1,0:T(8,128)(2,1)S(1)}, bf16[128,64]{1,0:T(8,128)(2,1)S(1)}, u32[]{:S(2)}, u32[]{:S(2)}) collective-permute-start(bf16[128,64]{1,0:T(8,128)(2,1)S(1)} %get-tuple-element.96), channel_id=1, source_target_pairs={{0,1},{1,0},{2,3},{3,2},{4,5},{5,4},{6,7},{7,6},{8,9},{9,8},{10,11... | collective-permute-start | bytes 49160 | tf_op jit(solution)/shard_map/ppermute | solution.py:99
  52.6 3.7 %collective-permute-done.14 = bf16[128,64]{1,0:T(8,128)(2,1)S(1)} collective-permute-done((bf16[128,64]{1,0:T(8,128)(2,1)S(1)}, bf16[128,64]{1,0:T(8,128)(2,1)S(1)}, u32[]{:S(2)}, u32[]{:S(2)}) %collective-permute-start.14) | collective-permute-done | bytes 16416 | tf_op jit(solution)/shard_map/ppermute | solution.py:99
  57.9 2.5 %collective-permute-start.15 = (bf16[128,64]{1,0:T(8,128)(2,1)S(1)}, bf16[128,64]{1,0:T(8,128)(2,1)S(1)}, u32[]{:S(2)}, u32[]{:S(2)}) collective-permute-start(bf16[128,64]{1,0:T(8,128)(2,1)S(1)} %get-tuple-element.88), channel_id=1, source_target_pairs={{0,1},{1,0},{2,3},{3,2},{4,5},{5,4},{6,7},{7,6},{8,9},{9,8},{10,11... | collective-permute-start | bytes 49160 | tf_op jit(solution)/shard_map/ppermute | solution.py:99
  61.5 3.7 %collective-permute-done.16 = bf16[128,64]{1,0:T(8,128)(2,1)S(1)} collective-permute-done((bf16[128,64]{1,0:T(8,128)(2,1)S(1)}, bf16[128,64]{1,0:T(8,128)(2,1)S(1)}, u32[]{:S(2)}, u32[]{:S(2)}) %collective-permute-start.16) | collective-permute-done | bytes 16416 | tf_op jit(solution)/shard_map/ppermute | solution.py:99
  66.8 2.3 %collective-permute-start.17 = (bf16[128,64]{1,0:T(8,128)(2,1)S(1)}, bf16[128,64]{1,0:T(8,128)(2,1)S(1)}, u32[]{:S(2)}, u32[]{:S(2)}) collective-permute-start(bf16[128,64]{1,0:T(8,128)(2,1)S(1)} %get-tuple-element.80), channel_id=1, source_target_pairs={{0,1},{1,0},{2,3},{3,2},{4,5},{5,4},{6,7},{7,6},{8,9},{9,8},{10,11... | collective-permute-start | bytes 49160 | tf_op jit(solution)/shard_map/ppermute | solution.py:99
  70.2 3.7 %collective-permute-done.18 = bf16[128,64]{1,0:T(8,128)(2,1)S(1)} collective-permute-done((bf16[128,64]{1,0:T(8,128)(2,1)S(1)}, bf16[128,64]{1,0:T(8,128)(2,1)S(1)}, u32[]{:S(2)}, u32[]{:S(2)}) %collective-permute-start.18) | collective-permute-done | bytes 16416 | tf_op jit(solution)/shard_map/ppermute | solution.py:99
  75.6 2.3 %collective-permute-start.19 = (bf16[128,64]{1,0:T(8,128)(2,1)S(1)}, bf16[128,64]{1,0:T(8,128)(2,1)S(1)}, u32[]{:S(2)}, u32[]{:S(2)}) collective-permute-start(bf16[128,64]{1,0:T(8,128)(2,1)S(1)} %get-tuple-element.72), channel_id=1, source_target_pairs={{0,1},{1,0},{2,3},{3,2},{4,5},{5,4},{6,7},{7,6},{8,9},{9,8},{10,11... | collective-permute-start | bytes 49160 | tf_op jit(solution)/shard_map/ppermute | solution.py:99
  79.0 3.7 %collective-permute-done.20 = bf16[128,64]{1,0:T(8,128)(2,1)S(1)} collective-permute-done((bf16[128,64]{1,0:T(8,128)(2,1)S(1)}, bf16[128,64]{1,0:T(8,128)(2,1)S(1)}, u32[]{:S(2)}, u32[]{:S(2)}) %collective-permute-start.20) | collective-permute-done | bytes 16416 | tf_op jit(solution)/shard_map/ppermute | solution.py:99
  84.3 2.3 %collective-permute-start.21 = (bf16[128,64]{1,0:T(8,128)(2,1)S(1)}, bf16[128,64]{1,0:T(8,128)(2,1)S(1)}, u32[]{:S(2)}, u32[]{:S(2)}) collective-permute-start(bf16[128,64]{1,0:T(8,128)(2,1)S(1)} %get-tuple-element.64), channel_id=1, source_target_pairs={{0,1},{1,0},{2,3},{3,2},{4,5},{5,4},{6,7},{7,6},{8,9},{9,8},{10,11... | collective-permute-start | bytes 49160 | tf_op jit(solution)/shard_map/ppermute | solution.py:99
  87.4 4.0 %collective-permute-done.22 = bf16[128,64]{1,0:T(8,128)(2,1)S(1)} collective-permute-done((bf16[128,64]{1,0:T(8,128)(2,1)S(1)}, bf16[128,64]{1,0:T(8,128)(2,1)S(1)}, u32[]{:S(2)}, u32[]{:S(2)}) %collective-permute-start.22) | collective-permute-done | bytes 16416 | tf_op jit(solution)/shard_map/ppermute | solution.py:99
  91.7 3.4 %collective-permute-start.23 = (bf16[128,512]{1,0:T(8,128)(2,1)S(1)}, bf16[128,512]{1,0:T(8,128)(2,1)S(1)}, u32[]{:S(2)}, u32[]{:S(2)}) collective-permute-start(bf16[128,512]{1,0:T(8,128)(2,1)S(1)} %get-tuple-element.7), channel_id=1, source_target_pairs={{0,160},{32,128},{64,224},{96,192},{128,32},{160,0},{192,96},{224,... | collective-permute-start | bytes 393224 | tf_op jit(solution)/shard_map/ppermute | solution.py:99
  95.1 2.4 %collective-permute-start.25 = (bf16[128,512]{1,0:T(8,128)(2,1)S(1)}, bf16[128,512]{1,0:T(8,128)(2,1)S(1)}, u32[]{:S(2)}, u32[]{:S(2)}) collective-permute-start(bf16[128,512]{1,0:T(8,128)(2,1)S(1)} %get-tuple-element.7), channel_id=1, source_target_pairs={{0,96},{32,64},{64,32},{96,0},{128,224},{160,192},{192,160},{224,1... | collective-permute-start | bytes 393224 | tf_op jit(solution)/shard_map/ppermute | solution.py:99
  105.6 3.1 %collective-permute-done.27 = bf16[128,512]{1,0:T(8,128)(2,1)S(1)} collective-permute-done((bf16[128,512]{1,0:T(8,128)(2,1)S(1)}, bf16[128,512]{1,0:T(8,128)(2,1)S(1)}, u32[]{:S(2)}, u32[]{:S(2)}) %collective-permute-start.27) | collective-permute-done | bytes 131104 | tf_op jit(solution)/shard_map/ppermute | solution.py:99
  110.8 4.3 %collective-permute-start.30 = (bf16[128,64]{1,0:T(8,128)(2,1)S(1)}, bf16[128,64]{1,0:T(8,128)(2,1)S(1)}, u32[]{:S(2)}, u32[]{:S(2)}) collective-permute-start(bf16[128,64]{1,0:T(8,128)(2,1)S(1)} %get-tuple-element.56), channel_id=1, source_target_pairs={{0,1},{1,0},{2,3},{3,2},{4,5},{5,4},{6,7},{7,6},{8,9},{9,8},{10,11... | collective-permute-start | bytes 49160 | tf_op jit(solution)/shard_map/ppermute | solution.py:99
  116.3 3.7 %collective-permute-done.31 = bf16[128,64]{1,0:T(8,128)(2,1)S(1)} collective-permute-done((bf16[128,64]{1,0:T(8,128)(2,1)S(1)}, bf16[128,64]{1,0:T(8,128)(2,1)S(1)}, u32[]{:S(2)}, u32[]{:S(2)}) %collective-permute-start.31) | collective-permute-done | bytes 16416 | tf_op jit(solution)/shard_map/ppermute | solution.py:99
  121.6 2.3 %collective-permute-start.32 = (bf16[128,64]{1,0:T(8,128)(2,1)S(1)}, bf16[128,64]{1,0:T(8,128)(2,1)S(1)}, u32[]{:S(2)}, u32[]{:S(2)}) collective-permute-start(bf16[128,64]{1,0:T(8,128)(2,1)S(1)} %get-tuple-element.48), channel_id=1, source_target_pairs={{0,1},{1,0},{2,3},{3,2},{4,5},{5,4},{6,7},{7,6},{8,9},{9,8},{10,11... | collective-permute-start | bytes 49160 | tf_op jit(solution)/shard_map/ppermute | solution.py:99
  125.0 3.7 %collective-permute-done.33 = bf16[128,64]{1,0:T(8,128)(2,1)S(1)} collective-permute-done((bf16[128,64]{1,0:T(8,128)(2,1)S(1)}, bf16[128,64]{1,0:T(8,128)(2,1)S(1)}, u32[]{:S(2)}, u32[]{:S(2)}) %collective-permute-start.33) | collective-permute-done | bytes 16416 | tf_op jit(solution)/shard_map/ppermute | solution.py:99
  130.3 2.3 %collective-permute-start.34 = (bf16[128,64]{1,0:T(8,128)(2,1)S(1)}, bf16[128,64]{1,0:T(8,128)(2,1)S(1)}, u32[]{:S(2)}, u32[]{:S(2)}) collective-permute-start(bf16[128,64]{1,0:T(8,128)(2,1)S(1)} %get-tuple-element.40), channel_id=1, source_target_pairs={{0,1},{1,0},{2,3},{3,2},{4,5},{5,4},{6,7},{7,6},{8,9},{9,8},{10,11... | collective-permute-start | bytes 49160 | tf_op jit(solution)/shard_map/ppermute | solution.py:99
  133.7 3.7 %collective-permute-done.35 = bf16[128,64]{1,0:T(8,128)(2,1)S(1)} collective-permute-done((bf16[128,64]{1,0:T(8,128)(2,1)S(1)}, bf16[128,64]{1,0:T(8,128)(2,1)S(1)}, u32[]{:S(2)}, u32[]{:S(2)}) %collective-permute-start.35) | collective-permute-done | bytes 16416 | tf_op jit(solution)/shard_map/ppermute | solution.py:99
  139.0 2.3 %collective-permute-start.36 = (bf16[128,64]{1,0:T(8,128)(2,1)S(1)}, bf16[128,64]{1,0:T(8,128)(2,1)S(1)}, u32[]{:S(2)}, u32[]{:S(2)}) collective-permute-start(bf16[128,64]{1,0:T(8,128)(2,1)S(1)} %get-tuple-element.32), channel_id=1, source_target_pairs={{0,1},{1,0},{2,3},{3,2},{4,5},{5,4},{6,7},{7,6},{8,9},{9,8},{10,11... | collective-permute-start | bytes 49160 | tf_op jit(solution)/shard_map/ppermute | solution.py:99
  142.4 3.7 %collective-permute-done.37 = bf16[128,64]{1,0:T(8,128)(2,1)S(1)} collective-permute-done((bf16[128,64]{1,0:T(8,128)(2,1)S(1)}, bf16[128,64]{1,0:T(8,128)(2,1)S(1)}, u32[]{:S(2)}, u32[]{:S(2)}) %collective-permute-start.37) | collective-permute-done | bytes 16416 | tf_op jit(solution)/shard_map/ppermute | solution.py:99
  147.7 2.3 %collective-permute-start.38 = (bf16[128,64]{1,0:T(8,128)(2,1)S(1)}, bf16[128,64]{1,0:T(8,128)(2,1)S(1)}, u32[]{:S(2)}, u32[]{:S(2)}) collective-permute-start(bf16[128,64]{1,0:T(8,128)(2,1)S(1)} %get-tuple-element.24), channel_id=1, source_target_pairs={{0,1},{1,0},{2,3},{3,2},{4,5},{5,4},{6,7},{7,6},{8,9},{9,8},{10,11... | collective-permute-start | bytes 49160 | tf_op jit(solution)/shard_map/ppermute | solution.py:99
  151.1 3.7 %collective-permute-done.39 = bf16[128,64]{1,0:T(8,128)(2,1)S(1)} collective-permute-done((bf16[128,64]{1,0:T(8,128)(2,1)S(1)}, bf16[128,64]{1,0:T(8,128)(2,1)S(1)}, u32[]{:S(2)}, u32[]{:S(2)}) %collective-permute-start.39) | collective-permute-done | bytes 16416 | tf_op jit(solution)/shard_map/ppermute | solution.py:99
  156.5 2.3 %collective-permute-start.40 = (bf16[128,64]{1,0:T(8,128)(2,1)S(1)}, bf16[128,64]{1,0:T(8,128)(2,1)S(1)}, u32[]{:S(2)}, u32[]{:S(2)}) collective-permute-start(bf16[128,64]{1,0:T(8,128)(2,1)S(1)} %get-tuple-element.16), channel_id=1, source_target_pairs={{0,1},{1,0},{2,3},{3,2},{4,5},{5,4},{6,7},{7,6},{8,9},{9,8},{10,11... | collective-permute-start | bytes 49160 | tf_op jit(solution)/shard_map/ppermute | solution.py:99
  159.9 3.7 %collective-permute-done.41 = bf16[128,64]{1,0:T(8,128)(2,1)S(1)} collective-permute-done((bf16[128,64]{1,0:T(8,128)(2,1)S(1)}, bf16[128,64]{1,0:T(8,128)(2,1)S(1)}, u32[]{:S(2)}, u32[]{:S(2)}) %collective-permute-start.41) | collective-permute-done | bytes 16416 | tf_op jit(solution)/shard_map/ppermute | solution.py:99
  (359 shorter events, 57.5 us)
Async XLA Ops:
  1.1 9.2 %collective-permute-start = (bf16[128,64]{1,0:T(8,128)(2,1)S(1)}, bf16[128,64]{1,0:T(8,128)(2,1)S(1)}, u32[]{:S(2)}, u32[]{:S(2)}) collective-permute-start(bf16[128,64]{1,0:T(8,128)(2,1)S(1)} %get-tuple-element.120), channel_id=1, source_target_pairs={{0,1},{1,0},{2,3},{3,2},{4,5},{5,4},{6,7},{7,6},{8,9},{9,8},{10,11... | collective-permute-start | bytes 49160 | tf_op jit(solution)/shard_map/ppermute | solution.py:99
  4.4 5.9 %collective-permute-start.1 = (bf16[128,64]{1,0:T(8,128)(2,1)S(1)}, bf16[128,64]{1,0:T(8,128)(2,1)S(1)}, u32[]{:S(2)}, u32[]{:S(2)}) collective-permute-start(bf16[128,64]{1,0:T(8,128)(2,1)S(1)} %get-tuple-element.121), channel_id=1, source_target_pairs={{0,31},{1,2},{2,1},{3,4},{4,3},{5,6},{6,5},{7,8},{8,7},{9,10},{10,... | collective-permute-start | bytes 49160 | tf_op jit(solution)/shard_map/ppermute | solution.py:99
  10.6 7.6 %collective-permute-start.2 = (bf16[128,512]{1,0:T(8,128)(2,1)S(1)}, bf16[128,512]{1,0:T(8,128)(2,1)S(1)}, u32[]{:S(2)}, u32[]{:S(2)}) collective-permute-start(bf16[128,512]{1,0:T(8,128)(2,1)S(1)} %get-tuple-element.9), channel_id=1, source_target_pairs={{0,160},{32,128},{64,224},{96,192},{128,32},{160,0},{192,96},{224,... | collective-permute-start | bytes 393224 | tf_op jit(solution)/shard_map/ppermute | solution.py:99
  13.6 6.1 %collective-permute-start.3 = (bf16[128,512]{1,0:T(8,128)(2,1)S(1)}, bf16[128,512]{1,0:T(8,128)(2,1)S(1)}, u32[]{:S(2)}, u32[]{:S(2)}) collective-permute-start(bf16[128,512]{1,0:T(8,128)(2,1)S(1)} %get-tuple-element.9), channel_id=1, source_target_pairs={{0,128},{32,160},{64,192},{96,224},{128,0},{160,32},{192,64},{224,... | collective-permute-start | bytes 393224 | tf_op jit(solution)/shard_map/ppermute | solution.py:99
  13.7 6.4 %collective-permute-start.4 = (bf16[128,512]{1,0:T(8,128)(2,1)S(1)}, bf16[128,512]{1,0:T(8,128)(2,1)S(1)}, u32[]{:S(2)}, u32[]{:S(2)}) collective-permute-start(bf16[128,512]{1,0:T(8,128)(2,1)S(1)} %get-tuple-element.9), channel_id=1, source_target_pairs={{0,96},{32,64},{64,32},{96,0},{128,224},{160,192},{192,160},{224,1... | collective-permute-start | bytes 393224 | tf_op jit(solution)/shard_map/ppermute | solution.py:99
  15.9 6.2 %collective-permute-start.5 = (bf16[128,512]{1,0:T(8,128)(2,1)S(1)}, bf16[128,512]{1,0:T(8,128)(2,1)S(1)}, u32[]{:S(2)}, u32[]{:S(2)}) collective-permute-start(bf16[128,512]{1,0:T(8,128)(2,1)S(1)} %get-tuple-element.9), channel_id=1, source_target_pairs={{0,224},{32,192},{64,160},{96,128},{128,96},{160,64},{192,32},{224... | collective-permute-start | bytes 393224 | tf_op jit(solution)/shard_map/ppermute | solution.py:99
  17.8 4.3 %collective-permute-start.6 = (bf16[128,512]{1,0:T(8,128)(2,1)S(1)}, bf16[128,512]{1,0:T(8,128)(2,1)S(1)}, u32[]{:S(2)}, u32[]{:S(2)}) collective-permute-start(bf16[128,512]{1,0:T(8,128)(2,1)S(1)} %get-tuple-element.9), channel_id=1, source_target_pairs={{0,64},{32,96},{64,0},{96,32},{128,192},{160,224},{192,128},{224,1... | collective-permute-start | bytes 393224 | tf_op jit(solution)/shard_map/ppermute | solution.py:99
  18.2 8.0 %collective-permute-start.7 = (bf16[128,512]{1,0:T(8,128)(2,1)S(1)}, bf16[128,512]{1,0:T(8,128)(2,1)S(1)}, u32[]{:S(2)}, u32[]{:S(2)}) collective-permute-start(bf16[128,512]{1,0:T(8,128)(2,1)S(1)} %get-tuple-element.9), channel_id=1, source_target_pairs={{0,192},{32,224},{64,128},{96,160},{128,64},{160,96},{192,0},{224,... | collective-permute-start | bytes 393224 | tf_op jit(solution)/shard_map/ppermute | solution.py:99
  19.8 6.4 %collective-permute-start.8 = (bf16[128,512]{1,0:T(8,128)(2,1)S(1)}, bf16[128,512]{1,0:T(8,128)(2,1)S(1)}, u32[]{:S(2)}, u32[]{:S(2)}) collective-permute-start(bf16[128,512]{1,0:T(8,128)(2,1)S(1)} %get-tuple-element.9), channel_id=1, source_target_pairs={{0,32},{32,0},{64,96},{96,64},{128,160},{160,128},{192,224},{224,1... | collective-permute-start | bytes 393224 | tf_op jit(solution)/shard_map/ppermute | solution.py:99
  28.1 12.5 %collective-permute-start.10 = (bf16[128,64]{1,0:T(8,128)(2,1)S(1)}, bf16[128,64]{1,0:T(8,128)(2,1)S(1)}, u32[]{:S(2)}, u32[]{:S(2)}) collective-permute-start(bf16[128,64]{1,0:T(8,128)(2,1)S(1)} %get-tuple-element.113), channel_id=1, source_target_pairs={{0,31},{1,2},{2,1},{3,4},{4,3},{5,6},{6,5},{7,8},{8,7},{9,10},{10,... | collective-permute-start | bytes 49160 | tf_op jit(solution)/shard_map/ppermute | solution.py:99
  34.9 5.7 %collective-permute-start.9 = (bf16[128,64]{1,0:T(8,128)(2,1)S(1)}, bf16[128,64]{1,0:T(8,128)(2,1)S(1)}, u32[]{:S(2)}, u32[]{:S(2)}) collective-permute-start(bf16[128,64]{1,0:T(8,128)(2,1)S(1)} %get-tuple-element.112), channel_id=1, source_target_pairs={{0,1},{1,0},{2,3},{3,2},{4,5},{5,4},{6,7},{7,6},{8,9},{9,8},{10,11... | collective-permute-start | bytes 49160 | tf_op jit(solution)/shard_map/ppermute | solution.py:99
  42.8 4.8 %collective-permute-start.12 = (bf16[128,64]{1,0:T(8,128)(2,1)S(1)}, bf16[128,64]{1,0:T(8,128)(2,1)S(1)}, u32[]{:S(2)}, u32[]{:S(2)}) collective-permute-start(bf16[128,64]{1,0:T(8,128)(2,1)S(1)} %get-tuple-element.105), channel_id=1, source_target_pairs={{0,31},{1,2},{2,1},{3,4},{4,3},{5,6},{6,5},{7,8},{8,7},{9,10},{10,... | collective-permute-start | bytes 49160 | tf_op jit(solution)/shard_map/ppermute | solution.py:99
  51.5 4.8 %collective-permute-start.14 = (bf16[128,64]{1,0:T(8,128)(2,1)S(1)}, bf16[128,64]{1,0:T(8,128)(2,1)S(1)}, u32[]{:S(2)}, u32[]{:S(2)}) collective-permute-start(bf16[128,64]{1,0:T(8,128)(2,1)S(1)} %get-tuple-element.97), channel_id=1, source_target_pairs={{0,31},{1,2},{2,1},{3,4},{4,3},{5,6},{6,5},{7,8},{8,7},{9,10},{10,... | collective-permute-start | bytes 49160 | tf_op jit(solution)/shard_map/ppermute | solution.py:99
  57.9 3.6 %collective-permute-start.15 = (bf16[128,64]{1,0:T(8,128)(2,1)S(1)}, bf16[128,64]{1,0:T(8,128)(2,1)S(1)}, u32[]{:S(2)}, u32[]{:S(2)}) collective-permute-start(bf16[128,64]{1,0:T(8,128)(2,1)S(1)} %get-tuple-element.88), channel_id=1, source_target_pairs={{0,1},{1,0},{2,3},{3,2},{4,5},{5,4},{6,7},{7,6},{8,9},{9,8},{10,11... | collective-permute-start | bytes 49160 | tf_op jit(solution)/shard_map/ppermute | solution.py:99
  60.4 4.8 %collective-permute-start.16 = (bf16[128,64]{1,0:T(8,128)(2,1)S(1)}, bf16[128,64]{1,0:T(8,128)(2,1)S(1)}, u32[]{:S(2)}, u32[]{:S(2)}) collective-permute-start(bf16[128,64]{1,0:T(8,128)(2,1)S(1)} %get-tuple-element.89), channel_id=1, source_target_pairs={{0,31},{1,2},{2,1},{3,4},{4,3},{5,6},{6,5},{7,8},{8,7},{9,10},{10,... | collective-permute-start | bytes 49160 | tf_op jit(solution)/shard_map/ppermute | solution.py:99
  69.1 4.8 %collective-permute-start.18 = (bf16[128,64]{1,0:T(8,128)(2,1)S(1)}, bf16[128,64]{1,0:T(8,128)(2,1)S(1)}, u32[]{:S(2)}, u32[]{:S(2)}) collective-permute-start(bf16[128,64]{1,0:T(8,128)(2,1)S(1)} %get-tuple-element.81), channel_id=1, source_target_pairs={{0,31},{1,2},{2,1},{3,4},{4,3},{5,6},{6,5},{7,8},{8,7},{9,10},{10,... | collective-permute-start | bytes 49160 | tf_op jit(solution)/shard_map/ppermute | solution.py:99
  77.9 4.8 %collective-permute-start.20 = (bf16[128,64]{1,0:T(8,128)(2,1)S(1)}, bf16[128,64]{1,0:T(8,128)(2,1)S(1)}, u32[]{:S(2)}, u32[]{:S(2)}) collective-permute-start(bf16[128,64]{1,0:T(8,128)(2,1)S(1)} %get-tuple-element.73), channel_id=1, source_target_pairs={{0,31},{1,2},{2,1},{3,4},{4,3},{5,6},{6,5},{7,8},{8,7},{9,10},{10,... | collective-permute-start | bytes 49160 | tf_op jit(solution)/shard_map/ppermute | solution.py:99
  86.6 4.8 %collective-permute-start.22 = (bf16[128,64]{1,0:T(8,128)(2,1)S(1)}, bf16[128,64]{1,0:T(8,128)(2,1)S(1)}, u32[]{:S(2)}, u32[]{:S(2)}) collective-permute-start(bf16[128,64]{1,0:T(8,128)(2,1)S(1)} %get-tuple-element.65), channel_id=1, source_target_pairs={{0,31},{1,2},{2,1},{3,4},{4,3},{5,6},{6,5},{7,8},{8,7},{9,10},{10,... | collective-permute-start | bytes 49160 | tf_op jit(solution)/shard_map/ppermute | solution.py:99
  91.7 9.0 %collective-permute-start.23 = (bf16[128,512]{1,0:T(8,128)(2,1)S(1)}, bf16[128,512]{1,0:T(8,128)(2,1)S(1)}, u32[]{:S(2)}, u32[]{:S(2)}) collective-permute-start(bf16[128,512]{1,0:T(8,128)(2,1)S(1)} %get-tuple-element.7), channel_id=1, source_target_pairs={{0,160},{32,128},{64,224},{96,192},{128,32},{160,0},{192,96},{224,... | collective-permute-start | bytes 393224 | tf_op jit(solution)/shard_map/ppermute | solution.py:99
  95.1 6.7 %collective-permute-start.24 = (bf16[128,512]{1,0:T(8,128)(2,1)S(1)}, bf16[128,512]{1,0:T(8,128)(2,1)S(1)}, u32[]{:S(2)}, u32[]{:S(2)}) collective-permute-start(bf16[128,512]{1,0:T(8,128)(2,1)S(1)} %get-tuple-element.7), channel_id=1, source_target_pairs={{0,128},{32,160},{64,192},{96,224},{128,0},{160,32},{192,64},{224,... | collective-permute-start | bytes 393224 | tf_op jit(solution)/shard_map/ppermute | solution.py:99
  95.1 8.4 %collective-permute-start.25 = (bf16[128,512]{1,0:T(8,128)(2,1)S(1)}, bf16[128,512]{1,0:T(8,128)(2,1)S(1)}, u32[]{:S(2)}, u32[]{:S(2)}) collective-permute-start(bf16[128,512]{1,0:T(8,128)(2,1)S(1)} %get-tuple-element.7), channel_id=1, source_target_pairs={{0,96},{32,64},{64,32},{96,0},{128,224},{160,192},{192,160},{224,1... | collective-permute-start | bytes 393224 | tf_op jit(solution)/shard_map/ppermute | solution.py:99
  97.5 8.1 %collective-permute-start.26 = (bf16[128,512]{1,0:T(8,128)(2,1)S(1)}, bf16[128,512]{1,0:T(8,128)(2,1)S(1)}, u32[]{:S(2)}, u32[]{:S(2)}) collective-permute-start(bf16[128,512]{1,0:T(8,128)(2,1)S(1)} %get-tuple-element.7), channel_id=1, source_target_pairs={{0,224},{32,192},{64,160},{96,128},{128,96},{160,64},{192,32},{224... | collective-permute-start | bytes 393224 | tf_op jit(solution)/shard_map/ppermute | solution.py:99
  99.2 9.5 %collective-permute-start.27 = (bf16[128,512]{1,0:T(8,128)(2,1)S(1)}, bf16[128,512]{1,0:T(8,128)(2,1)S(1)}, u32[]{:S(2)}, u32[]{:S(2)}) collective-permute-start(bf16[128,512]{1,0:T(8,128)(2,1)S(1)} %get-tuple-element.7), channel_id=1, source_target_pairs={{0,64},{32,96},{64,0},{96,32},{128,192},{160,224},{192,128},{224,1... | collective-permute-start | bytes 393224 | tf_op jit(solution)/shard_map/ppermute | solution.py:99
  100.7 8.4 %collective-permute-start.28 = (bf16[128,512]{1,0:T(8,128)(2,1)S(1)}, bf16[128,512]{1,0:T(8,128)(2,1)S(1)}, u32[]{:S(2)}, u32[]{:S(2)}) collective-permute-start(bf16[128,512]{1,0:T(8,128)(2,1)S(1)} %get-tuple-element.7), channel_id=1, source_target_pairs={{0,192},{32,224},{64,128},{96,160},{128,64},{160,96},{192,0},{224,... | collective-permute-start | bytes 393224 | tf_op jit(solution)/shard_map/ppermute | solution.py:99
  101.8 7.3 %collective-permute-start.29 = (bf16[128,512]{1,0:T(8,128)(2,1)S(1)}, bf16[128,512]{1,0:T(8,128)(2,1)S(1)}, u32[]{:S(2)}, u32[]{:S(2)}) collective-permute-start(bf16[128,512]{1,0:T(8,128)(2,1)S(1)} %get-tuple-element.7), channel_id=1, source_target_pairs={{0,32},{32,0},{64,96},{96,64},{128,160},{160,128},{192,224},{224,1... | collective-permute-start | bytes 393224 | tf_op jit(solution)/shard_map/ppermute | solution.py:99
  110.8 5.4 %collective-permute-start.30 = (bf16[128,64]{1,0:T(8,128)(2,1)S(1)}, bf16[128,64]{1,0:T(8,128)(2,1)S(1)}, u32[]{:S(2)}, u32[]{:S(2)}) collective-permute-start(bf16[128,64]{1,0:T(8,128)(2,1)S(1)} %get-tuple-element.56), channel_id=1, source_target_pairs={{0,1},{1,0},{2,3},{3,2},{4,5},{5,4},{6,7},{7,6},{8,9},{9,8},{10,11... | collective-permute-start | bytes 49160 | tf_op jit(solution)/shard_map/ppermute | solution.py:99
  115.1 4.8 %collective-permute-start.31 = (bf16[128,64]{1,0:T(8,128)(2,1)S(1)}, bf16[128,64]{1,0:T(8,128)(2,1)S(1)}, u32[]{:S(2)}, u32[]{:S(2)}) collective-permute-start(bf16[128,64]{1,0:T(8,128)(2,1)S(1)} %get-tuple-element.57), channel_id=1, source_target_pairs={{0,31},{1,2},{2,1},{3,4},{4,3},{5,6},{6,5},{7,8},{8,7},{9,10},{10,... | collective-permute-start | bytes 49160 | tf_op jit(solution)/shard_map/ppermute | solution.py:99
  123.9 4.8 %collective-permute-start.33 = (bf16[128,64]{1,0:T(8,128)(2,1)S(1)}, bf16[128,64]{1,0:T(8,128)(2,1)S(1)}, u32[]{:S(2)}, u32[]{:S(2)}) collective-permute-start(bf16[128,64]{1,0:T(8,128)(2,1)S(1)} %get-tuple-element.49), channel_id=1, source_target_pairs={{0,31},{1,2},{2,1},{3,4},{4,3},{5,6},{6,5},{7,8},{8,7},{9,10},{10,... | collective-permute-start | bytes 49160 | tf_op jit(solution)/shard_map/ppermute | solution.py:99
  132.6 4.8 %collective-permute-start.35 = (bf16[128,64]{1,0:T(8,128)(2,1)S(1)}, bf16[128,64]{1,0:T(8,128)(2,1)S(1)}, u32[]{:S(2)}, u32[]{:S(2)}) collective-permute-start(bf16[128,64]{1,0:T(8,128)(2,1)S(1)} %get-tuple-element.41), channel_id=1, source_target_pairs={{0,31},{1,2},{2,1},{3,4},{4,3},{5,6},{6,5},{7,8},{8,7},{9,10},{10,... | collective-permute-start | bytes 49160 | tf_op jit(solution)/shard_map/ppermute | solution.py:99
  141.3 4.8 %collective-permute-start.37 = (bf16[128,64]{1,0:T(8,128)(2,1)S(1)}, bf16[128,64]{1,0:T(8,128)(2,1)S(1)}, u32[]{:S(2)}, u32[]{:S(2)}) collective-permute-start(bf16[128,64]{1,0:T(8,128)(2,1)S(1)} %get-tuple-element.33), channel_id=1, source_target_pairs={{0,31},{1,2},{2,1},{3,4},{4,3},{5,6},{6,5},{7,8},{8,7},{9,10},{10,... | collective-permute-start | bytes 49160 | tf_op jit(solution)/shard_map/ppermute | solution.py:99
  150.0 4.8 %collective-permute-start.39 = (bf16[128,64]{1,0:T(8,128)(2,1)S(1)}, bf16[128,64]{1,0:T(8,128)(2,1)S(1)}, u32[]{:S(2)}, u32[]{:S(2)}) collective-permute-start(bf16[128,64]{1,0:T(8,128)(2,1)S(1)} %get-tuple-element.25), channel_id=1, source_target_pairs={{0,31},{1,2},{2,1},{3,4},{4,3},{5,6},{6,5},{7,8},{8,7},{9,10},{10,... | collective-permute-start | bytes 49160 | tf_op jit(solution)/shard_map/ppermute | solution.py:99
  158.8 4.8 %collective-permute-start.41 = (bf16[128,64]{1,0:T(8,128)(2,1)S(1)}, bf16[128,64]{1,0:T(8,128)(2,1)S(1)}, u32[]{:S(2)}, u32[]{:S(2)}) collective-permute-start(bf16[128,64]{1,0:T(8,128)(2,1)S(1)} %get-tuple-element.17), channel_id=1, source_target_pairs={{0,31},{1,2},{2,1},{3,4},{4,3},{5,6},{6,5},{7,8},{8,7},{9,10},{10,... | collective-permute-start | bytes 49160 | tf_op jit(solution)/shard_map/ppermute | solution.py:99
  (18 other events, 53.6 us)

commit v9 on v7

--- a/solution.py
+++ b/solution.py
@@ -157,7 +157,10 @@
         fixed_part = start + time_step * running_sum - own_scale * slopes
         iterate = start + time_step * running_sum
         for inner_step in range(INNER - 1):
-            iterate = fixed_part + own_scale * apply_operator(iterate, reaction, weights, x_lift, ny, nz)
+            own, rounded = local_terms(iterate, reaction, weights, ny, nz)
+            base = fixed_part + own_scale * own
+            faces = exchange_faces(rounded)
+            iterate = base + own_scale * jnp.dot(faces, x_lift, preferred_element_type=jnp.float32)
         states = iterate
     return states.reshape(shape)
 

time: 168 us -> 168 us (level)
  waiting for transfers between devices: 78 us -> 71.1 us
  matrix products: 18.2 us -> 24.9 us
    dot_general x14 -> x2, matrix products: 10.7 us -> 0.46 us  [apply_operator(): return own + jnp.dot(faces, x_lift, preferred_element_type=jnp.float32)]
    dot_general x0 -> x12, matrix products: none -> 10.2 us  [local(): jnp.dot(faces, x_lift, preferred_element_type=jnp.float32)]
    ppermute x36, waiting for transfers between devices: 78 us -> 71.1 us  [swapped(): lax.ppermute(array, axis, [(i, partner(i) % devices) for i in range(devic...]
    dot_general x14, matrix products: 3.83 us -> 10.5 us  [local_terms(): jnp.dot(inputs, stacked, preferred_element_type=jnp.float32)]
  transfers between devices with their start and end apart: 36 -> 36, of which waited for: 32 -> 21; matrix products, arithmetic and copies ran while one was open for 5% -> 9% of each run, Pallas kernels for 0% -> 0%
where the time goes in v9:
time: 168 us; the launch traced here: 167 us
  waiting for transfers between devices  71.1 us (42%)
  starting transfers between devices  53.6 us (32%)
  matrix products  24.9 us (15%)
  local copies, waits for them, and re-layouts  9.16 us (5%)
  other arithmetic  5.77 us (3%)
  between operations  2.27 us (1%)
    ppermute x36, waiting for transfers between devices, swapped(): lax.ppermute(array, axis, [(i, partner(i) % devices) for i in range(devic...  71.1 us
    ppermute x36, starting transfers between devices, swapped(): lax.ppermute(array, axis, [(i, partner(i) % devices) for i in range(devic...  53.6 us
    dot_general x14, matrix products, local_terms(): jnp.dot(inputs, stacked, preferred_element_type=jnp.float32)  10.5 us
    dot_general x12, matrix products, local(): jnp.dot(faces, x_lift, preferred_element_type=jnp.float32)  10.2 us
    dot_general x14, matrix products, local_terms(): jnp.dot(rounded, select, preferred_element_type=jnp.float32)  3.68 us
  transfers between devices with their start and end apart: 36, of which 21 were waited for; matrix products, arithmetic and copies ran while one was open for 9% of the time, Pallas kernels for 0%

profile of v9, /device:TPU:1, one launch (start us, length us, event | category | flops | bytes accessed | tf_op | source)
XLA Modules:
  0.0 166.8 jit_solution(6042354814253658772)
XLA Ops:
  1.1 3.3 %collective-permute-start = (bf16[128,64]{1,0:T(8,128)(2,1)S(1)}, bf16[128,64]{1,0:T(8,128)(2,1)S(1)}, u32[]{:S(2)}, u32[]{:S(2)}) collective-permute-start(bf16[128,64]{1,0:T(8,128)(2,1)S(1)} %get-tuple-element.120), channel_id=1, source_target_pairs={{0,1},{1,0},{2,3},{3,2},{4,5},{5,4},{6,7},{7,6},{8,9},{9,8},{10,11... | collective-permute-start | bytes 49160 | tf_op jit(solution)/shard_map/ppermute | solution.py:99
  11.0 2.5 %collective-permute-done.2 = bf16[128,512]{1,0:T(8,128)(2,1)S(1)} collective-permute-done((bf16[128,512]{1,0:T(8,128)(2,1)S(1)}, bf16[128,512]{1,0:T(8,128)(2,1)S(1)}, u32[]{:S(2)}, u32[]{:S(2)}) %collective-permute-start.2) | collective-permute-done | bytes 131104 | tf_op jit(solution)/shard_map/ppermute | solution.py:99
  17.1 3.3 %collective-permute-done.3 = bf16[128,1024]{1,0:T(8,128)(2,1)S(1)} collective-permute-done((bf16[128,1024]{1,0:T(8,128)(2,1)S(1)}, bf16[128,1024]{1,0:T(8,128)(2,1)S(1)}, u32[]{:S(2)}, u32[]{:S(2)}) %collective-permute-start.3) | collective-permute-done | bytes 262176 | tf_op jit(solution)/shard_map/ppermute | solution.py:99
  20.4 2.7 %collective-permute-done.4 = bf16[128,1024]{1,0:T(8,128)(2,1)S(1)} collective-permute-done((bf16[128,1024]{1,0:T(8,128)(2,1)S(1)}, bf16[128,1024]{1,0:T(8,128)(2,1)S(1)}, u32[]{:S(2)}, u32[]{:S(2)}) %collective-permute-start.4) | collective-permute-done | bytes 262176 | tf_op jit(solution)/shard_map/ppermute | solution.py:99
  25.6 7.9 %collective-permute-start.6 = (bf16[128,64]{1,0:T(8,128)(2,1)S(1)}, bf16[128,64]{1,0:T(8,128)(2,1)S(1)}, u32[]{:S(2)}, u32[]{:S(2)}) collective-permute-start(bf16[128,64]{1,0:T(8,128)(2,1)S(1)} %get-tuple-element.112), channel_id=1, source_target_pairs={{0,1},{1,0},{2,3},{3,2},{4,5},{5,4},{6,7},{7,6},{8,9},{9,8},{10,11... | collective-permute-start | bytes 49160 | tf_op jit(solution)/shard_map/ppermute | solution.py:99
  40.0 3.7 %collective-permute-start.8 = (bf16[128,64]{1,0:T(8,128)(2,1)S(1)}, bf16[128,64]{1,0:T(8,128)(2,1)S(1)}, u32[]{:S(2)}, u32[]{:S(2)}) collective-permute-start(bf16[128,64]{1,0:T(8,128)(2,1)S(1)} %get-tuple-element.104), channel_id=1, source_target_pairs={{0,1},{1,0},{2,3},{3,2},{4,5},{5,4},{6,7},{7,6},{8,9},{9,8},{10,11... | collective-permute-start | bytes 49160 | tf_op jit(solution)/shard_map/ppermute | solution.py:99
  44.6 3.9 %collective-permute-done.9 = bf16[128,64]{1,0:T(8,128)(2,1)S(1)} collective-permute-done((bf16[128,64]{1,0:T(8,128)(2,1)S(1)}, bf16[128,64]{1,0:T(8,128)(2,1)S(1)}, u32[]{:S(2)}, u32[]{:S(2)}) %collective-permute-start.9) | collective-permute-done | bytes 16416 | tf_op jit(solution)/shard_map/ppermute | solution.py:99
  50.1 2.3 %collective-permute-start.10 = (bf16[128,64]{1,0:T(8,128)(2,1)S(1)}, bf16[128,64]{1,0:T(8,128)(2,1)S(1)}, u32[]{:S(2)}, u32[]{:S(2)}) collective-permute-start(bf16[128,64]{1,0:T(8,128)(2,1)S(1)} %get-tuple-element.96), channel_id=1, source_target_pairs={{0,1},{1,0},{2,3},{3,2},{4,5},{5,4},{6,7},{7,6},{8,9},{9,8},{10,11... | collective-permute-start | bytes 49160 | tf_op jit(solution)/shard_map/ppermute | solution.py:99
  53.4 3.9 %collective-permute-done.11 = bf16[128,64]{1,0:T(8,128)(2,1)S(1)} collective-permute-done((bf16[128,64]{1,0:T(8,128)(2,1)S(1)}, bf16[128,64]{1,0:T(8,128)(2,1)S(1)}, u32[]{:S(2)}, u32[]{:S(2)}) %collective-permute-start.11) | collective-permute-done | bytes 16416 | tf_op jit(solution)/shard_map/ppermute | solution.py:99
  58.8 2.3 %collective-permute-start.12 = (bf16[128,64]{1,0:T(8,128)(2,1)S(1)}, bf16[128,64]{1,0:T(8,128)(2,1)S(1)}, u32[]{:S(2)}, u32[]{:S(2)}) collective-permute-start(bf16[128,64]{1,0:T(8,128)(2,1)S(1)} %get-tuple-element.88), channel_id=1, source_target_pairs={{0,1},{1,0},{2,3},{3,2},{4,5},{5,4},{6,7},{7,6},{8,9},{9,8},{10,11... | collective-permute-start | bytes 49160 | tf_op jit(solution)/shard_map/ppermute | solution.py:99
  62.1 3.9 %collective-permute-done.13 = bf16[128,64]{1,0:T(8,128)(2,1)S(1)} collective-permute-done((bf16[128,64]{1,0:T(8,128)(2,1)S(1)}, bf16[128,64]{1,0:T(8,128)(2,1)S(1)}, u32[]{:S(2)}, u32[]{:S(2)}) %collective-permute-start.13) | collective-permute-done | bytes 16416 | tf_op jit(solution)/shard_map/ppermute | solution.py:99
  67.6 2.5 %collective-permute-start.14 = (bf16[128,64]{1,0:T(8,128)(2,1)S(1)}, bf16[128,64]{1,0:T(8,128)(2,1)S(1)}, u32[]{:S(2)}, u32[]{:S(2)}) collective-permute-start(bf16[128,64]{1,0:T(8,128)(2,1)S(1)} %get-tuple-element.80), channel_id=1, source_target_pairs={{0,1},{1,0},{2,3},{3,2},{4,5},{5,4},{6,7},{7,6},{8,9},{9,8},{10,11... | collective-permute-start | bytes 49160 | tf_op jit(solution)/shard_map/ppermute | solution.py:99
  71.0 3.9 %collective-permute-done.15 = bf16[128,64]{1,0:T(8,128)(2,1)S(1)} collective-permute-done((bf16[128,64]{1,0:T(8,128)(2,1)S(1)}, bf16[128,64]{1,0:T(8,128)(2,1)S(1)}, u32[]{:S(2)}, u32[]{:S(2)}) %collective-permute-start.15) | collective-permute-done | bytes 16416 | tf_op jit(solution)/shard_map/ppermute | solution.py:99
  76.5 2.3 %collective-permute-start.16 = (bf16[128,64]{1,0:T(8,128)(2,1)S(1)}, bf16[128,64]{1,0:T(8,128)(2,1)S(1)}, u32[]{:S(2)}, u32[]{:S(2)}) collective-permute-start(bf16[128,64]{1,0:T(8,128)(2,1)S(1)} %get-tuple-element.72), channel_id=1, source_target_pairs={{0,1},{1,0},{2,3},{3,2},{4,5},{5,4},{6,7},{7,6},{8,9},{9,8},{10,11... | collective-permute-start | bytes 49160 | tf_op jit(solution)/shard_map/ppermute | solution.py:99
  79.8 3.9 %collective-permute-done.17 = bf16[128,64]{1,0:T(8,128)(2,1)S(1)} collective-permute-done((bf16[128,64]{1,0:T(8,128)(2,1)S(1)}, bf16[128,64]{1,0:T(8,128)(2,1)S(1)}, u32[]{:S(2)}, u32[]{:S(2)}) %collective-permute-start.17) | collective-permute-done | bytes 16416 | tf_op jit(solution)/shard_map/ppermute | solution.py:99
  88.4 4.0 %collective-permute-done.19 = bf16[128,64]{1,0:T(8,128)(2,1)S(1)} collective-permute-done((bf16[128,64]{1,0:T(8,128)(2,1)S(1)}, bf16[128,64]{1,0:T(8,128)(2,1)S(1)}, u32[]{:S(2)}, u32[]{:S(2)}) %collective-permute-start.19) | collective-permute-done | bytes 16416 | tf_op jit(solution)/shard_map/ppermute | solution.py:99
  93.1 3.5 %collective-permute-done.20 = bf16[128,512]{1,0:T(8,128)(2,1)S(1)} collective-permute-done((bf16[128,512]{1,0:T(8,128)(2,1)S(1)}, bf16[128,512]{1,0:T(8,128)(2,1)S(1)}, u32[]{:S(2)}, u32[]{:S(2)}) %collective-permute-start.20) | collective-permute-done | bytes 131104 | tf_op jit(solution)/shard_map/ppermute | solution.py:99
  96.6 2.5 %collective-permute-start.21 = (bf16[128,1024]{1,0:T(8,128)(2,1)S(1)}, bf16[128,1024]{1,0:T(8,128)(2,1)S(1)}, u32[]{:S(2)}, u32[]{:S(2)}) collective-permute-start(bf16[128,1024]{1,0:T(8,128)(2,1)S(1)} %pad_maximum_fusion.2), channel_id=1, source_target_pairs={{0,128},{32,160},{64,192},{96,224},{128,0},{160,32},{192,64},{224,... | collective-permute-start | bytes 786440 | tf_op jit(solution)/shard_map/ppermute | solution.py:99
  100.4 3.1 %collective-permute-done.21 = bf16[128,1024]{1,0:T(8,128)(2,1)S(1)} collective-permute-done((bf16[128,1024]{1,0:T(8,128)(2,1)S(1)}, bf16[128,1024]{1,0:T(8,128)(2,1)S(1)}, u32[]{:S(2)}, u32[]{:S(2)}) %collective-permute-start.21) | collective-permute-done | bytes 262176 | tf_op jit(solution)/shard_map/ppermute | solution.py:99
  103.5 6.1 %collective-permute-done.22 = bf16[128,1024]{1,0:T(8,128)(2,1)S(1)} collective-permute-done((bf16[128,1024]{1,0:T(8,128)(2,1)S(1)}, bf16[128,1024]{1,0:T(8,128)(2,1)S(1)}, u32[]{:S(2)}, u32[]{:S(2)}) %collective-permute-start.22) | collective-permute-done | bytes 262176 | tf_op jit(solution)/shard_map/ppermute | solution.py:99
  111.4 3.4 %collective-permute-start.24 = (bf16[128,64]{1,0:T(8,128)(2,1)S(1)}, bf16[128,64]{1,0:T(8,128)(2,1)S(1)}, u32[]{:S(2)}, u32[]{:S(2)}) collective-permute-start(bf16[128,64]{1,0:T(8,128)(2,1)S(1)} %get-tuple-element.56), channel_id=1, source_target_pairs={{0,1},{1,0},{2,3},{3,2},{4,5},{5,4},{6,7},{7,6},{8,9},{9,8},{10,11... | collective-permute-start | bytes 49160 | tf_op jit(solution)/shard_map/ppermute | solution.py:99
  115.8 3.9 %collective-permute-done.25 = bf16[128,64]{1,0:T(8,128)(2,1)S(1)} collective-permute-done((bf16[128,64]{1,0:T(8,128)(2,1)S(1)}, bf16[128,64]{1,0:T(8,128)(2,1)S(1)}, u32[]{:S(2)}, u32[]{:S(2)}) %collective-permute-start.25) | collective-permute-done | bytes 16416 | tf_op jit(solution)/shard_map/ppermute | solution.py:99
  121.3 4.0 %collective-permute-start.26 = (bf16[128,64]{1,0:T(8,128)(2,1)S(1)}, bf16[128,64]{1,0:T(8,128)(2,1)S(1)}, u32[]{:S(2)}, u32[]{:S(2)}) collective-permute-start(bf16[128,64]{1,0:T(8,128)(2,1)S(1)} %get-tuple-element.48), channel_id=1, source_target_pairs={{0,1},{1,0},{2,3},{3,2},{4,5},{5,4},{6,7},{7,6},{8,9},{9,8},{10,11... | collective-permute-start | bytes 49160 | tf_op jit(solution)/shard_map/ppermute | solution.py:99
  126.2 3.9 %collective-permute-done.27 = bf16[128,64]{1,0:T(8,128)(2,1)S(1)} collective-permute-done((bf16[128,64]{1,0:T(8,128)(2,1)S(1)}, bf16[128,64]{1,0:T(8,128)(2,1)S(1)}, u32[]{:S(2)}, u32[]{:S(2)}) %collective-permute-start.27) | collective-permute-done | bytes 16416 | tf_op jit(solution)/shard_map/ppermute | solution.py:99
  131.7 2.5 %collective-permute-start.28 = (bf16[128,64]{1,0:T(8,128)(2,1)S(1)}, bf16[128,64]{1,0:T(8,128)(2,1)S(1)}, u32[]{:S(2)}, u32[]{:S(2)}) collective-permute-start(bf16[128,64]{1,0:T(8,128)(2,1)S(1)} %get-tuple-element.40), channel_id=1, source_target_pairs={{0,1},{1,0},{2,3},{3,2},{4,5},{5,4},{6,7},{7,6},{8,9},{9,8},{10,11... | collective-permute-start | bytes 49160 | tf_op jit(solution)/shard_map/ppermute | solution.py:99
  135.2 3.9 %collective-permute-done.29 = bf16[128,64]{1,0:T(8,128)(2,1)S(1)} collective-permute-done((bf16[128,64]{1,0:T(8,128)(2,1)S(1)}, bf16[128,64]{1,0:T(8,128)(2,1)S(1)}, u32[]{:S(2)}, u32[]{:S(2)}) %collective-permute-start.29) | collective-permute-done | bytes 16416 | tf_op jit(solution)/shard_map/ppermute | solution.py:99
  140.7 2.3 %collective-permute-start.30 = (bf16[128,64]{1,0:T(8,128)(2,1)S(1)}, bf16[128,64]{1,0:T(8,128)(2,1)S(1)}, u32[]{:S(2)}, u32[]{:S(2)}) collective-permute-start(bf16[128,64]{1,0:T(8,128)(2,1)S(1)} %get-tuple-element.32), channel_id=1, source_target_pairs={{0,1},{1,0},{2,3},{3,2},{4,5},{5,4},{6,7},{7,6},{8,9},{9,8},{10,11... | collective-permute-start | bytes 49160 | tf_op jit(solution)/shard_map/ppermute | solution.py:99
  143.9 3.9 %collective-permute-done.31 = bf16[128,64]{1,0:T(8,128)(2,1)S(1)} collective-permute-done((bf16[128,64]{1,0:T(8,128)(2,1)S(1)}, bf16[128,64]{1,0:T(8,128)(2,1)S(1)}, u32[]{:S(2)}, u32[]{:S(2)}) %collective-permute-start.31) | collective-permute-done | bytes 16416 | tf_op jit(solution)/shard_map/ppermute | solution.py:99
  149.4 2.3 %collective-permute-start.32 = (bf16[128,64]{1,0:T(8,128)(2,1)S(1)}, bf16[128,64]{1,0:T(8,128)(2,1)S(1)}, u32[]{:S(2)}, u32[]{:S(2)}) collective-permute-start(bf16[128,64]{1,0:T(8,128)(2,1)S(1)} %get-tuple-element.24), channel_id=1, source_target_pairs={{0,1},{1,0},{2,3},{3,2},{4,5},{5,4},{6,7},{7,6},{8,9},{9,8},{10,11... | collective-permute-start | bytes 49160 | tf_op jit(solution)/shard_map/ppermute | solution.py:99
  152.7 3.9 %collective-permute-done.33 = bf16[128,64]{1,0:T(8,128)(2,1)S(1)} collective-permute-done((bf16[128,64]{1,0:T(8,128)(2,1)S(1)}, bf16[128,64]{1,0:T(8,128)(2,1)S(1)}, u32[]{:S(2)}, u32[]{:S(2)}) %collective-permute-start.33) | collective-permute-done | bytes 16416 | tf_op jit(solution)/shard_map/ppermute | solution.py:99
  158.2 2.3 %collective-permute-start.34 = (bf16[128,64]{1,0:T(8,128)(2,1)S(1)}, bf16[128,64]{1,0:T(8,128)(2,1)S(1)}, u32[]{:S(2)}, u32[]{:S(2)}) collective-permute-start(bf16[128,64]{1,0:T(8,128)(2,1)S(1)} %get-tuple-element.16), channel_id=1, source_target_pairs={{0,1},{1,0},{2,3},{3,2},{4,5},{5,4},{6,7},{7,6},{8,9},{9,8},{10,11... | collective-permute-start | bytes 49160 | tf_op jit(solution)/shard_map/ppermute | solution.py:99
  161.4 3.9 %collective-permute-done.35 = bf16[128,64]{1,0:T(8,128)(2,1)S(1)} collective-permute-done((bf16[128,64]{1,0:T(8,128)(2,1)S(1)}, bf16[128,64]{1,0:T(8,128)(2,1)S(1)}, u32[]{:S(2)}, u32[]{:S(2)}) %collective-permute-start.35) | collective-permute-done | bytes 16416 | tf_op jit(solution)/shard_map/ppermute | solution.py:99
  (349 shorter events, 53.1 us)
Async XLA Ops:
  1.1 7.3 %collective-permute-start = (bf16[128,64]{1,0:T(8,128)(2,1)S(1)}, bf16[128,64]{1,0:T(8,128)(2,1)S(1)}, u32[]{:S(2)}, u32[]{:S(2)}) collective-permute-start(bf16[128,64]{1,0:T(8,128)(2,1)S(1)} %get-tuple-element.120), channel_id=1, source_target_pairs={{0,1},{1,0},{2,3},{3,2},{4,5},{5,4},{6,7},{7,6},{8,9},{9,8},{10,11... | collective-permute-start | bytes 49160 | tf_op jit(solution)/shard_map/ppermute | solution.py:99
  4.5 4.8 %collective-permute-start.1 = (bf16[128,64]{1,0:T(8,128)(2,1)S(1)}, bf16[128,64]{1,0:T(8,128)(2,1)S(1)}, u32[]{:S(2)}, u32[]{:S(2)}) collective-permute-start(bf16[128,64]{1,0:T(8,128)(2,1)S(1)} %get-tuple-element.121), channel_id=1, source_target_pairs={{0,31},{1,2},{2,1},{3,4},{4,3},{5,6},{6,5},{7,8},{8,7},{9,10},{10,... | collective-permute-start | bytes 49160 | tf_op jit(solution)/shard_map/ppermute | solution.py:99
  9.6 3.9 %collective-permute-start.2 = (bf16[128,512]{1,0:T(8,128)(2,1)S(1)}, bf16[128,512]{1,0:T(8,128)(2,1)S(1)}, u32[]{:S(2)}, u32[]{:S(2)}) collective-permute-start(bf16[128,512]{1,0:T(8,128)(2,1)S(1)} %get-tuple-element.9), channel_id=1, source_target_pairs={{0,32},{32,0},{64,96},{96,64},{128,160},{160,128},{192,224},{224,1... | collective-permute-start | bytes 393224 | tf_op jit(solution)/shard_map/ppermute | solution.py:99
  13.5 6.9 %collective-permute-start.3 = (bf16[128,1024]{1,0:T(8,128)(2,1)S(1)}, bf16[128,1024]{1,0:T(8,128)(2,1)S(1)}, u32[]{:S(2)}, u32[]{:S(2)}) collective-permute-start(bf16[128,1024]{1,0:T(8,128)(2,1)S(1)} %pad_maximum_fusion.1), channel_id=1, source_target_pairs={{0,128},{32,160},{64,192},{96,224},{128,0},{160,32},{192,64},{224,... | collective-permute-start | bytes 786440 | tf_op jit(solution)/shard_map/ppermute | solution.py:99
  16.3 6.9 %collective-permute-start.4 = (bf16[128,1024]{1,0:T(8,128)(2,1)S(1)}, bf16[128,1024]{1,0:T(8,128)(2,1)S(1)}, u32[]{:S(2)}, u32[]{:S(2)}) collective-permute-start(bf16[128,1024]{1,0:T(8,128)(2,1)S(1)} %pad_maximum_fusion.1), channel_id=1, source_target_pairs={{0,192},{32,224},{64,128},{96,160},{128,64},{160,96},{192,0},{224,... | collective-permute-start | bytes 786440 | tf_op jit(solution)/shard_map/ppermute | solution.py:99
  17.1 6.1 %collective-permute-start.5 = (bf16[128,1024]{1,0:T(8,128)(2,1)S(1)}, bf16[128,1024]{1,0:T(8,128)(2,1)S(1)}, u32[]{:S(2)}, u32[]{:S(2)}) collective-permute-start(bf16[128,1024]{1,0:T(8,128)(2,1)S(1)} %pad_maximum_fusion.1), channel_id=1, source_target_pairs={{0,64},{32,96},{64,0},{96,32},{128,192},{160,224},{192,128},{224,1... | collective-permute-start | bytes 786440 | tf_op jit(solution)/shard_map/ppermute | solution.py:99
  25.6 10.8 %collective-permute-start.6 = (bf16[128,64]{1,0:T(8,128)(2,1)S(1)}, bf16[128,64]{1,0:T(8,128)(2,1)S(1)}, u32[]{:S(2)}, u32[]{:S(2)}) collective-permute-start(bf16[128,64]{1,0:T(8,128)(2,1)S(1)} %get-tuple-element.112), channel_id=1, source_target_pairs={{0,1},{1,0},{2,3},{3,2},{4,5},{5,4},{6,7},{7,6},{8,9},{9,8},{10,11... | collective-permute-start | bytes 49160 | tf_op jit(solution)/shard_map/ppermute | solution.py:99
  33.5 4.8 %collective-permute-start.7 = (bf16[128,64]{1,0:T(8,128)(2,1)S(1)}, bf16[128,64]{1,0:T(8,128)(2,1)S(1)}, u32[]{:S(2)}, u32[]{:S(2)}) collective-permute-start(bf16[128,64]{1,0:T(8,128)(2,1)S(1)} %get-tuple-element.113), channel_id=1, source_target_pairs={{0,31},{1,2},{2,1},{3,4},{4,3},{5,6},{6,5},{7,8},{8,7},{9,10},{10,... | collective-permute-start | bytes 49160 | tf_op jit(solution)/shard_map/ppermute | solution.py:99
  40.0 4.6 %collective-permute-start.8 = (bf16[128,64]{1,0:T(8,128)(2,1)S(1)}, bf16[128,64]{1,0:T(8,128)(2,1)S(1)}, u32[]{:S(2)}, u32[]{:S(2)}) collective-permute-start(bf16[128,64]{1,0:T(8,128)(2,1)S(1)} %get-tuple-element.104), channel_id=1, source_target_pairs={{0,1},{1,0},{2,3},{3,2},{4,5},{5,4},{6,7},{7,6},{8,9},{9,8},{10,11... | collective-permute-start | bytes 49160 | tf_op jit(solution)/shard_map/ppermute | solution.py:99
  43.7 4.8 %collective-permute-start.9 = (bf16[128,64]{1,0:T(8,128)(2,1)S(1)}, bf16[128,64]{1,0:T(8,128)(2,1)S(1)}, u32[]{:S(2)}, u32[]{:S(2)}) collective-permute-start(bf16[128,64]{1,0:T(8,128)(2,1)S(1)} %get-tuple-element.105), channel_id=1, source_target_pairs={{0,31},{1,2},{2,1},{3,4},{4,3},{5,6},{6,5},{7,8},{8,7},{9,10},{10,... | collective-permute-start | bytes 49160 | tf_op jit(solution)/shard_map/ppermute | solution.py:99
  52.4 4.8 %collective-permute-start.11 = (bf16[128,64]{1,0:T(8,128)(2,1)S(1)}, bf16[128,64]{1,0:T(8,128)(2,1)S(1)}, u32[]{:S(2)}, u32[]{:S(2)}) collective-permute-start(bf16[128,64]{1,0:T(8,128)(2,1)S(1)} %get-tuple-element.97), channel_id=1, source_target_pairs={{0,31},{1,2},{2,1},{3,4},{4,3},{5,6},{6,5},{7,8},{8,7},{9,10},{10,... | collective-permute-start | bytes 49160 | tf_op jit(solution)/shard_map/ppermute | solution.py:99
  58.8 3.3 %collective-permute-start.12 = (bf16[128,64]{1,0:T(8,128)(2,1)S(1)}, bf16[128,64]{1,0:T(8,128)(2,1)S(1)}, u32[]{:S(2)}, u32[]{:S(2)}) collective-permute-start(bf16[128,64]{1,0:T(8,128)(2,1)S(1)} %get-tuple-element.88), channel_id=1, source_target_pairs={{0,1},{1,0},{2,3},{3,2},{4,5},{5,4},{6,7},{7,6},{8,9},{9,8},{10,11... | collective-permute-start | bytes 49160 | tf_op jit(solution)/shard_map/ppermute | solution.py:99
  61.1 4.8 %collective-permute-start.13 = (bf16[128,64]{1,0:T(8,128)(2,1)S(1)}, bf16[128,64]{1,0:T(8,128)(2,1)S(1)}, u32[]{:S(2)}, u32[]{:S(2)}) collective-permute-start(bf16[128,64]{1,0:T(8,128)(2,1)S(1)} %get-tuple-element.89), channel_id=1, source_target_pairs={{0,31},{1,2},{2,1},{3,4},{4,3},{5,6},{6,5},{7,8},{8,7},{9,10},{10,... | collective-permute-start | bytes 49160 | tf_op jit(solution)/shard_map/ppermute | solution.py:99
  67.6 3.4 %collective-permute-start.14 = (bf16[128,64]{1,0:T(8,128)(2,1)S(1)}, bf16[128,64]{1,0:T(8,128)(2,1)S(1)}, u32[]{:S(2)}, u32[]{:S(2)}) collective-permute-start(bf16[128,64]{1,0:T(8,128)(2,1)S(1)} %get-tuple-element.80), channel_id=1, source_target_pairs={{0,1},{1,0},{2,3},{3,2},{4,5},{5,4},{6,7},{7,6},{8,9},{9,8},{10,11... | collective-permute-start | bytes 49160 | tf_op jit(solution)/shard_map/ppermute | solution.py:99
  70.1 4.8 %collective-permute-start.15 = (bf16[128,64]{1,0:T(8,128)(2,1)S(1)}, bf16[128,64]{1,0:T(8,128)(2,1)S(1)}, u32[]{:S(2)}, u32[]{:S(2)}) collective-permute-start(bf16[128,64]{1,0:T(8,128)(2,1)S(1)} %get-tuple-element.81), channel_id=1, source_target_pairs={{0,31},{1,2},{2,1},{3,4},{4,3},{5,6},{6,5},{7,8},{8,7},{9,10},{10,... | collective-permute-start | bytes 49160 | tf_op jit(solution)/shard_map/ppermute | solution.py:99
  78.8 4.8 %collective-permute-start.17 = (bf16[128,64]{1,0:T(8,128)(2,1)S(1)}, bf16[128,64]{1,0:T(8,128)(2,1)S(1)}, u32[]{:S(2)}, u32[]{:S(2)}) collective-permute-start(bf16[128,64]{1,0:T(8,128)(2,1)S(1)} %get-tuple-element.73), channel_id=1, source_target_pairs={{0,31},{1,2},{2,1},{3,4},{4,3},{5,6},{6,5},{7,8},{8,7},{9,10},{10,... | collective-permute-start | bytes 49160 | tf_op jit(solution)/shard_map/ppermute | solution.py:99
  87.6 4.8 %collective-permute-start.19 = (bf16[128,64]{1,0:T(8,128)(2,1)S(1)}, bf16[128,64]{1,0:T(8,128)(2,1)S(1)}, u32[]{:S(2)}, u32[]{:S(2)}) collective-permute-start(bf16[128,64]{1,0:T(8,128)(2,1)S(1)} %get-tuple-element.65), channel_id=1, source_target_pairs={{0,31},{1,2},{2,1},{3,4},{4,3},{5,6},{6,5},{7,8},{8,7},{9,10},{10,... | collective-permute-start | bytes 49160 | tf_op jit(solution)/shard_map/ppermute | solution.py:99
  92.7 3.9 %collective-permute-start.20 = (bf16[128,512]{1,0:T(8,128)(2,1)S(1)}, bf16[128,512]{1,0:T(8,128)(2,1)S(1)}, u32[]{:S(2)}, u32[]{:S(2)}) collective-permute-start(bf16[128,512]{1,0:T(8,128)(2,1)S(1)} %get-tuple-element.7), channel_id=1, source_target_pairs={{0,32},{32,0},{64,96},{96,64},{128,160},{160,128},{192,224},{224,1... | collective-permute-start | bytes 393224 | tf_op jit(solution)/shard_map/ppermute | solution.py:99
  96.6 6.9 %collective-permute-start.21 = (bf16[128,1024]{1,0:T(8,128)(2,1)S(1)}, bf16[128,1024]{1,0:T(8,128)(2,1)S(1)}, u32[]{:S(2)}, u32[]{:S(2)}) collective-permute-start(bf16[128,1024]{1,0:T(8,128)(2,1)S(1)} %pad_maximum_fusion.2), channel_id=1, source_target_pairs={{0,128},{32,160},{64,192},{96,224},{128,0},{160,32},{192,64},{224,... | collective-permute-start | bytes 786440 | tf_op jit(solution)/shard_map/ppermute | solution.py:99
  99.1 10.5 %collective-permute-start.22 = (bf16[128,1024]{1,0:T(8,128)(2,1)S(1)}, bf16[128,1024]{1,0:T(8,128)(2,1)S(1)}, u32[]{:S(2)}, u32[]{:S(2)}) collective-permute-start(bf16[128,1024]{1,0:T(8,128)(2,1)S(1)} %pad_maximum_fusion.2), channel_id=1, source_target_pairs={{0,192},{32,224},{64,128},{96,160},{128,64},{160,96},{192,0},{224,... | collective-permute-start | bytes 786440 | tf_op jit(solution)/shard_map/ppermute | solution.py:99
  100.4 9.3 %collective-permute-start.23 = (bf16[128,1024]{1,0:T(8,128)(2,1)S(1)}, bf16[128,1024]{1,0:T(8,128)(2,1)S(1)}, u32[]{:S(2)}, u32[]{:S(2)}) collective-permute-start(bf16[128,1024]{1,0:T(8,128)(2,1)S(1)} %pad_maximum_fusion.2), channel_id=1, source_target_pairs={{0,64},{32,96},{64,0},{96,32},{128,192},{160,224},{192,128},{224,1... | collective-permute-start | bytes 786440 | tf_op jit(solution)/shard_map/ppermute | solution.py:99
  111.4 4.3 %collective-permute-start.24 = (bf16[128,64]{1,0:T(8,128)(2,1)S(1)}, bf16[128,64]{1,0:T(8,128)(2,1)S(1)}, u32[]{:S(2)}, u32[]{:S(2)}) collective-permute-start(bf16[128,64]{1,0:T(8,128)(2,1)S(1)} %get-tuple-element.56), channel_id=1, source_target_pairs={{0,1},{1,0},{2,3},{3,2},{4,5},{5,4},{6,7},{7,6},{8,9},{9,8},{10,11... | collective-permute-start | bytes 49160 | tf_op jit(solution)/shard_map/ppermute | solution.py:99
  114.8 4.8 %collective-permute-start.25 = (bf16[128,64]{1,0:T(8,128)(2,1)S(1)}, bf16[128,64]{1,0:T(8,128)(2,1)S(1)}, u32[]{:S(2)}, u32[]{:S(2)}) collective-permute-start(bf16[128,64]{1,0:T(8,128)(2,1)S(1)} %get-tuple-element.57), channel_id=1, source_target_pairs={{0,31},{1,2},{2,1},{3,4},{4,3},{5,6},{6,5},{7,8},{8,7},{9,10},{10,... | collective-permute-start | bytes 49160 | tf_op jit(solution)/shard_map/ppermute | solution.py:99
  121.3 5.0 %collective-permute-start.26 = (bf16[128,64]{1,0:T(8,128)(2,1)S(1)}, bf16[128,64]{1,0:T(8,128)(2,1)S(1)}, u32[]{:S(2)}, u32[]{:S(2)}) collective-permute-start(bf16[128,64]{1,0:T(8,128)(2,1)S(1)} %get-tuple-element.48), channel_id=1, source_target_pairs={{0,1},{1,0},{2,3},{3,2},{4,5},{5,4},{6,7},{7,6},{8,9},{9,8},{10,11... | collective-permute-start | bytes 49160 | tf_op jit(solution)/shard_map/ppermute | solution.py:99
  125.3 4.8 %collective-permute-start.27 = (bf16[128,64]{1,0:T(8,128)(2,1)S(1)}, bf16[128,64]{1,0:T(8,128)(2,1)S(1)}, u32[]{:S(2)}, u32[]{:S(2)}) collective-permute-start(bf16[128,64]{1,0:T(8,128)(2,1)S(1)} %get-tuple-element.49), channel_id=1, source_target_pairs={{0,31},{1,2},{2,1},{3,4},{4,3},{5,6},{6,5},{7,8},{8,7},{9,10},{10,... | collective-permute-start | bytes 49160 | tf_op jit(solution)/shard_map/ppermute | solution.py:99
  131.7 3.5 %collective-permute-start.28 = (bf16[128,64]{1,0:T(8,128)(2,1)S(1)}, bf16[128,64]{1,0:T(8,128)(2,1)S(1)}, u32[]{:S(2)}, u32[]{:S(2)}) collective-permute-start(bf16[128,64]{1,0:T(8,128)(2,1)S(1)} %get-tuple-element.40), channel_id=1, source_target_pairs={{0,1},{1,0},{2,3},{3,2},{4,5},{5,4},{6,7},{7,6},{8,9},{9,8},{10,11... | collective-permute-start | bytes 49160 | tf_op jit(solution)/shard_map/ppermute | solution.py:99
  134.2 4.8 %collective-permute-start.29 = (bf16[128,64]{1,0:T(8,128)(2,1)S(1)}, bf16[128,64]{1,0:T(8,128)(2,1)S(1)}, u32[]{:S(2)}, u32[]{:S(2)}) collective-permute-start(bf16[128,64]{1,0:T(8,128)(2,1)S(1)} %get-tuple-element.41), channel_id=1, source_target_pairs={{0,31},{1,2},{2,1},{3,4},{4,3},{5,6},{6,5},{7,8},{8,7},{9,10},{10,... | collective-permute-start | bytes 49160 | tf_op jit(solution)/shard_map/ppermute | solution.py:99
  140.7 3.3 %collective-permute-start.30 = (bf16[128,64]{1,0:T(8,128)(2,1)S(1)}, bf16[128,64]{1,0:T(8,128)(2,1)S(1)}, u32[]{:S(2)}, u32[]{:S(2)}) collective-permute-start(bf16[128,64]{1,0:T(8,128)(2,1)S(1)} %get-tuple-element.32), channel_id=1, source_target_pairs={{0,1},{1,0},{2,3},{3,2},{4,5},{5,4},{6,7},{7,6},{8,9},{9,8},{10,11... | collective-permute-start | bytes 49160 | tf_op jit(solution)/shard_map/ppermute | solution.py:99
  143.0 4.8 %collective-permute-start.31 = (bf16[128,64]{1,0:T(8,128)(2,1)S(1)}, bf16[128,64]{1,0:T(8,128)(2,1)S(1)}, u32[]{:S(2)}, u32[]{:S(2)}) collective-permute-start(bf16[128,64]{1,0:T(8,128)(2,1)S(1)} %get-tuple-element.33), channel_id=1, source_target_pairs={{0,31},{1,2},{2,1},{3,4},{4,3},{5,6},{6,5},{7,8},{8,7},{9,10},{10,... | collective-permute-start | bytes 49160 | tf_op jit(solution)/shard_map/ppermute | solution.py:99
  149.4 3.3 %collective-permute-start.32 = (bf16[128,64]{1,0:T(8,128)(2,1)S(1)}, bf16[128,64]{1,0:T(8,128)(2,1)S(1)}, u32[]{:S(2)}, u32[]{:S(2)}) collective-permute-start(bf16[128,64]{1,0:T(8,128)(2,1)S(1)} %get-tuple-element.24), channel_id=1, source_target_pairs={{0,1},{1,0},{2,3},{3,2},{4,5},{5,4},{6,7},{7,6},{8,9},{9,8},{10,11... | collective-permute-start | bytes 49160 | tf_op jit(solution)/shard_map/ppermute | solution.py:99
  151.7 4.8 %collective-permute-start.33 = (bf16[128,64]{1,0:T(8,128)(2,1)S(1)}, bf16[128,64]{1,0:T(8,128)(2,1)S(1)}, u32[]{:S(2)}, u32[]{:S(2)}) collective-permute-start(bf16[128,64]{1,0:T(8,128)(2,1)S(1)} %get-tuple-element.25), channel_id=1, source_target_pairs={{0,31},{1,2},{2,1},{3,4},{4,3},{5,6},{6,5},{7,8},{8,7},{9,10},{10,... | collective-permute-start | bytes 49160 | tf_op jit(solution)/shard_map/ppermute | solution.py:99
  160.5 4.8 %collective-permute-start.35 = (bf16[128,64]{1,0:T(8,128)(2,1)S(1)}, bf16[128,64]{1,0:T(8,128)(2,1)S(1)}, u32[]{:S(2)}, u32[]{:S(2)}) collective-permute-start(bf16[128,64]{1,0:T(8,128)(2,1)S(1)} %get-tuple-element.17), channel_id=1, source_target_pairs={{0,31},{1,2},{2,1},{3,4},{4,3},{5,6},{6,5},{7,8},{8,7},{9,10},{10,... | collective-permute-start | bytes 49160 | tf_op jit(solution)/shard_map/ppermute | solution.py:99
  (12 other events, 38.8 us)
